TPU v7x, 512 devices: a whole 4x4x16 slice. The times are simulated.
512 devices in a mesh: aux: 16 (over x, y_lo, core), row: 32 (over y_hi, z).
Axes of the slice: x: 4, y: 4 (y_hi: 2, y_lo: 2; y = y_hi * 2 + y_lo), z: 16, core: 2. Of those that a mesh axis runs over, the one named last changes fastest.
Arguments:
- chol_vectors: bfloat16 [16, 6144, 6144], P('aux', 'row'), may hold values from -0.078125 to 0.078125
- occ_coeff: bfloat16 [6144, 512], P('row'), may hold values from -4 to 4
- tile_pairs: int32 [528, 2], replicated, may hold values from 0 to 31, as said below
- tile_owner: int32 [32, 17], P('row'), may hold values from 0 to 527, as said below
Outputs:
- ktiles: float32 [544, 192, 192], P('row', 'aux')
Inputs may be any that keep to these rules, and one draw needn't show every extreme that they name: `tile_pairs`: each entry is a pair (i, j) with i <= j, and every such pair of 32 blocks appears exactly once. `tile_owner`: every tile index appears at least once, a few twice.
All inputs are finite; a program needn't handle non-finite values.
Results may differ from a plain program's by a relative error of at most 0.0022.
Values may be sent and summed in bfloat16 or wider, within the bound.
No kernel may reach another device: no remote copies, remote signals or barrier semaphores. Data moves between devices by JAX's collectives and lax.ppermute only.
A program may use at most 64 MiB of HBM per device.

v0:
```python
import jax
import jax.numpy as jnp
from jax import lax
from jax.sharding import PartitionSpec as P


def local(chol_vectors, occ_coeff, tile_pairs, tile_owner):
    block = chol_vectors.shape[1]
    coeff_full = lax.all_gather(occ_coeff, "row", axis=0, tiled=True)
    half = jnp.einsum(
        "qbn,no->qbo", chol_vectors, coeff_full, preferred_element_type=jnp.float32
    ).astype(jnp.bfloat16)
    gathered = lax.all_gather(half, "row", axis=1, tiled=True)
    chosen = tile_pairs[tile_owner[0]]

    def take_rows(blockid):
        return lax.dynamic_slice_in_dim(gathered, blockid * block, block, 1)

    left_rows = jax.vmap(take_rows)(chosen[:, 0])
    right_rows = jax.vmap(take_rows)(chosen[:, 1])
    partial_tiles = jnp.einsum(
        "sqao,sqbo->sab", left_rows, right_rows, preferred_element_type=jnp.float32
    )
    result = lax.psum_scatter(partial_tiles, "aux", scatter_dimension=1, tiled=True)
    return result


def solution(mesh):
    placed = (P("aux", "row", None), P("row", None), P(), P("row", None))
    return jax.shard_map(
        local, mesh=mesh, in_specs=placed, out_specs=P("row", "aux", None), check_vma=False
    )
```

profile of v0, /device:TPU:1, one launch (start us, length us, event | category | flops | bytes accessed | tf_op | source)
XLA Modules:
  0.0 625.8 jit_solution(15321455764275538283)
XLA Ops:
  7.3 177.8 %all-gather.4.cloned.1.call-done = bf16[6144,512]{1,0:T(8,128)(2,1)} async-done(((bf16[192,512]{1,0:T(8,128)(2,1)}), bf16[6144,512]{1,0:T(8,128)(2,1)}) %all-gather.4.cloned.1.call-update) | async-done | bytes 6291472 | tf_op jit(solution)/shard_map/all_gather | solution.py:9
  185.2 4.8 fusion.5
  191.3 171.2 %all-gather.6.cloned.1.call-done = bf16[6144,512]{1,0:T(8,128)(2,1)} async-done(((bf16[192,512]{1,0:T(8,128)(2,1)}), bf16[6144,512]{1,0:T(8,128)(2,1)}) %all-gather.6.cloned.1.call-update) | async-done | bytes 6291472 | tf_op jit(solution)/shard_map/all_gather | solution.py:13
  364.7 49.4 %while.2 = (s32[]{:T(128)}, bf16[1,6144,512]{2,1,0:T(8,128)(2,1)}, s32[17,3]{0,1:T(4,128)S(1)}, bf16[17,1,192,512]{3,2,1,0:T(8,128)(2,1)}, s32[]{:T(128)}) while((s32[]{:T(128)}, bf16[1,6144,512]{2,1,0:T(8,128)(2,1)}, s32[17,3]{0,1:T(4,128)S(1)}, bf16[17,1,192,512]{3,2,1,0:T(8,128)(2,1)}, s32[]{:T(128)}) %tuple.45), condition=%wide.while_cond, body=%wide.while_body.sunk | while | flops 2 | bytes 394337 | solution.py:17
  368.1 2.3 bitcast_dynamic-update-slice_fusion.4
  371.0 2.3 bitcast_dynamic-update-slice_fusion.4
  376.8 2.3 bitcast_dynamic-update-slice_fusion.4
  391.3 2.3 bitcast_dynamic-update-slice_fusion.4
  397.1 2.3 bitcast_dynamic-update-slice_fusion.4
  400.1 2.3 bitcast_dynamic-update-slice_fusion.4
  403.0 2.3 bitcast_dynamic-update-slice_fusion.4
  405.9 2.3 bitcast_dynamic-update-slice_fusion.4
  416.1 49.4 %while.3 = (s32[]{:T(128)}, bf16[1,6144,512]{2,1,0:T(8,128)(2,1)}, s32[17,3]{0,1:T(4,128)S(1)}, bf16[17,1,192,512]{3,2,1,0:T(8,128)(2,1)}, s32[]{:T(128)}) while((s32[]{:T(128)}, bf16[1,6144,512]{2,1,0:T(8,128)(2,1)}, s32[17,3]{0,1:T(4,128)S(1)}, bf16[17,1,192,512]{3,2,1,0:T(8,128)(2,1)}, s32[]{:T(128)}) %tuple.46), condition=%wide.while_cond.1, body=%wide.while_body.1.sunk | while | flops 2 | bytes 394337 | solution.py:17
  416.7 2.3 bitcast_dynamic-update-slice_fusion.5
  425.4 2.3 bitcast_dynamic-update-slice_fusion.5
  428.3 2.3 bitcast_dynamic-update-slice_fusion.5
  431.2 2.3 bitcast_dynamic-update-slice_fusion.5
  437.0 2.3 bitcast_dynamic-update-slice_fusion.5
  451.5 2.3 bitcast_dynamic-update-slice_fusion.5
  454.4 2.3 bitcast_dynamic-update-slice_fusion.5
  457.3 2.3 bitcast_dynamic-update-slice_fusion.5
  463.1 2.3 bitcast_dynamic-update-slice_fusion.5
  465.5 5.7 fusion
  473.1 144.4 %all-reduce.3.cloned.1.call-done = f32[17,192,192]{2,1,0:T(8,128)} async-done(((f32[17,192,192]{2,1,0:T(8,128)}), f32[17,192,192]{2,1,0:T(8,128)}) %all-reduce.3.cloned.1.call-update) | async-done | bytes 2506768
  (111 shorter events, 68.4 us)
Async XLA Ops:
  6.5 178.6 %copy-start = (bf16[1,192,6144]{2,1,0:T(8,128)(2,1)S(1)}, bf16[1,192,6144]{2,1,0:T(8,128)(2,1)}, u32[]{:S(2)}) copy-start(bf16[1,192,6144]{2,1,0:T(8,128)(2,1)} %param.4) | copy-start | bytes 7077892
  6.5 178.6 %all-gather.4.cloned.1.call-start = ((), (), s32[]{:S(2)}) async-start(), calls=%async_computation | async-start | bytes 6488064 | tf_op jit(solution)/shard_map/all_gather | solution.py:9
  7.3 182.8 %copy-start.1 = (s32[528,2]{0,1:T(2,128)S(1)}, s32[528,2]{0,1:T(2,128)}, u32[]{:S(2)}) copy-start(s32[528,2]{0,1:T(2,128)} %param.6) | copy-start | bytes 12676
  7.3 183.0 %copy-start.2 = (s32[1,17]{1,0:T(1,128)S(1)}, s32[1,17]{1,0:T(1,128)}, u32[]{:S(2)}) copy-start(s32[1,17]{1,0:T(1,128)} %param.7) | copy-start | bytes 208
  7.3 355.3 %all-gather.6.cloned.1.call-start = ((), (), s32[]{:S(2)}) async-start(), calls=%async_computation.1 | async-start | bytes 6488064 | tf_op jit(solution)/shard_map/all_gather | solution.py:13
  190.0 427.5 %all-reduce.3.cloned.1.call-start = ((), (), s32[]{:S(2)}) async-start(), calls=%async_computation.2 | async-start | bytes 6684672
Sparse Core Ops, SparseCore 0:
  10.4 174.6 all-gather.3
  190.2 172.3 all-gather.5
  471.3 146.1 all-reduce.2
where the time goes:
time: 627 us; the launch traced here: 626 us
  waiting for transfers between devices  494 us (79%)
  local copies, waits for them, and re-layouts  107 us (17%)
  between operations  13.8 us (2%)
  matrix products  10.6 us (2%)
    all_gather x1, waiting for transfers between devices, local(): coeff_full = lax.all_gather(occ_coeff, 'row', axis=0, tiled=True)  178 us
    all_gather x1, waiting for transfers between devices, local(): gathered = lax.all_gather(half, 'row', axis=1, tiled=True)  171 us
    unnamed x4, waiting for transfers between devices  145 us
    gather x102, local copies, waits for them, and re-layouts  98.7 us
  transfers between devices with their start and end apart: 3, of which 3 were waited for; matrix products, arithmetic and copies ran while one was open for 0% of the time, Pallas kernels for 0%

commit v1 on v0

v1 whole, which is shorter than its diff:
```python
import jax
import jax.numpy as jnp
from jax import lax
from jax.sharding import PartitionSpec as P


def local(chol_vectors, occ_coeff, tile_pairs, tile_owner):
    block = chol_vectors.shape[1]
    nocc = occ_coeff.shape[1]
    nblk = lax.axis_size("row")
    naux = lax.axis_size("aux")
    half_cols = nocc // 2

    core = lax.axis_index("aux") % 2
    mine = lax.dynamic_slice_in_dim(occ_coeff, core * half_cols, half_cols, 1)
    mine_full = lax.all_gather(mine, "row", axis=0, tiled=True)
    partner = [(i, i ^ 1) for i in range(naux)]
    other_full = lax.ppermute(mine_full, "aux", partner)

    chol = chol_vectors[0]
    half_mine = jnp.dot(chol, mine_full, preferred_element_type=jnp.float32).astype(jnp.bfloat16)
    half_other = jnp.dot(chol, other_full, preferred_element_type=jnp.float32).astype(jnp.bfloat16)
    half = jnp.where(
        core == 0,
        jnp.concatenate([half_mine, half_other], axis=1),
        jnp.concatenate([half_other, half_mine], axis=1),
    )

    gathered = lax.all_gather(half, "row", axis=0, tiled=True)
    blocks = gathered.reshape(nblk, block, nocc)
    chosen = tile_pairs[tile_owner[0]]
    left_rows = jnp.take(blocks, chosen[:, 0], axis=0)
    right_rows = jnp.take(blocks, chosen[:, 1], axis=0)
    partial_tiles = jnp.einsum(
        "sao,sbo->sab", left_rows, right_rows, preferred_element_type=jnp.float32
    )
    slots = partial_tiles.shape[0]
    split = partial_tiles.reshape(slots, naux, block // naux, block).transpose(1, 0, 2, 3)
    pieces = lax.all_to_all(split, "aux", 0, 0, tiled=True)
    return jnp.sum(pieces, axis=0)


def solution(mesh):
    placed = (P("aux", "row", None), P("row", None), P(), P("row", None))
    return jax.shard_map(
        local, mesh=mesh, in_specs=placed, out_specs=P("row", "aux", None), check_vma=False
    )
```

time: 627 us -> 448 us (0.71)
  waiting for transfers between devices: 494 us -> 320 us
  local copies, waits for them, and re-layouts: 107 us -> 21 us
  blocking collectives: 0 us -> 65 us
  starting transfers between devices: 0.08 us -> 12.5 us
    unnamed x4 -> x2, waiting for transfers between devices: 145 us -> 0.03 us
    gather x102 -> x2, local copies, waits for them, and re-layouts: 98.7 us -> 11.1 us  [the longest x1 5.55 us: local(): left_rows = jnp.take(blocks, chosen[:, 0], axis=0)]
    all_to_all x0 -> x1, blocking collectives: none -> 65 us  [local(): pieces = lax.all_to_all(split, 'aux', 0, 0, tiled=True)]
    all_gather x2, waiting for transfers between devices: 349 us -> 317 us  [the longest x1 162 us: local(): gathered = lax.all_gather(half, 'row', axis=0, tiled=True)]
    ppermute x0 -> x1, starting transfers between devices: none -> 12.5 us  [local(): other_full = lax.ppermute(mine_full, 'aux', partner)]
    unnamed x11 -> x7, local copies, waits for them, and re-layouts: 7.38 us -> 0.16 us
  transfers between devices with their start and end apart: 3 -> 3, of which waited for: 3 -> 3; matrix products, arithmetic and copies ran while one was open for 0% -> 1% of each run, Pallas kernels for 0% -> 0%
where the time goes in v1:
time: 448 us
  waiting for transfers between devices  320 us (71%)
  blocking collectives  65 us (15%)
  local copies, waits for them, and re-layouts  21 us (5%)
  between operations  13.5 us (3%)
  starting transfers between devices  12.5 us (3%)
  matrix products  11.3 us (3%)
    all_gather x1, waiting for transfers between devices, local(): gathered = lax.all_gather(half, 'row', axis=0, tiled=True)  162 us
    all_gather x1, waiting for transfers between devices, local(): mine_full = lax.all_gather(mine, 'row', axis=0, tiled=True)  154 us
    all_to_all x1, blocking collectives, local(): pieces = lax.all_to_all(split, 'aux', 0, 0, tiled=True)  65 us
    ppermute x1, starting transfers between devices, local(): other_full = lax.ppermute(mine_full, 'aux', partner)  12.5 us
  transfers between devices with their start and end apart: 3, of which 3 were waited for; matrix products, arithmetic and copies ran while one was open for 1% of the time, Pallas kernels for 0%

profile of v1, /device:TPU:1, one launch (start us, length us, event | category | flops | bytes accessed | tf_op | source)
XLA Modules:
  0.0 447.5 jit_solution(477083212773906559)
XLA Ops:
  6.5 1.7 constant_dynamic-slice_fusion
  8.2 0.0 all-gather.3.cloned.1.call-update
  8.3 0.0 all-gather.5.cloned.1.call-start
  8.3 154.5 %all-gather.3.cloned.1.call-done = bf16[6144,256]{1,0:T(8,128)(2,1)} async-done(((bf16[192,256]{1,0:T(8,128)(2,1)}), bf16[6144,256]{1,0:T(8,128)(2,1)}) %all-gather.3.cloned.1.call-update) | async-done | bytes 3145744 | tf_op jit(solution)/shard_map/all_gather | solution.py:16
  162.8 12.5 %collective-permute-start = (bf16[6144,256]{1,0:T(8,128)(2,1)}, bf16[6144,256]{1,0:T(8,128)(2,1)}, u32[]{:S(2)}, u32[]{:S(2)}) collective-permute-start(bf16[6144,256]{1,0:T(8,128)(2,1)} %all-gather.3.cloned.1.call-done), channel_id=1, source_target_pairs={{0,32},{32,0},{64,96},{96,64},{128,160},{160,128},{192,224},{224,1... | collective-permute-start | bytes 9437192 | tf_op jit(solution)/shard_map/ppermute | solution.py:18
  175.3 0.0 copy-done
  175.3 2.7 fusion.16
  178.0 0.0 copy-start.1
  178.0 0.0 copy-start.2
  178.0 2.9 collective-permute-done
  180.9 2.7 fusion.19
  183.6 0.8 maximum_select_fusion
  184.3 0.0 all-gather.5.cloned.1.call-update
  184.3 0.1 copy.7
  184.5 0.6 gather_fusion
  185.1 0.2 slice_reduce_fusion.1
  185.3 162.4 %all-gather.5.cloned.1.call-done = bf16[6144,512]{1,0:T(8,128)(2,1)} async-done(((bf16[192,512]{1,0:T(8,128)(2,1)}), bf16[6144,512]{1,0:T(8,128)(2,1)}) %all-gather.5.cloned.1.call-update) | async-done | bytes 6291472 | tf_op jit(solution)/shard_map/all_gather | solution.py:29
  347.7 5.5 %gather_fusion.2 = bf16[17,192,512]{2,1,0:T(8,128)(2,1)} fusion(bf16[32,192,512]{2,1,0:T(8,128)(2,1)} %bitcast.26, s32[1024]{0:T(1024)S(1)} %pad_clamp_fusion), kind=kCustom, calls=%fused_computation.1.clone | custom fusion | bytes 6684740 | tf_op jit(solution)/shard_map/jit(_take)/gather | solution.py:33
  353.3 5.6 %gather_fusion.1 = bf16[17,192,512]{2,1,0:T(8,128)(2,1)} fusion(bf16[32,192,512]{2,1,0:T(8,128)(2,1)} %bitcast.27, s32[1024]{0:T(1024)S(1)} %pad_clamp_fusion.1), kind=kCustom, calls=%fused_computation.clone | custom fusion | bytes 6684740 | tf_op jit(solution)/shard_map/jit(_take)/gather | solution.py:32
  358.8 6.0 %fusion = f32[17,192,192]{2,1,0:T(8,128)} fusion(bf16[17,192,512]{2,1,0:T(8,128)(2,1)} %gather_fusion.2, bf16[17,192,512]{2,1,0:T(8,128)(2,1)} %gather_fusion.1, pred[17]{0:T(512)(128)(4,1)S(1)} %get-tuple-element.10, pred[17]{0:T(512)(128)(4,1)S(1)} %get-tuple-element.11), kind=kOutput, calls=%fused_computation.3 | convolution fusion | flops 645070848 | bytes 9191458 | tf_op jit(solution)/shard_map/sao,sbo->sab/dot_general | solution.py:34
  364.8 4.6 %reshape.40 = f32[17,16,12,192]{3,2,1,0:T(8,128)} reshape(f32[17,192,192]{2,1,0:T(8,128)} %fusion) | data formatting | bytes 5013504 | tf_op jit(solution)/shard_map/reshape | solution.py:38
  369.4 2.8 copy.8
  372.1 65.0 %all_to_all.5 = f32[16,17,12,192]{3,2,1,0:T(8,128)} all-to-all(f32[16,17,12,192]{3,2,1,0:T(8,128)S(1)} %copy.8), channel_id=1, replica_groups=mesh['aux'=16,'row'=32] {'aux'}, dimensions={0} | all-to-all | bytes 5013504 | tf_op jit(solution)/shard_map/all_to_all | solution.py:39
  437.1 3.5 reduce_sum.9
  (10 shorter events, 0.0 us)
Async XLA Ops:
  6.5 168.7 %copy-start = (bf16[1,192,6144]{2,1,0:T(8,128)(2,1)S(1)}, bf16[1,192,6144]{2,1,0:T(8,128)(2,1)}, u32[]{:S(2)}) copy-start(bf16[1,192,6144]{2,1,0:T(8,128)(2,1)} %param.6) | copy-start | bytes 7077892
  6.5 156.2 %all-gather.3.cloned.1.call-start = ((), (), s32[]{:S(2)}) async-start(), calls=%async_computation.1 | async-start | bytes 3244032 | tf_op jit(solution)/shard_map/all_gather | solution.py:16
  8.3 339.5 %all-gather.5.cloned.1.call-start = ((), (), s32[]{:S(2)}) async-start(), calls=%async_computation.2 | async-start | bytes 6488064 | tf_op jit(solution)/shard_map/all_gather | solution.py:29
  162.8 18.1 %collective-permute-start = (bf16[6144,256]{1,0:T(8,128)(2,1)}, bf16[6144,256]{1,0:T(8,128)(2,1)}, u32[]{:S(2)}, u32[]{:S(2)}) collective-permute-start(bf16[6144,256]{1,0:T(8,128)(2,1)} %all-gather.3.cloned.1.call-done), channel_id=1, source_target_pairs={{0,32},{32,0},{64,96},{96,64},{128,160},{160,128},{192,224},{224,1... | collective-permute-start | bytes 9437192 | tf_op jit(solution)/shard_map/ppermute | solution.py:18
  178.0 6.4 %copy-start.1 = (s32[528,2]{0,1:T(2,128)S(1)}, s32[528,2]{0,1:T(2,128)}, u32[]{:S(2)}) copy-start(s32[528,2]{0,1:T(2,128)} %param.8) | copy-start | bytes 12676
  178.0 6.5 %copy-start.2 = (s32[1,17]{1,0:T(1,128)S(1)}, s32[1,17]{1,0:T(1,128)}, u32[]{:S(2)}) copy-start(s32[1,17]{1,0:T(1,128)} %param.9) | copy-start | bytes 208
Sparse Core Ops, SparseCore 0:
  10.4 152.3 all-gather.2
  184.5 163.2 all-gather.4

commit v2 on v1

v2 whole, which is shorter than its diff:
```python
import jax
import jax.numpy as jnp
from jax import lax
from jax.sharding import PartitionSpec as P


def ring_gather(x, nrow, ring):
    pairs = nrow // ring
    r = lax.axis_index("row")
    yh = r // ring
    z = r % ring
    other = lax.ppermute(x, "row", [(i, i ^ ring) for i in range(nrow)])
    pair = jnp.where(yh == 0, jnp.stack([x, other]), jnp.stack([other, x]))
    send_right = [(i, (i // ring) * ring + (i % ring + 1) % ring) for i in range(nrow)]
    send_left = [(i, (i // ring) * ring + (i % ring - 1) % ring) for i in range(nrow)]
    got = [None] * ring
    got[0] = pair
    from_left = pair
    from_right = pair
    for t in range(1, ring // 2):
        from_left = lax.ppermute(from_left, "row", send_right)
        from_right = lax.ppermute(from_right, "row", send_left)
        got[t] = from_left
        got[ring - t] = from_right
    low = lax.ppermute(from_left[0], "row", send_right)
    high = lax.ppermute(from_right[1], "row", send_left)
    got[ring // 2] = jnp.stack([low, high])
    stacked = jnp.stack(got)
    return stacked.reshape((ring * pairs,) + x.shape), z


def position_of(k, z, ring):
    return ((z - k % ring) % ring) * 2 + k // ring


def local(chol_vectors, occ_coeff, tile_pairs, tile_owner):
    block = chol_vectors.shape[1]
    nbf = chol_vectors.shape[2]
    nocc = occ_coeff.shape[1]
    nrow = lax.axis_size("row")
    naux = lax.axis_size("aux")
    ring = nrow // 2
    half_cols = nocc // 2

    core = lax.axis_index("aux") % 2
    mine = lax.dynamic_slice_in_dim(occ_coeff, core * half_cols, half_cols, 1)
    mine_ring, z = ring_gather(mine, nrow, ring)
    partner = [(i, i ^ 1) for i in range(naux)]
    other_ring = lax.ppermute(mine_ring, "aux", partner)
    coeff_ring = jnp.where(
        core == 0,
        jnp.concatenate([mine_ring, other_ring], axis=2),
        jnp.concatenate([other_ring, mine_ring], axis=2),
    )

    p = jnp.arange(nrow)
    block_at = (p % 2) * ring + (z - p // 2) % ring
    chol = chol_vectors[0].reshape(block, nrow, nbf // nrow)
    chol_ring = jnp.take(chol, block_at, axis=1).reshape(block, nbf)
    half = jnp.dot(
        chol_ring, coeff_ring.reshape(nbf, nocc), preferred_element_type=jnp.float32
    ).astype(jnp.bfloat16)

    half_ring, _ = ring_gather(half, nrow, ring)
    chosen = tile_pairs[tile_owner[0]]
    left_rows = jnp.take(half_ring, position_of(chosen[:, 0], z, ring), axis=0)
    right_rows = jnp.take(half_ring, position_of(chosen[:, 1], z, ring), axis=0)
    partial_tiles = jnp.einsum(
        "sao,sbo->sab", left_rows, right_rows, preferred_element_type=jnp.float32
    )
    slots = partial_tiles.shape[0]
    split = partial_tiles.reshape(slots, naux, block // naux, block).transpose(1, 0, 2, 3)
    pieces = lax.all_to_all(split, "aux", 0, 0, tiled=True)
    return jnp.sum(pieces, axis=0)


def solution(mesh):
    placed = (P("aux", "row", None), P("row", None), P(), P("row", None))
    return jax.shard_map(
        local, mesh=mesh, in_specs=placed, out_specs=P("row", "aux", None), check_vma=False
    )
```

time: 448 us -> 315 us (0.70)
  waiting for transfers between devices: 320 us -> 42.2 us
  starting transfers between devices: 12.5 us -> 135 us
  local copies, waits for them, and re-layouts: 21 us -> 49.7 us
  between operations: 13.5 us -> 0.62 us
    all_gather x2 -> x0, waiting for transfers between devices: 317 us -> none  [the longest x1 162 us: local(): gathered = lax.all_gather(half, 'row', axis=0, tiled=True)]
    ppermute x1 -> x35, starting transfers between devices: 12.5 us -> 135 us  [the longest x14 70.1 us: ring_gather(): from_right = lax.ppermute(from_right, 'row', send_left)]
    ppermute x1 -> x35, waiting for transfers between devices: 2.89 us -> 42.2 us  [the longest x14 30.4 us: ring_gather(): from_left = lax.ppermute(from_left, 'row', send_right)]
    unnamed x7 -> x35, local copies, waits for them, and re-layouts: 0.16 us -> 20.3 us
    another operation x0 -> x6, local copies, waits for them, and re-layouts: none -> 9.72 us  [the longest x2 8.22 us: local(): chol = chol_vectors[0].reshape(block, nrow, nbf // nrow)]
    gather x2 -> x3, local copies, waits for them, and re-layouts: 11.1 us -> 11.6 us  [the longest x1 5.57 us: local(): right_rows = jnp.take(half_ring, position_of(chosen[:, 1], z, ring), axis=0)]
  transfers between devices with their start and end apart: 3 -> 35, of which waited for: 3 -> 20; matrix products, arithmetic and copies ran while one was open for 1% -> 8% of each run, Pallas kernels for 0% -> 0%
where the time goes in v2:
time: 315 us; the launch traced here: 314 us
  starting transfers between devices  135 us (43%)
  blocking collectives  66.1 us (21%)
  local copies, waits for them, and re-layouts  49.7 us (16%)
  waiting for transfers between devices  42.2 us (13%)
  matrix products  13.4 us (4%)
  other arithmetic  6.72 us (2%)
    ppermute x14, starting transfers between devices, ring_gather(): from_right = lax.ppermute(from_right, 'row', send_left)  70.1 us
    all_to_all x1, blocking collectives, local(): pieces = lax.all_to_all(split, 'aux', 0, 0, tiled=True)  66.1 us
    ppermute x14, waiting for transfers between devices, ring_gather(): from_left = lax.ppermute(from_left, 'row', send_right)  30.4 us
    ppermute x14, starting transfers between devices, ring_gather(): from_left = lax.ppermute(from_left, 'row', send_right)  28.4 us
    unnamed x35, local copies, waits for them, and re-layouts  20.3 us
    ppermute x1, starting transfers between devices, local(): other_ring = lax.ppermute(mine_ring, 'aux', partner)  12.1 us
    ppermute x2, starting transfers between devices, ring_gather(): other = lax.ppermute(x, 'row', [(i, i ^ ring) for i in range(nrow)])  10.5 us
    ppermute x2, starting transfers between devices, ring_gather(): high = lax.ppermute(from_right[1], 'row', send_left)  10.1 us
  transfers between devices with their start and end apart: 35, of which 20 were waited for; matrix products, arithmetic and copies ran while one was open for 8% of the time, Pallas kernels for 0%

profile of v2, /device:TPU:1, one launch (start us, length us, event | category | flops | bytes accessed | tf_op | source)
XLA Modules:
  0.0 313.8 jit_solution(17237789200099726534)
XLA Ops:
  0.9 5.6 %collective-permute-start = (bf16[192,256]{1,0:T(8,128)(2,1)S(1)}, bf16[192,256]{1,0:T(8,128)(2,1)S(1)}, u32[]{:S(2)}, u32[]{:S(2)}) collective-permute-start(bf16[192,256]{1,0:T(8,128)(2,1)S(1)} %constant_dynamic-slice_fusion), channel_id=1, source_target_pairs={{0,16},{1,17},{2,18},{3,19},{4,20},{5,21},{6,22},{7,23},{8,24},{9,... | collective-permute-start | bytes 294920 | tf_op jit(solution)/shard_map/ppermute | solution.py:12
  12.2 9.5 %collective-permute-start.9 = (bf16[2,192,256]{2,1,0:T(8,128)(2,1)S(1)}, bf16[2,192,256]{2,1,0:T(8,128)(2,1)S(1)}, u32[]{:S(2)}, u32[]{:S(2)}) collective-permute-start(bf16[2,192,256]{2,1,0:T(8,128)(2,1)S(1)} %maximum_select_fusion.9), channel_id=1, source_target_pairs={{0,15},{1,0},{2,1},{3,2},{4,3},{5,4},{6,5},{7,6},{8,7},{9,8},{10,9... | collective-permute-start | bytes 589832 | tf_op jit(solution)/shard_map/ppermute | solution.py:22
  25.1 4.6 %collective-permute-start.10 = (bf16[2,192,256]{2,1,0:T(8,128)(2,1)S(1)}, bf16[2,192,256]{2,1,0:T(8,128)(2,1)S(1)}, u32[]{:S(2)}, u32[]{:S(2)}) collective-permute-start(bf16[2,192,256]{2,1,0:T(8,128)(2,1)S(1)} %collective-permute-done.9), channel_id=1, source_target_pairs={{0,15},{1,0},{2,1},{3,2},{4,3},{5,4},{6,5},{7,6},{8,7},{9,8},{10,9... | collective-permute-start | bytes 589832 | tf_op jit(solution)/shard_map/ppermute | solution.py:22
  32.7 4.6 %collective-permute-start.11 = (bf16[2,192,256]{2,1,0:T(8,128)(2,1)S(1)}, bf16[2,192,256]{2,1,0:T(8,128)(2,1)S(1)}, u32[]{:S(2)}, u32[]{:S(2)}) collective-permute-start(bf16[2,192,256]{2,1,0:T(8,128)(2,1)S(1)} %collective-permute-done.10), channel_id=1, source_target_pairs={{0,15},{1,0},{2,1},{3,2},{4,3},{5,4},{6,5},{7,6},{8,7},{9,8},{10,9... | collective-permute-start | bytes 589832 | tf_op jit(solution)/shard_map/ppermute | solution.py:22
  40.4 4.6 %collective-permute-start.12 = (bf16[2,192,256]{2,1,0:T(8,128)(2,1)S(1)}, bf16[2,192,256]{2,1,0:T(8,128)(2,1)S(1)}, u32[]{:S(2)}, u32[]{:S(2)}) collective-permute-start(bf16[2,192,256]{2,1,0:T(8,128)(2,1)S(1)} %collective-permute-done.11), channel_id=1, source_target_pairs={{0,15},{1,0},{2,1},{3,2},{4,3},{5,4},{6,5},{7,6},{8,7},{9,8},{10,9... | collective-permute-start | bytes 589832 | tf_op jit(solution)/shard_map/ppermute | solution.py:22
  64.0 4.9 %collective-permute-start.15 = (bf16[2,192,256]{2,1,0:T(8,128)(2,1)S(1)}, bf16[2,192,256]{2,1,0:T(8,128)(2,1)S(1)}, u32[]{:S(2)}, u32[]{:S(2)}) collective-permute-start(bf16[2,192,256]{2,1,0:T(8,128)(2,1)S(1)} %collective-permute-done.14), channel_id=1, source_target_pairs={{0,15},{1,0},{2,1},{3,2},{4,3},{5,4},{6,5},{7,6},{8,7},{9,8},{10,9... | collective-permute-start | bytes 589832 | tf_op jit(solution)/shard_map/ppermute | solution.py:22
  73.7 5.0 %collective-permute-start.16 = (bf16[192,256]{1,0:T(8,128)(2,1)S(1)}, bf16[192,256]{1,0:T(8,128)(2,1)S(1)}, u32[]{:S(2)}, u32[]{:S(2)}) collective-permute-start(bf16[192,256]{1,0:T(8,128)(2,1)S(1)} %slice_bitcast_fusion.2), channel_id=1, source_target_pairs={{0,15},{1,0},{2,1},{3,2},{4,3},{5,4},{6,5},{7,6},{8,7},{9,8},{10,9... | collective-permute-start | bytes 294920 | tf_op jit(solution)/shard_map/ppermute | solution.py:26
  86.0 12.1 %collective-permute-start.17 = (bf16[32,192,256]{2,1,0:T(8,128)(2,1)}, bf16[32,192,256]{2,1,0:T(8,128)(2,1)}, u32[]{:S(2)}, u32[]{:S(2)}) collective-permute-start(bf16[32,192,256]{2,1,0:T(8,128)(2,1)} %bitcast.27), channel_id=1, source_target_pairs={{0,32},{32,0},{64,96},{96,64},{128,160},{160,128},{192,224},{224,1... | collective-permute-start | bytes 9437192 | tf_op jit(solution)/shard_map/ppermute | solution.py:49
  108.9 8.5 %fusion.20 = bf16[192,512]{1,0:T(8,128)(2,1)S(1)} fusion(bf16[32,192,256]{2,1,0:T(8,128)(2,1)} %collective-permute-done.17, bf16[32,192,256]{2,1,0:T(8,128)(2,1)} %bitcast.27, pred[]{:T(512)S(6)} %eq.19, bf16[32,192,192]{2,1,0:T(8,128)(2,1)} %gather_fusion, pred[32]{0:T(512)(128)(4,1)S(1)} %compare_and_fusion.2), kind=kOutput, calls=%fused_computation.23 | convolution fusion | flops 1237549056 | bytes 8847393 | tf_op jit(solution)/shard_map/dot_general | solution.py:60
  117.4 4.8 %collective-permute-start.18 = (bf16[192,512]{1,0:T(8,128)(2,1)S(1)}, bf16[192,512]{1,0:T(8,128)(2,1)S(1)}, u32[]{:S(2)}, u32[]{:S(2)}) collective-permute-start(bf16[192,512]{1,0:T(8,128)(2,1)S(1)} %fusion.20), channel_id=1, source_target_pairs={{0,16},{1,17},{2,18},{3,19},{4,20},{5,21},{6,22},{7,23},{8,24},{9,... | collective-permute-start | bytes 589832 | tf_op jit(solution)/shard_map/ppermute | solution.py:12
  122.2 5.0 %collective-permute-done.18 = bf16[192,512]{1,0:T(8,128)(2,1)S(1)} collective-permute-done((bf16[192,512]{1,0:T(8,128)(2,1)S(1)}, bf16[192,512]{1,0:T(8,128)(2,1)S(1)}, u32[]{:S(2)}, u32[]{:S(2)}) %collective-permute-start.18) | collective-permute-done | bytes 196640 | tf_op jit(solution)/shard_map/ppermute | solution.py:12
  129.2 5.2 %collective-permute-start.27 = (bf16[2,192,512]{2,1,0:T(8,128)(2,1)S(1)}, bf16[2,192,512]{2,1,0:T(8,128)(2,1)S(1)}, u32[]{:S(2)}, u32[]{:S(2)}) collective-permute-start(bf16[2,192,512]{2,1,0:T(8,128)(2,1)S(1)} %maximum_select_fusion.7), channel_id=1, source_target_pairs={{0,15},{1,0},{2,1},{3,2},{4,3},{5,4},{6,5},{7,6},{8,7},{9,8},{10,9... | collective-permute-start | bytes 1179656 | tf_op jit(solution)/shard_map/ppermute | solution.py:22
  134.5 6.7 %collective-permute-done.19 = bf16[2,192,512]{2,1,0:T(8,128)(2,1)S(1)} collective-permute-done((bf16[2,192,512]{2,1,0:T(8,128)(2,1)S(1)}, bf16[2,192,512]{2,1,0:T(8,128)(2,1)S(1)}, u32[]{:S(2)}, u32[]{:S(2)}) %collective-permute-start.19) | collective-permute-done | bytes 393248 | tf_op jit(solution)/shard_map/ppermute | solution.py:21
  143.1 4.6 %collective-permute-start.28 = (bf16[2,192,512]{2,1,0:T(8,128)(2,1)S(1)}, bf16[2,192,512]{2,1,0:T(8,128)(2,1)S(1)}, u32[]{:S(2)}, u32[]{:S(2)}) collective-permute-start(bf16[2,192,512]{2,1,0:T(8,128)(2,1)S(1)} %collective-permute-done.27), channel_id=1, source_target_pairs={{0,15},{1,0},{2,1},{3,2},{4,3},{5,4},{6,5},{7,6},{8,7},{9,8},{10,9... | collective-permute-start | bytes 1179656 | tf_op jit(solution)/shard_map/ppermute | solution.py:22
  147.8 5.7 %collective-permute-done.20 = bf16[2,192,512]{2,1,0:T(8,128)(2,1)S(1)} collective-permute-done((bf16[2,192,512]{2,1,0:T(8,128)(2,1)S(1)}, bf16[2,192,512]{2,1,0:T(8,128)(2,1)S(1)}, u32[]{:S(2)}, u32[]{:S(2)}) %collective-permute-start.20) | collective-permute-done | bytes 393248 | tf_op jit(solution)/shard_map/ppermute | solution.py:21
  156.0 4.6 %collective-permute-start.29 = (bf16[2,192,512]{2,1,0:T(8,128)(2,1)S(1)}, bf16[2,192,512]{2,1,0:T(8,128)(2,1)S(1)}, u32[]{:S(2)}, u32[]{:S(2)}) collective-permute-start(bf16[2,192,512]{2,1,0:T(8,128)(2,1)S(1)} %collective-permute-done.28), channel_id=1, source_target_pairs={{0,15},{1,0},{2,1},{3,2},{4,3},{5,4},{6,5},{7,6},{8,7},{9,8},{10,9... | collective-permute-start | bytes 1179656 | tf_op jit(solution)/shard_map/ppermute | solution.py:22
  166.9 4.8 %collective-permute-start.30 = (bf16[2,192,512]{2,1,0:T(8,128)(2,1)S(1)}, bf16[2,192,512]{2,1,0:T(8,128)(2,1)S(1)}, u32[]{:S(2)}, u32[]{:S(2)}) collective-permute-start(bf16[2,192,512]{2,1,0:T(8,128)(2,1)S(1)} %collective-permute-done.29), channel_id=1, source_target_pairs={{0,15},{1,0},{2,1},{3,2},{4,3},{5,4},{6,5},{7,6},{8,7},{9,8},{10,9... | collective-permute-start | bytes 1179656 | tf_op jit(solution)/shard_map/ppermute | solution.py:22
  188.0 4.6 %collective-permute-start.32 = (bf16[2,192,512]{2,1,0:T(8,128)(2,1)S(1)}, bf16[2,192,512]{2,1,0:T(8,128)(2,1)S(1)}, u32[]{:S(2)}, u32[]{:S(2)}) collective-permute-start(bf16[2,192,512]{2,1,0:T(8,128)(2,1)S(1)} %collective-permute-done.31), channel_id=1, source_target_pairs={{0,15},{1,0},{2,1},{3,2},{4,3},{5,4},{6,5},{7,6},{8,7},{9,8},{10,9... | collective-permute-start | bytes 1179656 | tf_op jit(solution)/shard_map/ppermute | solution.py:22
  197.7 4.6 %collective-permute-start.33 = (bf16[2,192,512]{2,1,0:T(8,128)(2,1)S(1)}, bf16[2,192,512]{2,1,0:T(8,128)(2,1)S(1)}, u32[]{:S(2)}, u32[]{:S(2)}) collective-permute-start(bf16[2,192,512]{2,1,0:T(8,128)(2,1)S(1)} %collective-permute-done.32), channel_id=1, source_target_pairs={{0,15},{1,0},{2,1},{3,2},{4,3},{5,4},{6,5},{7,6},{8,7},{9,8},{10,9... | collective-permute-start | bytes 1179656 | tf_op jit(solution)/shard_map/ppermute | solution.py:22
  207.4 5.0 %collective-permute-start.34 = (bf16[192,512]{1,0:T(8,128)(2,1)S(1)}, bf16[192,512]{1,0:T(8,128)(2,1)S(1)}, u32[]{:S(2)}, u32[]{:S(2)}) collective-permute-start(bf16[192,512]{1,0:T(8,128)(2,1)S(1)} %slice_bitcast_fusion), channel_id=1, source_target_pairs={{0,15},{1,0},{2,1},{3,2},{4,3},{5,4},{6,5},{7,6},{8,7},{9,8},{10,9... | collective-permute-start | bytes 589832 | tf_op jit(solution)/shard_map/ppermute | solution.py:26
  226.3 5.6 %gather_fusion.3 = bf16[17,192,512]{2,1,0:T(8,128)(2,1)} fusion(bf16[32,192,512]{2,1,0:T(8,128)(2,1)} %bitcast.52, s32[1024]{0:T(1024)S(1)} %pad_clamp_fusion), kind=kCustom, calls=%fused_computation.1.clone | custom fusion | bytes 6684740 | tf_op jit(solution)/shard_map/jit(_take)/gather | solution.py:67
  231.9 4.9 %fusion.7 = f32[17,192,192]{2,1,0:T(8,128)} fusion(bf16[17,192,512]{2,1,0:T(8,128)(2,1)} %gather_fusion.3, bf16[17,192,512]{2,1,0:T(8,128)(2,1)S(1)} %gather_fusion.2, pred[17]{0:T(512)(128)(4,1)S(1)} %get-tuple-element.10, pred[17]{0:T(512)(128)(4,1)S(1)} %get-tuple-element.12), kind=kOutput, calls=%fused_computation.12 | convolution fusion | flops 645070848 | bytes 9191458 | tf_op jit(solution)/shard_map/sao,sbo->sab/dot_general | solution.py:68
  236.8 4.6 %reshape.269 = f32[17,16,12,192]{3,2,1,0:T(8,128)} reshape(f32[17,192,192]{2,1,0:T(8,128)} %fusion.7) | data formatting | bytes 5013504 | tf_op jit(solution)/shard_map/reshape | solution.py:72
  244.2 66.1 %all_to_all.5 = f32[16,17,12,192]{3,2,1,0:T(8,128)} all-to-all(f32[16,17,12,192]{3,2,1,0:T(8,128)S(1)} %copy.11), channel_id=1, replica_groups=mesh['aux'=16,'row'=32] {'aux'}, dimensions={0} | all-to-all | bytes 5013504 | tf_op jit(solution)/shard_map/all_to_all | solution.py:73
  (117 shorter events, 117.1 us)
Async XLA Ops:
  8.6 14.6 %collective-permute-start.1 = (bf16[2,192,256]{2,1,0:T(8,128)(2,1)S(1)}, bf16[2,192,256]{2,1,0:T(8,128)(2,1)S(1)}, u32[]{:S(2)}, u32[]{:S(2)}) collective-permute-start(bf16[2,192,256]{2,1,0:T(8,128)(2,1)S(1)} %maximum_select_fusion.9), channel_id=1, source_target_pairs={{0,1},{1,2},{2,3},{3,4},{4,5},{5,6},{6,7},{7,8},{8,9},{9,10},{10,1... | collective-permute-start | bytes 589832 | tf_op jit(solution)/shard_map/ppermute | solution.py:21
  12.2 12.9 %collective-permute-start.9 = (bf16[2,192,256]{2,1,0:T(8,128)(2,1)S(1)}, bf16[2,192,256]{2,1,0:T(8,128)(2,1)S(1)}, u32[]{:S(2)}, u32[]{:S(2)}) collective-permute-start(bf16[2,192,256]{2,1,0:T(8,128)(2,1)S(1)} %maximum_select_fusion.9), channel_id=1, source_target_pairs={{0,15},{1,0},{2,1},{3,2},{4,3},{5,4},{6,5},{7,6},{8,7},{9,8},{10,9... | collective-permute-start | bytes 589832 | tf_op jit(solution)/shard_map/ppermute | solution.py:22
  53.7 8.4 %collective-permute-start.6 = (bf16[2,192,256]{2,1,0:T(8,128)(2,1)S(1)}, bf16[2,192,256]{2,1,0:T(8,128)(2,1)S(1)}, u32[]{:S(2)}, u32[]{:S(2)}) collective-permute-start(bf16[2,192,256]{2,1,0:T(8,128)(2,1)S(1)} %collective-permute-done.5), channel_id=1, source_target_pairs={{0,1},{1,2},{2,3},{3,4},{4,5},{5,6},{6,7},{7,8},{8,9},{9,10},{10,1... | collective-permute-start | bytes 589832 | tf_op jit(solution)/shard_map/ppermute | solution.py:21
  55.6 8.4 %collective-permute-start.14 = (bf16[2,192,256]{2,1,0:T(8,128)(2,1)S(1)}, bf16[2,192,256]{2,1,0:T(8,128)(2,1)S(1)}, u32[]{:S(2)}, u32[]{:S(2)}) collective-permute-start(bf16[2,192,256]{2,1,0:T(8,128)(2,1)S(1)} %collective-permute-done.13), channel_id=1, source_target_pairs={{0,15},{1,0},{2,1},{3,2},{4,3},{5,4},{6,5},{7,6},{8,7},{9,8},{10,9... | collective-permute-start | bytes 589832 | tf_op jit(solution)/shard_map/ppermute | solution.py:22
  62.1 9.7 %collective-permute-start.7 = (bf16[2,192,256]{2,1,0:T(8,128)(2,1)S(1)}, bf16[2,192,256]{2,1,0:T(8,128)(2,1)S(1)}, u32[]{:S(2)}, u32[]{:S(2)}) collective-permute-start(bf16[2,192,256]{2,1,0:T(8,128)(2,1)S(1)} %collective-permute-done.6), channel_id=1, source_target_pairs={{0,1},{1,2},{2,3},{3,4},{4,5},{5,6},{6,7},{7,8},{8,9},{9,10},{10,1... | collective-permute-start | bytes 589832 | tf_op jit(solution)/shard_map/ppermute | solution.py:21
  64.0 9.7 %collective-permute-start.15 = (bf16[2,192,256]{2,1,0:T(8,128)(2,1)S(1)}, bf16[2,192,256]{2,1,0:T(8,128)(2,1)S(1)}, u32[]{:S(2)}, u32[]{:S(2)}) collective-permute-start(bf16[2,192,256]{2,1,0:T(8,128)(2,1)S(1)} %collective-permute-done.14), channel_id=1, source_target_pairs={{0,15},{1,0},{2,1},{3,2},{4,3},{5,4},{6,5},{7,6},{8,7},{9,8},{10,9... | collective-permute-start | bytes 589832 | tf_op jit(solution)/shard_map/ppermute | solution.py:22
  86.0 22.9 %collective-permute-start.17 = (bf16[32,192,256]{2,1,0:T(8,128)(2,1)}, bf16[32,192,256]{2,1,0:T(8,128)(2,1)}, u32[]{:S(2)}, u32[]{:S(2)}) collective-permute-start(bf16[32,192,256]{2,1,0:T(8,128)(2,1)} %bitcast.27), channel_id=1, source_target_pairs={{0,32},{32,0},{64,96},{96,64},{128,160},{160,128},{192,224},{224,1... | collective-permute-start | bytes 9437192 | tf_op jit(solution)/shard_map/ppermute | solution.py:49
  117.4 9.8 %collective-permute-start.18 = (bf16[192,512]{1,0:T(8,128)(2,1)S(1)}, bf16[192,512]{1,0:T(8,128)(2,1)S(1)}, u32[]{:S(2)}, u32[]{:S(2)}) collective-permute-start(bf16[192,512]{1,0:T(8,128)(2,1)S(1)} %fusion.20), channel_id=1, source_target_pairs={{0,16},{1,17},{2,18},{3,19},{4,20},{5,21},{6,22},{7,23},{8,24},{9,... | collective-permute-start | bytes 589832 | tf_op jit(solution)/shard_map/ppermute | solution.py:12
  127.3 13.9 %collective-permute-start.19 = (bf16[2,192,512]{2,1,0:T(8,128)(2,1)S(1)}, bf16[2,192,512]{2,1,0:T(8,128)(2,1)S(1)}, u32[]{:S(2)}, u32[]{:S(2)}) collective-permute-start(bf16[2,192,512]{2,1,0:T(8,128)(2,1)S(1)} %maximum_select_fusion.7), channel_id=1, source_target_pairs={{0,1},{1,2},{2,3},{3,4},{4,5},{5,6},{6,7},{7,8},{8,9},{9,10},{10,1... | collective-permute-start | bytes 1179656 | tf_op jit(solution)/shard_map/ppermute | solution.py:21
  129.2 13.8 %collective-permute-start.27 = (bf16[2,192,512]{2,1,0:T(8,128)(2,1)S(1)}, bf16[2,192,512]{2,1,0:T(8,128)(2,1)S(1)}, u32[]{:S(2)}, u32[]{:S(2)}) collective-permute-start(bf16[2,192,512]{2,1,0:T(8,128)(2,1)S(1)} %maximum_select_fusion.7), channel_id=1, source_target_pairs={{0,15},{1,0},{2,1},{3,2},{4,3},{5,4},{6,5},{7,6},{8,7},{9,8},{10,9... | collective-permute-start | bytes 1179656 | tf_op jit(solution)/shard_map/ppermute | solution.py:22
  141.2 12.3 %collective-permute-start.20 = (bf16[2,192,512]{2,1,0:T(8,128)(2,1)S(1)}, bf16[2,192,512]{2,1,0:T(8,128)(2,1)S(1)}, u32[]{:S(2)}, u32[]{:S(2)}) collective-permute-start(bf16[2,192,512]{2,1,0:T(8,128)(2,1)S(1)} %collective-permute-done.19), channel_id=1, source_target_pairs={{0,1},{1,2},{2,3},{3,4},{4,5},{5,6},{6,7},{7,8},{8,9},{9,10},{10,1... | collective-permute-start | bytes 1179656 | tf_op jit(solution)/shard_map/ppermute | solution.py:21
  143.1 12.9 %collective-permute-start.28 = (bf16[2,192,512]{2,1,0:T(8,128)(2,1)S(1)}, bf16[2,192,512]{2,1,0:T(8,128)(2,1)S(1)}, u32[]{:S(2)}, u32[]{:S(2)}) collective-permute-start(bf16[2,192,512]{2,1,0:T(8,128)(2,1)S(1)} %collective-permute-done.27), channel_id=1, source_target_pairs={{0,15},{1,0},{2,1},{3,2},{4,3},{5,4},{6,5},{7,6},{8,7},{9,8},{10,9... | collective-permute-start | bytes 1179656 | tf_op jit(solution)/shard_map/ppermute | solution.py:22
  153.5 11.5 %collective-permute-start.21 = (bf16[2,192,512]{2,1,0:T(8,128)(2,1)S(1)}, bf16[2,192,512]{2,1,0:T(8,128)(2,1)S(1)}, u32[]{:S(2)}, u32[]{:S(2)}) collective-permute-start(bf16[2,192,512]{2,1,0:T(8,128)(2,1)S(1)} %collective-permute-done.20), channel_id=1, source_target_pairs={{0,1},{1,2},{2,3},{3,4},{4,5},{5,6},{6,7},{7,8},{8,9},{9,10},{10,1... | collective-permute-start | bytes 1179656 | tf_op jit(solution)/shard_map/ppermute | solution.py:21
  156.0 10.9 %collective-permute-start.29 = (bf16[2,192,512]{2,1,0:T(8,128)(2,1)S(1)}, bf16[2,192,512]{2,1,0:T(8,128)(2,1)S(1)}, u32[]{:S(2)}, u32[]{:S(2)}) collective-permute-start(bf16[2,192,512]{2,1,0:T(8,128)(2,1)S(1)} %collective-permute-done.28), channel_id=1, source_target_pairs={{0,15},{1,0},{2,1},{3,2},{4,3},{5,4},{6,5},{7,6},{8,7},{9,8},{10,9... | collective-permute-start | bytes 1179656 | tf_op jit(solution)/shard_map/ppermute | solution.py:22
  164.9 10.6 %collective-permute-start.22 = (bf16[2,192,512]{2,1,0:T(8,128)(2,1)S(1)}, bf16[2,192,512]{2,1,0:T(8,128)(2,1)S(1)}, u32[]{:S(2)}, u32[]{:S(2)}) collective-permute-start(bf16[2,192,512]{2,1,0:T(8,128)(2,1)S(1)} %collective-permute-done.21), channel_id=1, source_target_pairs={{0,1},{1,2},{2,3},{3,4},{4,5},{5,6},{6,7},{7,8},{8,9},{9,10},{10,1... | collective-permute-start | bytes 1179656 | tf_op jit(solution)/shard_map/ppermute | solution.py:21
  166.9 11.3 %collective-permute-start.30 = (bf16[2,192,512]{2,1,0:T(8,128)(2,1)S(1)}, bf16[2,192,512]{2,1,0:T(8,128)(2,1)S(1)}, u32[]{:S(2)}, u32[]{:S(2)}) collective-permute-start(bf16[2,192,512]{2,1,0:T(8,128)(2,1)S(1)} %collective-permute-done.29), channel_id=1, source_target_pairs={{0,15},{1,0},{2,1},{3,2},{4,3},{5,4},{6,5},{7,6},{8,7},{9,8},{10,9... | collective-permute-start | bytes 1179656 | tf_op jit(solution)/shard_map/ppermute | solution.py:22
  175.6 9.7 %collective-permute-start.23 = (bf16[2,192,512]{2,1,0:T(8,128)(2,1)S(1)}, bf16[2,192,512]{2,1,0:T(8,128)(2,1)S(1)}, u32[]{:S(2)}, u32[]{:S(2)}) collective-permute-start(bf16[2,192,512]{2,1,0:T(8,128)(2,1)S(1)} %collective-permute-done.22), channel_id=1, source_target_pairs={{0,1},{1,2},{2,3},{3,4},{4,5},{5,6},{6,7},{7,8},{8,9},{9,10},{10,1... | collective-permute-start | bytes 1179656 | tf_op jit(solution)/shard_map/ppermute | solution.py:21
  178.3 9.7 %collective-permute-start.31 = (bf16[2,192,512]{2,1,0:T(8,128)(2,1)S(1)}, bf16[2,192,512]{2,1,0:T(8,128)(2,1)S(1)}, u32[]{:S(2)}, u32[]{:S(2)}) collective-permute-start(bf16[2,192,512]{2,1,0:T(8,128)(2,1)S(1)} %collective-permute-done.30), channel_id=1, source_target_pairs={{0,15},{1,0},{2,1},{3,2},{4,3},{5,4},{6,5},{7,6},{8,7},{9,8},{10,9... | collective-permute-start | bytes 1179656 | tf_op jit(solution)/shard_map/ppermute | solution.py:22
  185.3 9.7 %collective-permute-start.24 = (bf16[2,192,512]{2,1,0:T(8,128)(2,1)S(1)}, bf16[2,192,512]{2,1,0:T(8,128)(2,1)S(1)}, u32[]{:S(2)}, u32[]{:S(2)}) collective-permute-start(bf16[2,192,512]{2,1,0:T(8,128)(2,1)S(1)} %collective-permute-done.23), channel_id=1, source_target_pairs={{0,1},{1,2},{2,3},{3,4},{4,5},{5,6},{6,7},{7,8},{8,9},{9,10},{10,1... | collective-permute-start | bytes 1179656 | tf_op jit(solution)/shard_map/ppermute | solution.py:21
  188.0 9.7 %collective-permute-start.32 = (bf16[2,192,512]{2,1,0:T(8,128)(2,1)S(1)}, bf16[2,192,512]{2,1,0:T(8,128)(2,1)S(1)}, u32[]{:S(2)}, u32[]{:S(2)}) collective-permute-start(bf16[2,192,512]{2,1,0:T(8,128)(2,1)S(1)} %collective-permute-done.31), channel_id=1, source_target_pairs={{0,15},{1,0},{2,1},{3,2},{4,3},{5,4},{6,5},{7,6},{8,7},{9,8},{10,9... | collective-permute-start | bytes 1179656 | tf_op jit(solution)/shard_map/ppermute | solution.py:22
  195.0 9.8 %collective-permute-start.25 = (bf16[2,192,512]{2,1,0:T(8,128)(2,1)S(1)}, bf16[2,192,512]{2,1,0:T(8,128)(2,1)S(1)}, u32[]{:S(2)}, u32[]{:S(2)}) collective-permute-start(bf16[2,192,512]{2,1,0:T(8,128)(2,1)S(1)} %collective-permute-done.24), channel_id=1, source_target_pairs={{0,1},{1,2},{2,3},{3,4},{4,5},{5,6},{6,7},{7,8},{8,9},{9,10},{10,1... | collective-permute-start | bytes 1179656 | tf_op jit(solution)/shard_map/ppermute | solution.py:21
  197.7 9.7 %collective-permute-start.33 = (bf16[2,192,512]{2,1,0:T(8,128)(2,1)S(1)}, bf16[2,192,512]{2,1,0:T(8,128)(2,1)S(1)}, u32[]{:S(2)}, u32[]{:S(2)}) collective-permute-start(bf16[2,192,512]{2,1,0:T(8,128)(2,1)S(1)} %collective-permute-done.32), channel_id=1, source_target_pairs={{0,15},{1,0},{2,1},{3,2},{4,3},{5,4},{6,5},{7,6},{8,7},{9,8},{10,9... | collective-permute-start | bytes 1179656 | tf_op jit(solution)/shard_map/ppermute | solution.py:22
  204.9 8.9 %collective-permute-start.26 = (bf16[192,512]{1,0:T(8,128)(2,1)S(1)}, bf16[192,512]{1,0:T(8,128)(2,1)S(1)}, u32[]{:S(2)}, u32[]{:S(2)}) collective-permute-start(bf16[192,512]{1,0:T(8,128)(2,1)S(1)} %slice_bitcast_fusion.1), channel_id=1, source_target_pairs={{0,1},{1,2},{2,3},{3,4},{4,5},{5,6},{6,7},{7,8},{8,9},{9,10},{10,1... | collective-permute-start | bytes 589832 | tf_op jit(solution)/shard_map/ppermute | solution.py:25
  207.4 9.1 %collective-permute-start.34 = (bf16[192,512]{1,0:T(8,128)(2,1)S(1)}, bf16[192,512]{1,0:T(8,128)(2,1)S(1)}, u32[]{:S(2)}, u32[]{:S(2)}) collective-permute-start(bf16[192,512]{1,0:T(8,128)(2,1)S(1)} %slice_bitcast_fusion), channel_id=1, source_target_pairs={{0,15},{1,0},{2,1},{3,2},{4,3},{5,4},{6,5},{7,6},{8,7},{9,8},{10,9... | collective-permute-start | bytes 589832 | tf_op jit(solution)/shard_map/ppermute | solution.py:26
  (15 other events, 245.5 us)

commit v3 on v1

v3 whole, which is shorter than its diff:
```python
import jax
import jax.numpy as jnp
from jax import lax
from jax.sharding import PartitionSpec as P


def y_pair(x, nrow, ring):
    yh = lax.axis_index("row") // ring
    other = lax.ppermute(x, "row", [(i, i ^ ring) for i in range(nrow)])
    return jnp.where(yh == 0, jnp.stack([x, other]), jnp.stack([other, x]))


def one_way_ring(x, naux, nrow, ring):
    perm = []
    for a in range(naux):
        for r in range(nrow):
            base = (r // ring) * ring
            step = 1 if a % 2 == 0 else -1
            perm.append((a * nrow + r, a * nrow + base + (r % ring + step) % ring))
    got = []
    for _ in range(ring // 2):
        x = lax.ppermute(x, ("aux", "row"), perm)
        got.append(x)
    return jnp.stack(got)


def slot_of(k, z, core, ring):
    y = k // ring
    d = (z - k % ring) % ring
    hr = ring // 2
    idx0 = jnp.where(d == 0, 0, jnp.where(d <= hr, d, hr + ring - d))
    idx1 = jnp.where(d == 0, 0, jnp.where(d >= hr, ring - d, hr + d))
    return jnp.where(core == 0, idx0, idx1) * 2 + y


def local(chol_vectors, occ_coeff, tile_pairs, tile_owner):
    block = chol_vectors.shape[1]
    nbf = chol_vectors.shape[2]
    nocc = occ_coeff.shape[1]
    nrow = lax.axis_size("row")
    naux = lax.axis_size("aux")
    ring = nrow // 2
    core = lax.axis_index("aux") % 2
    z = lax.axis_index("row") % ring
    partner = [(i, i ^ 1) for i in range(naux)]
    k = jnp.arange(nrow)

    pair_c = y_pair(occ_coeff, nrow, ring)
    stream_c = one_way_ring(pair_c, naux, nrow, ring)
    swapped_c = lax.ppermute(stream_c, "aux", partner)
    all_c = jnp.concatenate([pair_c[None], stream_c, swapped_c]).reshape(
        (-1, block, nocc)
    )
    coeff = jnp.take(all_c, slot_of(k, z, core, ring), axis=0).reshape(nbf, nocc)
    half = jnp.dot(chol_vectors[0], coeff, preferred_element_type=jnp.float32).astype(
        jnp.bfloat16
    )

    pair_h = y_pair(half, nrow, ring)
    partner_h = lax.ppermute(pair_h, "aux", partner)
    quad = jnp.stack([pair_h, partner_h])
    stream_h = one_way_ring(quad, naux, nrow, ring)
    swapped_h = lax.ppermute(stream_h[:, 1], "aux", partner)
    all_h = jnp.concatenate([pair_h[None], stream_h[:, 0], swapped_h]).reshape(
        (-1, block, nocc)
    )

    chosen = tile_pairs[tile_owner[0]]
    left_rows = jnp.take(all_h, slot_of(chosen[:, 0], z, core, ring), axis=0)
    right_rows = jnp.take(all_h, slot_of(chosen[:, 1], z, core, ring), axis=0)
    partial_tiles = jnp.einsum(
        "sao,sbo->sab", left_rows, right_rows, preferred_element_type=jnp.float32
    )
    slots = partial_tiles.shape[0]
    split = partial_tiles.reshape(slots, naux, block // naux, block).transpose(1, 0, 2, 3)
    pieces = lax.all_to_all(split, "aux", 0, 0, tiled=True)
    return jnp.sum(pieces, axis=0)


def solution(mesh):
    placed = (P("aux", "row", None), P("row", None), P(), P("row", None))
    return jax.shard_map(
        local, mesh=mesh, in_specs=placed, out_specs=P("row", "aux", None), check_vma=False
    )
```

time: 448 us -> 370 us (0.83)
  waiting for transfers between devices: 320 us -> 123 us
  starting transfers between devices: 12.5 us -> 122 us
  local copies, waits for them, and re-layouts: 21 us -> 41.6 us
  between operations: 13.5 us -> 0.44 us
  other arithmetic: 4.32 us -> 16.8 us
  blocking collectives: 65 us -> 57.9 us
    all_gather x2 -> x0, waiting for transfers between devices: 317 us -> none  [the longest x1 162 us: local(): gathered = lax.all_gather(half, 'row', axis=0, tiled=True)]
    ppermute x1 -> x21, waiting for transfers between devices: 2.89 us -> 123 us  [the longest x16 104 us: one_way_ring(): x = lax.ppermute(x, ('aux', 'row'), perm)]
    ppermute x1 -> x21, starting transfers between devices: 12.5 us -> 122 us  [the longest x16 80.7 us: one_way_ring(): x = lax.ppermute(x, ('aux', 'row'), perm)]
    unnamed x7 -> x23, local copies, waits for them, and re-layouts: 0.16 us -> 7.35 us
    all_to_all x1, blocking collectives: 65 us -> 57.9 us  [local(): pieces = lax.all_to_all(split, 'aux', 0, 0, tiled=True)]
    gather x2 -> x3, local copies, waits for them, and re-layouts: 11.1 us -> 18 us  [the longest x1 6.53 us: local(): jnp.take(all_c, slot_of(k, z, core, ring), axis=0).reshape(nbf, nocc)]
    concatenate x0 -> x1, other arithmetic: none -> 6.57 us  [local(): jnp.concatenate([pair_h[None], stream_h[:, 0], swapped_h])]
  transfers between devices with their start and end apart: 3 -> 21, of which waited for: 3 -> 21; matrix products, arithmetic and copies ran while one was open for 1% -> 3% of each run, Pallas kernels for 0% -> 0%
where the time goes in v3:
time: 370 us; the launch traced here: 369 us
  waiting for transfers between devices  123 us (33%)
  starting transfers between devices  122 us (33%)
  blocking collectives  57.9 us (16%)
  local copies, waits for them, and re-layouts  41.6 us (11%)
  other arithmetic  16.8 us (5%)
  matrix products  7.28 us (2%)
    ppermute x16, waiting for transfers between devices, one_way_ring(): x = lax.ppermute(x, ('aux', 'row'), perm)  104 us
    ppermute x16, starting transfers between devices, one_way_ring(): x = lax.ppermute(x, ('aux', 'row'), perm)  80.7 us
    all_to_all x1, blocking collectives, local(): pieces = lax.all_to_all(split, 'aux', 0, 0, tiled=True)  57.9 us
    ppermute x1, starting transfers between devices, local(): swapped_h = lax.ppermute(stream_h[:, 1], 'aux', partner)  14.6 us
    ppermute x1, starting transfers between devices, local(): swapped_c = lax.ppermute(stream_c, 'aux', partner)  12.8 us
    ppermute x2, starting transfers between devices, y_pair(): other = lax.ppermute(x, 'row', [(i, i ^ ring) for i in range(nrow)])  10.6 us
    ppermute x2, waiting for transfers between devices, y_pair(): other = lax.ppermute(x, 'row', [(i, i ^ ring) for i in range(nrow)])  7.89 us
  transfers between devices with their start and end apart: 21, of which 21 were waited for; matrix products, arithmetic and copies ran while one was open for 3% of the time, Pallas kernels for 0%

profile of v3, /device:TPU:1, one launch (start us, length us, event | category | flops | bytes accessed | tf_op | source)
XLA Modules:
  0.0 368.7 jit_solution(15377900236096405312)
XLA Ops:
  0.0 5.8 %collective-permute-start = (bf16[192,512]{1,0:T(8,128)(2,1)}, bf16[192,512]{1,0:T(8,128)(2,1)S(1)}, u32[]{:S(2)}, u32[]{:S(2)}) collective-permute-start(bf16[192,512]{1,0:T(8,128)(2,1)} %param.7), channel_id=1, source_target_pairs={{0,16},{1,17},{2,18},{3,19},{4,20},{5,21},{6,22},{7,23},{8,24},{9,... | collective-permute-start | bytes 589832 | tf_op jit(solution)/shard_map/ppermute | solution.py:9
  10.1 12.4 %collective-permute-start.1 = (bf16[2,192,512]{2,1,0:T(8,128)(2,1)S(1)}, bf16[2,192,512]{2,1,0:T(8,128)(2,1)S(1)}, u32[]{:S(2)}, u32[]{:S(2)}) collective-permute-start(bf16[2,192,512]{2,1,0:T(8,128)(2,1)S(1)} %maximum_select_fusion.1), channel_id=1, source_target_pairs={{0,1},{1,2},{2,3},{3,4},{4,5},{5,6},{6,7},{7,8},{8,9},{9,10},{10,1... | collective-permute-start | bytes 1179656 | tf_op jit(solution)/shard_map/ppermute | solution.py:22
  27.2 5.0 %collective-permute-start.2 = (bf16[2,192,512]{2,1,0:T(8,128)(2,1)S(1)}, bf16[2,192,512]{2,1,0:T(8,128)(2,1)S(1)}, u32[]{:S(2)}, u32[]{:S(2)}) collective-permute-start(bf16[2,192,512]{2,1,0:T(8,128)(2,1)S(1)} %collective-permute-done.1), channel_id=1, source_target_pairs={{0,1},{1,2},{2,3},{3,4},{4,5},{5,6},{6,7},{7,8},{8,9},{9,10},{10,1... | collective-permute-start | bytes 1179656 | tf_op jit(solution)/shard_map/ppermute | solution.py:22
  37.0 5.0 %collective-permute-start.3 = (bf16[2,192,512]{2,1,0:T(8,128)(2,1)S(1)}, bf16[2,192,512]{2,1,0:T(8,128)(2,1)S(1)}, u32[]{:S(2)}, u32[]{:S(2)}) collective-permute-start(bf16[2,192,512]{2,1,0:T(8,128)(2,1)S(1)} %collective-permute-done.2), channel_id=1, source_target_pairs={{0,1},{1,2},{2,3},{3,4},{4,5},{5,6},{6,7},{7,8},{8,9},{9,10},{10,1... | collective-permute-start | bytes 1179656 | tf_op jit(solution)/shard_map/ppermute | solution.py:22
  56.4 5.0 %collective-permute-start.5 = (bf16[2,192,512]{2,1,0:T(8,128)(2,1)S(1)}, bf16[2,192,512]{2,1,0:T(8,128)(2,1)S(1)}, u32[]{:S(2)}, u32[]{:S(2)}) collective-permute-start(bf16[2,192,512]{2,1,0:T(8,128)(2,1)S(1)} %collective-permute-done.4), channel_id=1, source_target_pairs={{0,1},{1,2},{2,3},{3,4},{4,5},{5,6},{6,7},{7,8},{8,9},{9,10},{10,1... | collective-permute-start | bytes 1179656 | tf_op jit(solution)/shard_map/ppermute | solution.py:22
  66.1 5.0 %collective-permute-start.6 = (bf16[2,192,512]{2,1,0:T(8,128)(2,1)S(1)}, bf16[2,192,512]{2,1,0:T(8,128)(2,1)S(1)}, u32[]{:S(2)}, u32[]{:S(2)}) collective-permute-start(bf16[2,192,512]{2,1,0:T(8,128)(2,1)S(1)} %collective-permute-done.5), channel_id=1, source_target_pairs={{0,1},{1,2},{2,3},{3,4},{4,5},{5,6},{6,7},{7,8},{8,9},{9,10},{10,1... | collective-permute-start | bytes 1179656 | tf_op jit(solution)/shard_map/ppermute | solution.py:22
  85.6 5.0 %collective-permute-start.8 = (bf16[2,192,512]{2,1,0:T(8,128)(2,1)S(1)}, bf16[2,192,512]{2,1,0:T(8,128)(2,1)S(1)}, u32[]{:S(2)}, u32[]{:S(2)}) collective-permute-start(bf16[2,192,512]{2,1,0:T(8,128)(2,1)S(1)} %collective-permute-done.7), channel_id=1, source_target_pairs={{0,1},{1,2},{2,3},{3,4},{4,5},{5,6},{6,7},{7,8},{8,9},{9,10},{10,1... | collective-permute-start | bytes 1179656 | tf_op jit(solution)/shard_map/ppermute | solution.py:22
  96.3 12.8 %collective-permute-start.9 = (bf16[8,2,192,512]{3,2,1,0:T(8,128)(2,1)}, bf16[8,2,192,512]{3,2,1,0:T(8,128)(2,1)}, u32[]{:S(2)}, u32[]{:S(2)}) collective-permute-start(bf16[8,2,192,512]{3,2,1,0:T(8,128)(2,1)} %get-tuple-element.14), channel_id=1, source_target_pairs={{0,32},{32,0},{64,96},{96,64},{128,160},{160,128},{192,224},{224,1... | collective-permute-start | bytes 9437192 | tf_op jit(solution)/shard_map/ppermute | solution.py:50
  109.2 5.5 %collective-permute-done.9 = bf16[8,2,192,512]{3,2,1,0:T(8,128)(2,1)} collective-permute-done((bf16[8,2,192,512]{3,2,1,0:T(8,128)(2,1)}, bf16[8,2,192,512]{3,2,1,0:T(8,128)(2,1)}, u32[]{:S(2)}, u32[]{:S(2)}) %collective-permute-start.9) | collective-permute-done | bytes 3145760 | tf_op jit(solution)/shard_map/ppermute | solution.py:50
  118.5 6.5 %gather_fusion = bf16[32,192,512]{2,1,0:T(8,128)(2,1)} fusion(bf16[34,192,512]{2,1,0:T(8,128)(2,1)} %bitcast.14, s32[1024]{0:T(1024)S(1)} %pad_clamp_fusion.2), kind=kCustom, calls=%fused_computation.2 | custom fusion | bytes 12583040 | tf_op jit(solution)/shard_map/jit(_take)/gather | solution.py:54
  145.9 11.1 %collective-permute-done.12 = bf16[2,2,192,512]{3,2,1,0:T(8,128)(2,1)S(1)} collective-permute-done((bf16[2,2,192,512]{3,2,1,0:T(8,128)(2,1)S(1)}, bf16[2,2,192,512]{3,2,1,0:T(8,128)(2,1)S(1)}, u32[]{:S(2)}, u32[]{:S(2)}) %collective-permute-start.12) | collective-permute-done | bytes 786464 | tf_op jit(solution)/shard_map/ppermute | solution.py:22
  159.9 10.2 %collective-permute-done.13 = bf16[2,2,192,512]{3,2,1,0:T(8,128)(2,1)S(1)} collective-permute-done((bf16[2,2,192,512]{3,2,1,0:T(8,128)(2,1)S(1)}, bf16[2,2,192,512]{3,2,1,0:T(8,128)(2,1)S(1)}, u32[]{:S(2)}, u32[]{:S(2)}) %collective-permute-start.13) | collective-permute-done | bytes 786464 | tf_op jit(solution)/shard_map/ppermute | solution.py:22
  173.8 9.3 %collective-permute-done.14 = bf16[2,2,192,512]{3,2,1,0:T(8,128)(2,1)S(1)} collective-permute-done((bf16[2,2,192,512]{3,2,1,0:T(8,128)(2,1)S(1)}, bf16[2,2,192,512]{3,2,1,0:T(8,128)(2,1)S(1)}, u32[]{:S(2)}, u32[]{:S(2)}) %collective-permute-start.14) | collective-permute-done | bytes 786464 | tf_op jit(solution)/shard_map/ppermute | solution.py:22
  187.7 8.9 %collective-permute-done.15 = bf16[2,2,192,512]{3,2,1,0:T(8,128)(2,1)S(1)} collective-permute-done((bf16[2,2,192,512]{3,2,1,0:T(8,128)(2,1)S(1)}, bf16[2,2,192,512]{3,2,1,0:T(8,128)(2,1)S(1)}, u32[]{:S(2)}, u32[]{:S(2)}) %collective-permute-start.15) | collective-permute-done | bytes 786464 | tf_op jit(solution)/shard_map/ppermute | solution.py:22
  201.7 8.9 %collective-permute-done.16 = bf16[2,2,192,512]{3,2,1,0:T(8,128)(2,1)S(1)} collective-permute-done((bf16[2,2,192,512]{3,2,1,0:T(8,128)(2,1)S(1)}, bf16[2,2,192,512]{3,2,1,0:T(8,128)(2,1)S(1)}, u32[]{:S(2)}, u32[]{:S(2)}) %collective-permute-start.16) | collective-permute-done | bytes 786464 | tf_op jit(solution)/shard_map/ppermute | solution.py:22
  215.7 8.9 %collective-permute-done.17 = bf16[2,2,192,512]{3,2,1,0:T(8,128)(2,1)S(1)} collective-permute-done((bf16[2,2,192,512]{3,2,1,0:T(8,128)(2,1)S(1)}, bf16[2,2,192,512]{3,2,1,0:T(8,128)(2,1)S(1)}, u32[]{:S(2)}, u32[]{:S(2)}) %collective-permute-start.17) | collective-permute-done | bytes 786464 | tf_op jit(solution)/shard_map/ppermute | solution.py:22
  229.7 8.7 %collective-permute-done.18 = bf16[2,2,192,512]{3,2,1,0:T(8,128)(2,1)S(1)} collective-permute-done((bf16[2,2,192,512]{3,2,1,0:T(8,128)(2,1)S(1)}, bf16[2,2,192,512]{3,2,1,0:T(8,128)(2,1)S(1)}, u32[]{:S(2)}, u32[]{:S(2)}) %collective-permute-start.18) | collective-permute-done | bytes 786464 | tf_op jit(solution)/shard_map/ppermute | solution.py:22
  243.6 8.7 %collective-permute-done.19 = bf16[2,2,192,512]{3,2,1,0:T(8,128)(2,1)S(1)} collective-permute-done((bf16[2,2,192,512]{3,2,1,0:T(8,128)(2,1)S(1)}, bf16[2,2,192,512]{3,2,1,0:T(8,128)(2,1)S(1)}, u32[]{:S(2)}, u32[]{:S(2)}) %collective-permute-start.19) | collective-permute-done | bytes 786464 | tf_op jit(solution)/shard_map/ppermute | solution.py:22
  255.6 14.6 %collective-permute-start.20 = (bf16[8,2,192,512]{3,2,1,0:T(8,128)(2,1)}, bf16[8,2,192,512]{3,2,1,0:T(8,128)(2,1)}, u32[]{:S(2)}, u32[]{:S(2)}) collective-permute-start(bf16[8,2,192,512]{3,2,1,0:T(8,128)(2,1)} %get-tuple-element.13), channel_id=1, source_target_pairs={{0,32},{32,0},{64,96},{96,64},{128,160},{160,128},{192,224},{224,1... | collective-permute-start | bytes 9437192 | tf_op jit(solution)/shard_map/ppermute | solution.py:63
  275.8 6.6 %pad_maximum_fusion = bf16[17,2,192,512]{3,2,1,0:T(8,128)(2,1)} fusion(bf16[8,2,192,512]{3,2,1,0:T(8,128)(2,1)} %collective-permute-done.20, bf16[8,2,192,512]{3,2,1,0:T(8,128)(2,1)} %get-tuple-element.12, bf16[1,2,192,512]{3,2,1,0:T(8,128)(2,1)S(1)} %maximum_select_fusion.2), kind=kLoop, calls=%fused_computation.4 | loop fusion | flops 6684672 | bytes 13369344 | tf_op jit(solution)/shard_map/concatenate | solution.py:64
  282.4 5.8 %gather_fusion.2 = bf16[17,192,512]{2,1,0:T(8,128)(2,1)} fusion(bf16[34,192,512]{2,1,0:T(8,128)(2,1)} %bitcast.74, s32[1024]{0:T(1024)S(1)} %pad_clamp_fusion.1), kind=kCustom, calls=%fused_computation.clone | custom fusion | bytes 6684740 | tf_op jit(solution)/shard_map/jit(_take)/gather | solution.py:69
  288.1 5.7 %gather_fusion.3 = bf16[17,192,512]{2,1,0:T(8,128)(2,1)} fusion(bf16[34,192,512]{2,1,0:T(8,128)(2,1)} %bitcast.75, s32[1024]{0:T(1024)S(1)} %pad_clamp_fusion), kind=kCustom, calls=%fused_computation.1.clone | custom fusion | bytes 6684740 | tf_op jit(solution)/shard_map/jit(_take)/gather | solution.py:70
  293.8 5.9 %fusion = f32[17,192,192]{2,1,0:T(8,128)} fusion(bf16[17,192,512]{2,1,0:T(8,128)(2,1)} %gather_fusion.3, bf16[17,192,512]{2,1,0:T(8,128)(2,1)} %gather_fusion.2, pred[17]{0:T(512)(128)(4,1)S(1)} %get-tuple-element.10, pred[17]{0:T(512)(128)(4,1)S(1)} %get-tuple-element.30), kind=kOutput, calls=%fused_computation.6 | convolution fusion | flops 645070848 | bytes 9191458 | tf_op jit(solution)/shard_map/sao,sbo->sab/dot_general | solution.py:71
  307.3 57.9 %all_to_all.5 = f32[16,17,12,192]{3,2,1,0:T(8,128)} all-to-all(f32[16,17,12,192]{3,2,1,0:T(8,128)S(1)} %copy.11), channel_id=1, replica_groups=mesh['aux'=16,'row'=32] {'aux'}, dimensions={0} | all-to-all | bytes 5013504 | tf_op jit(solution)/shard_map/all_to_all | solution.py:76
  (71 shorter events, 129.1 us)
Async XLA Ops:
  0.0 128.5 %copy-start = (bf16[1,192,6144]{2,1,0:T(8,128)(2,1)S(1)}, bf16[1,192,6144]{2,1,0:T(8,128)(2,1)}, u32[]{:S(2)}) copy-start(bf16[1,192,6144]{2,1,0:T(8,128)(2,1)} %param.6) | copy-start | bytes 7077892
  0.0 9.0 %collective-permute-start = (bf16[192,512]{1,0:T(8,128)(2,1)}, bf16[192,512]{1,0:T(8,128)(2,1)S(1)}, u32[]{:S(2)}, u32[]{:S(2)}) collective-permute-start(bf16[192,512]{1,0:T(8,128)(2,1)} %param.7), channel_id=1, source_target_pairs={{0,16},{1,17},{2,18},{3,19},{4,20},{5,21},{6,22},{7,23},{8,24},{9,... | collective-permute-start | bytes 589832 | tf_op jit(solution)/shard_map/ppermute | solution.py:9
  10.1 17.1 %collective-permute-start.1 = (bf16[2,192,512]{2,1,0:T(8,128)(2,1)S(1)}, bf16[2,192,512]{2,1,0:T(8,128)(2,1)S(1)}, u32[]{:S(2)}, u32[]{:S(2)}) collective-permute-start(bf16[2,192,512]{2,1,0:T(8,128)(2,1)S(1)} %maximum_select_fusion.1), channel_id=1, source_target_pairs={{0,1},{1,2},{2,3},{3,4},{4,5},{5,6},{6,7},{7,8},{8,9},{9,10},{10,1... | collective-permute-start | bytes 1179656 | tf_op jit(solution)/shard_map/ppermute | solution.py:22
  27.2 9.7 %collective-permute-start.2 = (bf16[2,192,512]{2,1,0:T(8,128)(2,1)S(1)}, bf16[2,192,512]{2,1,0:T(8,128)(2,1)S(1)}, u32[]{:S(2)}, u32[]{:S(2)}) collective-permute-start(bf16[2,192,512]{2,1,0:T(8,128)(2,1)S(1)} %collective-permute-done.1), channel_id=1, source_target_pairs={{0,1},{1,2},{2,3},{3,4},{4,5},{5,6},{6,7},{7,8},{8,9},{9,10},{10,1... | collective-permute-start | bytes 1179656 | tf_op jit(solution)/shard_map/ppermute | solution.py:22
  37.0 9.7 %collective-permute-start.3 = (bf16[2,192,512]{2,1,0:T(8,128)(2,1)S(1)}, bf16[2,192,512]{2,1,0:T(8,128)(2,1)S(1)}, u32[]{:S(2)}, u32[]{:S(2)}) collective-permute-start(bf16[2,192,512]{2,1,0:T(8,128)(2,1)S(1)} %collective-permute-done.2), channel_id=1, source_target_pairs={{0,1},{1,2},{2,3},{3,4},{4,5},{5,6},{6,7},{7,8},{8,9},{9,10},{10,1... | collective-permute-start | bytes 1179656 | tf_op jit(solution)/shard_map/ppermute | solution.py:22
  46.7 9.7 %collective-permute-start.4 = (bf16[2,192,512]{2,1,0:T(8,128)(2,1)S(1)}, bf16[2,192,512]{2,1,0:T(8,128)(2,1)S(1)}, u32[]{:S(2)}, u32[]{:S(2)}) collective-permute-start(bf16[2,192,512]{2,1,0:T(8,128)(2,1)S(1)} %collective-permute-done.3), channel_id=1, source_target_pairs={{0,1},{1,2},{2,3},{3,4},{4,5},{5,6},{6,7},{7,8},{8,9},{9,10},{10,1... | collective-permute-start | bytes 1179656 | tf_op jit(solution)/shard_map/ppermute | solution.py:22
  56.4 9.7 %collective-permute-start.5 = (bf16[2,192,512]{2,1,0:T(8,128)(2,1)S(1)}, bf16[2,192,512]{2,1,0:T(8,128)(2,1)S(1)}, u32[]{:S(2)}, u32[]{:S(2)}) collective-permute-start(bf16[2,192,512]{2,1,0:T(8,128)(2,1)S(1)} %collective-permute-done.4), channel_id=1, source_target_pairs={{0,1},{1,2},{2,3},{3,4},{4,5},{5,6},{6,7},{7,8},{8,9},{9,10},{10,1... | collective-permute-start | bytes 1179656 | tf_op jit(solution)/shard_map/ppermute | solution.py:22
  66.1 9.7 %collective-permute-start.6 = (bf16[2,192,512]{2,1,0:T(8,128)(2,1)S(1)}, bf16[2,192,512]{2,1,0:T(8,128)(2,1)S(1)}, u32[]{:S(2)}, u32[]{:S(2)}) collective-permute-start(bf16[2,192,512]{2,1,0:T(8,128)(2,1)S(1)} %collective-permute-done.5), channel_id=1, source_target_pairs={{0,1},{1,2},{2,3},{3,4},{4,5},{5,6},{6,7},{7,8},{8,9},{9,10},{10,1... | collective-permute-start | bytes 1179656 | tf_op jit(solution)/shard_map/ppermute | solution.py:22
  75.9 9.7 %collective-permute-start.7 = (bf16[2,192,512]{2,1,0:T(8,128)(2,1)S(1)}, bf16[2,192,512]{2,1,0:T(8,128)(2,1)S(1)}, u32[]{:S(2)}, u32[]{:S(2)}) collective-permute-start(bf16[2,192,512]{2,1,0:T(8,128)(2,1)S(1)} %collective-permute-done.6), channel_id=1, source_target_pairs={{0,1},{1,2},{2,3},{3,4},{4,5},{5,6},{6,7},{7,8},{8,9},{9,10},{10,1... | collective-permute-start | bytes 1179656 | tf_op jit(solution)/shard_map/ppermute | solution.py:22
  85.6 9.7 %collective-permute-start.8 = (bf16[2,192,512]{2,1,0:T(8,128)(2,1)S(1)}, bf16[2,192,512]{2,1,0:T(8,128)(2,1)S(1)}, u32[]{:S(2)}, u32[]{:S(2)}) collective-permute-start(bf16[2,192,512]{2,1,0:T(8,128)(2,1)S(1)} %collective-permute-done.7), channel_id=1, source_target_pairs={{0,1},{1,2},{2,3},{3,4},{4,5},{5,6},{6,7},{7,8},{8,9},{9,10},{10,1... | collective-permute-start | bytes 1179656 | tf_op jit(solution)/shard_map/ppermute | solution.py:22
  96.3 18.4 %collective-permute-start.9 = (bf16[8,2,192,512]{3,2,1,0:T(8,128)(2,1)}, bf16[8,2,192,512]{3,2,1,0:T(8,128)(2,1)}, u32[]{:S(2)}, u32[]{:S(2)}) collective-permute-start(bf16[8,2,192,512]{3,2,1,0:T(8,128)(2,1)} %get-tuple-element.14), channel_id=1, source_target_pairs={{0,32},{32,0},{64,96},{96,64},{128,160},{160,128},{192,224},{224,1... | collective-permute-start | bytes 9437192 | tf_op jit(solution)/shard_map/ppermute | solution.py:50
  129.9 9.5 %collective-permute-start.10 = (bf16[192,512]{1,0:T(8,128)(2,1)S(1)}, bf16[192,512]{1,0:T(8,128)(2,1)S(1)}, u32[]{:S(2)}, u32[]{:S(2)}) collective-permute-start(bf16[192,512]{1,0:T(8,128)(2,1)S(1)} %bitcast.82), channel_id=1, source_target_pairs={{0,16},{1,17},{2,18},{3,19},{4,20},{5,21},{6,22},{7,23},{8,24},{9,... | collective-permute-start | bytes 589832 | tf_op jit(solution)/shard_map/ppermute | solution.py:9
  139.4 4.5 %collective-permute-start.11 = (bf16[2,192,512]{2,1,0:T(8,128)(2,1)S(1)}, bf16[2,192,512]{2,1,0:T(8,128)(2,1)S(1)}, u32[]{:S(2)}, u32[]{:S(2)}) collective-permute-start(bf16[2,192,512]{2,1,0:T(8,128)(2,1)S(1)} %maximum_select_fusion.3), channel_id=1, source_target_pairs={{0,32},{32,0},{64,96},{96,64},{128,160},{160,128},{192,224},{224,1... | collective-permute-start | bytes 1179656 | tf_op jit(solution)/shard_map/ppermute | solution.py:60
  144.0 13.0 %collective-permute-start.12 = (bf16[2,2,192,512]{3,2,1,0:T(8,128)(2,1)S(1)}, bf16[2,2,192,512]{3,2,1,0:T(8,128)(2,1)S(1)}, u32[]{:S(2)}, u32[]{:S(2)}) collective-permute-start(bf16[2,2,192,512]{3,2,1,0:T(8,128)(2,1)S(1)} %pad_maximum_fusion.1), channel_id=1, source_target_pairs={{0,1},{1,2},{2,3},{3,4},{4,5},{5,6},{6,7},{7,8},{8,9},{9,10},{10,1... | collective-permute-start | bytes 2359304 | tf_op jit(solution)/shard_map/ppermute | solution.py:22
  157.0 13.0 %collective-permute-start.13 = (bf16[2,2,192,512]{3,2,1,0:T(8,128)(2,1)S(1)}, bf16[2,2,192,512]{3,2,1,0:T(8,128)(2,1)S(1)}, u32[]{:S(2)}, u32[]{:S(2)}) collective-permute-start(bf16[2,2,192,512]{3,2,1,0:T(8,128)(2,1)S(1)} %collective-permute-done.12), channel_id=1, source_target_pairs={{0,1},{1,2},{2,3},{3,4},{4,5},{5,6},{6,7},{7,8},{8,9},{9,10},{10,1... | collective-permute-start | bytes 2359304 | tf_op jit(solution)/shard_map/ppermute | solution.py:22
  170.0 13.0 %collective-permute-start.14 = (bf16[2,2,192,512]{3,2,1,0:T(8,128)(2,1)S(1)}, bf16[2,2,192,512]{3,2,1,0:T(8,128)(2,1)S(1)}, u32[]{:S(2)}, u32[]{:S(2)}) collective-permute-start(bf16[2,2,192,512]{3,2,1,0:T(8,128)(2,1)S(1)} %collective-permute-done.13), channel_id=1, source_target_pairs={{0,1},{1,2},{2,3},{3,4},{4,5},{5,6},{6,7},{7,8},{8,9},{9,10},{10,1... | collective-permute-start | bytes 2359304 | tf_op jit(solution)/shard_map/ppermute | solution.py:22
  183.1 13.6 %collective-permute-start.15 = (bf16[2,2,192,512]{3,2,1,0:T(8,128)(2,1)S(1)}, bf16[2,2,192,512]{3,2,1,0:T(8,128)(2,1)S(1)}, u32[]{:S(2)}, u32[]{:S(2)}) collective-permute-start(bf16[2,2,192,512]{3,2,1,0:T(8,128)(2,1)S(1)} %collective-permute-done.14), channel_id=1, source_target_pairs={{0,1},{1,2},{2,3},{3,4},{4,5},{5,6},{6,7},{7,8},{8,9},{9,10},{10,1... | collective-permute-start | bytes 2359304 | tf_op jit(solution)/shard_map/ppermute | solution.py:22
  196.6 13.9 %collective-permute-start.16 = (bf16[2,2,192,512]{3,2,1,0:T(8,128)(2,1)S(1)}, bf16[2,2,192,512]{3,2,1,0:T(8,128)(2,1)S(1)}, u32[]{:S(2)}, u32[]{:S(2)}) collective-permute-start(bf16[2,2,192,512]{3,2,1,0:T(8,128)(2,1)S(1)} %collective-permute-done.15), channel_id=1, source_target_pairs={{0,1},{1,2},{2,3},{3,4},{4,5},{5,6},{6,7},{7,8},{8,9},{9,10},{10,1... | collective-permute-start | bytes 2359304 | tf_op jit(solution)/shard_map/ppermute | solution.py:22
  210.6 13.9 %collective-permute-start.17 = (bf16[2,2,192,512]{3,2,1,0:T(8,128)(2,1)S(1)}, bf16[2,2,192,512]{3,2,1,0:T(8,128)(2,1)S(1)}, u32[]{:S(2)}, u32[]{:S(2)}) collective-permute-start(bf16[2,2,192,512]{3,2,1,0:T(8,128)(2,1)S(1)} %collective-permute-done.16), channel_id=1, source_target_pairs={{0,1},{1,2},{2,3},{3,4},{4,5},{5,6},{6,7},{7,8},{8,9},{9,10},{10,1... | collective-permute-start | bytes 2359304 | tf_op jit(solution)/shard_map/ppermute | solution.py:22
  224.5 13.9 %collective-permute-start.18 = (bf16[2,2,192,512]{3,2,1,0:T(8,128)(2,1)S(1)}, bf16[2,2,192,512]{3,2,1,0:T(8,128)(2,1)S(1)}, u32[]{:S(2)}, u32[]{:S(2)}) collective-permute-start(bf16[2,2,192,512]{3,2,1,0:T(8,128)(2,1)S(1)} %collective-permute-done.17), channel_id=1, source_target_pairs={{0,1},{1,2},{2,3},{3,4},{4,5},{5,6},{6,7},{7,8},{8,9},{9,10},{10,1... | collective-permute-start | bytes 2359304 | tf_op jit(solution)/shard_map/ppermute | solution.py:22
  238.4 13.9 %collective-permute-start.19 = (bf16[2,2,192,512]{3,2,1,0:T(8,128)(2,1)S(1)}, bf16[2,2,192,512]{3,2,1,0:T(8,128)(2,1)S(1)}, u32[]{:S(2)}, u32[]{:S(2)}) collective-permute-start(bf16[2,2,192,512]{3,2,1,0:T(8,128)(2,1)S(1)} %collective-permute-done.18), channel_id=1, source_target_pairs={{0,1},{1,2},{2,3},{3,4},{4,5},{5,6},{6,7},{7,8},{8,9},{9,10},{10,1... | collective-permute-start | bytes 2359304 | tf_op jit(solution)/shard_map/ppermute | solution.py:22
  252.4 17.9 %copy-start.3 = (s32[1,17]{1,0:T(1,128)S(1)}, s32[1,17]{1,0:T(1,128)}, u32[]{:S(2)}) copy-start(s32[1,17]{1,0:T(1,128)} %param.9) | copy-start | bytes 208
  255.6 20.2 %collective-permute-start.20 = (bf16[8,2,192,512]{3,2,1,0:T(8,128)(2,1)}, bf16[8,2,192,512]{3,2,1,0:T(8,128)(2,1)}, u32[]{:S(2)}, u32[]{:S(2)}) collective-permute-start(bf16[8,2,192,512]{3,2,1,0:T(8,128)(2,1)} %get-tuple-element.13), channel_id=1, source_target_pairs={{0,32},{32,0},{64,96},{96,64},{128,160},{160,128},{192,224},{224,1... | collective-permute-start | bytes 9437192 | tf_op jit(solution)/shard_map/ppermute | solution.py:63
  304.4 64.4 %copy-start.1 = (bf16[1,192,6144]{2,1,0:T(8,128)(2,1)S(1)}, bf16[1,192,6144]{2,1,0:T(8,128)(2,1)}, u32[]{:S(2)}) copy-start(bf16[1,192,6144]{2,1,0:T(8,128)(2,1)} %param.6) | copy-start | bytes 7077892
  (1 other events, 17.7 us)

commit v4 on v2

--- a/solution.py
+++ b/solution.py
@@ -31,6 +31,27 @@
 
 def position_of(k, z, ring):
     return ((z - k % ring) % ring) * 2 + k // ring
+
+
+def reduce_scatter_aux(parts, naux):
+    nx = naux // 4
+    me = lax.axis_index("aux")
+    c_me = me % 2
+    y_me = (me // 2) % 2
+    x_me = me // 4
+    shaped = parts.reshape((parts.shape[0], nx, 2, 2) + parts.shape[2:])
+    keep = jnp.take(shaped, c_me, axis=3)
+    send = jnp.take(shaped, 1 - c_me, axis=3)
+    on_chip = keep + lax.ppermute(send, "aux", [(i, i ^ 1) for i in range(naux)])
+    total = jnp.take(on_chip, x_me, axis=1)
+    for dx in range(1, nx):
+        perm = [(i, ((i // 4 + dx) % nx) * 4 + i % 4) for i in range(naux)]
+        total = total + lax.ppermute(
+            jnp.take(on_chip, (x_me + dx) % nx, axis=1), "aux", perm
+        )
+    mine = jnp.take(total, y_me, axis=1)
+    theirs = jnp.take(total, 1 - y_me, axis=1)
+    return mine + lax.ppermute(theirs, "aux", [(i, i ^ 2) for i in range(naux)])
 
 
 def local(chol_vectors, occ_coeff, tile_pairs, tile_owner):
@@ -69,9 +90,8 @@
         "sao,sbo->sab", left_rows, right_rows, preferred_element_type=jnp.float32
     )
     slots = partial_tiles.shape[0]
-    split = partial_tiles.reshape(slots, naux, block // naux, block).transpose(1, 0, 2, 3)
-    pieces = lax.all_to_all(split, "aux", 0, 0, tiled=True)
-    return jnp.sum(pieces, axis=0)
+    split = partial_tiles.reshape(slots, naux, block // naux, block)
+    return reduce_scatter_aux(split, naux)
 
 
 def solution(mesh):

time: 315 us -> 306 us (0.971); the launches traced: 314 us -> 302 us
  blocking collectives: 66.1 us -> 0 us
  starting transfers between devices: 135 us -> 160 us
  waiting for transfers between devices: 42.2 us -> 62.8 us
  local copies, waits for them, and re-layouts: 49.7 us -> 54.6 us
  other arithmetic: 6.72 us -> 10.2 us
    all_to_all x1 -> x0, blocking collectives: 66.1 us -> none  [local(): pieces = lax.all_to_all(split, 'aux', 0, 0, tiled=True)]
    ppermute x0 -> x5, starting transfers between devices: none -> 24.3 us  [the longest x1 10.5 us: reduce_scatter_aux(): lax.ppermute(send, 'aux', [(i, i ^ 1) for i in range(naux)])]
    ppermute x0 -> x5, waiting for transfers between devices: none -> 21.5 us  [the longest x3 13 us: reduce_scatter_aux(): lax.ppermute(jnp.take(on_chip, (x_me + dx) % nx, axis=1), 'aux', perm)]
    add x0 -> x3, other arithmetic: none -> 4.87 us  [the longest x1 2.8 us: reduce_scatter_aux(): keep + lax.ppermute(send, 'aux', [(i, i ^ 1) for i in range(naux)])]
    select_n x0 -> x4, local copies, waits for them, and re-layouts: none -> 4.72 us  [the longest x3 3.27 us: reduce_scatter_aux(): jnp.take(on_chip, (x_me + dx) % nx, axis=1)]
    another operation x0 -> x1, local copies, waits for them, and re-layouts: none -> 4.64 us  [reduce_scatter_aux(): shaped = parts.reshape((parts.shape[0], nx, 2, 2) + parts.shape[2:])]
    reshape x1 -> x0, local copies, waits for them, and re-layouts: 4.62 us -> none  [local(): partial_tiles.reshape(slots, naux, block // naux, block)]
    reduce_sum x1 -> x0, other arithmetic: 3.54 us -> none  [local(): return jnp.sum(pieces, axis=0)]
  transfers between devices with their start and end apart: 35 -> 40, of which waited for: 20 -> 24; matrix products, arithmetic and copies ran while one was open for 8% -> 9% of each run, Pallas kernels for 0% -> 0%
where the time goes in v4:
time: 306 us; the launch traced here: 302 us
  starting transfers between devices  160 us (52%)
  waiting for transfers between devices  62.8 us (21%)
  local copies, waits for them, and re-layouts  54.6 us (18%)
  matrix products  13.4 us (4%)
  other arithmetic  10.2 us (3%)
    ppermute x14, starting transfers between devices, ring_gather(): from_right = lax.ppermute(from_right, 'row', send_left)  70.4 us
    ppermute x14, waiting for transfers between devices, ring_gather(): from_left = lax.ppermute(from_left, 'row', send_right)  28.6 us
    ppermute x14, starting transfers between devices, ring_gather(): from_left = lax.ppermute(from_left, 'row', send_right)  28.4 us
    unnamed x37, local copies, waits for them, and re-layouts  23.1 us
    ppermute x3, waiting for transfers between devices, reduce_scatter_aux(): lax.ppermute(jnp.take(on_chip, (x_me + dx) % nx, axis=1), 'aux', perm)  13 us
    ppermute x1, starting transfers between devices, local(): other_ring = lax.ppermute(mine_ring, 'aux', partner)  12.1 us
    ppermute x1, starting transfers between devices, reduce_scatter_aux(): lax.ppermute(send, 'aux', [(i, i ^ 1) for i in range(naux)])  10.5 us
    ppermute x3, starting transfers between devices, reduce_scatter_aux(): lax.ppermute(jnp.take(on_chip, (x_me + dx) % nx, axis=1), 'aux', perm)  10.5 us
  transfers between devices with their start and end apart: 40, of which 24 were waited for; matrix products, arithmetic and copies ran while one was open for 9% of the time, Pallas kernels for 0%

profile of v4, /device:TPU:1, one launch (start us, length us, event | category | flops | bytes accessed | tf_op | source)
XLA Modules:
  0.0 301.5 jit_solution(8113107486351850205)
XLA Ops:
  0.9 5.6 %collective-permute-start = (bf16[192,256]{1,0:T(8,128)(2,1)S(1)}, bf16[192,256]{1,0:T(8,128)(2,1)S(1)}, u32[]{:S(2)}, u32[]{:S(2)}) collective-permute-start(bf16[192,256]{1,0:T(8,128)(2,1)S(1)} %constant_dynamic-slice_fusion), channel_id=1, source_target_pairs={{0,16},{1,17},{2,18},{3,19},{4,20},{5,21},{6,22},{7,23},{8,24},{9,... | collective-permute-start | bytes 294920 | tf_op jit(solution)/shard_map/ppermute | solution.py:12
  12.2 9.5 %collective-permute-start.9 = (bf16[2,192,256]{2,1,0:T(8,128)(2,1)S(1)}, bf16[2,192,256]{2,1,0:T(8,128)(2,1)S(1)}, u32[]{:S(2)}, u32[]{:S(2)}) collective-permute-start(bf16[2,192,256]{2,1,0:T(8,128)(2,1)S(1)} %maximum_select_fusion.9), channel_id=1, source_target_pairs={{0,15},{1,0},{2,1},{3,2},{4,3},{5,4},{6,5},{7,6},{8,7},{9,8},{10,9... | collective-permute-start | bytes 589832 | tf_op jit(solution)/shard_map/ppermute | solution.py:22
  32.7 4.6 %collective-permute-start.11 = (bf16[2,192,256]{2,1,0:T(8,128)(2,1)S(1)}, bf16[2,192,256]{2,1,0:T(8,128)(2,1)S(1)}, u32[]{:S(2)}, u32[]{:S(2)}) collective-permute-start(bf16[2,192,256]{2,1,0:T(8,128)(2,1)S(1)} %collective-permute-done.10), channel_id=1, source_target_pairs={{0,15},{1,0},{2,1},{3,2},{4,3},{5,4},{6,5},{7,6},{8,7},{9,8},{10,9... | collective-permute-start | bytes 589832 | tf_op jit(solution)/shard_map/ppermute | solution.py:22
  40.4 4.6 %collective-permute-start.12 = (bf16[2,192,256]{2,1,0:T(8,128)(2,1)S(1)}, bf16[2,192,256]{2,1,0:T(8,128)(2,1)S(1)}, u32[]{:S(2)}, u32[]{:S(2)}) collective-permute-start(bf16[2,192,256]{2,1,0:T(8,128)(2,1)S(1)} %collective-permute-done.11), channel_id=1, source_target_pairs={{0,15},{1,0},{2,1},{3,2},{4,3},{5,4},{6,5},{7,6},{8,7},{9,8},{10,9... | collective-permute-start | bytes 589832 | tf_op jit(solution)/shard_map/ppermute | solution.py:22
  48.0 4.6 %collective-permute-start.13 = (bf16[2,192,256]{2,1,0:T(8,128)(2,1)S(1)}, bf16[2,192,256]{2,1,0:T(8,128)(2,1)S(1)}, u32[]{:S(2)}, u32[]{:S(2)}) collective-permute-start(bf16[2,192,256]{2,1,0:T(8,128)(2,1)S(1)} %collective-permute-done.12), channel_id=1, source_target_pairs={{0,15},{1,0},{2,1},{3,2},{4,3},{5,4},{6,5},{7,6},{8,7},{9,8},{10,9... | collective-permute-start | bytes 589832 | tf_op jit(solution)/shard_map/ppermute | solution.py:22
  64.0 4.9 %collective-permute-start.15 = (bf16[2,192,256]{2,1,0:T(8,128)(2,1)S(1)}, bf16[2,192,256]{2,1,0:T(8,128)(2,1)S(1)}, u32[]{:S(2)}, u32[]{:S(2)}) collective-permute-start(bf16[2,192,256]{2,1,0:T(8,128)(2,1)S(1)} %collective-permute-done.14), channel_id=1, source_target_pairs={{0,15},{1,0},{2,1},{3,2},{4,3},{5,4},{6,5},{7,6},{8,7},{9,8},{10,9... | collective-permute-start | bytes 589832 | tf_op jit(solution)/shard_map/ppermute | solution.py:22
  73.7 5.0 %collective-permute-start.16 = (bf16[192,256]{1,0:T(8,128)(2,1)S(1)}, bf16[192,256]{1,0:T(8,128)(2,1)S(1)}, u32[]{:S(2)}, u32[]{:S(2)}) collective-permute-start(bf16[192,256]{1,0:T(8,128)(2,1)S(1)} %slice_bitcast_fusion.2), channel_id=1, source_target_pairs={{0,15},{1,0},{2,1},{3,2},{4,3},{5,4},{6,5},{7,6},{8,7},{9,8},{10,9... | collective-permute-start | bytes 294920 | tf_op jit(solution)/shard_map/ppermute | solution.py:26
  86.0 12.1 %collective-permute-start.17 = (bf16[32,192,256]{2,1,0:T(8,128)(2,1)}, bf16[32,192,256]{2,1,0:T(8,128)(2,1)}, u32[]{:S(2)}, u32[]{:S(2)}) collective-permute-start(bf16[32,192,256]{2,1,0:T(8,128)(2,1)} %bitcast.27), channel_id=1, source_target_pairs={{0,32},{32,0},{64,96},{96,64},{128,160},{160,128},{192,224},{224,1... | collective-permute-start | bytes 9437192 | tf_op jit(solution)/shard_map/ppermute | solution.py:70
  108.9 8.4 %fusion.20 = bf16[192,512]{1,0:T(8,128)(2,1)S(1)} fusion(bf16[32,192,256]{2,1,0:T(8,128)(2,1)} %collective-permute-done.17, bf16[32,192,256]{2,1,0:T(8,128)(2,1)} %bitcast.27, pred[]{:T(512)S(6)} %eq.24, bf16[32,192,192]{2,1,0:T(8,128)(2,1)} %gather_fusion, pred[32]{0:T(512)(128)(4,1)S(1)} %compare_and_fusion.2), kind=kOutput, calls=%fused_computation.25 | convolution fusion | flops 1237549056 | bytes 8847393 | tf_op jit(solution)/shard_map/dot_general | solution.py:81
  117.3 4.8 %collective-permute-start.18 = (bf16[192,512]{1,0:T(8,128)(2,1)S(1)}, bf16[192,512]{1,0:T(8,128)(2,1)S(1)}, u32[]{:S(2)}, u32[]{:S(2)}) collective-permute-start(bf16[192,512]{1,0:T(8,128)(2,1)S(1)} %fusion.20), channel_id=1, source_target_pairs={{0,16},{1,17},{2,18},{3,19},{4,20},{5,21},{6,22},{7,23},{8,24},{9,... | collective-permute-start | bytes 589832 | tf_op jit(solution)/shard_map/ppermute | solution.py:12
  122.1 5.1 %collective-permute-done.18 = bf16[192,512]{1,0:T(8,128)(2,1)S(1)} collective-permute-done((bf16[192,512]{1,0:T(8,128)(2,1)S(1)}, bf16[192,512]{1,0:T(8,128)(2,1)S(1)}, u32[]{:S(2)}, u32[]{:S(2)}) %collective-permute-start.18) | collective-permute-done | bytes 196640 | tf_op jit(solution)/shard_map/ppermute | solution.py:12
  129.2 5.2 %collective-permute-start.27 = (bf16[2,192,512]{2,1,0:T(8,128)(2,1)S(1)}, bf16[2,192,512]{2,1,0:T(8,128)(2,1)S(1)}, u32[]{:S(2)}, u32[]{:S(2)}) collective-permute-start(bf16[2,192,512]{2,1,0:T(8,128)(2,1)S(1)} %maximum_select_fusion.7), channel_id=1, source_target_pairs={{0,15},{1,0},{2,1},{3,2},{4,3},{5,4},{6,5},{7,6},{8,7},{9,8},{10,9... | collective-permute-start | bytes 1179656 | tf_op jit(solution)/shard_map/ppermute | solution.py:22
  134.3 6.7 %collective-permute-done.19 = bf16[2,192,512]{2,1,0:T(8,128)(2,1)S(1)} collective-permute-done((bf16[2,192,512]{2,1,0:T(8,128)(2,1)S(1)}, bf16[2,192,512]{2,1,0:T(8,128)(2,1)S(1)}, u32[]{:S(2)}, u32[]{:S(2)}) %collective-permute-start.19) | collective-permute-done | bytes 393248 | tf_op jit(solution)/shard_map/ppermute | solution.py:21
  142.9 4.6 %collective-permute-start.28 = (bf16[2,192,512]{2,1,0:T(8,128)(2,1)S(1)}, bf16[2,192,512]{2,1,0:T(8,128)(2,1)S(1)}, u32[]{:S(2)}, u32[]{:S(2)}) collective-permute-start(bf16[2,192,512]{2,1,0:T(8,128)(2,1)S(1)} %collective-permute-done.27), channel_id=1, source_target_pairs={{0,15},{1,0},{2,1},{3,2},{4,3},{5,4},{6,5},{7,6},{8,7},{9,8},{10,9... | collective-permute-start | bytes 1179656 | tf_op jit(solution)/shard_map/ppermute | solution.py:22
  147.7 5.6 %collective-permute-done.20 = bf16[2,192,512]{2,1,0:T(8,128)(2,1)S(1)} collective-permute-done((bf16[2,192,512]{2,1,0:T(8,128)(2,1)S(1)}, bf16[2,192,512]{2,1,0:T(8,128)(2,1)S(1)}, u32[]{:S(2)}, u32[]{:S(2)}) %collective-permute-start.20) | collective-permute-done | bytes 393248 | tf_op jit(solution)/shard_map/ppermute | solution.py:21
  166.9 4.7 %collective-permute-start.30 = (bf16[2,192,512]{2,1,0:T(8,128)(2,1)S(1)}, bf16[2,192,512]{2,1,0:T(8,128)(2,1)S(1)}, u32[]{:S(2)}, u32[]{:S(2)}) collective-permute-start(bf16[2,192,512]{2,1,0:T(8,128)(2,1)S(1)} %collective-permute-done.29), channel_id=1, source_target_pairs={{0,15},{1,0},{2,1},{3,2},{4,3},{5,4},{6,5},{7,6},{8,7},{9,8},{10,9... | collective-permute-start | bytes 1179656 | tf_op jit(solution)/shard_map/ppermute | solution.py:22
  198.7 5.0 %collective-permute-start.33 = (bf16[2,192,512]{2,1,0:T(8,128)(2,1)S(1)}, bf16[2,192,512]{2,1,0:T(8,128)(2,1)S(1)}, u32[]{:S(2)}, u32[]{:S(2)}) collective-permute-start(bf16[2,192,512]{2,1,0:T(8,128)(2,1)S(1)} %collective-permute-done.32), channel_id=1, source_target_pairs={{0,15},{1,0},{2,1},{3,2},{4,3},{5,4},{6,5},{7,6},{8,7},{9,8},{10,9... | collective-permute-start | bytes 1179656 | tf_op jit(solution)/shard_map/ppermute | solution.py:22
  208.8 5.2 %collective-permute-start.34 = (bf16[192,512]{1,0:T(8,128)(2,1)S(1)}, bf16[192,512]{1,0:T(8,128)(2,1)S(1)}, u32[]{:S(2)}, u32[]{:S(2)}) collective-permute-start(bf16[192,512]{1,0:T(8,128)(2,1)S(1)} %slice_bitcast_fusion), channel_id=1, source_target_pairs={{0,15},{1,0},{2,1},{3,2},{4,3},{5,4},{6,5},{7,6},{8,7},{9,8},{10,9... | collective-permute-start | bytes 589832 | tf_op jit(solution)/shard_map/ppermute | solution.py:26
  227.8 5.6 %gather_fusion.3 = bf16[17,192,512]{2,1,0:T(8,128)(2,1)} fusion(bf16[32,192,512]{2,1,0:T(8,128)(2,1)} %bitcast.52, s32[1024]{0:T(1024)S(1)} %pad_clamp_fusion), kind=kCustom, calls=%fused_computation.1.clone | custom fusion | bytes 6684740 | tf_op jit(solution)/shard_map/jit(_take)/gather | solution.py:88
  233.4 5.0 %fusion.7 = f32[17,192,192]{2,1,0:T(8,128)} fusion(bf16[17,192,512]{2,1,0:T(8,128)(2,1)} %gather_fusion.3, bf16[17,192,512]{2,1,0:T(8,128)(2,1)S(1)} %gather_fusion.2, pred[17]{0:T(512)(128)(4,1)S(1)} %get-tuple-element.46, pred[17]{0:T(512)(128)(4,1)S(1)} %get-tuple-element.51), kind=kOutput, calls=%fused_computation.12 | convolution fusion | flops 645070848 | bytes 9191458 | tf_op jit(solution)/shard_map/sao,sbo->sab/dot_general | solution.py:89
  238.4 4.6 %reshape_reshape.3 = f32[17,4,2,2,12,192]{5,4,3,2,1,0:T(8,128)} reshape(f32[17,192,192]{2,1,0:T(8,128)} %fusion.7) | data formatting | bytes 5013504 | tf_op jit(solution)/shard_map/reshape;reshape | solution.py:42
  246.4 10.5 %collective-permute-start.35 = (f32[17,4,2,12,192]{4,1,3,2,0:T(4,128)S(1)}, f32[17,4,2,12,192]{4,1,3,2,0:T(4,128)}, u32[]{:S(2)}, u32[]{:S(2)}) collective-permute-start(f32[17,4,2,12,192]{4,1,3,2,0:T(4,128)S(1)} %copy.23), channel_id=1, source_target_pairs={{0,32},{32,0},{64,96},{96,64},{128,160},{160,128},{192,224},{224,1... | collective-permute-start | bytes 3760136 | tf_op jit(solution)/shard_map/ppermute | solution.py:45
  278.5 10.0 %collective-permute-done.37 = f32[17,2,12,192]{3,1,2,0:T(2,128)S(1)} collective-permute-done((f32[17,2,12,192]{3,1,2,0:T(2,128)}, f32[17,2,12,192]{3,1,2,0:T(2,128)S(1)}, u32[]{:S(2)}, u32[]{:S(2)}) %collective-permute-start.37) | collective-permute-done | bytes 313376 | tf_op jit(solution)/shard_map/ppermute | solution.py:49
  295.5 5.3 %collective-permute-done.39 = f32[17,12,192]{2,1,0:T(8,128)S(1)} collective-permute-done((f32[17,12,192]{2,1,0:T(8,128)S(1)}, f32[17,12,192]{2,1,0:T(8,128)S(1)}, u32[]{:S(2)}, u32[]{:S(2)}) %collective-permute-start.39) | collective-permute-done | bytes 156704 | tf_op jit(solution)/shard_map/ppermute | solution.py:54
  (136 shorter events, 153.5 us)
Async XLA Ops:
  8.6 14.6 %collective-permute-start.1 = (bf16[2,192,256]{2,1,0:T(8,128)(2,1)S(1)}, bf16[2,192,256]{2,1,0:T(8,128)(2,1)S(1)}, u32[]{:S(2)}, u32[]{:S(2)}) collective-permute-start(bf16[2,192,256]{2,1,0:T(8,128)(2,1)S(1)} %maximum_select_fusion.9), channel_id=1, source_target_pairs={{0,1},{1,2},{2,3},{3,4},{4,5},{5,6},{6,7},{7,8},{8,9},{9,10},{10,1... | collective-permute-start | bytes 589832 | tf_op jit(solution)/shard_map/ppermute | solution.py:21
  12.2 12.9 %collective-permute-start.9 = (bf16[2,192,256]{2,1,0:T(8,128)(2,1)S(1)}, bf16[2,192,256]{2,1,0:T(8,128)(2,1)S(1)}, u32[]{:S(2)}, u32[]{:S(2)}) collective-permute-start(bf16[2,192,256]{2,1,0:T(8,128)(2,1)S(1)} %maximum_select_fusion.9), channel_id=1, source_target_pairs={{0,15},{1,0},{2,1},{3,2},{4,3},{5,4},{6,5},{7,6},{8,7},{9,8},{10,9... | collective-permute-start | bytes 589832 | tf_op jit(solution)/shard_map/ppermute | solution.py:22
  62.1 9.7 %collective-permute-start.7 = (bf16[2,192,256]{2,1,0:T(8,128)(2,1)S(1)}, bf16[2,192,256]{2,1,0:T(8,128)(2,1)S(1)}, u32[]{:S(2)}, u32[]{:S(2)}) collective-permute-start(bf16[2,192,256]{2,1,0:T(8,128)(2,1)S(1)} %collective-permute-done.6), channel_id=1, source_target_pairs={{0,1},{1,2},{2,3},{3,4},{4,5},{5,6},{6,7},{7,8},{8,9},{9,10},{10,1... | collective-permute-start | bytes 589832 | tf_op jit(solution)/shard_map/ppermute | solution.py:21
  64.0 9.7 %collective-permute-start.15 = (bf16[2,192,256]{2,1,0:T(8,128)(2,1)S(1)}, bf16[2,192,256]{2,1,0:T(8,128)(2,1)S(1)}, u32[]{:S(2)}, u32[]{:S(2)}) collective-permute-start(bf16[2,192,256]{2,1,0:T(8,128)(2,1)S(1)} %collective-permute-done.14), channel_id=1, source_target_pairs={{0,15},{1,0},{2,1},{3,2},{4,3},{5,4},{6,5},{7,6},{8,7},{9,8},{10,9... | collective-permute-start | bytes 589832 | tf_op jit(solution)/shard_map/ppermute | solution.py:22
  86.0 22.9 %collective-permute-start.17 = (bf16[32,192,256]{2,1,0:T(8,128)(2,1)}, bf16[32,192,256]{2,1,0:T(8,128)(2,1)}, u32[]{:S(2)}, u32[]{:S(2)}) collective-permute-start(bf16[32,192,256]{2,1,0:T(8,128)(2,1)} %bitcast.27), channel_id=1, source_target_pairs={{0,32},{32,0},{64,96},{96,64},{128,160},{160,128},{192,224},{224,1... | collective-permute-start | bytes 9437192 | tf_op jit(solution)/shard_map/ppermute | solution.py:70
  117.3 9.9 %collective-permute-start.18 = (bf16[192,512]{1,0:T(8,128)(2,1)S(1)}, bf16[192,512]{1,0:T(8,128)(2,1)S(1)}, u32[]{:S(2)}, u32[]{:S(2)}) collective-permute-start(bf16[192,512]{1,0:T(8,128)(2,1)S(1)} %fusion.20), channel_id=1, source_target_pairs={{0,16},{1,17},{2,18},{3,19},{4,20},{5,21},{6,22},{7,23},{8,24},{9,... | collective-permute-start | bytes 589832 | tf_op jit(solution)/shard_map/ppermute | solution.py:12
  127.2 13.8 %collective-permute-start.19 = (bf16[2,192,512]{2,1,0:T(8,128)(2,1)S(1)}, bf16[2,192,512]{2,1,0:T(8,128)(2,1)S(1)}, u32[]{:S(2)}, u32[]{:S(2)}) collective-permute-start(bf16[2,192,512]{2,1,0:T(8,128)(2,1)S(1)} %maximum_select_fusion.7), channel_id=1, source_target_pairs={{0,1},{1,2},{2,3},{3,4},{4,5},{5,6},{6,7},{7,8},{8,9},{9,10},{10,1... | collective-permute-start | bytes 1179656 | tf_op jit(solution)/shard_map/ppermute | solution.py:21
  129.2 13.8 %collective-permute-start.27 = (bf16[2,192,512]{2,1,0:T(8,128)(2,1)S(1)}, bf16[2,192,512]{2,1,0:T(8,128)(2,1)S(1)}, u32[]{:S(2)}, u32[]{:S(2)}) collective-permute-start(bf16[2,192,512]{2,1,0:T(8,128)(2,1)S(1)} %maximum_select_fusion.7), channel_id=1, source_target_pairs={{0,15},{1,0},{2,1},{3,2},{4,3},{5,4},{6,5},{7,6},{8,7},{9,8},{10,9... | collective-permute-start | bytes 1179656 | tf_op jit(solution)/shard_map/ppermute | solution.py:22
  141.0 12.3 %collective-permute-start.20 = (bf16[2,192,512]{2,1,0:T(8,128)(2,1)S(1)}, bf16[2,192,512]{2,1,0:T(8,128)(2,1)S(1)}, u32[]{:S(2)}, u32[]{:S(2)}) collective-permute-start(bf16[2,192,512]{2,1,0:T(8,128)(2,1)S(1)} %collective-permute-done.19), channel_id=1, source_target_pairs={{0,1},{1,2},{2,3},{3,4},{4,5},{5,6},{6,7},{7,8},{8,9},{9,10},{10,1... | collective-permute-start | bytes 1179656 | tf_op jit(solution)/shard_map/ppermute | solution.py:21
  142.9 12.9 %collective-permute-start.28 = (bf16[2,192,512]{2,1,0:T(8,128)(2,1)S(1)}, bf16[2,192,512]{2,1,0:T(8,128)(2,1)S(1)}, u32[]{:S(2)}, u32[]{:S(2)}) collective-permute-start(bf16[2,192,512]{2,1,0:T(8,128)(2,1)S(1)} %collective-permute-done.27), channel_id=1, source_target_pairs={{0,15},{1,0},{2,1},{3,2},{4,3},{5,4},{6,5},{7,6},{8,7},{9,8},{10,9... | collective-permute-start | bytes 1179656 | tf_op jit(solution)/shard_map/ppermute | solution.py:22
  153.3 11.6 %collective-permute-start.21 = (bf16[2,192,512]{2,1,0:T(8,128)(2,1)S(1)}, bf16[2,192,512]{2,1,0:T(8,128)(2,1)}, u32[]{:S(2)}, u32[]{:S(2)}) collective-permute-start(bf16[2,192,512]{2,1,0:T(8,128)(2,1)S(1)} %collective-permute-done.20), channel_id=1, source_target_pairs={{0,1},{1,2},{2,3},{3,4},{4,5},{5,6},{6,7},{7,8},{8,9},{9,10},{10,1... | collective-permute-start | bytes 1179656 | tf_op jit(solution)/shard_map/ppermute | solution.py:21
  155.8 11.0 %collective-permute-start.29 = (bf16[2,192,512]{2,1,0:T(8,128)(2,1)S(1)}, bf16[2,192,512]{2,1,0:T(8,128)(2,1)S(1)}, u32[]{:S(2)}, u32[]{:S(2)}) collective-permute-start(bf16[2,192,512]{2,1,0:T(8,128)(2,1)S(1)} %collective-permute-done.28), channel_id=1, source_target_pairs={{0,15},{1,0},{2,1},{3,2},{4,3},{5,4},{6,5},{7,6},{8,7},{9,8},{10,9... | collective-permute-start | bytes 1179656 | tf_op jit(solution)/shard_map/ppermute | solution.py:22
  164.9 10.9 %collective-permute-start.22 = (bf16[2,192,512]{2,1,0:T(8,128)(2,1)}, bf16[2,192,512]{2,1,0:T(8,128)(2,1)}, u32[]{:S(2)}, u32[]{:S(2)}) collective-permute-start(bf16[2,192,512]{2,1,0:T(8,128)(2,1)} %collective-permute-done.21), channel_id=1, source_target_pairs={{0,1},{1,2},{2,3},{3,4},{4,5},{5,6},{6,7},{7,8},{8,9},{9,10},{10,1... | collective-permute-start | bytes 1179656 | tf_op jit(solution)/shard_map/ppermute | solution.py:21
  166.9 11.6 %collective-permute-start.30 = (bf16[2,192,512]{2,1,0:T(8,128)(2,1)S(1)}, bf16[2,192,512]{2,1,0:T(8,128)(2,1)S(1)}, u32[]{:S(2)}, u32[]{:S(2)}) collective-permute-start(bf16[2,192,512]{2,1,0:T(8,128)(2,1)S(1)} %collective-permute-done.29), channel_id=1, source_target_pairs={{0,15},{1,0},{2,1},{3,2},{4,3},{5,4},{6,5},{7,6},{8,7},{9,8},{10,9... | collective-permute-start | bytes 1179656 | tf_op jit(solution)/shard_map/ppermute | solution.py:22
  175.8 9.9 %collective-permute-start.23 = (bf16[2,192,512]{2,1,0:T(8,128)(2,1)}, bf16[2,192,512]{2,1,0:T(8,128)(2,1)S(1)}, u32[]{:S(2)}, u32[]{:S(2)}) collective-permute-start(bf16[2,192,512]{2,1,0:T(8,128)(2,1)} %collective-permute-done.22), channel_id=1, source_target_pairs={{0,1},{1,2},{2,3},{3,4},{4,5},{5,6},{6,7},{7,8},{8,9},{9,10},{10,1... | collective-permute-start | bytes 1179656 | tf_op jit(solution)/shard_map/ppermute | solution.py:21
  178.5 10.9 %collective-permute-start.31 = (bf16[2,192,512]{2,1,0:T(8,128)(2,1)S(1)}, bf16[2,192,512]{2,1,0:T(8,128)(2,1)S(1)}, u32[]{:S(2)}, u32[]{:S(2)}) collective-permute-start(bf16[2,192,512]{2,1,0:T(8,128)(2,1)S(1)} %collective-permute-done.30), channel_id=1, source_target_pairs={{0,15},{1,0},{2,1},{3,2},{4,3},{5,4},{6,5},{7,6},{8,7},{9,8},{10,9... | collective-permute-start | bytes 1179656 | tf_op jit(solution)/shard_map/ppermute | solution.py:22
  185.7 10.0 %collective-permute-start.24 = (bf16[2,192,512]{2,1,0:T(8,128)(2,1)S(1)}, bf16[2,192,512]{2,1,0:T(8,128)(2,1)S(1)}, u32[]{:S(2)}, u32[]{:S(2)}) collective-permute-start(bf16[2,192,512]{2,1,0:T(8,128)(2,1)S(1)} %collective-permute-done.23), channel_id=1, source_target_pairs={{0,1},{1,2},{2,3},{3,4},{4,5},{5,6},{6,7},{7,8},{8,9},{9,10},{10,1... | collective-permute-start | bytes 1179656 | tf_op jit(solution)/shard_map/ppermute | solution.py:21
  195.8 9.7 %collective-permute-start.25 = (bf16[2,192,512]{2,1,0:T(8,128)(2,1)S(1)}, bf16[2,192,512]{2,1,0:T(8,128)(2,1)S(1)}, u32[]{:S(2)}, u32[]{:S(2)}) collective-permute-start(bf16[2,192,512]{2,1,0:T(8,128)(2,1)S(1)} %collective-permute-done.24), channel_id=1, source_target_pairs={{0,1},{1,2},{2,3},{3,4},{4,5},{5,6},{6,7},{7,8},{8,9},{9,10},{10,1... | collective-permute-start | bytes 1179656 | tf_op jit(solution)/shard_map/ppermute | solution.py:21
  198.7 10.1 %collective-permute-start.33 = (bf16[2,192,512]{2,1,0:T(8,128)(2,1)S(1)}, bf16[2,192,512]{2,1,0:T(8,128)(2,1)S(1)}, u32[]{:S(2)}, u32[]{:S(2)}) collective-permute-start(bf16[2,192,512]{2,1,0:T(8,128)(2,1)S(1)} %collective-permute-done.32), channel_id=1, source_target_pairs={{0,15},{1,0},{2,1},{3,2},{4,3},{5,4},{6,5},{7,6},{8,7},{9,8},{10,9... | collective-permute-start | bytes 1179656 | tf_op jit(solution)/shard_map/ppermute | solution.py:22
  205.5 9.3 %collective-permute-start.26 = (bf16[192,512]{1,0:T(8,128)(2,1)S(1)}, bf16[192,512]{1,0:T(8,128)(2,1)S(1)}, u32[]{:S(2)}, u32[]{:S(2)}) collective-permute-start(bf16[192,512]{1,0:T(8,128)(2,1)S(1)} %slice_bitcast_fusion.1), channel_id=1, source_target_pairs={{0,1},{1,2},{2,3},{3,4},{4,5},{5,6},{6,7},{7,8},{8,9},{9,10},{10,1... | collective-permute-start | bytes 589832 | tf_op jit(solution)/shard_map/ppermute | solution.py:25
  246.4 13.8 %collective-permute-start.35 = (f32[17,4,2,12,192]{4,1,3,2,0:T(4,128)S(1)}, f32[17,4,2,12,192]{4,1,3,2,0:T(4,128)}, u32[]{:S(2)}, u32[]{:S(2)}) collective-permute-start(f32[17,4,2,12,192]{4,1,3,2,0:T(4,128)S(1)} %copy.23), channel_id=1, source_target_pairs={{0,32},{32,0},{64,96},{96,64},{128,160},{160,128},{192,224},{224,1... | collective-permute-start | bytes 3760136 | tf_op jit(solution)/shard_map/ppermute | solution.py:45
  264.3 14.1 %collective-permute-start.36 = (f32[17,2,12,192]{3,1,2,0:T(2,128)}, f32[17,2,12,192]{3,1,2,0:T(2,128)S(1)}, u32[]{:S(2)}, u32[]{:S(2)}) collective-permute-start(f32[17,2,12,192]{3,1,2,0:T(2,128)} %copy.25), channel_id=1, source_target_pairs={{0,128},{32,160},{64,192},{96,224},{128,256},{160,288},{192,320},{... | collective-permute-start | bytes 940040 | tf_op jit(solution)/shard_map/ppermute | solution.py:49
  268.6 19.9 %collective-permute-start.37 = (f32[17,2,12,192]{3,1,2,0:T(2,128)}, f32[17,2,12,192]{3,1,2,0:T(2,128)S(1)}, u32[]{:S(2)}, u32[]{:S(2)}) collective-permute-start(f32[17,2,12,192]{3,1,2,0:T(2,128)} %copy.27), channel_id=1, source_target_pairs={{0,256},{32,288},{64,320},{96,352},{128,384},{160,416},{192,448},{... | collective-permute-start | bytes 940040 | tf_op jit(solution)/shard_map/ppermute | solution.py:49
  274.0 16.8 %collective-permute-start.38 = (f32[17,2,12,192]{3,1,2,0:T(2,128)}, f32[17,2,12,192]{3,1,2,0:T(2,128)}, u32[]{:S(2)}, u32[]{:S(2)}) collective-permute-start(f32[17,2,12,192]{3,1,2,0:T(2,128)} %copy.29), channel_id=1, source_target_pairs={{0,384},{32,416},{64,448},{96,480},{128,0},{160,32},{192,64},{224,... | collective-permute-start | bytes 940040 | tf_op jit(solution)/shard_map/ppermute | solution.py:49
  (21 other events, 289.9 us)

commit v5 on v4

--- a/solution.py
+++ b/solution.py
@@ -5,32 +5,37 @@
 
 
 def ring_gather(x, nrow, ring):
-    pairs = nrow // ring
     r = lax.axis_index("row")
-    yh = r // ring
     z = r % ring
-    other = lax.ppermute(x, "row", [(i, i ^ ring) for i in range(nrow)])
-    pair = jnp.where(yh == 0, jnp.stack([x, other]), jnp.stack([other, x]))
     send_right = [(i, (i // ring) * ring + (i % ring + 1) % ring) for i in range(nrow)]
     send_left = [(i, (i // ring) * ring + (i % ring - 1) % ring) for i in range(nrow)]
-    got = [None] * ring
-    got[0] = pair
-    from_left = pair
-    from_right = pair
-    for t in range(1, ring // 2):
+    across = [(i, i ^ ring) for i in range(nrow)]
+    own = [None] * ring
+    far = [None] * ring
+    own[0] = x
+    far[0] = lax.ppermute(x, "row", across)
+    from_left = lax.ppermute(x, "row", send_right)
+    from_right = lax.ppermute(x, "row", send_left)
+    own[1] = from_left
+    own[ring - 1] = from_right
+    for t in range(2, ring // 2):
+        far[t - 1] = lax.ppermute(from_left, "row", across)
+        far[ring - t + 1] = lax.ppermute(from_right, "row", across)
         from_left = lax.ppermute(from_left, "row", send_right)
         from_right = lax.ppermute(from_right, "row", send_left)
-        got[t] = from_left
-        got[ring - t] = from_right
-    low = lax.ppermute(from_left[0], "row", send_right)
-    high = lax.ppermute(from_right[1], "row", send_left)
-    got[ring // 2] = jnp.stack([low, high])
-    stacked = jnp.stack(got)
-    return stacked.reshape((ring * pairs,) + x.shape), z
+        own[t] = from_left
+        own[ring - t] = from_right
+    t = ring // 2
+    far[t - 1] = lax.ppermute(from_left, "row", across)
+    far[ring - t + 1] = lax.ppermute(from_right, "row", across)
+    own[t] = lax.ppermute(from_left, "row", send_right)
+    far[t] = lax.ppermute(own[t], "row", across)
+    return jnp.stack(own + far), z
 
 
 def position_of(k, z, ring):
-    return ((z - k % ring) % ring) * 2 + k // ring
+    yh = lax.axis_index("row") // ring
+    return jnp.where(k // ring == yh, 0, ring) + (z - k % ring) % ring
 
 
 def reduce_scatter_aux(parts, naux):
@@ -68,18 +73,22 @@
     mine_ring, z = ring_gather(mine, nrow, ring)
     partner = [(i, i ^ 1) for i in range(naux)]
     other_ring = lax.ppermute(mine_ring, "aux", partner)
-    coeff_ring = jnp.where(
-        core == 0,
-        jnp.concatenate([mine_ring, other_ring], axis=2),
-        jnp.concatenate([other_ring, mine_ring], axis=2),
-    )
 
     p = jnp.arange(nrow)
-    block_at = (p % 2) * ring + (z - p // 2) % ring
+    yh = lax.axis_index("row") // ring
+    block_at = jnp.where(p // ring == 0, yh, 1 - yh) * ring + (z - p % ring) % ring
     chol = chol_vectors[0].reshape(block, nrow, nbf // nrow)
     chol_ring = jnp.take(chol, block_at, axis=1).reshape(block, nbf)
-    half = jnp.dot(
-        chol_ring, coeff_ring.reshape(nbf, nocc), preferred_element_type=jnp.float32
+    half_mine = jnp.dot(
+        chol_ring, mine_ring.reshape(nbf, half_cols), preferred_element_type=jnp.float32
+    )
+    half_other = jnp.dot(
+        chol_ring, other_ring.reshape(nbf, half_cols), preferred_element_type=jnp.float32
+    )
+    half = jnp.where(
+        core == 0,
+        jnp.concatenate([half_mine, half_other], axis=1),
+        jnp.concatenate([half_other, half_mine], axis=1),
     ).astype(jnp.bfloat16)
 
     half_ring, _ = ring_gather(half, nrow, ring)

time: 306 us -> 453 us (1.48)
  starting transfers between devices: 160 us -> 248 us
  waiting for transfers between devices: 62.8 us -> 105 us
  local copies, waits for them, and re-layouts: 54.6 us -> 73.8 us
    ppermute x6 -> x38, starting transfers between devices: 24.5 us -> 124 us  [the longest x14 42.8 us: ring_gather(): far[t - 1] = lax.ppermute(from_left, 'row', across)]
    ppermute x6 -> x38, waiting for transfers between devices: 11.1 us -> 65 us  [the longest x14 26.1 us: ring_gather(): far[t - 1] = lax.ppermute(from_left, 'row', across)]
    ppermute x14 -> x12, starting transfers between devices: 70.4 us -> 50.1 us  [ring_gather(): from_right = lax.ppermute(from_right, 'row', send_left)]
    unnamed x37 -> x72, local copies, waits for them, and re-layouts: 23.1 us -> 42.5 us
    ppermute x14 -> x12, waiting for transfers between devices: 28.6 us -> 11.1 us  [ring_gather(): from_left = lax.ppermute(from_left, 'row', send_right)]
    ppermute x1, starting transfers between devices: 10.5 us -> 20.1 us  [reduce_scatter_aux(): lax.ppermute(send, 'aux', [(i, i ^ 1) for i in range(naux)])]
    ppermute x14 -> x12, starting transfers between devices: 28.4 us -> 23 us  [ring_gather(): from_left = lax.ppermute(from_left, 'row', send_right)]
    ppermute x1, starting transfers between devices: 12.1 us -> 17.6 us  [local(): other_ring = lax.ppermute(mine_ring, 'aux', partner)]
  transfers between devices with their start and end apart: 40 -> 68, of which waited for: 24 -> 30; matrix products, arithmetic and copies ran while one was open for 9% -> 13% of each run, Pallas kernels for 0% -> 0%
where the time goes in v5:
time: 453 us; the launch traced here: 448 us
  starting transfers between devices  248 us (55%)
  waiting for transfers between devices  105 us (23%)
  local copies, waits for them, and re-layouts  73.8 us (16%)
  matrix products  12.2 us (3%)
  other arithmetic  7.9 us (2%)
    ppermute x12, starting transfers between devices, ring_gather(): from_right = lax.ppermute(from_right, 'row', send_left)  50.1 us
    ppermute x14, starting transfers between devices, ring_gather(): far[t - 1] = lax.ppermute(from_left, 'row', across)  42.8 us
    ppermute x14, starting transfers between devices, ring_gather(): far[ring - t + 1] = lax.ppermute(from_right, 'row', across)  42.6 us
    unnamed x72, local copies, waits for them, and re-layouts  42.5 us
    ppermute x14, waiting for transfers between devices, ring_gather(): far[t - 1] = lax.ppermute(from_left, 'row', across)  26.1 us
    ppermute x14, waiting for transfers between devices, ring_gather(): far[ring - t + 1] = lax.ppermute(from_right, 'row', across)  24.7 us
    ppermute x12, starting transfers between devices, ring_gather(): from_left = lax.ppermute(from_left, 'row', send_right)  23 us
    ppermute x1, starting transfers between devices, reduce_scatter_aux(): lax.ppermute(send, 'aux', [(i, i ^ 1) for i in range(naux)])  20.1 us
  transfers between devices with their start and end apart: 68, of which 30 were waited for; matrix products, arithmetic and copies ran while one was open for 13% of the time, Pallas kernels for 0%

profile of v5, /device:TPU:1, one launch (start us, length us, event | category | flops | bytes accessed | tf_op | source)
XLA Modules:
  0.0 448.0 jit_solution(4677431917311662837)
XLA Ops:
  6.0 9.5 %collective-permute-start.8 = (bf16[192,256]{1,0:T(8,128)(2,1)S(1)}, bf16[192,256]{1,0:T(8,128)(2,1)S(1)}, u32[]{:S(2)}, u32[]{:S(2)}) collective-permute-start(bf16[192,256]{1,0:T(8,128)(2,1)S(1)} %get-tuple-element.49), channel_id=1, source_target_pairs={{0,15},{1,0},{2,1},{3,2},{4,3},{5,4},{6,5},{7,6},{8,7},{9,8},{10,9... | collective-permute-start | bytes 294920 | tf_op jit(solution)/shard_map/ppermute | solution.py:18
  15.5 4.8 %collective-permute-start.15 = (bf16[192,256]{1,0:T(8,128)(2,1)S(1)}, bf16[192,256]{1,0:T(8,128)(2,1)S(1)}, u32[]{:S(2)}, u32[]{:S(2)}) collective-permute-start(bf16[192,256]{1,0:T(8,128)(2,1)S(1)} %get-tuple-element.49), channel_id=1, source_target_pairs={{0,16},{1,17},{2,18},{3,19},{4,20},{5,21},{6,22},{7,23},{8,24},{9,... | collective-permute-start | bytes 294920 | tf_op jit(solution)/shard_map/ppermute | solution.py:16
  24.3 4.6 %collective-permute-start.9 = (bf16[192,256]{1,0:T(8,128)(2,1)S(1)}, bf16[192,256]{1,0:T(8,128)(2,1)S(1)}, u32[]{:S(2)}, u32[]{:S(2)}) collective-permute-start(bf16[192,256]{1,0:T(8,128)(2,1)S(1)} %collective-permute-done.8), channel_id=1, source_target_pairs={{0,15},{1,0},{2,1},{3,2},{4,3},{5,4},{6,5},{7,6},{8,7},{9,8},{10,9... | collective-permute-start | bytes 294920 | tf_op jit(solution)/shard_map/ppermute | solution.py:25
  28.9 4.8 %collective-permute-start.30 = (bf16[192,256]{1,0:T(8,128)(2,1)S(1)}, bf16[192,256]{1,0:T(8,128)(2,1)S(1)}, u32[]{:S(2)}, u32[]{:S(2)}) collective-permute-start(bf16[192,256]{1,0:T(8,128)(2,1)S(1)} %collective-permute-done.8), channel_id=1, source_target_pairs={{0,16},{1,17},{2,18},{3,19},{4,20},{5,21},{6,22},{7,23},{8,24},{9,... | collective-permute-start | bytes 294920 | tf_op jit(solution)/shard_map/ppermute | solution.py:23
  157.9 17.6 %collective-permute-start.31 = (bf16[32,192,256]{2,1,0:T(8,128)(2,1)}, bf16[32,192,256]{2,1,0:T(8,128)(2,1)}, u32[]{:S(2)}, u32[]{:S(2)}) collective-permute-start(bf16[32,192,256]{2,1,0:T(8,128)(2,1)} %constant_dynamic-update-slice_fusion), channel_id=1, source_target_pairs={{0,32},{32,0},{64,96},{96,64},{128,160},{160,128},{192,224},{224,1... | collective-permute-start | bytes 9437192 | tf_op jit(solution)/shard_map/ppermute | solution.py:75
  175.6 4.6 %reshape_squeeze.3 = bf16[192,32,192]{2,1,0:T(8,128)(2,1)} reshape(bf16[1,192,6144]{2,1,0:T(8,128)(2,1)S(1)} %copy-done.1) | data formatting | bytes 4718592 | tf_op jit(solution)/shard_map/reshape;squeeze | solution.py:80
  196.5 5.8 %collective-permute-start.40 = (bf16[192,512]{1,0:T(8,128)(2,1)S(1)}, bf16[192,512]{1,0:T(8,128)(2,1)S(1)}, u32[]{:S(2)}, u32[]{:S(2)}) collective-permute-start(bf16[192,512]{1,0:T(8,128)(2,1)S(1)} %fusion.13), channel_id=1, source_target_pairs={{0,15},{1,0},{2,1},{3,2},{4,3},{5,4},{6,5},{7,6},{8,7},{9,8},{10,9... | collective-permute-start | bytes 589832 | tf_op jit(solution)/shard_map/ppermute | solution.py:18
  211.8 4.6 %collective-permute-start.41 = (bf16[192,512]{1,0:T(8,128)(2,1)S(1)}, bf16[192,512]{1,0:T(8,128)(2,1)S(1)}, u32[]{:S(2)}, u32[]{:S(2)}) collective-permute-start(bf16[192,512]{1,0:T(8,128)(2,1)S(1)} %collective-permute-done.40), channel_id=1, source_target_pairs={{0,15},{1,0},{2,1},{3,2},{4,3},{5,4},{6,5},{7,6},{8,7},{9,8},{10,9... | collective-permute-start | bytes 589832 | tf_op jit(solution)/shard_map/ppermute | solution.py:25
  230.3 4.6 %collective-permute-start.43 = (bf16[192,512]{1,0:T(8,128)(2,1)S(1)}, bf16[192,512]{1,0:T(8,128)(2,1)S(1)}, u32[]{:S(2)}, u32[]{:S(2)}) collective-permute-start(bf16[192,512]{1,0:T(8,128)(2,1)S(1)} %collective-permute-done.42), channel_id=1, source_target_pairs={{0,15},{1,0},{2,1},{3,2},{4,3},{5,4},{6,5},{7,6},{8,7},{9,8},{10,9... | collective-permute-start | bytes 589832 | tf_op jit(solution)/shard_map/ppermute | solution.py:25
  238.0 4.6 %collective-permute-start.44 = (bf16[192,512]{1,0:T(8,128)(2,1)S(1)}, bf16[192,512]{1,0:T(8,128)(2,1)S(1)}, u32[]{:S(2)}, u32[]{:S(2)}) collective-permute-start(bf16[192,512]{1,0:T(8,128)(2,1)S(1)} %collective-permute-done.43), channel_id=1, source_target_pairs={{0,15},{1,0},{2,1},{3,2},{4,3},{5,4},{6,5},{7,6},{8,7},{9,8},{10,9... | collective-permute-start | bytes 589832 | tf_op jit(solution)/shard_map/ppermute | solution.py:25
  253.9 5.4 %collective-permute-done.38 = bf16[192,512]{1,0:T(8,128)(2,1)S(1)} collective-permute-done((bf16[192,512]{1,0:T(8,128)(2,1)S(1)}, bf16[192,512]{1,0:T(8,128)(2,1)S(1)}, u32[]{:S(2)}, u32[]{:S(2)}) %collective-permute-start.38) | collective-permute-done | bytes 196640 | tf_op jit(solution)/shard_map/ppermute | solution.py:24
  303.7 5.4 %collective-permute-done.52 = bf16[192,512]{1,0:T(8,128)(2,1)S(1)} collective-permute-done((bf16[192,512]{1,0:T(8,128)(2,1)S(1)}, bf16[192,512]{1,0:T(8,128)(2,1)S(1)}, u32[]{:S(2)}, u32[]{:S(2)}) %collective-permute-start.52) | collective-permute-done | bytes 196640 | tf_op jit(solution)/shard_map/ppermute | solution.py:22
  312.0 5.0 %collective-permute-done.53 = bf16[192,512]{1,0:T(8,128)(2,1)S(1)} collective-permute-done((bf16[192,512]{1,0:T(8,128)(2,1)S(1)}, bf16[192,512]{1,0:T(8,128)(2,1)S(1)}, u32[]{:S(2)}, u32[]{:S(2)}) %collective-permute-start.53) | collective-permute-done | bytes 196640 | tf_op jit(solution)/shard_map/ppermute | solution.py:22
  320.0 5.0 %collective-permute-done.54 = bf16[192,512]{1,0:T(8,128)(2,1)S(1)} collective-permute-done((bf16[192,512]{1,0:T(8,128)(2,1)S(1)}, bf16[192,512]{1,0:T(8,128)(2,1)S(1)}, u32[]{:S(2)}, u32[]{:S(2)}) %collective-permute-start.54) | collective-permute-done | bytes 196640 | tf_op jit(solution)/shard_map/ppermute | solution.py:29
  327.9 5.0 %collective-permute-done.55 = bf16[192,512]{1,0:T(8,128)(2,1)S(1)} collective-permute-done((bf16[192,512]{1,0:T(8,128)(2,1)S(1)}, bf16[192,512]{1,0:T(8,128)(2,1)S(1)}, u32[]{:S(2)}, u32[]{:S(2)}) %collective-permute-start.55) | collective-permute-done | bytes 196640 | tf_op jit(solution)/shard_map/ppermute | solution.py:32
  335.8 5.0 %collective-permute-done.56 = bf16[192,512]{1,0:T(8,128)(2,1)S(1)} collective-permute-done((bf16[192,512]{1,0:T(8,128)(2,1)S(1)}, bf16[192,512]{1,0:T(8,128)(2,1)S(1)}, u32[]{:S(2)}, u32[]{:S(2)}) %collective-permute-start.56) | collective-permute-done | bytes 196640 | tf_op jit(solution)/shard_map/ppermute | solution.py:30
  343.7 5.0 %collective-permute-done.57 = bf16[192,512]{1,0:T(8,128)(2,1)S(1)} collective-permute-done((bf16[192,512]{1,0:T(8,128)(2,1)S(1)}, bf16[192,512]{1,0:T(8,128)(2,1)S(1)}, u32[]{:S(2)}, u32[]{:S(2)}) %collective-permute-start.57) | collective-permute-done | bytes 196640 | tf_op jit(solution)/shard_map/ppermute | solution.py:23
  353.0 4.6 %collective-permute-done.58 = bf16[192,512]{1,0:T(8,128)(2,1)S(1)} collective-permute-done((bf16[192,512]{1,0:T(8,128)(2,1)S(1)}, bf16[192,512]{1,0:T(8,128)(2,1)S(1)}, u32[]{:S(2)}, u32[]{:S(2)}) %collective-permute-start.58) | collective-permute-done | bytes 196640 | tf_op jit(solution)/shard_map/ppermute | solution.py:23
  364.6 5.6 %gather_fusion.3 = bf16[17,192,512]{2,1,0:T(8,128)(2,1)} fusion(bf16[32,192,512]{2,1,0:T(8,128)(2,1)} %bitcast_dynamic-update-slice_fusion, s32[1024]{0:T(1024)S(1)} %pad_clamp_fusion), kind=kCustom, calls=%fused_computation.1.clone | custom fusion | bytes 6684740 | tf_op jit(solution)/shard_map/jit(_take)/gather | solution.py:97
  370.3 5.0 %fusion = f32[17,192,192]{2,1,0:T(8,128)} fusion(bf16[17,192,512]{2,1,0:T(8,128)(2,1)} %gather_fusion.3, bf16[17,192,512]{2,1,0:T(8,128)(2,1)S(1)} %gather_fusion.2, pred[17]{0:T(512)(128)(4,1)S(1)} %get-tuple-element.46, pred[17]{0:T(512)(128)(4,1)S(1)} %get-tuple-element.53), kind=kOutput, calls=%fused_computation.4 | convolution fusion | flops 645070848 | bytes 9191458 | tf_op jit(solution)/shard_map/sao,sbo->sab/dot_general | solution.py:98
  375.3 4.6 %reshape_reshape.3 = f32[17,4,2,2,12,192]{5,4,3,2,1,0:T(8,128)} reshape(f32[17,192,192]{2,1,0:T(8,128)} %fusion) | data formatting | bytes 5013504 | tf_op jit(solution)/shard_map/reshape;reshape | solution.py:47
  383.3 20.1 %collective-permute-start.63 = (f32[17,4,2,12,192]{4,1,3,2,0:T(4,128)S(1)}, f32[17,4,2,12,192]{4,1,3,2,0:T(4,128)}, u32[]{:S(2)}, u32[]{:S(2)}) collective-permute-start(f32[17,4,2,12,192]{4,1,3,2,0:T(4,128)S(1)} %copy.23), channel_id=1, source_target_pairs={{0,32},{32,0},{64,96},{96,64},{128,160},{160,128},{192,224},{224,1... | collective-permute-start | bytes 3760136 | tf_op jit(solution)/shard_map/ppermute | solution.py:50
  424.9 9.9 %collective-permute-done.65 = f32[17,2,12,192]{3,1,2,0:T(2,128)S(1)} collective-permute-done((f32[17,2,12,192]{3,1,2,0:T(2,128)}, f32[17,2,12,192]{3,1,2,0:T(2,128)S(1)}, u32[]{:S(2)}, u32[]{:S(2)}) %collective-permute-start.65) | collective-permute-done | bytes 313376 | tf_op jit(solution)/shard_map/ppermute | solution.py:54
  441.0 6.3 %collective-permute-done.67 = f32[17,12,192]{2,1,0:T(8,128)S(1)} collective-permute-done((f32[17,12,192]{2,1,0:T(8,128)S(1)}, f32[17,12,192]{2,1,0:T(8,128)S(1)}, u32[]{:S(2)}, u32[]{:S(2)}) %collective-permute-start.67) | collective-permute-done | bytes 156704 | tf_op jit(solution)/shard_map/ppermute | solution.py:59
  (217 shorter events, 289.6 us)
Async XLA Ops:
  1.5 18.8 %collective-permute-start = (bf16[192,256]{1,0:T(8,128)(2,1)S(1)}, bf16[192,256]{1,0:T(8,128)(2,1)S(1)}, u32[]{:S(2)}, u32[]{:S(2)}) collective-permute-start(bf16[192,256]{1,0:T(8,128)(2,1)S(1)} %get-tuple-element.49), channel_id=1, source_target_pairs={{0,1},{1,2},{2,3},{3,4},{4,5},{5,6},{6,7},{7,8},{8,9},{9,10},{10,1... | collective-permute-start | bytes 294920 | tf_op jit(solution)/shard_map/ppermute | solution.py:17
  6.0 18.2 %collective-permute-start.8 = (bf16[192,256]{1,0:T(8,128)(2,1)S(1)}, bf16[192,256]{1,0:T(8,128)(2,1)S(1)}, u32[]{:S(2)}, u32[]{:S(2)}) collective-permute-start(bf16[192,256]{1,0:T(8,128)(2,1)S(1)} %get-tuple-element.49), channel_id=1, source_target_pairs={{0,15},{1,0},{2,1},{3,2},{4,3},{5,4},{6,5},{7,6},{8,7},{9,8},{10,9... | collective-permute-start | bytes 294920 | tf_op jit(solution)/shard_map/ppermute | solution.py:18
  15.5 74.1 %collective-permute-start.15 = (bf16[192,256]{1,0:T(8,128)(2,1)S(1)}, bf16[192,256]{1,0:T(8,128)(2,1)S(1)}, u32[]{:S(2)}, u32[]{:S(2)}) collective-permute-start(bf16[192,256]{1,0:T(8,128)(2,1)S(1)} %get-tuple-element.49), channel_id=1, source_target_pairs={{0,16},{1,17},{2,18},{3,19},{4,20},{5,21},{6,22},{7,23},{8,24},{9,... | collective-permute-start | bytes 294920 | tf_op jit(solution)/shard_map/ppermute | solution.py:16
  22.3 71.4 %collective-permute-start.16 = (bf16[192,256]{1,0:T(8,128)(2,1)S(1)}, bf16[192,256]{1,0:T(8,128)(2,1)S(1)}, u32[]{:S(2)}, u32[]{:S(2)}) collective-permute-start(bf16[192,256]{1,0:T(8,128)(2,1)S(1)} %collective-permute-done), channel_id=1, source_target_pairs={{0,16},{1,17},{2,18},{3,19},{4,20},{5,21},{6,22},{7,23},{8,24},{9,... | collective-permute-start | bytes 294920 | tf_op jit(solution)/shard_map/ppermute | solution.py:22
  28.9 128.4 %collective-permute-start.30 = (bf16[192,256]{1,0:T(8,128)(2,1)S(1)}, bf16[192,256]{1,0:T(8,128)(2,1)S(1)}, u32[]{:S(2)}, u32[]{:S(2)}) collective-permute-start(bf16[192,256]{1,0:T(8,128)(2,1)S(1)} %collective-permute-done.8), channel_id=1, source_target_pairs={{0,16},{1,17},{2,18},{3,19},{4,20},{5,21},{6,22},{7,23},{8,24},{9,... | collective-permute-start | bytes 294920 | tf_op jit(solution)/shard_map/ppermute | solution.py:23
  72.1 25.6 %collective-permute-start.17 = (bf16[192,256]{1,0:T(8,128)(2,1)S(1)}, bf16[192,256]{1,0:T(8,128)(2,1)S(1)}, u32[]{:S(2)}, u32[]{:S(2)}) collective-permute-start(bf16[192,256]{1,0:T(8,128)(2,1)S(1)} %collective-permute-done.1), channel_id=1, source_target_pairs={{0,16},{1,17},{2,18},{3,19},{4,20},{5,21},{6,22},{7,23},{8,24},{9,... | collective-permute-start | bytes 294920 | tf_op jit(solution)/shard_map/ppermute | solution.py:22
  81.7 74.9 %collective-permute-start.29 = (bf16[192,256]{1,0:T(8,128)(2,1)S(1)}, bf16[192,256]{1,0:T(8,128)(2,1)S(1)}, u32[]{:S(2)}, u32[]{:S(2)}) collective-permute-start(bf16[192,256]{1,0:T(8,128)(2,1)S(1)} %collective-permute-done.9), channel_id=1, source_target_pairs={{0,16},{1,17},{2,18},{3,19},{4,20},{5,21},{6,22},{7,23},{8,24},{9,... | collective-permute-start | bytes 294920 | tf_op jit(solution)/shard_map/ppermute | solution.py:23
  93.7 62.3 %collective-permute-start.28 = (bf16[192,256]{1,0:T(8,128)(2,1)S(1)}, bf16[192,256]{1,0:T(8,128)(2,1)S(1)}, u32[]{:S(2)}, u32[]{:S(2)}) collective-permute-start(bf16[192,256]{1,0:T(8,128)(2,1)S(1)} %collective-permute-done.10), channel_id=1, source_target_pairs={{0,16},{1,17},{2,18},{3,19},{4,20},{5,21},{6,22},{7,23},{8,24},{9,... | collective-permute-start | bytes 294920 | tf_op jit(solution)/shard_map/ppermute | solution.py:23
  101.7 53.6 %collective-permute-start.27 = (bf16[192,256]{1,0:T(8,128)(2,1)S(1)}, bf16[192,256]{1,0:T(8,128)(2,1)S(1)}, u32[]{:S(2)}, u32[]{:S(2)}) collective-permute-start(bf16[192,256]{1,0:T(8,128)(2,1)S(1)} %collective-permute-done.11), channel_id=1, source_target_pairs={{0,16},{1,17},{2,18},{3,19},{4,20},{5,21},{6,22},{7,23},{8,24},{9,... | collective-permute-start | bytes 294920 | tf_op jit(solution)/shard_map/ppermute | solution.py:23
  157.9 33.5 %collective-permute-start.31 = (bf16[32,192,256]{2,1,0:T(8,128)(2,1)}, bf16[32,192,256]{2,1,0:T(8,128)(2,1)}, u32[]{:S(2)}, u32[]{:S(2)}) collective-permute-start(bf16[32,192,256]{2,1,0:T(8,128)(2,1)} %constant_dynamic-update-slice_fusion), channel_id=1, source_target_pairs={{0,32},{32,0},{64,96},{96,64},{128,160},{160,128},{192,224},{224,1... | collective-permute-start | bytes 9437192 | tf_op jit(solution)/shard_map/ppermute | solution.py:75
  196.5 15.2 %collective-permute-start.40 = (bf16[192,512]{1,0:T(8,128)(2,1)S(1)}, bf16[192,512]{1,0:T(8,128)(2,1)S(1)}, u32[]{:S(2)}, u32[]{:S(2)}) collective-permute-start(bf16[192,512]{1,0:T(8,128)(2,1)S(1)} %fusion.13), channel_id=1, source_target_pairs={{0,15},{1,0},{2,1},{3,2},{4,3},{5,4},{6,5},{7,6},{8,7},{9,8},{10,9... | collective-permute-start | bytes 589832 | tf_op jit(solution)/shard_map/ppermute | solution.py:18
  202.3 80.1 %collective-permute-start.47 = (bf16[192,512]{1,0:T(8,128)(2,1)S(1)}, bf16[192,512]{1,0:T(8,128)(2,1)S(1)}, u32[]{:S(2)}, u32[]{:S(2)}) collective-permute-start(bf16[192,512]{1,0:T(8,128)(2,1)S(1)} %fusion.13), channel_id=1, source_target_pairs={{0,16},{1,17},{2,18},{3,19},{4,20},{5,21},{6,22},{7,23},{8,24},{9,... | collective-permute-start | bytes 589832 | tf_op jit(solution)/shard_map/ppermute | solution.py:16
  206.8 14.0 %collective-permute-start.33 = (bf16[192,512]{1,0:T(8,128)(2,1)S(1)}, bf16[192,512]{1,0:T(8,128)(2,1)S(1)}, u32[]{:S(2)}, u32[]{:S(2)}) collective-permute-start(bf16[192,512]{1,0:T(8,128)(2,1)S(1)} %collective-permute-done.32), channel_id=1, source_target_pairs={{0,1},{1,2},{2,3},{3,4},{4,5},{5,6},{6,7},{7,8},{8,9},{9,10},{10,1... | collective-permute-start | bytes 589832 | tf_op jit(solution)/shard_map/ppermute | solution.py:24
  208.7 78.7 %collective-permute-start.48 = (bf16[192,512]{1,0:T(8,128)(2,1)S(1)}, bf16[192,512]{1,0:T(8,128)(2,1)S(1)}, u32[]{:S(2)}, u32[]{:S(2)}) collective-permute-start(bf16[192,512]{1,0:T(8,128)(2,1)S(1)} %collective-permute-done.32), channel_id=1, source_target_pairs={{0,16},{1,17},{2,18},{3,19},{4,20},{5,21},{6,22},{7,23},{8,24},{9,... | collective-permute-start | bytes 589832 | tf_op jit(solution)/shard_map/ppermute | solution.py:22
  216.4 144.0 %collective-permute-start.62 = (bf16[192,512]{1,0:T(8,128)(2,1)S(1)}, bf16[192,512]{1,0:T(8,128)(2,1)S(1)}, u32[]{:S(2)}, u32[]{:S(2)}) collective-permute-start(bf16[192,512]{1,0:T(8,128)(2,1)S(1)} %collective-permute-done.40), channel_id=1, source_target_pairs={{0,16},{1,17},{2,18},{3,19},{4,20},{5,21},{6,22},{7,23},{8,24},{9,... | collective-permute-start | bytes 589832 | tf_op jit(solution)/shard_map/ppermute | solution.py:23
  245.6 16.3 %collective-permute-start.45 = (bf16[192,512]{1,0:T(8,128)(2,1)S(1)}, bf16[192,512]{1,0:T(8,128)(2,1)S(1)}, u32[]{:S(2)}, u32[]{:S(2)}) collective-permute-start(bf16[192,512]{1,0:T(8,128)(2,1)S(1)} %collective-permute-done.44), channel_id=1, source_target_pairs={{0,15},{1,0},{2,1},{3,2},{4,3},{5,4},{6,5},{7,6},{8,7},{9,8},{10,9... | collective-permute-start | bytes 589832 | tf_op jit(solution)/shard_map/ppermute | solution.py:25
  261.9 28.7 %collective-permute-start.49 = (bf16[192,512]{1,0:T(8,128)(2,1)S(1)}, bf16[192,512]{1,0:T(8,128)(2,1)S(1)}, u32[]{:S(2)}, u32[]{:S(2)}) collective-permute-start(bf16[192,512]{1,0:T(8,128)(2,1)S(1)} %collective-permute-done.33), channel_id=1, source_target_pairs={{0,16},{1,17},{2,18},{3,19},{4,20},{5,21},{6,22},{7,23},{8,24},{9,... | collective-permute-start | bytes 589832 | tf_op jit(solution)/shard_map/ppermute | solution.py:22
  275.1 84.6 %collective-permute-start.61 = (bf16[192,512]{1,0:T(8,128)(2,1)S(1)}, bf16[192,512]{1,0:T(8,128)(2,1)S(1)}, u32[]{:S(2)}, u32[]{:S(2)}) collective-permute-start(bf16[192,512]{1,0:T(8,128)(2,1)S(1)} %collective-permute-done.41), channel_id=1, source_target_pairs={{0,16},{1,17},{2,18},{3,19},{4,20},{5,21},{6,22},{7,23},{8,24},{9,... | collective-permute-start | bytes 589832 | tf_op jit(solution)/shard_map/ppermute | solution.py:23
  287.4 71.6 %collective-permute-start.60 = (bf16[192,512]{1,0:T(8,128)(2,1)S(1)}, bf16[192,512]{1,0:T(8,128)(2,1)S(1)}, u32[]{:S(2)}, u32[]{:S(2)}) collective-permute-start(bf16[192,512]{1,0:T(8,128)(2,1)S(1)} %collective-permute-done.42), channel_id=1, source_target_pairs={{0,16},{1,17},{2,18},{3,19},{4,20},{5,21},{6,22},{7,23},{8,24},{9,... | collective-permute-start | bytes 589832 | tf_op jit(solution)/shard_map/ppermute | solution.py:23
  295.5 62.8 %collective-permute-start.59 = (bf16[192,512]{1,0:T(8,128)(2,1)S(1)}, bf16[192,512]{1,0:T(8,128)(2,1)S(1)}, u32[]{:S(2)}, u32[]{:S(2)}) collective-permute-start(bf16[192,512]{1,0:T(8,128)(2,1)S(1)} %collective-permute-done.43), channel_id=1, source_target_pairs={{0,16},{1,17},{2,18},{3,19},{4,20},{5,21},{6,22},{7,23},{8,24},{9,... | collective-permute-start | bytes 589832 | tf_op jit(solution)/shard_map/ppermute | solution.py:23
  383.3 23.4 %collective-permute-start.63 = (f32[17,4,2,12,192]{4,1,3,2,0:T(4,128)S(1)}, f32[17,4,2,12,192]{4,1,3,2,0:T(4,128)}, u32[]{:S(2)}, u32[]{:S(2)}) collective-permute-start(f32[17,4,2,12,192]{4,1,3,2,0:T(4,128)S(1)} %copy.23), channel_id=1, source_target_pairs={{0,32},{32,0},{64,96},{96,64},{128,160},{160,128},{192,224},{224,1... | collective-permute-start | bytes 3760136 | tf_op jit(solution)/shard_map/ppermute | solution.py:50
  410.8 14.1 %collective-permute-start.64 = (f32[17,2,12,192]{3,1,2,0:T(2,128)}, f32[17,2,12,192]{3,1,2,0:T(2,128)S(1)}, u32[]{:S(2)}, u32[]{:S(2)}) collective-permute-start(f32[17,2,12,192]{3,1,2,0:T(2,128)} %copy.25), channel_id=1, source_target_pairs={{0,128},{32,160},{64,192},{96,224},{128,256},{160,288},{192,320},{... | collective-permute-start | bytes 940040 | tf_op jit(solution)/shard_map/ppermute | solution.py:54
  415.1 19.8 %collective-permute-start.65 = (f32[17,2,12,192]{3,1,2,0:T(2,128)}, f32[17,2,12,192]{3,1,2,0:T(2,128)S(1)}, u32[]{:S(2)}, u32[]{:S(2)}) collective-permute-start(f32[17,2,12,192]{3,1,2,0:T(2,128)} %copy.27), channel_id=1, source_target_pairs={{0,256},{32,288},{64,320},{96,352},{128,384},{160,416},{192,448},{... | collective-permute-start | bytes 940040 | tf_op jit(solution)/shard_map/ppermute | solution.py:54
  420.5 16.9 %collective-permute-start.66 = (f32[17,2,12,192]{3,1,2,0:T(2,128)}, f32[17,2,12,192]{3,1,2,0:T(2,128)}, u32[]{:S(2)}, u32[]{:S(2)}) collective-permute-start(f32[17,2,12,192]{3,1,2,0:T(2,128)} %copy.29), channel_id=1, source_target_pairs={{0,384},{32,416},{64,448},{96,480},{128,0},{160,32},{192,64},{224,... | collective-permute-start | bytes 940040 | tf_op jit(solution)/shard_map/ppermute | solution.py:54
  (49 other events, 552.4 us)

commit v6 on v4

--- a/solution.py
+++ b/solution.py
@@ -35,20 +35,23 @@
 
 def reduce_scatter_aux(parts, naux):
     nx = naux // 4
+    slots, rows, cols = parts.shape
     me = lax.axis_index("aux")
     c_me = me % 2
     y_me = (me // 2) % 2
     x_me = me // 4
-    shaped = parts.reshape((parts.shape[0], nx, 2, 2) + parts.shape[2:])
-    keep = jnp.take(shaped, c_me, axis=3)
-    send = jnp.take(shaped, 1 - c_me, axis=3)
+    shaped = parts.reshape(slots, 2, rows // 2, cols)
+    keep = jnp.take(shaped, c_me, axis=1)
+    send = jnp.take(shaped, 1 - c_me, axis=1)
     on_chip = keep + lax.ppermute(send, "aux", [(i, i ^ 1) for i in range(naux)])
+    on_chip = on_chip.reshape(slots, nx, rows // (2 * nx), cols)
     total = jnp.take(on_chip, x_me, axis=1)
     for dx in range(1, nx):
         perm = [(i, ((i // 4 + dx) % nx) * 4 + i % 4) for i in range(naux)]
         total = total + lax.ppermute(
             jnp.take(on_chip, (x_me + dx) % nx, axis=1), "aux", perm
         )
+    total = total.reshape(slots, 2, rows // naux, cols)
     mine = jnp.take(total, y_me, axis=1)
     theirs = jnp.take(total, 1 - y_me, axis=1)
     return mine + lax.ppermute(theirs, "aux", [(i, i ^ 2) for i in range(naux)])
@@ -68,30 +71,37 @@
     mine_ring, z = ring_gather(mine, nrow, ring)
     partner = [(i, i ^ 1) for i in range(naux)]
     other_ring = lax.ppermute(mine_ring, "aux", partner)
-    coeff_ring = jnp.where(
-        core == 0,
-        jnp.concatenate([mine_ring, other_ring], axis=2),
-        jnp.concatenate([other_ring, mine_ring], axis=2),
-    )
 
     p = jnp.arange(nrow)
     block_at = (p % 2) * ring + (z - p // 2) % ring
     chol = chol_vectors[0].reshape(block, nrow, nbf // nrow)
     chol_ring = jnp.take(chol, block_at, axis=1).reshape(block, nbf)
-    half = jnp.dot(
-        chol_ring, coeff_ring.reshape(nbf, nocc), preferred_element_type=jnp.float32
+    half_mine = jnp.dot(
+        chol_ring, mine_ring.reshape(nbf, half_cols), preferred_element_type=jnp.float32
+    )
+    half_other = jnp.dot(
+        chol_ring, other_ring.reshape(nbf, half_cols), preferred_element_type=jnp.float32
+    )
+    half = jnp.where(
+        core == 0,
+        jnp.concatenate([half_mine, half_other], axis=1),
+        jnp.concatenate([half_other, half_mine], axis=1),
     ).astype(jnp.bfloat16)
 
     half_ring, _ = ring_gather(half, nrow, ring)
     chosen = tile_pairs[tile_owner[0]]
     left_rows = jnp.take(half_ring, position_of(chosen[:, 0], z, ring), axis=0)
+    slots = left_rows.shape[0]
+    left_rows = (
+        left_rows.reshape(slots, naux // 4, 2, 2, block // naux, nocc)
+        .transpose(0, 3, 1, 2, 4, 5)
+        .reshape(slots, block, nocc)
+    )
     right_rows = jnp.take(half_ring, position_of(chosen[:, 1], z, ring), axis=0)
     partial_tiles = jnp.einsum(
         "sao,sbo->sab", left_rows, right_rows, preferred_element_type=jnp.float32
     )
-    slots = partial_tiles.shape[0]
-    split = partial_tiles.reshape(slots, naux, block // naux, block)
-    return reduce_scatter_aux(split, naux)
+    return reduce_scatter_aux(partial_tiles, naux)
 
 
 def solution(mesh):

time: 306 us -> 317 us (1.036)
  local copies, waits for them, and re-layouts: 54.6 us -> 63 us
  waiting for transfers between devices: 62.8 us -> 69.5 us
  matrix products: 13.4 us -> 9.16 us
    reshape x0 -> x3, local copies, waits for them, and re-layouts: none -> 13.1 us  [the longest x1 6.59 us: local(): left_rows = left_rows.reshape(slots, naux // 4, 2, 2, block // naux, nocc...]
    unnamed x37 -> x41, local copies, waits for them, and re-layouts: 23.1 us -> 15.8 us
    ppermute x14, waiting for transfers between devices: 28.6 us -> 34.7 us  [ring_gather(): from_left = lax.ppermute(from_left, 'row', send_right)]
    transpose x0 -> x1, local copies, waits for them, and re-layouts: none -> 5.09 us  [local(): left_rows = left_rows.reshape(slots, naux // 4, 2, 2, block // naux, nocc...]
    select_n x4 -> x2, local copies, waits for them, and re-layouts: 4.72 us -> 9.62 us  [local(): chol_ring = jnp.take(chol, block_at, axis=1).reshape(block, nbf)]
    another operation x1 -> x0, local copies, waits for them, and re-layouts: 4.64 us -> none  [reduce_scatter_aux(): shaped = parts.reshape((parts.shape[0], nx, 2, 2) + parts.shape[2:])]
    dot_general x1 -> x2, matrix products: 8.44 us -> 6.09 us  [the longest x1 3.38 us: local(): jnp.dot(chol_ring, mine_ring.reshape(nbf, half_cols), preferred_element_t...]
  transfers between devices with their start and end apart: 40 -> 40, of which waited for: 24 -> 24; matrix products, arithmetic and copies ran while one was open for 9% -> 11% of each run, Pallas kernels for 0% -> 0%
where the time goes in v6:
time: 317 us; the launch traced here: 312 us
  starting transfers between devices  159 us (50%)
  waiting for transfers between devices  69.5 us (22%)
  local copies, waits for them, and re-layouts  63 us (20%)
  other arithmetic  10.2 us (3%)
  matrix products  9.16 us (3%)
    ppermute x14, starting transfers between devices, ring_gather(): from_right = lax.ppermute(from_right, 'row', send_left)  70.2 us
    ppermute x14, waiting for transfers between devices, ring_gather(): from_left = lax.ppermute(from_left, 'row', send_right)  34.7 us
    ppermute x14, starting transfers between devices, ring_gather(): from_left = lax.ppermute(from_left, 'row', send_right)  28.6 us
    unnamed x41, local copies, waits for them, and re-layouts  15.8 us
    ppermute x3, waiting for transfers between devices, reduce_scatter_aux(): lax.ppermute(jnp.take(on_chip, (x_me + dx) % nx, axis=1), 'aux', perm)  14.6 us
    ppermute x1, starting transfers between devices, local(): other_ring = lax.ppermute(mine_ring, 'aux', partner)  12.1 us
    ppermute x3, starting transfers between devices, reduce_scatter_aux(): lax.ppermute(jnp.take(on_chip, (x_me + dx) % nx, axis=1), 'aux', perm)  10.6 us
    ppermute x2, starting transfers between devices, ring_gather(): other = lax.ppermute(x, 'row', [(i, i ^ ring) for i in range(nrow)])  10.5 us
  transfers between devices with their start and end apart: 40, of which 24 were waited for; matrix products, arithmetic and copies ran while one was open for 11% of the time, Pallas kernels for 0%

profile of v6, /device:TPU:1, one launch (start us, length us, event | category | flops | bytes accessed | tf_op | source)
XLA Modules:
  0.0 312.2 jit_solution(18103005743667459610)
XLA Ops:
  0.9 5.6 %collective-permute-start = (bf16[192,256]{1,0:T(8,128)(2,1)S(1)}, bf16[192,256]{1,0:T(8,128)(2,1)S(1)}, u32[]{:S(2)}, u32[]{:S(2)}) collective-permute-start(bf16[192,256]{1,0:T(8,128)(2,1)S(1)} %constant_dynamic-slice_fusion), channel_id=1, source_target_pairs={{0,16},{1,17},{2,18},{3,19},{4,20},{5,21},{6,22},{7,23},{8,24},{9,... | collective-permute-start | bytes 294920 | tf_op jit(solution)/shard_map/ppermute | solution.py:12
  12.2 9.5 %collective-permute-start.9 = (bf16[2,192,256]{2,1,0:T(8,128)(2,1)S(1)}, bf16[2,192,256]{2,1,0:T(8,128)(2,1)S(1)}, u32[]{:S(2)}, u32[]{:S(2)}) collective-permute-start(bf16[2,192,256]{2,1,0:T(8,128)(2,1)S(1)} %maximum_select_fusion.5), channel_id=1, source_target_pairs={{0,15},{1,0},{2,1},{3,2},{4,3},{5,4},{6,5},{7,6},{8,7},{9,8},{10,9... | collective-permute-start | bytes 589832 | tf_op jit(solution)/shard_map/ppermute | solution.py:22
  32.7 4.6 %collective-permute-start.11 = (bf16[2,192,256]{2,1,0:T(8,128)(2,1)S(1)}, bf16[2,192,256]{2,1,0:T(8,128)(2,1)S(1)}, u32[]{:S(2)}, u32[]{:S(2)}) collective-permute-start(bf16[2,192,256]{2,1,0:T(8,128)(2,1)S(1)} %collective-permute-done.10), channel_id=1, source_target_pairs={{0,15},{1,0},{2,1},{3,2},{4,3},{5,4},{6,5},{7,6},{8,7},{9,8},{10,9... | collective-permute-start | bytes 589832 | tf_op jit(solution)/shard_map/ppermute | solution.py:22
  40.4 4.6 %collective-permute-start.12 = (bf16[2,192,256]{2,1,0:T(8,128)(2,1)S(1)}, bf16[2,192,256]{2,1,0:T(8,128)(2,1)S(1)}, u32[]{:S(2)}, u32[]{:S(2)}) collective-permute-start(bf16[2,192,256]{2,1,0:T(8,128)(2,1)S(1)} %collective-permute-done.11), channel_id=1, source_target_pairs={{0,15},{1,0},{2,1},{3,2},{4,3},{5,4},{6,5},{7,6},{8,7},{9,8},{10,9... | collective-permute-start | bytes 589832 | tf_op jit(solution)/shard_map/ppermute | solution.py:22
  48.0 4.6 %collective-permute-start.13 = (bf16[2,192,256]{2,1,0:T(8,128)(2,1)S(1)}, bf16[2,192,256]{2,1,0:T(8,128)(2,1)S(1)}, u32[]{:S(2)}, u32[]{:S(2)}) collective-permute-start(bf16[2,192,256]{2,1,0:T(8,128)(2,1)S(1)} %collective-permute-done.12), channel_id=1, source_target_pairs={{0,15},{1,0},{2,1},{3,2},{4,3},{5,4},{6,5},{7,6},{8,7},{9,8},{10,9... | collective-permute-start | bytes 589832 | tf_op jit(solution)/shard_map/ppermute | solution.py:22
  64.0 4.9 %collective-permute-start.15 = (bf16[2,192,256]{2,1,0:T(8,128)(2,1)S(1)}, bf16[2,192,256]{2,1,0:T(8,128)(2,1)S(1)}, u32[]{:S(2)}, u32[]{:S(2)}) collective-permute-start(bf16[2,192,256]{2,1,0:T(8,128)(2,1)S(1)} %collective-permute-done.14), channel_id=1, source_target_pairs={{0,15},{1,0},{2,1},{3,2},{4,3},{5,4},{6,5},{7,6},{8,7},{9,8},{10,9... | collective-permute-start | bytes 589832 | tf_op jit(solution)/shard_map/ppermute | solution.py:22
  73.7 5.0 %collective-permute-start.16 = (bf16[192,256]{1,0:T(8,128)(2,1)S(1)}, bf16[192,256]{1,0:T(8,128)(2,1)S(1)}, u32[]{:S(2)}, u32[]{:S(2)}) collective-permute-start(bf16[192,256]{1,0:T(8,128)(2,1)S(1)} %slice_bitcast_fusion.2), channel_id=1, source_target_pairs={{0,15},{1,0},{2,1},{3,2},{4,3},{5,4},{6,5},{7,6},{8,7},{9,8},{10,9... | collective-permute-start | bytes 294920 | tf_op jit(solution)/shard_map/ppermute | solution.py:26
  86.0 12.1 %collective-permute-start.17 = (bf16[32,192,256]{2,1,0:T(8,128)(2,1)}, bf16[32,192,256]{2,1,0:T(8,128)(2,1)}, u32[]{:S(2)}, u32[]{:S(2)}) collective-permute-start(bf16[32,192,256]{2,1,0:T(8,128)(2,1)} %bitcast.29), channel_id=1, source_target_pairs={{0,32},{32,0},{64,96},{96,64},{128,160},{160,128},{192,224},{224,1... | collective-permute-start | bytes 9437192 | tf_op jit(solution)/shard_map/ppermute | solution.py:73
  98.1 4.6 %reshape_squeeze.3 = bf16[192,32,192]{2,1,0:T(8,128)(2,1)} reshape(bf16[1,192,6144]{2,1,0:T(8,128)(2,1)S(1)} %copy-done.4) | data formatting | bytes 4718592 | tf_op jit(solution)/shard_map/reshape;squeeze | solution.py:77
  114.6 6.2 %select_n.260 = bf16[192,6144]{1,0:T(8,128)(2,1)} reshape(bf16[192,32,192]{2,1,0:T(8,128)(2,1)} %copy.18) | data formatting | bytes 4718592 | tf_op jit(solution)/shard_map/jit(_take)/select_n | solution.py:78
  127.0 4.8 %collective-permute-start.18 = (bf16[192,512]{1,0:T(8,128)(2,1)S(1)}, bf16[192,512]{1,0:T(8,128)(2,1)S(1)}, u32[]{:S(2)}, u32[]{:S(2)}) collective-permute-start(bf16[192,512]{1,0:T(8,128)(2,1)S(1)} %fusion.14), channel_id=1, source_target_pairs={{0,16},{1,17},{2,18},{3,19},{4,20},{5,21},{6,22},{7,23},{8,24},{9,... | collective-permute-start | bytes 589832 | tf_op jit(solution)/shard_map/ppermute | solution.py:12
  131.9 4.9 %collective-permute-done.18 = bf16[192,512]{1,0:T(8,128)(2,1)S(1)} collective-permute-done((bf16[192,512]{1,0:T(8,128)(2,1)S(1)}, bf16[192,512]{1,0:T(8,128)(2,1)S(1)}, u32[]{:S(2)}, u32[]{:S(2)}) %collective-permute-start.18) | collective-permute-done | bytes 196640 | tf_op jit(solution)/shard_map/ppermute | solution.py:12
  138.8 5.2 %collective-permute-start.27 = (bf16[2,192,512]{2,1,0:T(8,128)(2,1)S(1)}, bf16[2,192,512]{2,1,0:T(8,128)(2,1)S(1)}, u32[]{:S(2)}, u32[]{:S(2)}) collective-permute-start(bf16[2,192,512]{2,1,0:T(8,128)(2,1)S(1)} %maximum_select_fusion.3), channel_id=1, source_target_pairs={{0,15},{1,0},{2,1},{3,2},{4,3},{5,4},{6,5},{7,6},{8,7},{9,8},{10,9... | collective-permute-start | bytes 1179656 | tf_op jit(solution)/shard_map/ppermute | solution.py:22
  144.0 6.7 %collective-permute-done.19 = bf16[2,192,512]{2,1,0:T(8,128)(2,1)S(1)} collective-permute-done((bf16[2,192,512]{2,1,0:T(8,128)(2,1)S(1)}, bf16[2,192,512]{2,1,0:T(8,128)(2,1)S(1)}, u32[]{:S(2)}, u32[]{:S(2)}) %collective-permute-start.19) | collective-permute-done | bytes 393248 | tf_op jit(solution)/shard_map/ppermute | solution.py:21
  157.4 5.6 %collective-permute-done.20 = bf16[2,192,512]{2,1,0:T(8,128)(2,1)S(1)} collective-permute-done((bf16[2,192,512]{2,1,0:T(8,128)(2,1)S(1)}, bf16[2,192,512]{2,1,0:T(8,128)(2,1)S(1)}, u32[]{:S(2)}, u32[]{:S(2)}) %collective-permute-start.20) | collective-permute-done | bytes 393248 | tf_op jit(solution)/shard_map/ppermute | solution.py:21
  165.6 4.6 %collective-permute-start.29 = (bf16[2,192,512]{2,1,0:T(8,128)(2,1)S(1)}, bf16[2,192,512]{2,1,0:T(8,128)(2,1)S(1)}, u32[]{:S(2)}, u32[]{:S(2)}) collective-permute-start(bf16[2,192,512]{2,1,0:T(8,128)(2,1)S(1)} %collective-permute-done.28), channel_id=1, source_target_pairs={{0,15},{1,0},{2,1},{3,2},{4,3},{5,4},{6,5},{7,6},{8,7},{9,8},{10,9... | collective-permute-start | bytes 1179656 | tf_op jit(solution)/shard_map/ppermute | solution.py:22
  176.5 4.8 %collective-permute-start.30 = (bf16[2,192,512]{2,1,0:T(8,128)(2,1)S(1)}, bf16[2,192,512]{2,1,0:T(8,128)(2,1)S(1)}, u32[]{:S(2)}, u32[]{:S(2)}) collective-permute-start(bf16[2,192,512]{2,1,0:T(8,128)(2,1)S(1)} %collective-permute-done.29), channel_id=1, source_target_pairs={{0,15},{1,0},{2,1},{3,2},{4,3},{5,4},{6,5},{7,6},{8,7},{9,8},{10,9... | collective-permute-start | bytes 1179656 | tf_op jit(solution)/shard_map/ppermute | solution.py:22
  216.7 4.9 %collective-permute-start.34 = (bf16[192,512]{1,0:T(8,128)(2,1)S(1)}, bf16[192,512]{1,0:T(8,128)(2,1)S(1)}, u32[]{:S(2)}, u32[]{:S(2)}) collective-permute-start(bf16[192,512]{1,0:T(8,128)(2,1)S(1)} %slice_bitcast_fusion), channel_id=1, source_target_pairs={{0,15},{1,0},{2,1},{3,2},{4,3},{5,4},{6,5},{7,6},{8,7},{9,8},{10,9... | collective-permute-start | bytes 589832 | tf_op jit(solution)/shard_map/ppermute | solution.py:26
  234.2 6.5 %reshape.432 = bf16[17,4,2,2,12,512]{5,4,3,2,1,0:T(8,128)(2,1)} reshape(bf16[17,192,512]{2,1,0:T(8,128)(2,1)} %broadcast_select_fusion) | data formatting | bytes 6684672 | tf_op jit(solution)/shard_map/reshape | solution.py:96
  240.7 5.1 %copy.19 = bf16[17,2,4,2,12,512]{5,4,3,2,1,0:T(8,128)(2,1)} copy(bf16[17,2,4,2,12,512]{5,4,1,3,2,0:T(8,128)(2,1)} %bitcast.167) | data formatting | bytes 6684672 | tf_op jit(solution)/shard_map/transpose | solution.py:97
  245.8 6.6 %reshape.433 = bf16[17,192,512]{2,1,0:T(8,128)(2,1)} reshape(bf16[17,2,4,2,12,512]{5,4,3,2,1,0:T(8,128)(2,1)} %copy.19) | data formatting | bytes 6684672 | tf_op jit(solution)/shard_map/reshape | solution.py:98
  260.9 10.4 %collective-permute-start.35 = (f32[17,96,192]{2,1,0:T(8,128)S(1)}, f32[17,96,192]{2,1,0:T(8,128)S(1)}, u32[]{:S(2)}, u32[]{:S(2)}) collective-permute-start(f32[17,96,192]{2,1,0:T(8,128)S(1)} %fusion.3), channel_id=1, source_target_pairs={{0,32},{32,0},{64,96},{96,64},{128,160},{160,128},{192,224},{224,1... | collective-permute-start | bytes 3760136 | tf_op jit(solution)/shard_map/ppermute | solution.py:46
  290.1 10.0 %collective-permute-done.37 = f32[17,24,192]{2,1,0:T(8,128)} collective-permute-done((f32[17,24,192]{2,1,0:T(8,128)S(1)}, f32[17,24,192]{2,1,0:T(8,128)}, u32[]{:S(2)}, u32[]{:S(2)}) %collective-permute-start.37) | collective-permute-done | bytes 313376 | tf_op jit(solution)/shard_map/ppermute | solution.py:51
  306.0 5.4 %collective-permute-done.39 = f32[17,12,192]{2,1,0:T(8,128)S(1)} collective-permute-done((f32[17,12,192]{2,1,0:T(8,128)S(1)}, f32[17,12,192]{2,1,0:T(8,128)S(1)}, u32[]{:S(2)}, u32[]{:S(2)}) %collective-permute-start.39) | collective-permute-done | bytes 156704 | tf_op jit(solution)/shard_map/ppermute | solution.py:57
  (147 shorter events, 163.9 us)
Async XLA Ops:
  8.6 14.6 %collective-permute-start.1 = (bf16[2,192,256]{2,1,0:T(8,128)(2,1)S(1)}, bf16[2,192,256]{2,1,0:T(8,128)(2,1)S(1)}, u32[]{:S(2)}, u32[]{:S(2)}) collective-permute-start(bf16[2,192,256]{2,1,0:T(8,128)(2,1)S(1)} %maximum_select_fusion.5), channel_id=1, source_target_pairs={{0,1},{1,2},{2,3},{3,4},{4,5},{5,6},{6,7},{7,8},{8,9},{9,10},{10,1... | collective-permute-start | bytes 589832 | tf_op jit(solution)/shard_map/ppermute | solution.py:21
  12.2 12.9 %collective-permute-start.9 = (bf16[2,192,256]{2,1,0:T(8,128)(2,1)S(1)}, bf16[2,192,256]{2,1,0:T(8,128)(2,1)S(1)}, u32[]{:S(2)}, u32[]{:S(2)}) collective-permute-start(bf16[2,192,256]{2,1,0:T(8,128)(2,1)S(1)} %maximum_select_fusion.5), channel_id=1, source_target_pairs={{0,15},{1,0},{2,1},{3,2},{4,3},{5,4},{6,5},{7,6},{8,7},{9,8},{10,9... | collective-permute-start | bytes 589832 | tf_op jit(solution)/shard_map/ppermute | solution.py:22
  62.1 9.7 %collective-permute-start.7 = (bf16[2,192,256]{2,1,0:T(8,128)(2,1)S(1)}, bf16[2,192,256]{2,1,0:T(8,128)(2,1)S(1)}, u32[]{:S(2)}, u32[]{:S(2)}) collective-permute-start(bf16[2,192,256]{2,1,0:T(8,128)(2,1)S(1)} %collective-permute-done.6), channel_id=1, source_target_pairs={{0,1},{1,2},{2,3},{3,4},{4,5},{5,6},{6,7},{7,8},{8,9},{9,10},{10,1... | collective-permute-start | bytes 589832 | tf_op jit(solution)/shard_map/ppermute | solution.py:21
  64.0 9.7 %collective-permute-start.15 = (bf16[2,192,256]{2,1,0:T(8,128)(2,1)S(1)}, bf16[2,192,256]{2,1,0:T(8,128)(2,1)S(1)}, u32[]{:S(2)}, u32[]{:S(2)}) collective-permute-start(bf16[2,192,256]{2,1,0:T(8,128)(2,1)S(1)} %collective-permute-done.14), channel_id=1, source_target_pairs={{0,15},{1,0},{2,1},{3,2},{4,3},{5,4},{6,5},{7,6},{8,7},{9,8},{10,9... | collective-permute-start | bytes 589832 | tf_op jit(solution)/shard_map/ppermute | solution.py:22
  86.0 38.2 %collective-permute-start.17 = (bf16[32,192,256]{2,1,0:T(8,128)(2,1)}, bf16[32,192,256]{2,1,0:T(8,128)(2,1)}, u32[]{:S(2)}, u32[]{:S(2)}) collective-permute-start(bf16[32,192,256]{2,1,0:T(8,128)(2,1)} %bitcast.29), channel_id=1, source_target_pairs={{0,32},{32,0},{64,96},{96,64},{128,160},{160,128},{192,224},{224,1... | collective-permute-start | bytes 9437192 | tf_op jit(solution)/shard_map/ppermute | solution.py:73
  127.0 9.8 %collective-permute-start.18 = (bf16[192,512]{1,0:T(8,128)(2,1)S(1)}, bf16[192,512]{1,0:T(8,128)(2,1)S(1)}, u32[]{:S(2)}, u32[]{:S(2)}) collective-permute-start(bf16[192,512]{1,0:T(8,128)(2,1)S(1)} %fusion.14), channel_id=1, source_target_pairs={{0,16},{1,17},{2,18},{3,19},{4,20},{5,21},{6,22},{7,23},{8,24},{9,... | collective-permute-start | bytes 589832 | tf_op jit(solution)/shard_map/ppermute | solution.py:12
  136.9 13.9 %collective-permute-start.19 = (bf16[2,192,512]{2,1,0:T(8,128)(2,1)S(1)}, bf16[2,192,512]{2,1,0:T(8,128)(2,1)S(1)}, u32[]{:S(2)}, u32[]{:S(2)}) collective-permute-start(bf16[2,192,512]{2,1,0:T(8,128)(2,1)S(1)} %maximum_select_fusion.3), channel_id=1, source_target_pairs={{0,1},{1,2},{2,3},{3,4},{4,5},{5,6},{6,7},{7,8},{8,9},{9,10},{10,1... | collective-permute-start | bytes 1179656 | tf_op jit(solution)/shard_map/ppermute | solution.py:21
  138.8 13.8 %collective-permute-start.27 = (bf16[2,192,512]{2,1,0:T(8,128)(2,1)S(1)}, bf16[2,192,512]{2,1,0:T(8,128)(2,1)S(1)}, u32[]{:S(2)}, u32[]{:S(2)}) collective-permute-start(bf16[2,192,512]{2,1,0:T(8,128)(2,1)S(1)} %maximum_select_fusion.3), channel_id=1, source_target_pairs={{0,15},{1,0},{2,1},{3,2},{4,3},{5,4},{6,5},{7,6},{8,7},{9,8},{10,9... | collective-permute-start | bytes 1179656 | tf_op jit(solution)/shard_map/ppermute | solution.py:22
  150.7 12.3 %collective-permute-start.20 = (bf16[2,192,512]{2,1,0:T(8,128)(2,1)S(1)}, bf16[2,192,512]{2,1,0:T(8,128)(2,1)S(1)}, u32[]{:S(2)}, u32[]{:S(2)}) collective-permute-start(bf16[2,192,512]{2,1,0:T(8,128)(2,1)S(1)} %collective-permute-done.19), channel_id=1, source_target_pairs={{0,1},{1,2},{2,3},{3,4},{4,5},{5,6},{6,7},{7,8},{8,9},{9,10},{10,1... | collective-permute-start | bytes 1179656 | tf_op jit(solution)/shard_map/ppermute | solution.py:21
  152.6 12.9 %collective-permute-start.28 = (bf16[2,192,512]{2,1,0:T(8,128)(2,1)S(1)}, bf16[2,192,512]{2,1,0:T(8,128)(2,1)S(1)}, u32[]{:S(2)}, u32[]{:S(2)}) collective-permute-start(bf16[2,192,512]{2,1,0:T(8,128)(2,1)S(1)} %collective-permute-done.27), channel_id=1, source_target_pairs={{0,15},{1,0},{2,1},{3,2},{4,3},{5,4},{6,5},{7,6},{8,7},{9,8},{10,9... | collective-permute-start | bytes 1179656 | tf_op jit(solution)/shard_map/ppermute | solution.py:22
  163.0 11.5 %collective-permute-start.21 = (bf16[2,192,512]{2,1,0:T(8,128)(2,1)S(1)}, bf16[2,192,512]{2,1,0:T(8,128)(2,1)S(1)}, u32[]{:S(2)}, u32[]{:S(2)}) collective-permute-start(bf16[2,192,512]{2,1,0:T(8,128)(2,1)S(1)} %collective-permute-done.20), channel_id=1, source_target_pairs={{0,1},{1,2},{2,3},{3,4},{4,5},{5,6},{6,7},{7,8},{8,9},{9,10},{10,1... | collective-permute-start | bytes 1179656 | tf_op jit(solution)/shard_map/ppermute | solution.py:21
  165.6 10.9 %collective-permute-start.29 = (bf16[2,192,512]{2,1,0:T(8,128)(2,1)S(1)}, bf16[2,192,512]{2,1,0:T(8,128)(2,1)S(1)}, u32[]{:S(2)}, u32[]{:S(2)}) collective-permute-start(bf16[2,192,512]{2,1,0:T(8,128)(2,1)S(1)} %collective-permute-done.28), channel_id=1, source_target_pairs={{0,15},{1,0},{2,1},{3,2},{4,3},{5,4},{6,5},{7,6},{8,7},{9,8},{10,9... | collective-permute-start | bytes 1179656 | tf_op jit(solution)/shard_map/ppermute | solution.py:22
  174.5 10.7 %collective-permute-start.22 = (bf16[2,192,512]{2,1,0:T(8,128)(2,1)S(1)}, bf16[2,192,512]{2,1,0:T(8,128)(2,1)}, u32[]{:S(2)}, u32[]{:S(2)}) collective-permute-start(bf16[2,192,512]{2,1,0:T(8,128)(2,1)S(1)} %collective-permute-done.21), channel_id=1, source_target_pairs={{0,1},{1,2},{2,3},{3,4},{4,5},{5,6},{6,7},{7,8},{8,9},{9,10},{10,1... | collective-permute-start | bytes 1179656 | tf_op jit(solution)/shard_map/ppermute | solution.py:21
  176.5 10.7 %collective-permute-start.30 = (bf16[2,192,512]{2,1,0:T(8,128)(2,1)S(1)}, bf16[2,192,512]{2,1,0:T(8,128)(2,1)S(1)}, u32[]{:S(2)}, u32[]{:S(2)}) collective-permute-start(bf16[2,192,512]{2,1,0:T(8,128)(2,1)S(1)} %collective-permute-done.29), channel_id=1, source_target_pairs={{0,15},{1,0},{2,1},{3,2},{4,3},{5,4},{6,5},{7,6},{8,7},{9,8},{10,9... | collective-permute-start | bytes 1179656 | tf_op jit(solution)/shard_map/ppermute | solution.py:22
  185.2 9.9 %collective-permute-start.23 = (bf16[2,192,512]{2,1,0:T(8,128)(2,1)}, bf16[2,192,512]{2,1,0:T(8,128)(2,1)S(1)}, u32[]{:S(2)}, u32[]{:S(2)}) collective-permute-start(bf16[2,192,512]{2,1,0:T(8,128)(2,1)} %collective-permute-done.22), channel_id=1, source_target_pairs={{0,1},{1,2},{2,3},{3,4},{4,5},{5,6},{6,7},{7,8},{8,9},{9,10},{10,1... | collective-permute-start | bytes 1179656 | tf_op jit(solution)/shard_map/ppermute | solution.py:21
  187.2 9.9 %collective-permute-start.31 = (bf16[2,192,512]{2,1,0:T(8,128)(2,1)S(1)}, bf16[2,192,512]{2,1,0:T(8,128)(2,1)S(1)}, u32[]{:S(2)}, u32[]{:S(2)}) collective-permute-start(bf16[2,192,512]{2,1,0:T(8,128)(2,1)S(1)} %collective-permute-done.30), channel_id=1, source_target_pairs={{0,15},{1,0},{2,1},{3,2},{4,3},{5,4},{6,5},{7,6},{8,7},{9,8},{10,9... | collective-permute-start | bytes 1179656 | tf_op jit(solution)/shard_map/ppermute | solution.py:22
  195.1 9.7 %collective-permute-start.24 = (bf16[2,192,512]{2,1,0:T(8,128)(2,1)S(1)}, bf16[2,192,512]{2,1,0:T(8,128)(2,1)S(1)}, u32[]{:S(2)}, u32[]{:S(2)}) collective-permute-start(bf16[2,192,512]{2,1,0:T(8,128)(2,1)S(1)} %collective-permute-done.23), channel_id=1, source_target_pairs={{0,1},{1,2},{2,3},{3,4},{4,5},{5,6},{6,7},{7,8},{8,9},{9,10},{10,1... | collective-permute-start | bytes 1179656 | tf_op jit(solution)/shard_map/ppermute | solution.py:21
  197.1 9.9 %collective-permute-start.32 = (bf16[2,192,512]{2,1,0:T(8,128)(2,1)S(1)}, bf16[2,192,512]{2,1,0:T(8,128)(2,1)S(1)}, u32[]{:S(2)}, u32[]{:S(2)}) collective-permute-start(bf16[2,192,512]{2,1,0:T(8,128)(2,1)S(1)} %collective-permute-done.31), channel_id=1, source_target_pairs={{0,15},{1,0},{2,1},{3,2},{4,3},{5,4},{6,5},{7,6},{8,7},{9,8},{10,9... | collective-permute-start | bytes 1179656 | tf_op jit(solution)/shard_map/ppermute | solution.py:22
  204.9 9.8 %collective-permute-start.25 = (bf16[2,192,512]{2,1,0:T(8,128)(2,1)S(1)}, bf16[2,192,512]{2,1,0:T(8,128)(2,1)S(1)}, u32[]{:S(2)}, u32[]{:S(2)}) collective-permute-start(bf16[2,192,512]{2,1,0:T(8,128)(2,1)S(1)} %collective-permute-done.24), channel_id=1, source_target_pairs={{0,1},{1,2},{2,3},{3,4},{4,5},{5,6},{6,7},{7,8},{8,9},{9,10},{10,1... | collective-permute-start | bytes 1179656 | tf_op jit(solution)/shard_map/ppermute | solution.py:21
  207.0 9.6 %collective-permute-start.33 = (bf16[2,192,512]{2,1,0:T(8,128)(2,1)S(1)}, bf16[2,192,512]{2,1,0:T(8,128)(2,1)S(1)}, u32[]{:S(2)}, u32[]{:S(2)}) collective-permute-start(bf16[2,192,512]{2,1,0:T(8,128)(2,1)S(1)} %collective-permute-done.32), channel_id=1, source_target_pairs={{0,15},{1,0},{2,1},{3,2},{4,3},{5,4},{6,5},{7,6},{8,7},{9,8},{10,9... | collective-permute-start | bytes 1179656 | tf_op jit(solution)/shard_map/ppermute | solution.py:22
  260.9 13.6 %collective-permute-start.35 = (f32[17,96,192]{2,1,0:T(8,128)S(1)}, f32[17,96,192]{2,1,0:T(8,128)S(1)}, u32[]{:S(2)}, u32[]{:S(2)}) collective-permute-start(f32[17,96,192]{2,1,0:T(8,128)S(1)} %fusion.3), channel_id=1, source_target_pairs={{0,32},{32,0},{64,96},{96,64},{128,160},{160,128},{192,224},{224,1... | collective-permute-start | bytes 3760136 | tf_op jit(solution)/shard_map/ppermute | solution.py:46
  276.2 13.9 %collective-permute-start.36 = (f32[17,24,192]{2,1,0:T(8,128)S(1)}, f32[17,24,192]{2,1,0:T(8,128)S(1)}, u32[]{:S(2)}, u32[]{:S(2)}) collective-permute-start(f32[17,24,192]{2,1,0:T(8,128)S(1)} %get-tuple-element.48), channel_id=1, source_target_pairs={{0,128},{32,160},{64,192},{96,224},{128,256},{160,288},{192,320},{... | collective-permute-start | bytes 940040 | tf_op jit(solution)/shard_map/ppermute | solution.py:51
  279.3 20.8 %collective-permute-start.37 = (f32[17,24,192]{2,1,0:T(8,128)S(1)}, f32[17,24,192]{2,1,0:T(8,128)}, u32[]{:S(2)}, u32[]{:S(2)}) collective-permute-start(f32[17,24,192]{2,1,0:T(8,128)S(1)} %get-tuple-element.49), channel_id=1, source_target_pairs={{0,256},{32,288},{64,320},{96,352},{128,384},{160,416},{192,448},{... | collective-permute-start | bytes 940040 | tf_op jit(solution)/shard_map/ppermute | solution.py:51
  283.7 17.7 %collective-permute-start.38 = (f32[17,24,192]{2,1,0:T(8,128)S(1)}, f32[17,24,192]{2,1,0:T(8,128)}, u32[]{:S(2)}, u32[]{:S(2)}) collective-permute-start(f32[17,24,192]{2,1,0:T(8,128)S(1)} %select_bitcast_fusion.1), channel_id=1, source_target_pairs={{0,384},{32,416},{64,448},{96,480},{128,0},{160,32},{192,64},{224,... | collective-permute-start | bytes 940040 | tf_op jit(solution)/shard_map/ppermute | solution.py:51
  (23 other events, 317.0 us)

commit v7 on v4

--- a/solution.py
+++ b/solution.py
@@ -11,20 +11,25 @@
     z = r % ring
     other = lax.ppermute(x, "row", [(i, i ^ ring) for i in range(nrow)])
     pair = jnp.where(yh == 0, jnp.stack([x, other]), jnp.stack([other, x]))
-    send_right = [(i, (i // ring) * ring + (i % ring + 1) % ring) for i in range(nrow)]
-    send_left = [(i, (i // ring) * ring + (i % ring - 1) % ring) for i in range(nrow)]
+
+    def shift(d):
+        return [(i, (i // ring) * ring + (i % ring + d) % ring) for i in range(nrow)]
+
+    steps = ring // 4
     got = [None] * ring
     got[0] = pair
-    from_left = pair
-    from_right = pair
-    for t in range(1, ring // 2):
-        from_left = lax.ppermute(from_left, "row", send_right)
-        from_right = lax.ppermute(from_right, "row", send_left)
-        got[t] = from_left
-        got[ring - t] = from_right
-    low = lax.ppermute(from_left[0], "row", send_right)
-    high = lax.ppermute(from_right[1], "row", send_left)
-    got[ring // 2] = jnp.stack([low, high])
+    near_r = near_l = far_r = far_l = pair
+    for t in range(1, steps + 1):
+        hop = steps + 1 if t == 1 else 1
+        near_r = lax.ppermute(near_r, "row", shift(1))
+        near_l = lax.ppermute(near_l, "row", shift(-1))
+        far_r = lax.ppermute(far_r, "row", shift(hop))
+        got[t] = near_r
+        got[ring - t] = near_l
+        got[steps + t] = far_r
+        if t < steps:
+            far_l = lax.ppermute(far_l, "row", shift(-hop))
+            got[ring - steps - t] = far_l
     stacked = jnp.stack(got)
     return stacked.reshape((ring * pairs,) + x.shape), z
 

time: 306 us -> 316 us (1.033)
  waiting for transfers between devices: 62.8 us -> 75.1 us
  starting transfers between devices: 160 us -> 156 us
    ppermute x32 -> x30, waiting for transfers between devices: 34.3 us -> 46.4 us  [the longest x8 42 us: ring_gather(): far_r = lax.ppermute(far_r, 'row', shift(hop))]
    ppermute x32 -> x30, starting transfers between devices: 113 us -> 121 us  [the longest x6 34.1 us: ring_gather(): far_l = lax.ppermute(far_l, 'row', shift(-hop))]
    ppermute x1, starting transfers between devices: 12.1 us -> 5.88 us  [local(): other_ring = lax.ppermute(mine_ring, 'aux', partner)]
    ppermute x1, starting transfers between devices: 10.5 us -> 5.18 us  [reduce_scatter_aux(): lax.ppermute(send, 'aux', [(i, i ^ 1) for i in range(naux)])]
    unnamed x37 -> x39, local copies, waits for them, and re-layouts: 23.1 us -> 25.5 us
  transfers between devices with their start and end apart: 40 -> 38, of which waited for: 24 -> 13; matrix products, arithmetic and copies ran while one was open for 9% -> 11% of each run, Pallas kernels for 0% -> 0%
where the time goes in v7:
time: 316 us; the launch traced here: 311 us
  starting transfers between devices  156 us (49%)
  waiting for transfers between devices  75.1 us (24%)
  local copies, waits for them, and re-layouts  57 us (18%)
  matrix products  13.4 us (4%)
  other arithmetic  8.7 us (3%)
    ppermute x8, waiting for transfers between devices, ring_gather(): far_r = lax.ppermute(far_r, 'row', shift(hop))  42 us
    ppermute x6, starting transfers between devices, ring_gather(): far_l = lax.ppermute(far_l, 'row', shift(-hop))  34.1 us
    ppermute x8, starting transfers between devices, ring_gather(): near_l = lax.ppermute(near_l, 'row', shift(-1))  34 us
    ppermute x8, starting transfers between devices, ring_gather(): far_r = lax.ppermute(far_r, 'row', shift(hop))  32.9 us
    unnamed x39, local copies, waits for them, and re-layouts  25.5 us
    ppermute x8, starting transfers between devices, ring_gather(): near_r = lax.ppermute(near_r, 'row', shift(1))  20.2 us
    ppermute x3, waiting for transfers between devices, reduce_scatter_aux(): lax.ppermute(jnp.take(on_chip, (x_me + dx) % nx, axis=1), 'aux', perm)  13.1 us
    ppermute x2, starting transfers between devices, ring_gather(): other = lax.ppermute(x, 'row', [(i, i ^ ring) for i in range(nrow)])  10.5 us
  transfers between devices with their start and end apart: 38, of which 13 were waited for; matrix products, arithmetic and copies ran while one was open for 11% of the time, Pallas kernels for 0%

profile of v7, /device:TPU:1, one launch (start us, length us, event | category | flops | bytes accessed | tf_op | source)
XLA Modules:
  0.0 311.3 jit_solution(17048572521838794710)
XLA Ops:
  0.9 5.6 %collective-permute-start = (bf16[192,256]{1,0:T(8,128)(2,1)S(1)}, bf16[192,256]{1,0:T(8,128)(2,1)S(1)}, u32[]{:S(2)}, u32[]{:S(2)}) collective-permute-start(bf16[192,256]{1,0:T(8,128)(2,1)S(1)} %constant_dynamic-slice_fusion), channel_id=1, source_target_pairs={{0,16},{1,17},{2,18},{3,19},{4,20},{5,21},{6,22},{7,23},{8,24},{9,... | collective-permute-start | bytes 294920 | tf_op jit(solution)/shard_map/ppermute | solution.py:12
  12.3 10.2 %collective-permute-start.5 = (bf16[2,192,256]{2,1,0:T(8,128)(2,1)S(1)}, bf16[2,192,256]{2,1,0:T(8,128)(2,1)S(1)}, u32[]{:S(2)}, u32[]{:S(2)}) collective-permute-start(bf16[2,192,256]{2,1,0:T(8,128)(2,1)S(1)} %maximum_select_fusion.9), channel_id=1, source_target_pairs={{0,5},{1,6},{2,7},{3,8},{4,9},{5,10},{6,11},{7,12},{8,13},{9,14},{... | collective-permute-start | bytes 589832 | tf_op jit(solution)/shard_map/ppermute | solution.py:26
  22.5 5.0 %collective-permute-start.9 = (bf16[2,192,256]{2,1,0:T(8,128)(2,1)S(1)}, bf16[2,192,256]{2,1,0:T(8,128)(2,1)S(1)}, u32[]{:S(2)}, u32[]{:S(2)}) collective-permute-start(bf16[2,192,256]{2,1,0:T(8,128)(2,1)S(1)} %maximum_select_fusion.9), channel_id=1, source_target_pairs={{0,11},{1,12},{2,13},{3,14},{4,15},{5,0},{6,1},{7,2},{8,3},{9,4},{... | collective-permute-start | bytes 589832 | tf_op jit(solution)/shard_map/ppermute | solution.py:31
  36.3 5.3 %collective-permute-start.6 = (bf16[2,192,256]{2,1,0:T(8,128)(2,1)S(1)}, bf16[2,192,256]{2,1,0:T(8,128)(2,1)S(1)}, u32[]{:S(2)}, u32[]{:S(2)}) collective-permute-start(bf16[2,192,256]{2,1,0:T(8,128)(2,1)S(1)} %collective-permute-done.5), channel_id=1, source_target_pairs={{0,1},{1,2},{2,3},{3,4},{4,5},{5,6},{6,7},{7,8},{8,9},{9,10},{10,1... | collective-permute-start | bytes 589832 | tf_op jit(solution)/shard_map/ppermute | solution.py:26
  41.6 11.5 %collective-permute-start.10 = (bf16[2,192,256]{2,1,0:T(8,128)(2,1)S(1)}, bf16[2,192,256]{2,1,0:T(8,128)(2,1)S(1)}, u32[]{:S(2)}, u32[]{:S(2)}) collective-permute-start(bf16[2,192,256]{2,1,0:T(8,128)(2,1)S(1)} %collective-permute-done.9), channel_id=1, source_target_pairs={{0,15},{1,0},{2,1},{3,2},{4,3},{5,4},{6,5},{7,6},{8,7},{9,8},{10,9... | collective-permute-start | bytes 589832 | tf_op jit(solution)/shard_map/ppermute | solution.py:31
  53.1 4.6 %collective-permute-start.13 = (bf16[2,192,256]{2,1,0:T(8,128)(2,1)S(1)}, bf16[2,192,256]{2,1,0:T(8,128)(2,1)S(1)}, u32[]{:S(2)}, u32[]{:S(2)}) collective-permute-start(bf16[2,192,256]{2,1,0:T(8,128)(2,1)S(1)} %collective-permute-done.12), channel_id=1, source_target_pairs={{0,15},{1,0},{2,1},{3,2},{4,3},{5,4},{6,5},{7,6},{8,7},{9,8},{10,9... | collective-permute-start | bytes 589832 | tf_op jit(solution)/shard_map/ppermute | solution.py:25
  89.1 5.9 %collective-permute-start.16 = (bf16[32,192,256]{2,1,0:T(8,128)(2,1)}, bf16[32,192,256]{2,1,0:T(8,128)(2,1)}, u32[]{:S(2)}, u32[]{:S(2)}) collective-permute-start(bf16[32,192,256]{2,1,0:T(8,128)(2,1)} %bitcast.23), channel_id=1, source_target_pairs={{0,32},{32,0},{64,96},{96,64},{128,160},{160,128},{192,224},{224,1... | collective-permute-start | bytes 9437192 | tf_op jit(solution)/shard_map/ppermute | solution.py:75
  95.0 4.6 %reshape_squeeze.3 = bf16[192,32,192]{2,1,0:T(8,128)(2,1)} reshape(bf16[1,192,6144]{2,1,0:T(8,128)(2,1)S(1)} %copy-done.1) | data formatting | bytes 4718592 | tf_op jit(solution)/shard_map/reshape;squeeze | solution.py:84
  105.8 8.4 %fusion.20 = bf16[192,512]{1,0:T(8,128)(2,1)S(1)} fusion(bf16[32,192,256]{2,1,0:T(8,128)(2,1)} %collective-permute-done.16, bf16[32,192,256]{2,1,0:T(8,128)(2,1)} %bitcast.23, pred[]{:T(512)S(6)} %eq.24, bf16[32,192,192]{2,1,0:T(8,128)(2,1)} %gather_fusion, pred[32]{0:T(512)(128)(4,1)S(1)} %compare_and_fusion.2), kind=kOutput, calls=%fused_computation.25 | convolution fusion | flops 1237549056 | bytes 8847393 | tf_op jit(solution)/shard_map/dot_general | solution.py:86
  114.2 4.8 %collective-permute-start.17 = (bf16[192,512]{1,0:T(8,128)(2,1)S(1)}, bf16[192,512]{1,0:T(8,128)(2,1)S(1)}, u32[]{:S(2)}, u32[]{:S(2)}) collective-permute-start(bf16[192,512]{1,0:T(8,128)(2,1)S(1)} %fusion.20), channel_id=1, source_target_pairs={{0,16},{1,17},{2,18},{3,19},{4,20},{5,21},{6,22},{7,23},{8,24},{9,... | collective-permute-start | bytes 589832 | tf_op jit(solution)/shard_map/ppermute | solution.py:12
  119.0 5.0 %collective-permute-done.17 = bf16[192,512]{1,0:T(8,128)(2,1)S(1)} collective-permute-done((bf16[192,512]{1,0:T(8,128)(2,1)S(1)}, bf16[192,512]{1,0:T(8,128)(2,1)S(1)}, u32[]{:S(2)}, u32[]{:S(2)}) %collective-permute-start.17) | collective-permute-done | bytes 196640 | tf_op jit(solution)/shard_map/ppermute | solution.py:12
  127.8 6.2 %collective-permute-start.22 = (bf16[2,192,512]{2,1,0:T(8,128)(2,1)S(1)}, bf16[2,192,512]{2,1,0:T(8,128)(2,1)S(1)}, u32[]{:S(2)}, u32[]{:S(2)}) collective-permute-start(bf16[2,192,512]{2,1,0:T(8,128)(2,1)S(1)} %maximum_select_fusion.7), channel_id=1, source_target_pairs={{0,5},{1,6},{2,7},{3,8},{4,9},{5,10},{6,11},{7,12},{8,13},{9,14},{... | collective-permute-start | bytes 1179656 | tf_op jit(solution)/shard_map/ppermute | solution.py:26
  145.2 35.6 %collective-permute-done.22 = bf16[2,192,512]{2,1,0:T(8,128)(2,1)S(1)} collective-permute-done((bf16[2,192,512]{2,1,0:T(8,128)(2,1)S(1)}, bf16[2,192,512]{2,1,0:T(8,128)(2,1)S(1)}, u32[]{:S(2)}, u32[]{:S(2)}) %collective-permute-start.22) | collective-permute-done | bytes 393248 | tf_op jit(solution)/shard_map/ppermute | solution.py:26
  182.7 4.6 %collective-permute-start.30 = (bf16[2,192,512]{2,1,0:T(8,128)(2,1)S(1)}, bf16[2,192,512]{2,1,0:T(8,128)(2,1)S(1)}, u32[]{:S(2)}, u32[]{:S(2)}) collective-permute-start(bf16[2,192,512]{2,1,0:T(8,128)(2,1)S(1)} %collective-permute-done.29), channel_id=1, source_target_pairs={{0,15},{1,0},{2,1},{3,2},{4,3},{5,4},{6,5},{7,6},{8,7},{9,8},{10,9... | collective-permute-start | bytes 1179656 | tf_op jit(solution)/shard_map/ppermute | solution.py:25
  187.5 7.1 %collective-permute-start.27 = (bf16[2,192,512]{2,1,0:T(8,128)(2,1)S(1)}, bf16[2,192,512]{2,1,0:T(8,128)(2,1)S(1)}, u32[]{:S(2)}, u32[]{:S(2)}) collective-permute-start(bf16[2,192,512]{2,1,0:T(8,128)(2,1)S(1)} %collective-permute-done.26), channel_id=1, source_target_pairs={{0,15},{1,0},{2,1},{3,2},{4,3},{5,4},{6,5},{7,6},{8,7},{9,8},{10,9... | collective-permute-start | bytes 1179656 | tf_op jit(solution)/shard_map/ppermute | solution.py:31
  218.7 4.8 %collective-permute-start.32 = (bf16[2,192,512]{2,1,0:T(8,128)(2,1)S(1)}, bf16[2,192,512]{2,1,0:T(8,128)(2,1)S(1)}, u32[]{:S(2)}, u32[]{:S(2)}) collective-permute-start(bf16[2,192,512]{2,1,0:T(8,128)(2,1)S(1)} %collective-permute-done.31), channel_id=1, source_target_pairs={{0,15},{1,0},{2,1},{3,2},{4,3},{5,4},{6,5},{7,6},{8,7},{9,8},{10,9... | collective-permute-start | bytes 1179656 | tf_op jit(solution)/shard_map/ppermute | solution.py:25
  228.4 4.7 %collective-permute-done.25 = bf16[2,192,512]{2,1,0:T(8,128)(2,1)S(1)} collective-permute-done((bf16[2,192,512]{2,1,0:T(8,128)(2,1)S(1)}, bf16[2,192,512]{2,1,0:T(8,128)(2,1)S(1)}, u32[]{:S(2)}, u32[]{:S(2)}) %collective-permute-start.25) | collective-permute-done | bytes 393248 | tf_op jit(solution)/shard_map/ppermute | solution.py:26
  242.9 5.6 %gather_fusion.3 = bf16[17,192,512]{2,1,0:T(8,128)(2,1)} fusion(bf16[32,192,512]{2,1,0:T(8,128)(2,1)} %bitcast.44, s32[1024]{0:T(1024)S(1)} %pad_clamp_fusion), kind=kCustom, calls=%fused_computation.1.clone | custom fusion | bytes 6684740 | tf_op jit(solution)/shard_map/jit(_take)/gather | solution.py:93
  248.5 5.0 %fusion.7 = f32[17,192,192]{2,1,0:T(8,128)} fusion(bf16[17,192,512]{2,1,0:T(8,128)(2,1)} %gather_fusion.3, bf16[17,192,512]{2,1,0:T(8,128)(2,1)S(1)} %gather_fusion.2, pred[17]{0:T(512)(128)(4,1)S(1)} %get-tuple-element.46, pred[17]{0:T(512)(128)(4,1)S(1)} %get-tuple-element.51), kind=kOutput, calls=%fused_computation.12 | convolution fusion | flops 645070848 | bytes 9191458 | tf_op jit(solution)/shard_map/sao,sbo->sab/dot_general | solution.py:94
  253.4 4.6 %reshape_reshape.3 = f32[17,4,2,2,12,192]{5,4,3,2,1,0:T(8,128)} reshape(f32[17,192,192]{2,1,0:T(8,128)} %fusion.7) | data formatting | bytes 5013504 | tf_op jit(solution)/shard_map/reshape;reshape | solution.py:47
  261.5 5.2 %collective-permute-start.33 = (f32[17,4,2,12,192]{4,1,3,2,0:T(4,128)S(1)}, f32[17,4,2,12,192]{4,1,3,2,0:T(4,128)}, u32[]{:S(2)}, u32[]{:S(2)}) collective-permute-start(f32[17,4,2,12,192]{4,1,3,2,0:T(4,128)S(1)} %copy.23), channel_id=1, source_target_pairs={{0,32},{32,0},{64,96},{96,64},{128,160},{160,128},{192,224},{224,1... | collective-permute-start | bytes 3760136 | tf_op jit(solution)/shard_map/ppermute | solution.py:50
  278.1 4.5 %collective-permute-start.35 = (f32[17,2,12,192]{3,1,2,0:T(2,128)}, f32[17,2,12,192]{3,1,2,0:T(2,128)S(1)}, u32[]{:S(2)}, u32[]{:S(2)}) collective-permute-start(f32[17,2,12,192]{3,1,2,0:T(2,128)} %copy.27), channel_id=1, source_target_pairs={{0,256},{32,288},{64,320},{96,352},{128,384},{160,416},{192,448},{... | collective-permute-start | bytes 940040 | tf_op jit(solution)/shard_map/ppermute | solution.py:54
  288.2 9.9 %collective-permute-done.35 = f32[17,2,12,192]{3,1,2,0:T(2,128)S(1)} collective-permute-done((f32[17,2,12,192]{3,1,2,0:T(2,128)}, f32[17,2,12,192]{3,1,2,0:T(2,128)S(1)}, u32[]{:S(2)}, u32[]{:S(2)}) %collective-permute-start.35) | collective-permute-done | bytes 313376 | tf_op jit(solution)/shard_map/ppermute | solution.py:54
  305.1 5.4 %collective-permute-done.37 = f32[17,12,192]{2,1,0:T(8,128)S(1)} collective-permute-done((f32[17,12,192]{2,1,0:T(8,128)S(1)}, f32[17,12,192]{2,1,0:T(8,128)S(1)}, u32[]{:S(2)}, u32[]{:S(2)}) %collective-permute-start.37) | collective-permute-done | bytes 156704 | tf_op jit(solution)/shard_map/ppermute | solution.py:59
  (128 shorter events, 136.5 us)
Async XLA Ops:
  8.6 24.1 %collective-permute-start.1 = (bf16[2,192,256]{2,1,0:T(8,128)(2,1)S(1)}, bf16[2,192,256]{2,1,0:T(8,128)(2,1)S(1)}, u32[]{:S(2)}, u32[]{:S(2)}) collective-permute-start(bf16[2,192,256]{2,1,0:T(8,128)(2,1)S(1)} %maximum_select_fusion.9), channel_id=1, source_target_pairs={{0,1},{1,2},{2,3},{3,4},{4,5},{5,6},{6,7},{7,8},{8,9},{9,10},{10,1... | collective-permute-start | bytes 589832 | tf_op jit(solution)/shard_map/ppermute | solution.py:24
  12.3 24.0 %collective-permute-start.5 = (bf16[2,192,256]{2,1,0:T(8,128)(2,1)S(1)}, bf16[2,192,256]{2,1,0:T(8,128)(2,1)S(1)}, u32[]{:S(2)}, u32[]{:S(2)}) collective-permute-start(bf16[2,192,256]{2,1,0:T(8,128)(2,1)S(1)} %maximum_select_fusion.9), channel_id=1, source_target_pairs={{0,5},{1,6},{2,7},{3,8},{4,9},{5,10},{6,11},{7,12},{8,13},{9,14},{... | collective-permute-start | bytes 589832 | tf_op jit(solution)/shard_map/ppermute | solution.py:26
  22.5 19.1 %collective-permute-start.9 = (bf16[2,192,256]{2,1,0:T(8,128)(2,1)S(1)}, bf16[2,192,256]{2,1,0:T(8,128)(2,1)S(1)}, u32[]{:S(2)}, u32[]{:S(2)}) collective-permute-start(bf16[2,192,256]{2,1,0:T(8,128)(2,1)S(1)} %maximum_select_fusion.9), channel_id=1, source_target_pairs={{0,11},{1,12},{2,13},{3,14},{4,15},{5,0},{6,1},{7,2},{8,3},{9,4},{... | collective-permute-start | bytes 589832 | tf_op jit(solution)/shard_map/ppermute | solution.py:31
  27.5 25.7 %collective-permute-start.12 = (bf16[2,192,256]{2,1,0:T(8,128)(2,1)S(1)}, bf16[2,192,256]{2,1,0:T(8,128)(2,1)S(1)}, u32[]{:S(2)}, u32[]{:S(2)}) collective-permute-start(bf16[2,192,256]{2,1,0:T(8,128)(2,1)S(1)} %maximum_select_fusion.9), channel_id=1, source_target_pairs={{0,15},{1,0},{2,1},{3,2},{4,3},{5,4},{6,5},{7,6},{8,7},{9,8},{10,9... | collective-permute-start | bytes 589832 | tf_op jit(solution)/shard_map/ppermute | solution.py:25
  32.7 25.7 %collective-permute-start.2 = (bf16[2,192,256]{2,1,0:T(8,128)(2,1)S(1)}, bf16[2,192,256]{2,1,0:T(8,128)(2,1)S(1)}, u32[]{:S(2)}, u32[]{:S(2)}) collective-permute-start(bf16[2,192,256]{2,1,0:T(8,128)(2,1)S(1)} %collective-permute-done.1), channel_id=1, source_target_pairs={{0,1},{1,2},{2,3},{3,4},{4,5},{5,6},{6,7},{7,8},{8,9},{9,10},{10,1... | collective-permute-start | bytes 589832 | tf_op jit(solution)/shard_map/ppermute | solution.py:24
  36.3 24.0 %collective-permute-start.6 = (bf16[2,192,256]{2,1,0:T(8,128)(2,1)S(1)}, bf16[2,192,256]{2,1,0:T(8,128)(2,1)S(1)}, u32[]{:S(2)}, u32[]{:S(2)}) collective-permute-start(bf16[2,192,256]{2,1,0:T(8,128)(2,1)S(1)} %collective-permute-done.5), channel_id=1, source_target_pairs={{0,1},{1,2},{2,3},{3,4},{4,5},{5,6},{6,7},{7,8},{8,9},{9,10},{10,1... | collective-permute-start | bytes 589832 | tf_op jit(solution)/shard_map/ppermute | solution.py:26
  41.6 21.3 %collective-permute-start.10 = (bf16[2,192,256]{2,1,0:T(8,128)(2,1)S(1)}, bf16[2,192,256]{2,1,0:T(8,128)(2,1)S(1)}, u32[]{:S(2)}, u32[]{:S(2)}) collective-permute-start(bf16[2,192,256]{2,1,0:T(8,128)(2,1)S(1)} %collective-permute-done.9), channel_id=1, source_target_pairs={{0,15},{1,0},{2,1},{3,2},{4,3},{5,4},{6,5},{7,6},{8,7},{9,8},{10,9... | collective-permute-start | bytes 589832 | tf_op jit(solution)/shard_map/ppermute | solution.py:31
  62.9 21.3 %collective-permute-start.11 = (bf16[2,192,256]{2,1,0:T(8,128)(2,1)S(1)}, bf16[2,192,256]{2,1,0:T(8,128)(2,1)S(1)}, u32[]{:S(2)}, u32[]{:S(2)}) collective-permute-start(bf16[2,192,256]{2,1,0:T(8,128)(2,1)S(1)} %collective-permute-done.10), channel_id=1, source_target_pairs={{0,15},{1,0},{2,1},{3,2},{4,3},{5,4},{6,5},{7,6},{8,7},{9,8},{10,9... | collective-permute-start | bytes 589832 | tf_op jit(solution)/shard_map/ppermute | solution.py:31
  89.1 16.7 %collective-permute-start.16 = (bf16[32,192,256]{2,1,0:T(8,128)(2,1)}, bf16[32,192,256]{2,1,0:T(8,128)(2,1)}, u32[]{:S(2)}, u32[]{:S(2)}) collective-permute-start(bf16[32,192,256]{2,1,0:T(8,128)(2,1)} %bitcast.23), channel_id=1, source_target_pairs={{0,32},{32,0},{64,96},{96,64},{128,160},{160,128},{192,224},{224,1... | collective-permute-start | bytes 9437192 | tf_op jit(solution)/shard_map/ppermute | solution.py:75
  124.1 17.6 %collective-permute-start.18 = (bf16[2,192,512]{2,1,0:T(8,128)(2,1)S(1)}, bf16[2,192,512]{2,1,0:T(8,128)(2,1)}, u32[]{:S(2)}, u32[]{:S(2)}) collective-permute-start(bf16[2,192,512]{2,1,0:T(8,128)(2,1)S(1)} %maximum_select_fusion.7), channel_id=1, source_target_pairs={{0,1},{1,2},{2,3},{3,4},{4,5},{5,6},{6,7},{7,8},{8,9},{9,10},{10,1... | collective-permute-start | bytes 1179656 | tf_op jit(solution)/shard_map/ppermute | solution.py:24
  127.8 53.0 %collective-permute-start.22 = (bf16[2,192,512]{2,1,0:T(8,128)(2,1)S(1)}, bf16[2,192,512]{2,1,0:T(8,128)(2,1)S(1)}, u32[]{:S(2)}, u32[]{:S(2)}) collective-permute-start(bf16[2,192,512]{2,1,0:T(8,128)(2,1)S(1)} %maximum_select_fusion.7), channel_id=1, source_target_pairs={{0,5},{1,6},{2,7},{3,8},{4,9},{5,10},{6,11},{7,12},{8,13},{9,14},{... | collective-permute-start | bytes 1179656 | tf_op jit(solution)/shard_map/ppermute | solution.py:26
  134.0 48.8 %collective-permute-start.29 = (bf16[2,192,512]{2,1,0:T(8,128)(2,1)S(1)}, bf16[2,192,512]{2,1,0:T(8,128)(2,1)S(1)}, u32[]{:S(2)}, u32[]{:S(2)}) collective-permute-start(bf16[2,192,512]{2,1,0:T(8,128)(2,1)S(1)} %maximum_select_fusion.7), channel_id=1, source_target_pairs={{0,15},{1,0},{2,1},{3,2},{4,3},{5,4},{6,5},{7,6},{8,7},{9,8},{10,9... | collective-permute-start | bytes 1179656 | tf_op jit(solution)/shard_map/ppermute | solution.py:25
  138.9 48.6 %collective-permute-start.26 = (bf16[2,192,512]{2,1,0:T(8,128)(2,1)S(1)}, bf16[2,192,512]{2,1,0:T(8,128)(2,1)S(1)}, u32[]{:S(2)}, u32[]{:S(2)}) collective-permute-start(bf16[2,192,512]{2,1,0:T(8,128)(2,1)S(1)} %maximum_select_fusion.7), channel_id=1, source_target_pairs={{0,11},{1,12},{2,13},{3,14},{4,15},{5,0},{6,1},{7,2},{8,3},{9,4},{... | collective-permute-start | bytes 1179656 | tf_op jit(solution)/shard_map/ppermute | solution.py:31
  141.7 52.9 %collective-permute-start.19 = (bf16[2,192,512]{2,1,0:T(8,128)(2,1)}, bf16[2,192,512]{2,1,0:T(8,128)(2,1)}, u32[]{:S(2)}, u32[]{:S(2)}) collective-permute-start(bf16[2,192,512]{2,1,0:T(8,128)(2,1)} %collective-permute-done.18), channel_id=1, source_target_pairs={{0,1},{1,2},{2,3},{3,4},{4,5},{5,6},{6,7},{7,8},{8,9},{9,10},{10,1... | collective-permute-start | bytes 1179656 | tf_op jit(solution)/shard_map/ppermute | solution.py:24
  180.8 16.6 %collective-permute-start.23 = (bf16[2,192,512]{2,1,0:T(8,128)(2,1)S(1)}, bf16[2,192,512]{2,1,0:T(8,128)(2,1)S(1)}, u32[]{:S(2)}, u32[]{:S(2)}) collective-permute-start(bf16[2,192,512]{2,1,0:T(8,128)(2,1)S(1)} %collective-permute-done.22), channel_id=1, source_target_pairs={{0,1},{1,2},{2,3},{3,4},{4,5},{5,6},{6,7},{7,8},{8,9},{9,10},{10,1... | collective-permute-start | bytes 1179656 | tf_op jit(solution)/shard_map/ppermute | solution.py:26
  182.7 18.0 %collective-permute-start.30 = (bf16[2,192,512]{2,1,0:T(8,128)(2,1)S(1)}, bf16[2,192,512]{2,1,0:T(8,128)(2,1)S(1)}, u32[]{:S(2)}, u32[]{:S(2)}) collective-permute-start(bf16[2,192,512]{2,1,0:T(8,128)(2,1)S(1)} %collective-permute-done.29), channel_id=1, source_target_pairs={{0,15},{1,0},{2,1},{3,2},{4,3},{5,4},{6,5},{7,6},{8,7},{9,8},{10,9... | collective-permute-start | bytes 1179656 | tf_op jit(solution)/shard_map/ppermute | solution.py:25
  187.5 21.8 %collective-permute-start.27 = (bf16[2,192,512]{2,1,0:T(8,128)(2,1)S(1)}, bf16[2,192,512]{2,1,0:T(8,128)(2,1)S(1)}, u32[]{:S(2)}, u32[]{:S(2)}) collective-permute-start(bf16[2,192,512]{2,1,0:T(8,128)(2,1)S(1)} %collective-permute-done.26), channel_id=1, source_target_pairs={{0,15},{1,0},{2,1},{3,2},{4,3},{5,4},{6,5},{7,6},{8,7},{9,8},{10,9... | collective-permute-start | bytes 1179656 | tf_op jit(solution)/shard_map/ppermute | solution.py:31
  194.6 18.5 %collective-permute-start.20 = (bf16[2,192,512]{2,1,0:T(8,128)(2,1)}, bf16[2,192,512]{2,1,0:T(8,128)(2,1)}, u32[]{:S(2)}, u32[]{:S(2)}) collective-permute-start(bf16[2,192,512]{2,1,0:T(8,128)(2,1)} %collective-permute-done.19), channel_id=1, source_target_pairs={{0,1},{1,2},{2,3},{3,4},{4,5},{5,6},{6,7},{7,8},{8,9},{9,10},{10,1... | collective-permute-start | bytes 1179656 | tf_op jit(solution)/shard_map/ppermute | solution.py:24
  197.4 19.4 %collective-permute-start.24 = (bf16[2,192,512]{2,1,0:T(8,128)(2,1)S(1)}, bf16[2,192,512]{2,1,0:T(8,128)(2,1)S(1)}, u32[]{:S(2)}, u32[]{:S(2)}) collective-permute-start(bf16[2,192,512]{2,1,0:T(8,128)(2,1)S(1)} %collective-permute-done.23), channel_id=1, source_target_pairs={{0,1},{1,2},{2,3},{3,4},{4,5},{5,6},{6,7},{7,8},{8,9},{9,10},{10,1... | collective-permute-start | bytes 1179656 | tf_op jit(solution)/shard_map/ppermute | solution.py:26
  200.7 18.0 %collective-permute-start.31 = (bf16[2,192,512]{2,1,0:T(8,128)(2,1)S(1)}, bf16[2,192,512]{2,1,0:T(8,128)(2,1)S(1)}, u32[]{:S(2)}, u32[]{:S(2)}) collective-permute-start(bf16[2,192,512]{2,1,0:T(8,128)(2,1)S(1)} %collective-permute-done.30), channel_id=1, source_target_pairs={{0,15},{1,0},{2,1},{3,2},{4,3},{5,4},{6,5},{7,6},{8,7},{9,8},{10,9... | collective-permute-start | bytes 1179656 | tf_op jit(solution)/shard_map/ppermute | solution.py:25
  209.3 24.6 %collective-permute-start.28 = (bf16[2,192,512]{2,1,0:T(8,128)(2,1)S(1)}, bf16[2,192,512]{2,1,0:T(8,128)(2,1)S(1)}, u32[]{:S(2)}, u32[]{:S(2)}) collective-permute-start(bf16[2,192,512]{2,1,0:T(8,128)(2,1)S(1)} %collective-permute-done.27), channel_id=1, source_target_pairs={{0,15},{1,0},{2,1},{3,2},{4,3},{5,4},{6,5},{7,6},{8,7},{9,8},{10,9... | collective-permute-start | bytes 1179656 | tf_op jit(solution)/shard_map/ppermute | solution.py:31
  218.7 17.5 %collective-permute-start.32 = (bf16[2,192,512]{2,1,0:T(8,128)(2,1)S(1)}, bf16[2,192,512]{2,1,0:T(8,128)(2,1)S(1)}, u32[]{:S(2)}, u32[]{:S(2)}) collective-permute-start(bf16[2,192,512]{2,1,0:T(8,128)(2,1)S(1)} %collective-permute-done.31), channel_id=1, source_target_pairs={{0,15},{1,0},{2,1},{3,2},{4,3},{5,4},{6,5},{7,6},{8,7},{9,8},{10,9... | collective-permute-start | bytes 1179656 | tf_op jit(solution)/shard_map/ppermute | solution.py:25
  278.1 20.0 %collective-permute-start.35 = (f32[17,2,12,192]{3,1,2,0:T(2,128)}, f32[17,2,12,192]{3,1,2,0:T(2,128)S(1)}, u32[]{:S(2)}, u32[]{:S(2)}) collective-permute-start(f32[17,2,12,192]{3,1,2,0:T(2,128)} %copy.27), channel_id=1, source_target_pairs={{0,256},{32,288},{64,320},{96,352},{128,384},{160,416},{192,448},{... | collective-permute-start | bytes 940040 | tf_op jit(solution)/shard_map/ppermute | solution.py:54
  283.7 16.9 %collective-permute-start.36 = (f32[17,2,12,192]{3,1,2,0:T(2,128)}, f32[17,2,12,192]{3,1,2,0:T(2,128)}, u32[]{:S(2)}, u32[]{:S(2)}) collective-permute-start(f32[17,2,12,192]{3,1,2,0:T(2,128)} %copy.29), channel_id=1, source_target_pairs={{0,384},{32,416},{64,448},{96,480},{128,0},{160,32},{192,64},{224,... | collective-permute-start | bytes 940040 | tf_op jit(solution)/shard_map/ppermute | solution.py:54
  (19 other events, 298.3 us)

commit v8 on v7

--- a/solution.py
+++ b/solution.py
@@ -5,6 +5,31 @@
 
 
 def ring_gather(x, nrow, ring):
+    pairs = nrow // ring
+    r = lax.axis_index("row")
+    yh = r // ring
+    z = r % ring
+    other = lax.ppermute(x, "row", [(i, i ^ ring) for i in range(nrow)])
+    pair = jnp.where(yh == 0, jnp.stack([x, other]), jnp.stack([other, x]))
+    send_right = [(i, (i // ring) * ring + (i % ring + 1) % ring) for i in range(nrow)]
+    send_left = [(i, (i // ring) * ring + (i % ring - 1) % ring) for i in range(nrow)]
+    got = [None] * ring
+    got[0] = pair
+    from_left = pair
+    from_right = pair
+    for t in range(1, ring // 2):
+        from_left = lax.ppermute(from_left, "row", send_right)
+        from_right = lax.ppermute(from_right, "row", send_left)
+        got[t] = from_left
+        got[ring - t] = from_right
+    low = lax.ppermute(from_left[0], "row", send_right)
+    high = lax.ppermute(from_right[1], "row", send_left)
+    got[ring // 2] = jnp.stack([low, high])
+    stacked = jnp.stack(got)
+    return stacked.reshape((ring * pairs,) + x.shape), z
+
+
+def ring_gather_jump(x, nrow, ring):
     pairs = nrow // ring
     r = lax.axis_index("row")
     yh = r // ring
@@ -70,7 +95,7 @@
 
     core = lax.axis_index("aux") % 2
     mine = lax.dynamic_slice_in_dim(occ_coeff, core * half_cols, half_cols, 1)
-    mine_ring, z = ring_gather(mine, nrow, ring)
+    mine_ring, z = ring_gather_jump(mine, nrow, ring)
     partner = [(i, i ^ 1) for i in range(naux)]
     other_ring = lax.ppermute(mine_ring, "aux", partner)
     coeff_ring = jnp.where(

time: 316 us -> 304 us (0.962)
  the two profiles are of different devices: /device:TPU:1 before, /device:TPU:106 now
where the time goes in v8:
time: 304 us; the launch traced here: 303 us
  starting transfers between devices  138 us (45%)
  waiting for transfers between devices  85.8 us (28%)
  local copies, waits for them, and re-layouts  55.1 us (18%)
  matrix products  13.4 us (4%)
  other arithmetic  9.47 us (3%)
    ppermute x7, starting transfers between devices, ring_gather(): from_left = lax.ppermute(from_left, 'row', send_right)  35.2 us
    unnamed x38, local copies, waits for them, and re-layouts  23.7 us
    ppermute x7, waiting for transfers between devices, ring_gather(): from_left = lax.ppermute(from_left, 'row', send_right)  22.1 us
    ppermute x4, starting transfers between devices, ring_gather_jump(): near_r = lax.ppermute(near_r, 'row', shift(1))  19.5 us
    ppermute x4, starting transfers between devices, ring_gather_jump(): far_r = lax.ppermute(far_r, 'row', shift(hop))  15.3 us
    ppermute x3, waiting for transfers between devices, reduce_scatter_aux(): lax.ppermute(jnp.take(on_chip, (x_me + dx) % nx, axis=1), 'aux', perm)  15 us
    ppermute x7, starting transfers between devices, ring_gather(): from_right = lax.ppermute(from_right, 'row', send_left)  14.2 us
    ppermute x4, waiting for transfers between devices, ring_gather_jump(): far_r = lax.ppermute(far_r, 'row', shift(hop))  14 us
  transfers between devices with their start and end apart: 39, of which 19 were waited for; matrix products, arithmetic and copies ran while one was open for 10% of the time, Pallas kernels for 0%

profile of v8, /device:TPU:106, one launch (start us, length us, event | category | flops | bytes accessed | tf_op | source)
XLA Modules:
  0.0 302.8 jit_solution(8605086776709855217)
XLA Ops:
  9.0 5.2 %collective-permute-start.1 = (bf16[2,192,256]{2,1,0:T(8,128)(2,1)S(1)}, bf16[2,192,256]{2,1,0:T(8,128)(2,1)S(1)}, u32[]{:S(2)}, u32[]{:S(2)}) collective-permute-start(bf16[2,192,256]{2,1,0:T(8,128)(2,1)S(1)} %maximum_select_fusion.9), channel_id=1, source_target_pairs={{0,1},{1,2},{2,3},{3,4},{4,5},{5,6},{6,7},{7,8},{8,9},{9,10},{10,1... | collective-permute-start | bytes 589832 | tf_op jit(solution)/shard_map/ppermute | solution.py:49
  14.2 9.6 %collective-permute-start.5 = (bf16[2,192,256]{2,1,0:T(8,128)(2,1)S(1)}, bf16[2,192,256]{2,1,0:T(8,128)(2,1)S(1)}, u32[]{:S(2)}, u32[]{:S(2)}) collective-permute-start(bf16[2,192,256]{2,1,0:T(8,128)(2,1)S(1)} %maximum_select_fusion.9), channel_id=1, source_target_pairs={{0,5},{1,6},{2,7},{3,8},{4,9},{5,10},{6,11},{7,12},{8,13},{9,14},{... | collective-permute-start | bytes 589832 | tf_op jit(solution)/shard_map/ppermute | solution.py:51
  33.4 14.0 %collective-permute-done.5 = bf16[2,192,256]{2,1,0:T(8,128)(2,1)S(1)} collective-permute-done((bf16[2,192,256]{2,1,0:T(8,128)(2,1)S(1)}, bf16[2,192,256]{2,1,0:T(8,128)(2,1)S(1)}, u32[]{:S(2)}, u32[]{:S(2)}) %collective-permute-start.5) | collective-permute-done | bytes 196640 | tf_op jit(solution)/shard_map/ppermute | solution.py:51
  51.6 4.5 %collective-permute-start.10 = (bf16[2,192,256]{2,1,0:T(8,128)(2,1)S(1)}, bf16[2,192,256]{2,1,0:T(8,128)(2,1)S(1)}, u32[]{:S(2)}, u32[]{:S(2)}) collective-permute-start(bf16[2,192,256]{2,1,0:T(8,128)(2,1)S(1)} %collective-permute-done.9), channel_id=1, source_target_pairs={{0,15},{1,0},{2,1},{3,2},{4,3},{5,4},{6,5},{7,6},{8,7},{9,8},{10,9... | collective-permute-start | bytes 589832 | tf_op jit(solution)/shard_map/ppermute | solution.py:56
  58.7 5.1 %collective-permute-start.3 = (bf16[2,192,256]{2,1,0:T(8,128)(2,1)S(1)}, bf16[2,192,256]{2,1,0:T(8,128)(2,1)S(1)}, u32[]{:S(2)}, u32[]{:S(2)}) collective-permute-start(bf16[2,192,256]{2,1,0:T(8,128)(2,1)S(1)} %collective-permute-done.2), channel_id=1, source_target_pairs={{0,1},{1,2},{2,3},{3,4},{4,5},{5,6},{6,7},{7,8},{8,9},{9,10},{10,1... | collective-permute-start | bytes 589832 | tf_op jit(solution)/shard_map/ppermute | solution.py:49
  72.4 5.1 %collective-permute-start.4 = (bf16[2,192,256]{2,1,0:T(8,128)(2,1)S(1)}, bf16[2,192,256]{2,1,0:T(8,128)(2,1)S(1)}, u32[]{:S(2)}, u32[]{:S(2)}) collective-permute-start(bf16[2,192,256]{2,1,0:T(8,128)(2,1)S(1)} %collective-permute-done.3), channel_id=1, source_target_pairs={{0,1},{1,2},{2,3},{3,4},{4,5},{5,6},{6,7},{7,8},{8,9},{9,10},{10,1... | collective-permute-start | bytes 589832 | tf_op jit(solution)/shard_map/ppermute | solution.py:49
  94.3 4.6 %reshape_squeeze.3 = bf16[192,32,192]{2,1,0:T(8,128)(2,1)} reshape(bf16[1,192,6144]{2,1,0:T(8,128)(2,1)S(1)} %copy-done.1) | data formatting | bytes 4718592 | tf_op jit(solution)/shard_map/reshape;squeeze | solution.py:109
  105.1 8.4 %fusion.20 = bf16[192,512]{1,0:T(8,128)(2,1)S(1)} fusion(bf16[32,192,256]{2,1,0:T(8,128)(2,1)} %collective-permute-done.16, bf16[32,192,256]{2,1,0:T(8,128)(2,1)} %bitcast.23, pred[]{:T(512)S(6)} %eq.24, bf16[32,192,192]{2,1,0:T(8,128)(2,1)} %gather_fusion, pred[32]{0:T(512)(128)(4,1)S(1)} %compare_and_fusion.2), kind=kOutput, calls=%fused_computation.25 | convolution fusion | flops 1237549056 | bytes 8847393 | tf_op jit(solution)/shard_map/dot_general | solution.py:111
  117.8 6.5 %collective-permute-done.17 = bf16[192,512]{1,0:T(8,128)(2,1)S(1)} collective-permute-done((bf16[192,512]{1,0:T(8,128)(2,1)S(1)}, bf16[192,512]{1,0:T(8,128)(2,1)S(1)}, u32[]{:S(2)}, u32[]{:S(2)}) %collective-permute-start.17) | collective-permute-done | bytes 196640 | tf_op jit(solution)/shard_map/ppermute | solution.py:12
  130.1 6.7 %collective-permute-done.18 = bf16[2,192,512]{2,1,0:T(8,128)(2,1)S(1)} collective-permute-done((bf16[2,192,512]{2,1,0:T(8,128)(2,1)S(1)}, bf16[2,192,512]{2,1,0:T(8,128)(2,1)S(1)}, u32[]{:S(2)}, u32[]{:S(2)}) %collective-permute-start.18) | collective-permute-done | bytes 393248 | tf_op jit(solution)/shard_map/ppermute | solution.py:21
  143.3 5.2 %collective-permute-done.19 = bf16[2,192,512]{2,1,0:T(8,128)(2,1)S(1)} collective-permute-done((bf16[2,192,512]{2,1,0:T(8,128)(2,1)S(1)}, bf16[2,192,512]{2,1,0:T(8,128)(2,1)S(1)}, u32[]{:S(2)}, u32[]{:S(2)}) %collective-permute-start.19) | collective-permute-done | bytes 393248 | tf_op jit(solution)/shard_map/ppermute | solution.py:21
  148.5 5.5 %collective-permute-start.20 = (bf16[2,192,512]{2,1,0:T(8,128)(2,1)S(1)}, bf16[2,192,512]{2,1,0:T(8,128)(2,1)}, u32[]{:S(2)}, u32[]{:S(2)}) collective-permute-start(bf16[2,192,512]{2,1,0:T(8,128)(2,1)S(1)} %collective-permute-done.19), channel_id=1, source_target_pairs={{0,1},{1,2},{2,3},{3,4},{4,5},{5,6},{6,7},{7,8},{8,9},{9,10},{10,1... | collective-permute-start | bytes 1179656 | tf_op jit(solution)/shard_map/ppermute | solution.py:21
  160.5 5.7 %collective-permute-start.21 = (bf16[2,192,512]{2,1,0:T(8,128)(2,1)}, bf16[2,192,512]{2,1,0:T(8,128)(2,1)}, u32[]{:S(2)}, u32[]{:S(2)}) collective-permute-start(bf16[2,192,512]{2,1,0:T(8,128)(2,1)} %collective-permute-done.20), channel_id=1, source_target_pairs={{0,1},{1,2},{2,3},{3,4},{4,5},{5,6},{6,7},{7,8},{8,9},{9,10},{10,1... | collective-permute-start | bytes 1179656 | tf_op jit(solution)/shard_map/ppermute | solution.py:21
  172.1 5.6 %collective-permute-start.22 = (bf16[2,192,512]{2,1,0:T(8,128)(2,1)}, bf16[2,192,512]{2,1,0:T(8,128)(2,1)S(1)}, u32[]{:S(2)}, u32[]{:S(2)}) collective-permute-start(bf16[2,192,512]{2,1,0:T(8,128)(2,1)} %collective-permute-done.21), channel_id=1, source_target_pairs={{0,1},{1,2},{2,3},{3,4},{4,5},{5,6},{6,7},{7,8},{8,9},{9,10},{10,1... | collective-permute-start | bytes 1179656 | tf_op jit(solution)/shard_map/ppermute | solution.py:21
  183.3 5.5 %collective-permute-start.23 = (bf16[2,192,512]{2,1,0:T(8,128)(2,1)S(1)}, bf16[2,192,512]{2,1,0:T(8,128)(2,1)S(1)}, u32[]{:S(2)}, u32[]{:S(2)}) collective-permute-start(bf16[2,192,512]{2,1,0:T(8,128)(2,1)S(1)} %collective-permute-done.22), channel_id=1, source_target_pairs={{0,1},{1,2},{2,3},{3,4},{4,5},{5,6},{6,7},{7,8},{8,9},{9,10},{10,1... | collective-permute-start | bytes 1179656 | tf_op jit(solution)/shard_map/ppermute | solution.py:21
  194.2 5.5 %collective-permute-start.24 = (bf16[2,192,512]{2,1,0:T(8,128)(2,1)S(1)}, bf16[2,192,512]{2,1,0:T(8,128)(2,1)S(1)}, u32[]{:S(2)}, u32[]{:S(2)}) collective-permute-start(bf16[2,192,512]{2,1,0:T(8,128)(2,1)S(1)} %collective-permute-done.23), channel_id=1, source_target_pairs={{0,1},{1,2},{2,3},{3,4},{4,5},{5,6},{6,7},{7,8},{8,9},{9,10},{10,1... | collective-permute-start | bytes 1179656 | tf_op jit(solution)/shard_map/ppermute | solution.py:21
  206.2 5.6 %collective-permute-start.25 = (bf16[192,512]{1,0:T(8,128)(2,1)S(1)}, bf16[192,512]{1,0:T(8,128)(2,1)S(1)}, u32[]{:S(2)}, u32[]{:S(2)}) collective-permute-start(bf16[192,512]{1,0:T(8,128)(2,1)S(1)} %slice_bitcast_fusion.1), channel_id=1, source_target_pairs={{0,1},{1,2},{2,3},{3,4},{4,5},{5,6},{6,7},{7,8},{8,9},{9,10},{10,1... | collective-permute-start | bytes 589832 | tf_op jit(solution)/shard_map/ppermute | solution.py:25
  217.7 5.9 %collective-permute-done.33 = bf16[192,512]{1,0:T(8,128)(2,1)S(1)} collective-permute-done((bf16[192,512]{1,0:T(8,128)(2,1)S(1)}, bf16[192,512]{1,0:T(8,128)(2,1)S(1)}, u32[]{:S(2)}, u32[]{:S(2)}) %collective-permute-start.33) | collective-permute-done | bytes 196640 | tf_op jit(solution)/shard_map/ppermute | solution.py:26
  233.3 5.6 %gather_fusion.3 = bf16[17,192,512]{2,1,0:T(8,128)(2,1)} fusion(bf16[32,192,512]{2,1,0:T(8,128)(2,1)} %bitcast.48, s32[1024]{0:T(1024)S(1)} %pad_clamp_fusion), kind=kCustom, calls=%fused_computation.1.clone | custom fusion | bytes 6684740 | tf_op jit(solution)/shard_map/jit(_take)/gather | solution.py:118
  238.9 5.0 %fusion.7 = f32[17,192,192]{2,1,0:T(8,128)} fusion(bf16[17,192,512]{2,1,0:T(8,128)(2,1)} %gather_fusion.3, bf16[17,192,512]{2,1,0:T(8,128)(2,1)S(1)} %gather_fusion.2, pred[17]{0:T(512)(128)(4,1)S(1)} %get-tuple-element.46, pred[17]{0:T(512)(128)(4,1)S(1)} %get-tuple-element.51), kind=kOutput, calls=%fused_computation.12 | convolution fusion | flops 645070848 | bytes 9191458 | tf_op jit(solution)/shard_map/sao,sbo->sab/dot_general | solution.py:119
  243.9 4.6 %reshape_reshape.3 = f32[17,4,2,2,12,192]{5,4,3,2,1,0:T(8,128)} reshape(f32[17,192,192]{2,1,0:T(8,128)} %fusion.7) | data formatting | bytes 5013504 | tf_op jit(solution)/shard_map/reshape;reshape | solution.py:72
  276.2 6.1 %collective-permute-done.36 = f32[17,2,12,192]{3,1,2,0:T(2,128)S(1)} collective-permute-done((f32[17,2,12,192]{3,1,2,0:T(2,128)}, f32[17,2,12,192]{3,1,2,0:T(2,128)S(1)}, u32[]{:S(2)}, u32[]{:S(2)}) %collective-permute-start.36) | collective-permute-done | bytes 313376 | tf_op jit(solution)/shard_map/ppermute | solution.py:79
  283.1 7.2 %collective-permute-done.37 = f32[17,2,12,192]{3,1,2,0:T(2,128)} collective-permute-done((f32[17,2,12,192]{3,1,2,0:T(2,128)}, f32[17,2,12,192]{3,1,2,0:T(2,128)}, u32[]{:S(2)}, u32[]{:S(2)}) %collective-permute-start.37) | collective-permute-done | bytes 313376 | tf_op jit(solution)/shard_map/ppermute | solution.py:79
  293.9 8.1 %collective-permute-done.38 = f32[17,12,192]{2,1,0:T(8,128)S(1)} collective-permute-done((f32[17,12,192]{2,1,0:T(8,128)S(1)}, f32[17,12,192]{2,1,0:T(8,128)S(1)}, u32[]{:S(2)}, u32[]{:S(2)}) %collective-permute-start.38) | collective-permute-done | bytes 156704 | tf_op jit(solution)/shard_map/ppermute | solution.py:84
  (132 shorter events, 151.3 us)
Async XLA Ops:
  9.0 20.3 %collective-permute-start.1 = (bf16[2,192,256]{2,1,0:T(8,128)(2,1)S(1)}, bf16[2,192,256]{2,1,0:T(8,128)(2,1)S(1)}, u32[]{:S(2)}, u32[]{:S(2)}) collective-permute-start(bf16[2,192,256]{2,1,0:T(8,128)(2,1)S(1)} %maximum_select_fusion.9), channel_id=1, source_target_pairs={{0,1},{1,2},{2,3},{3,4},{4,5},{5,6},{6,7},{7,8},{8,9},{9,10},{10,1... | collective-permute-start | bytes 589832 | tf_op jit(solution)/shard_map/ppermute | solution.py:49
  14.2 33.3 %collective-permute-start.5 = (bf16[2,192,256]{2,1,0:T(8,128)(2,1)S(1)}, bf16[2,192,256]{2,1,0:T(8,128)(2,1)S(1)}, u32[]{:S(2)}, u32[]{:S(2)}) collective-permute-start(bf16[2,192,256]{2,1,0:T(8,128)(2,1)S(1)} %maximum_select_fusion.9), channel_id=1, source_target_pairs={{0,5},{1,6},{2,7},{3,8},{4,9},{5,10},{6,11},{7,12},{8,13},{9,14},{... | collective-permute-start | bytes 589832 | tf_op jit(solution)/shard_map/ppermute | solution.py:51
  23.7 27.8 %collective-permute-start.9 = (bf16[2,192,256]{2,1,0:T(8,128)(2,1)S(1)}, bf16[2,192,256]{2,1,0:T(8,128)(2,1)S(1)}, u32[]{:S(2)}, u32[]{:S(2)}) collective-permute-start(bf16[2,192,256]{2,1,0:T(8,128)(2,1)S(1)} %maximum_select_fusion.9), channel_id=1, source_target_pairs={{0,11},{1,12},{2,13},{3,14},{4,15},{5,0},{6,1},{7,2},{8,3},{9,4},{... | collective-permute-start | bytes 589832 | tf_op jit(solution)/shard_map/ppermute | solution.py:56
  25.6 30.4 %collective-permute-start.12 = (bf16[2,192,256]{2,1,0:T(8,128)(2,1)S(1)}, bf16[2,192,256]{2,1,0:T(8,128)(2,1)S(1)}, u32[]{:S(2)}, u32[]{:S(2)}) collective-permute-start(bf16[2,192,256]{2,1,0:T(8,128)(2,1)S(1)} %maximum_select_fusion.9), channel_id=1, source_target_pairs={{0,15},{1,0},{2,1},{3,2},{4,3},{5,4},{6,5},{7,6},{8,7},{9,8},{10,9... | collective-permute-start | bytes 589832 | tf_op jit(solution)/shard_map/ppermute | solution.py:50
  29.3 29.4 %collective-permute-start.2 = (bf16[2,192,256]{2,1,0:T(8,128)(2,1)S(1)}, bf16[2,192,256]{2,1,0:T(8,128)(2,1)S(1)}, u32[]{:S(2)}, u32[]{:S(2)}) collective-permute-start(bf16[2,192,256]{2,1,0:T(8,128)(2,1)S(1)} %collective-permute-done.1), channel_id=1, source_target_pairs={{0,1},{1,2},{2,3},{3,4},{4,5},{5,6},{6,7},{7,8},{8,9},{9,10},{10,1... | collective-permute-start | bytes 589832 | tf_op jit(solution)/shard_map/ppermute | solution.py:49
  47.4 16.4 %collective-permute-start.6 = (bf16[2,192,256]{2,1,0:T(8,128)(2,1)S(1)}, bf16[2,192,256]{2,1,0:T(8,128)(2,1)S(1)}, u32[]{:S(2)}, u32[]{:S(2)}) collective-permute-start(bf16[2,192,256]{2,1,0:T(8,128)(2,1)S(1)} %collective-permute-done.5), channel_id=1, source_target_pairs={{0,1},{1,2},{2,3},{3,4},{4,5},{5,6},{6,7},{7,8},{8,9},{9,10},{10,1... | collective-permute-start | bytes 589832 | tf_op jit(solution)/shard_map/ppermute | solution.py:51
  51.6 14.2 %collective-permute-start.10 = (bf16[2,192,256]{2,1,0:T(8,128)(2,1)S(1)}, bf16[2,192,256]{2,1,0:T(8,128)(2,1)S(1)}, u32[]{:S(2)}, u32[]{:S(2)}) collective-permute-start(bf16[2,192,256]{2,1,0:T(8,128)(2,1)S(1)} %collective-permute-done.9), channel_id=1, source_target_pairs={{0,15},{1,0},{2,1},{3,2},{4,3},{5,4},{6,5},{7,6},{8,7},{9,8},{10,9... | collective-permute-start | bytes 589832 | tf_op jit(solution)/shard_map/ppermute | solution.py:56
  56.1 13.6 %collective-permute-start.13 = (bf16[2,192,256]{2,1,0:T(8,128)(2,1)S(1)}, bf16[2,192,256]{2,1,0:T(8,128)(2,1)S(1)}, u32[]{:S(2)}, u32[]{:S(2)}) collective-permute-start(bf16[2,192,256]{2,1,0:T(8,128)(2,1)S(1)} %collective-permute-done.12), channel_id=1, source_target_pairs={{0,15},{1,0},{2,1},{3,2},{4,3},{5,4},{6,5},{7,6},{8,7},{9,8},{10,9... | collective-permute-start | bytes 589832 | tf_op jit(solution)/shard_map/ppermute | solution.py:50
  58.7 13.6 %collective-permute-start.3 = (bf16[2,192,256]{2,1,0:T(8,128)(2,1)S(1)}, bf16[2,192,256]{2,1,0:T(8,128)(2,1)S(1)}, u32[]{:S(2)}, u32[]{:S(2)}) collective-permute-start(bf16[2,192,256]{2,1,0:T(8,128)(2,1)S(1)} %collective-permute-done.2), channel_id=1, source_target_pairs={{0,1},{1,2},{2,3},{3,4},{4,5},{5,6},{6,7},{7,8},{8,9},{9,10},{10,1... | collective-permute-start | bytes 589832 | tf_op jit(solution)/shard_map/ppermute | solution.py:49
  63.9 13.6 %collective-permute-start.7 = (bf16[2,192,256]{2,1,0:T(8,128)(2,1)S(1)}, bf16[2,192,256]{2,1,0:T(8,128)(2,1)S(1)}, u32[]{:S(2)}, u32[]{:S(2)}) collective-permute-start(bf16[2,192,256]{2,1,0:T(8,128)(2,1)S(1)} %collective-permute-done.6), channel_id=1, source_target_pairs={{0,1},{1,2},{2,3},{3,4},{4,5},{5,6},{6,7},{7,8},{8,9},{9,10},{10,1... | collective-permute-start | bytes 589832 | tf_op jit(solution)/shard_map/ppermute | solution.py:51
  65.8 21.8 %collective-permute-start.11 = (bf16[2,192,256]{2,1,0:T(8,128)(2,1)S(1)}, bf16[2,192,256]{2,1,0:T(8,128)(2,1)S(1)}, u32[]{:S(2)}, u32[]{:S(2)}) collective-permute-start(bf16[2,192,256]{2,1,0:T(8,128)(2,1)S(1)} %collective-permute-done.10), channel_id=1, source_target_pairs={{0,15},{1,0},{2,1},{3,2},{4,3},{5,4},{6,5},{7,6},{8,7},{9,8},{10,9... | collective-permute-start | bytes 589832 | tf_op jit(solution)/shard_map/ppermute | solution.py:56
  92.4 12.7 %collective-permute-start.16 = (bf16[32,192,256]{2,1,0:T(8,128)(2,1)}, bf16[32,192,256]{2,1,0:T(8,128)(2,1)}, u32[]{:S(2)}, u32[]{:S(2)}) collective-permute-start(bf16[32,192,256]{2,1,0:T(8,128)(2,1)} %bitcast.23), channel_id=1, source_target_pairs={{0,32},{32,0},{64,96},{96,64},{128,160},{160,128},{192,224},{224,1... | collective-permute-start | bytes 9437192 | tf_op jit(solution)/shard_map/ppermute | solution.py:100
  124.3 12.6 %collective-permute-start.18 = (bf16[2,192,512]{2,1,0:T(8,128)(2,1)S(1)}, bf16[2,192,512]{2,1,0:T(8,128)(2,1)S(1)}, u32[]{:S(2)}, u32[]{:S(2)}) collective-permute-start(bf16[2,192,512]{2,1,0:T(8,128)(2,1)S(1)} %maximum_select_fusion.7), channel_id=1, source_target_pairs={{0,1},{1,2},{2,3},{3,4},{4,5},{5,6},{6,7},{7,8},{8,9},{9,10},{10,1... | collective-permute-start | bytes 1179656 | tf_op jit(solution)/shard_map/ppermute | solution.py:21
  127.4 13.8 %collective-permute-start.26 = (bf16[2,192,512]{2,1,0:T(8,128)(2,1)S(1)}, bf16[2,192,512]{2,1,0:T(8,128)(2,1)S(1)}, u32[]{:S(2)}, u32[]{:S(2)}) collective-permute-start(bf16[2,192,512]{2,1,0:T(8,128)(2,1)S(1)} %maximum_select_fusion.7), channel_id=1, source_target_pairs={{0,15},{1,0},{2,1},{3,2},{4,3},{5,4},{6,5},{7,6},{8,7},{9,8},{10,9... | collective-permute-start | bytes 1179656 | tf_op jit(solution)/shard_map/ppermute | solution.py:22
  141.2 13.5 %collective-permute-start.27 = (bf16[2,192,512]{2,1,0:T(8,128)(2,1)S(1)}, bf16[2,192,512]{2,1,0:T(8,128)(2,1)S(1)}, u32[]{:S(2)}, u32[]{:S(2)}) collective-permute-start(bf16[2,192,512]{2,1,0:T(8,128)(2,1)S(1)} %collective-permute-done.26), channel_id=1, source_target_pairs={{0,15},{1,0},{2,1},{3,2},{4,3},{5,4},{6,5},{7,6},{8,7},{9,8},{10,9... | collective-permute-start | bytes 1179656 | tf_op jit(solution)/shard_map/ppermute | solution.py:22
  148.5 12.0 %collective-permute-start.20 = (bf16[2,192,512]{2,1,0:T(8,128)(2,1)S(1)}, bf16[2,192,512]{2,1,0:T(8,128)(2,1)}, u32[]{:S(2)}, u32[]{:S(2)}) collective-permute-start(bf16[2,192,512]{2,1,0:T(8,128)(2,1)S(1)} %collective-permute-done.19), channel_id=1, source_target_pairs={{0,1},{1,2},{2,3},{3,4},{4,5},{5,6},{6,7},{7,8},{8,9},{9,10},{10,1... | collective-permute-start | bytes 1179656 | tf_op jit(solution)/shard_map/ppermute | solution.py:21
  154.7 11.8 %collective-permute-start.28 = (bf16[2,192,512]{2,1,0:T(8,128)(2,1)S(1)}, bf16[2,192,512]{2,1,0:T(8,128)(2,1)S(1)}, u32[]{:S(2)}, u32[]{:S(2)}) collective-permute-start(bf16[2,192,512]{2,1,0:T(8,128)(2,1)S(1)} %collective-permute-done.27), channel_id=1, source_target_pairs={{0,15},{1,0},{2,1},{3,2},{4,3},{5,4},{6,5},{7,6},{8,7},{9,8},{10,9... | collective-permute-start | bytes 1179656 | tf_op jit(solution)/shard_map/ppermute | solution.py:22
  166.4 12.0 %collective-permute-start.29 = (bf16[2,192,512]{2,1,0:T(8,128)(2,1)S(1)}, bf16[2,192,512]{2,1,0:T(8,128)(2,1)S(1)}, u32[]{:S(2)}, u32[]{:S(2)}) collective-permute-start(bf16[2,192,512]{2,1,0:T(8,128)(2,1)S(1)} %collective-permute-done.28), channel_id=1, source_target_pairs={{0,15},{1,0},{2,1},{3,2},{4,3},{5,4},{6,5},{7,6},{8,7},{9,8},{10,9... | collective-permute-start | bytes 1179656 | tf_op jit(solution)/shard_map/ppermute | solution.py:22
  178.5 12.1 %collective-permute-start.30 = (bf16[2,192,512]{2,1,0:T(8,128)(2,1)S(1)}, bf16[2,192,512]{2,1,0:T(8,128)(2,1)S(1)}, u32[]{:S(2)}, u32[]{:S(2)}) collective-permute-start(bf16[2,192,512]{2,1,0:T(8,128)(2,1)S(1)} %collective-permute-done.29), channel_id=1, source_target_pairs={{0,15},{1,0},{2,1},{3,2},{4,3},{5,4},{6,5},{7,6},{8,7},{9,8},{10,9... | collective-permute-start | bytes 1179656 | tf_op jit(solution)/shard_map/ppermute | solution.py:22
  194.2 11.9 %collective-permute-start.24 = (bf16[2,192,512]{2,1,0:T(8,128)(2,1)S(1)}, bf16[2,192,512]{2,1,0:T(8,128)(2,1)S(1)}, u32[]{:S(2)}, u32[]{:S(2)}) collective-permute-start(bf16[2,192,512]{2,1,0:T(8,128)(2,1)S(1)} %collective-permute-done.23), channel_id=1, source_target_pairs={{0,1},{1,2},{2,3},{3,4},{4,5},{5,6},{6,7},{7,8},{8,9},{9,10},{10,1... | collective-permute-start | bytes 1179656 | tf_op jit(solution)/shard_map/ppermute | solution.py:21
  202.1 12.7 %collective-permute-start.32 = (bf16[2,192,512]{2,1,0:T(8,128)(2,1)S(1)}, bf16[2,192,512]{2,1,0:T(8,128)(2,1)S(1)}, u32[]{:S(2)}, u32[]{:S(2)}) collective-permute-start(bf16[2,192,512]{2,1,0:T(8,128)(2,1)S(1)} %collective-permute-done.31), channel_id=1, source_target_pairs={{0,15},{1,0},{2,1},{3,2},{4,3},{5,4},{6,5},{7,6},{8,7},{9,8},{10,9... | collective-permute-start | bytes 1179656 | tf_op jit(solution)/shard_map/ppermute | solution.py:22
  261.6 14.6 %collective-permute-start.35 = (f32[17,2,12,192]{3,1,2,0:T(2,128)}, f32[17,2,12,192]{3,1,2,0:T(2,128)S(1)}, u32[]{:S(2)}, u32[]{:S(2)}) collective-permute-start(f32[17,2,12,192]{3,1,2,0:T(2,128)} %copy.25), channel_id=1, source_target_pairs={{0,128},{32,160},{64,192},{96,224},{128,256},{160,288},{192,320},{... | collective-permute-start | bytes 940040 | tf_op jit(solution)/shard_map/ppermute | solution.py:79
  266.1 16.2 %collective-permute-start.36 = (f32[17,2,12,192]{3,1,2,0:T(2,128)}, f32[17,2,12,192]{3,1,2,0:T(2,128)S(1)}, u32[]{:S(2)}, u32[]{:S(2)}) collective-permute-start(f32[17,2,12,192]{3,1,2,0:T(2,128)} %copy.27), channel_id=1, source_target_pairs={{0,256},{32,288},{64,320},{96,352},{128,384},{160,416},{192,448},{... | collective-permute-start | bytes 940040 | tf_op jit(solution)/shard_map/ppermute | solution.py:79
  270.3 19.9 %collective-permute-start.37 = (f32[17,2,12,192]{3,1,2,0:T(2,128)}, f32[17,2,12,192]{3,1,2,0:T(2,128)}, u32[]{:S(2)}, u32[]{:S(2)}) collective-permute-start(f32[17,2,12,192]{3,1,2,0:T(2,128)} %copy.29), channel_id=1, source_target_pairs={{0,384},{32,416},{64,448},{96,480},{128,0},{160,32},{192,64},{224,... | collective-permute-start | bytes 940040 | tf_op jit(solution)/shard_map/ppermute | solution.py:79
  (20 other events, 326.9 us)

commit v9 on v8

--- a/solution.py
+++ b/solution.py
@@ -65,14 +65,17 @@
 
 def reduce_scatter_aux(parts, naux):
     nx = naux // 4
+    slots, rows, cols = parts.shape
+    per = rows // naux
     me = lax.axis_index("aux")
     c_me = me % 2
     y_me = (me // 2) % 2
     x_me = me // 4
-    shaped = parts.reshape((parts.shape[0], nx, 2, 2) + parts.shape[2:])
-    keep = jnp.take(shaped, c_me, axis=3)
-    send = jnp.take(shaped, 1 - c_me, axis=3)
+    shaped = parts.reshape(slots, nx * 2, 2 * per, cols)
+    keep = lax.dynamic_slice_in_dim(shaped, c_me * per, per, axis=2)
+    send = lax.dynamic_slice_in_dim(shaped, (1 - c_me) * per, per, axis=2)
     on_chip = keep + lax.ppermute(send, "aux", [(i, i ^ 1) for i in range(naux)])
+    on_chip = on_chip.reshape(slots, nx, 2, per, cols)
     total = jnp.take(on_chip, x_me, axis=1)
     for dx in range(1, nx):
         perm = [(i, ((i // 4 + dx) % nx) * 4 + i % 4) for i in range(naux)]
@@ -119,9 +122,7 @@
     partial_tiles = jnp.einsum(
         "sao,sbo->sab", left_rows, right_rows, preferred_element_type=jnp.float32
     )
-    slots = partial_tiles.shape[0]
-    split = partial_tiles.reshape(slots, naux, block // naux, block)
-    return reduce_scatter_aux(split, naux)
+    return reduce_scatter_aux(partial_tiles, naux)
 
 
 def solution(mesh):

time: 304 us -> 300 us (0.987)
  local copies, waits for them, and re-layouts: 55.1 us -> 50.6 us
    select_n x4 -> x0, local copies, waits for them, and re-layouts: 4.72 us -> none  [the longest x3 3.26 us: reduce_scatter_aux(): jnp.take(on_chip, (x_me + dx) % nx, axis=1)]
    another operation x1 -> x0, local copies, waits for them, and re-layouts: 4.64 us -> none  [reduce_scatter_aux(): shaped = parts.reshape((parts.shape[0], nx, 2, 2) + parts.shape[2:])]
where the time goes in v9:
time: 300 us; the launch traced here: 299 us
  starting transfers between devices  138 us (46%)
  waiting for transfers between devices  87.8 us (29%)
  local copies, waits for them, and re-layouts  50.6 us (17%)
  matrix products  11.6 us (4%)
  other arithmetic  9.99 us (3%)
    ppermute x7, starting transfers between devices, ring_gather(): from_left = lax.ppermute(from_left, 'row', send_right)  35.2 us
    unnamed x38, local copies, waits for them, and re-layouts  25.6 us
    ppermute x7, waiting for transfers between devices, ring_gather(): from_left = lax.ppermute(from_left, 'row', send_right)  22.1 us
    ppermute x4, starting transfers between devices, ring_gather_jump(): near_r = lax.ppermute(near_r, 'row', shift(1))  19.5 us
    ppermute x3, waiting for transfers between devices, reduce_scatter_aux(): lax.ppermute(jnp.take(on_chip, (x_me + dx) % nx, axis=1), 'aux', perm)  16.8 us
    ppermute x4, starting transfers between devices, ring_gather_jump(): far_r = lax.ppermute(far_r, 'row', shift(hop))  15.3 us
    ppermute x7, starting transfers between devices, ring_gather(): from_right = lax.ppermute(from_right, 'row', send_left)  14.2 us
    ppermute x4, waiting for transfers between devices, ring_gather_jump(): far_r = lax.ppermute(far_r, 'row', shift(hop))  14 us
  transfers between devices with their start and end apart: 39, of which 19 were waited for; matrix products, arithmetic and copies ran while one was open for 10% of the time, Pallas kernels for 0%

profile of v9, /device:TPU:106, one launch (start us, length us, event | category | flops | bytes accessed | tf_op | source)
XLA Modules:
  0.0 298.8 jit_solution(3778607737920768339)
XLA Ops:
  9.0 5.2 %collective-permute-start.1 = (bf16[2,192,256]{2,1,0:T(8,128)(2,1)S(1)}, bf16[2,192,256]{2,1,0:T(8,128)(2,1)S(1)}, u32[]{:S(2)}, u32[]{:S(2)}) collective-permute-start(bf16[2,192,256]{2,1,0:T(8,128)(2,1)S(1)} %maximum_select_fusion.9), channel_id=1, source_target_pairs={{0,1},{1,2},{2,3},{3,4},{4,5},{5,6},{6,7},{7,8},{8,9},{9,10},{10,1... | collective-permute-start | bytes 589832 | tf_op jit(solution)/shard_map/ppermute | solution.py:49
  14.2 9.6 %collective-permute-start.5 = (bf16[2,192,256]{2,1,0:T(8,128)(2,1)S(1)}, bf16[2,192,256]{2,1,0:T(8,128)(2,1)S(1)}, u32[]{:S(2)}, u32[]{:S(2)}) collective-permute-start(bf16[2,192,256]{2,1,0:T(8,128)(2,1)S(1)} %maximum_select_fusion.9), channel_id=1, source_target_pairs={{0,5},{1,6},{2,7},{3,8},{4,9},{5,10},{6,11},{7,12},{8,13},{9,14},{... | collective-permute-start | bytes 589832 | tf_op jit(solution)/shard_map/ppermute | solution.py:51
  33.4 14.0 %collective-permute-done.5 = bf16[2,192,256]{2,1,0:T(8,128)(2,1)S(1)} collective-permute-done((bf16[2,192,256]{2,1,0:T(8,128)(2,1)S(1)}, bf16[2,192,256]{2,1,0:T(8,128)(2,1)S(1)}, u32[]{:S(2)}, u32[]{:S(2)}) %collective-permute-start.5) | collective-permute-done | bytes 196640 | tf_op jit(solution)/shard_map/ppermute | solution.py:51
  51.6 4.5 %collective-permute-start.10 = (bf16[2,192,256]{2,1,0:T(8,128)(2,1)S(1)}, bf16[2,192,256]{2,1,0:T(8,128)(2,1)S(1)}, u32[]{:S(2)}, u32[]{:S(2)}) collective-permute-start(bf16[2,192,256]{2,1,0:T(8,128)(2,1)S(1)} %collective-permute-done.9), channel_id=1, source_target_pairs={{0,15},{1,0},{2,1},{3,2},{4,3},{5,4},{6,5},{7,6},{8,7},{9,8},{10,9... | collective-permute-start | bytes 589832 | tf_op jit(solution)/shard_map/ppermute | solution.py:56
  58.7 5.1 %collective-permute-start.3 = (bf16[2,192,256]{2,1,0:T(8,128)(2,1)S(1)}, bf16[2,192,256]{2,1,0:T(8,128)(2,1)S(1)}, u32[]{:S(2)}, u32[]{:S(2)}) collective-permute-start(bf16[2,192,256]{2,1,0:T(8,128)(2,1)S(1)} %collective-permute-done.2), channel_id=1, source_target_pairs={{0,1},{1,2},{2,3},{3,4},{4,5},{5,6},{6,7},{7,8},{8,9},{9,10},{10,1... | collective-permute-start | bytes 589832 | tf_op jit(solution)/shard_map/ppermute | solution.py:49
  72.4 5.1 %collective-permute-start.4 = (bf16[2,192,256]{2,1,0:T(8,128)(2,1)S(1)}, bf16[2,192,256]{2,1,0:T(8,128)(2,1)S(1)}, u32[]{:S(2)}, u32[]{:S(2)}) collective-permute-start(bf16[2,192,256]{2,1,0:T(8,128)(2,1)S(1)} %collective-permute-done.3), channel_id=1, source_target_pairs={{0,1},{1,2},{2,3},{3,4},{4,5},{5,6},{6,7},{7,8},{8,9},{9,10},{10,1... | collective-permute-start | bytes 589832 | tf_op jit(solution)/shard_map/ppermute | solution.py:49
  94.4 4.6 %reshape_squeeze.3 = bf16[192,32,192]{2,1,0:T(8,128)(2,1)} reshape(bf16[1,192,6144]{2,1,0:T(8,128)(2,1)S(1)} %copy-done.1) | data formatting | bytes 4718592 | tf_op jit(solution)/shard_map/reshape;squeeze | solution.py:112
  105.2 8.4 %fusion.20 = bf16[192,512]{1,0:T(8,128)(2,1)S(1)} fusion(bf16[32,192,256]{2,1,0:T(8,128)(2,1)} %collective-permute-done.16, bf16[32,192,256]{2,1,0:T(8,128)(2,1)} %bitcast.23, pred[]{:T(512)S(6)} %eq.24, bf16[32,192,192]{2,1,0:T(8,128)(2,1)} %gather_fusion, pred[32]{0:T(512)(128)(4,1)S(1)} %compare_and_fusion.2), kind=kOutput, calls=%fused_computation.24 | convolution fusion | flops 1237549056 | bytes 8847393 | tf_op jit(solution)/shard_map/dot_general | solution.py:114
  113.6 4.2 %collective-permute-start.17 = (bf16[192,512]{1,0:T(8,128)(2,1)S(1)}, bf16[192,512]{1,0:T(8,128)(2,1)S(1)}, u32[]{:S(2)}, u32[]{:S(2)}) collective-permute-start(bf16[192,512]{1,0:T(8,128)(2,1)S(1)} %fusion.20), channel_id=1, source_target_pairs={{0,16},{1,17},{2,18},{3,19},{4,20},{5,21},{6,22},{7,23},{8,24},{9,... | collective-permute-start | bytes 589832 | tf_op jit(solution)/shard_map/ppermute | solution.py:12
  117.8 6.5 %collective-permute-done.17 = bf16[192,512]{1,0:T(8,128)(2,1)S(1)} collective-permute-done((bf16[192,512]{1,0:T(8,128)(2,1)S(1)}, bf16[192,512]{1,0:T(8,128)(2,1)S(1)}, u32[]{:S(2)}, u32[]{:S(2)}) %collective-permute-start.17) | collective-permute-done | bytes 196640 | tf_op jit(solution)/shard_map/ppermute | solution.py:12
  130.2 6.7 %collective-permute-done.18 = bf16[2,192,512]{2,1,0:T(8,128)(2,1)S(1)} collective-permute-done((bf16[2,192,512]{2,1,0:T(8,128)(2,1)S(1)}, bf16[2,192,512]{2,1,0:T(8,128)(2,1)S(1)}, u32[]{:S(2)}, u32[]{:S(2)}) %collective-permute-start.18) | collective-permute-done | bytes 393248 | tf_op jit(solution)/shard_map/ppermute | solution.py:21
  136.9 4.3 %collective-permute-start.19 = (bf16[2,192,512]{2,1,0:T(8,128)(2,1)S(1)}, bf16[2,192,512]{2,1,0:T(8,128)(2,1)S(1)}, u32[]{:S(2)}, u32[]{:S(2)}) collective-permute-start(bf16[2,192,512]{2,1,0:T(8,128)(2,1)S(1)} %collective-permute-done.18), channel_id=1, source_target_pairs={{0,1},{1,2},{2,3},{3,4},{4,5},{5,6},{6,7},{7,8},{8,9},{9,10},{10,1... | collective-permute-start | bytes 1179656 | tf_op jit(solution)/shard_map/ppermute | solution.py:21
  143.3 5.2 %collective-permute-done.19 = bf16[2,192,512]{2,1,0:T(8,128)(2,1)S(1)} collective-permute-done((bf16[2,192,512]{2,1,0:T(8,128)(2,1)S(1)}, bf16[2,192,512]{2,1,0:T(8,128)(2,1)S(1)}, u32[]{:S(2)}, u32[]{:S(2)}) %collective-permute-start.19) | collective-permute-done | bytes 393248 | tf_op jit(solution)/shard_map/ppermute | solution.py:21
  148.6 5.5 %collective-permute-start.20 = (bf16[2,192,512]{2,1,0:T(8,128)(2,1)S(1)}, bf16[2,192,512]{2,1,0:T(8,128)(2,1)}, u32[]{:S(2)}, u32[]{:S(2)}) collective-permute-start(bf16[2,192,512]{2,1,0:T(8,128)(2,1)S(1)} %collective-permute-done.19), channel_id=1, source_target_pairs={{0,1},{1,2},{2,3},{3,4},{4,5},{5,6},{6,7},{7,8},{8,9},{9,10},{10,1... | collective-permute-start | bytes 1179656 | tf_op jit(solution)/shard_map/ppermute | solution.py:21
  160.6 5.7 %collective-permute-start.21 = (bf16[2,192,512]{2,1,0:T(8,128)(2,1)}, bf16[2,192,512]{2,1,0:T(8,128)(2,1)}, u32[]{:S(2)}, u32[]{:S(2)}) collective-permute-start(bf16[2,192,512]{2,1,0:T(8,128)(2,1)} %collective-permute-done.20), channel_id=1, source_target_pairs={{0,1},{1,2},{2,3},{3,4},{4,5},{5,6},{6,7},{7,8},{8,9},{9,10},{10,1... | collective-permute-start | bytes 1179656 | tf_op jit(solution)/shard_map/ppermute | solution.py:21
  172.2 5.6 %collective-permute-start.22 = (bf16[2,192,512]{2,1,0:T(8,128)(2,1)}, bf16[2,192,512]{2,1,0:T(8,128)(2,1)S(1)}, u32[]{:S(2)}, u32[]{:S(2)}) collective-permute-start(bf16[2,192,512]{2,1,0:T(8,128)(2,1)} %collective-permute-done.21), channel_id=1, source_target_pairs={{0,1},{1,2},{2,3},{3,4},{4,5},{5,6},{6,7},{7,8},{8,9},{9,10},{10,1... | collective-permute-start | bytes 1179656 | tf_op jit(solution)/shard_map/ppermute | solution.py:21
  183.4 5.5 %collective-permute-start.23 = (bf16[2,192,512]{2,1,0:T(8,128)(2,1)S(1)}, bf16[2,192,512]{2,1,0:T(8,128)(2,1)S(1)}, u32[]{:S(2)}, u32[]{:S(2)}) collective-permute-start(bf16[2,192,512]{2,1,0:T(8,128)(2,1)S(1)} %collective-permute-done.22), channel_id=1, source_target_pairs={{0,1},{1,2},{2,3},{3,4},{4,5},{5,6},{6,7},{7,8},{8,9},{9,10},{10,1... | collective-permute-start | bytes 1179656 | tf_op jit(solution)/shard_map/ppermute | solution.py:21
  194.3 5.4 %collective-permute-start.24 = (bf16[2,192,512]{2,1,0:T(8,128)(2,1)S(1)}, bf16[2,192,512]{2,1,0:T(8,128)(2,1)S(1)}, u32[]{:S(2)}, u32[]{:S(2)}) collective-permute-start(bf16[2,192,512]{2,1,0:T(8,128)(2,1)S(1)} %collective-permute-done.23), channel_id=1, source_target_pairs={{0,1},{1,2},{2,3},{3,4},{4,5},{5,6},{6,7},{7,8},{8,9},{9,10},{10,1... | collective-permute-start | bytes 1179656 | tf_op jit(solution)/shard_map/ppermute | solution.py:21
  206.3 5.6 %collective-permute-start.25 = (bf16[192,512]{1,0:T(8,128)(2,1)S(1)}, bf16[192,512]{1,0:T(8,128)(2,1)S(1)}, u32[]{:S(2)}, u32[]{:S(2)}) collective-permute-start(bf16[192,512]{1,0:T(8,128)(2,1)S(1)} %slice_bitcast_fusion.1), channel_id=1, source_target_pairs={{0,1},{1,2},{2,3},{3,4},{4,5},{5,6},{6,7},{7,8},{8,9},{9,10},{10,1... | collective-permute-start | bytes 589832 | tf_op jit(solution)/shard_map/ppermute | solution.py:25
  217.8 5.9 %collective-permute-done.33 = bf16[192,512]{1,0:T(8,128)(2,1)S(1)} collective-permute-done((bf16[192,512]{1,0:T(8,128)(2,1)S(1)}, bf16[192,512]{1,0:T(8,128)(2,1)S(1)}, u32[]{:S(2)}, u32[]{:S(2)}) %collective-permute-start.33) | collective-permute-done | bytes 196640 | tf_op jit(solution)/shard_map/ppermute | solution.py:26
  233.5 5.6 %gather_fusion.3 = bf16[17,192,512]{2,1,0:T(8,128)(2,1)} fusion(bf16[32,192,512]{2,1,0:T(8,128)(2,1)} %bitcast.48, s32[1024]{0:T(1024)S(1)} %pad_clamp_fusion), kind=kCustom, calls=%fused_computation.1.clone | custom fusion | bytes 6684740 | tf_op jit(solution)/shard_map/jit(_take)/gather | solution.py:121
  272.7 5.1 %collective-permute-done.36 = f32[17,2,12,192]{3,1,2,0:T(2,128)} collective-permute-done((f32[17,2,12,192]{3,1,2,0:T(2,128)S(1)}, f32[17,2,12,192]{3,1,2,0:T(2,128)}, u32[]{:S(2)}, u32[]{:S(2)}) %collective-permute-start.36) | collective-permute-done | bytes 313376 | tf_op jit(solution)/shard_map/ppermute | solution.py:82
  277.8 7.8 %collective-permute-done.37 = f32[17,2,12,192]{3,1,2,0:T(2,128)} collective-permute-done((f32[17,2,12,192]{3,1,2,0:T(2,128)S(1)}, f32[17,2,12,192]{3,1,2,0:T(2,128)}, u32[]{:S(2)}, u32[]{:S(2)}) %collective-permute-start.37) | collective-permute-done | bytes 313376 | tf_op jit(solution)/shard_map/ppermute | solution.py:82
  290.0 8.1 %collective-permute-done.38 = f32[17,12,192]{2,1,0:T(8,128)S(1)} collective-permute-done((f32[17,12,192]{2,1,0:T(8,128)S(1)}, f32[17,12,192]{2,1,0:T(8,128)S(1)}, u32[]{:S(2)}, u32[]{:S(2)}) %collective-permute-start.38) | collective-permute-done | bytes 156704 | tf_op jit(solution)/shard_map/ppermute | solution.py:87
  (128 shorter events, 148.8 us)
Async XLA Ops:
  9.0 20.3 %collective-permute-start.1 = (bf16[2,192,256]{2,1,0:T(8,128)(2,1)S(1)}, bf16[2,192,256]{2,1,0:T(8,128)(2,1)S(1)}, u32[]{:S(2)}, u32[]{:S(2)}) collective-permute-start(bf16[2,192,256]{2,1,0:T(8,128)(2,1)S(1)} %maximum_select_fusion.9), channel_id=1, source_target_pairs={{0,1},{1,2},{2,3},{3,4},{4,5},{5,6},{6,7},{7,8},{8,9},{9,10},{10,1... | collective-permute-start | bytes 589832 | tf_op jit(solution)/shard_map/ppermute | solution.py:49
  14.2 33.3 %collective-permute-start.5 = (bf16[2,192,256]{2,1,0:T(8,128)(2,1)S(1)}, bf16[2,192,256]{2,1,0:T(8,128)(2,1)S(1)}, u32[]{:S(2)}, u32[]{:S(2)}) collective-permute-start(bf16[2,192,256]{2,1,0:T(8,128)(2,1)S(1)} %maximum_select_fusion.9), channel_id=1, source_target_pairs={{0,5},{1,6},{2,7},{3,8},{4,9},{5,10},{6,11},{7,12},{8,13},{9,14},{... | collective-permute-start | bytes 589832 | tf_op jit(solution)/shard_map/ppermute | solution.py:51
  23.7 27.8 %collective-permute-start.9 = (bf16[2,192,256]{2,1,0:T(8,128)(2,1)S(1)}, bf16[2,192,256]{2,1,0:T(8,128)(2,1)S(1)}, u32[]{:S(2)}, u32[]{:S(2)}) collective-permute-start(bf16[2,192,256]{2,1,0:T(8,128)(2,1)S(1)} %maximum_select_fusion.9), channel_id=1, source_target_pairs={{0,11},{1,12},{2,13},{3,14},{4,15},{5,0},{6,1},{7,2},{8,3},{9,4},{... | collective-permute-start | bytes 589832 | tf_op jit(solution)/shard_map/ppermute | solution.py:56
  25.6 30.4 %collective-permute-start.12 = (bf16[2,192,256]{2,1,0:T(8,128)(2,1)S(1)}, bf16[2,192,256]{2,1,0:T(8,128)(2,1)S(1)}, u32[]{:S(2)}, u32[]{:S(2)}) collective-permute-start(bf16[2,192,256]{2,1,0:T(8,128)(2,1)S(1)} %maximum_select_fusion.9), channel_id=1, source_target_pairs={{0,15},{1,0},{2,1},{3,2},{4,3},{5,4},{6,5},{7,6},{8,7},{9,8},{10,9... | collective-permute-start | bytes 589832 | tf_op jit(solution)/shard_map/ppermute | solution.py:50
  29.3 29.4 %collective-permute-start.2 = (bf16[2,192,256]{2,1,0:T(8,128)(2,1)S(1)}, bf16[2,192,256]{2,1,0:T(8,128)(2,1)S(1)}, u32[]{:S(2)}, u32[]{:S(2)}) collective-permute-start(bf16[2,192,256]{2,1,0:T(8,128)(2,1)S(1)} %collective-permute-done.1), channel_id=1, source_target_pairs={{0,1},{1,2},{2,3},{3,4},{4,5},{5,6},{6,7},{7,8},{8,9},{9,10},{10,1... | collective-permute-start | bytes 589832 | tf_op jit(solution)/shard_map/ppermute | solution.py:49
  47.4 16.4 %collective-permute-start.6 = (bf16[2,192,256]{2,1,0:T(8,128)(2,1)S(1)}, bf16[2,192,256]{2,1,0:T(8,128)(2,1)S(1)}, u32[]{:S(2)}, u32[]{:S(2)}) collective-permute-start(bf16[2,192,256]{2,1,0:T(8,128)(2,1)S(1)} %collective-permute-done.5), channel_id=1, source_target_pairs={{0,1},{1,2},{2,3},{3,4},{4,5},{5,6},{6,7},{7,8},{8,9},{9,10},{10,1... | collective-permute-start | bytes 589832 | tf_op jit(solution)/shard_map/ppermute | solution.py:51
  51.6 14.2 %collective-permute-start.10 = (bf16[2,192,256]{2,1,0:T(8,128)(2,1)S(1)}, bf16[2,192,256]{2,1,0:T(8,128)(2,1)S(1)}, u32[]{:S(2)}, u32[]{:S(2)}) collective-permute-start(bf16[2,192,256]{2,1,0:T(8,128)(2,1)S(1)} %collective-permute-done.9), channel_id=1, source_target_pairs={{0,15},{1,0},{2,1},{3,2},{4,3},{5,4},{6,5},{7,6},{8,7},{9,8},{10,9... | collective-permute-start | bytes 589832 | tf_op jit(solution)/shard_map/ppermute | solution.py:56
  56.1 13.6 %collective-permute-start.13 = (bf16[2,192,256]{2,1,0:T(8,128)(2,1)S(1)}, bf16[2,192,256]{2,1,0:T(8,128)(2,1)S(1)}, u32[]{:S(2)}, u32[]{:S(2)}) collective-permute-start(bf16[2,192,256]{2,1,0:T(8,128)(2,1)S(1)} %collective-permute-done.12), channel_id=1, source_target_pairs={{0,15},{1,0},{2,1},{3,2},{4,3},{5,4},{6,5},{7,6},{8,7},{9,8},{10,9... | collective-permute-start | bytes 589832 | tf_op jit(solution)/shard_map/ppermute | solution.py:50
  58.7 13.7 %collective-permute-start.3 = (bf16[2,192,256]{2,1,0:T(8,128)(2,1)S(1)}, bf16[2,192,256]{2,1,0:T(8,128)(2,1)S(1)}, u32[]{:S(2)}, u32[]{:S(2)}) collective-permute-start(bf16[2,192,256]{2,1,0:T(8,128)(2,1)S(1)} %collective-permute-done.2), channel_id=1, source_target_pairs={{0,1},{1,2},{2,3},{3,4},{4,5},{5,6},{6,7},{7,8},{8,9},{9,10},{10,1... | collective-permute-start | bytes 589832 | tf_op jit(solution)/shard_map/ppermute | solution.py:49
  63.9 13.6 %collective-permute-start.7 = (bf16[2,192,256]{2,1,0:T(8,128)(2,1)S(1)}, bf16[2,192,256]{2,1,0:T(8,128)(2,1)S(1)}, u32[]{:S(2)}, u32[]{:S(2)}) collective-permute-start(bf16[2,192,256]{2,1,0:T(8,128)(2,1)S(1)} %collective-permute-done.6), channel_id=1, source_target_pairs={{0,1},{1,2},{2,3},{3,4},{4,5},{5,6},{6,7},{7,8},{8,9},{9,10},{10,1... | collective-permute-start | bytes 589832 | tf_op jit(solution)/shard_map/ppermute | solution.py:51
  65.8 21.8 %collective-permute-start.11 = (bf16[2,192,256]{2,1,0:T(8,128)(2,1)S(1)}, bf16[2,192,256]{2,1,0:T(8,128)(2,1)S(1)}, u32[]{:S(2)}, u32[]{:S(2)}) collective-permute-start(bf16[2,192,256]{2,1,0:T(8,128)(2,1)S(1)} %collective-permute-done.10), channel_id=1, source_target_pairs={{0,15},{1,0},{2,1},{3,2},{4,3},{5,4},{6,5},{7,6},{8,7},{9,8},{10,9... | collective-permute-start | bytes 589832 | tf_op jit(solution)/shard_map/ppermute | solution.py:56
  92.5 12.7 %collective-permute-start.16 = (bf16[32,192,256]{2,1,0:T(8,128)(2,1)}, bf16[32,192,256]{2,1,0:T(8,128)(2,1)}, u32[]{:S(2)}, u32[]{:S(2)}) collective-permute-start(bf16[32,192,256]{2,1,0:T(8,128)(2,1)} %bitcast.23), channel_id=1, source_target_pairs={{0,32},{32,0},{64,96},{96,64},{128,160},{160,128},{192,224},{224,1... | collective-permute-start | bytes 9437192 | tf_op jit(solution)/shard_map/ppermute | solution.py:103
  124.3 12.6 %collective-permute-start.18 = (bf16[2,192,512]{2,1,0:T(8,128)(2,1)S(1)}, bf16[2,192,512]{2,1,0:T(8,128)(2,1)S(1)}, u32[]{:S(2)}, u32[]{:S(2)}) collective-permute-start(bf16[2,192,512]{2,1,0:T(8,128)(2,1)S(1)} %maximum_select_fusion.7), channel_id=1, source_target_pairs={{0,1},{1,2},{2,3},{3,4},{4,5},{5,6},{6,7},{7,8},{8,9},{9,10},{10,1... | collective-permute-start | bytes 1179656 | tf_op jit(solution)/shard_map/ppermute | solution.py:21
  127.5 13.8 %collective-permute-start.26 = (bf16[2,192,512]{2,1,0:T(8,128)(2,1)S(1)}, bf16[2,192,512]{2,1,0:T(8,128)(2,1)S(1)}, u32[]{:S(2)}, u32[]{:S(2)}) collective-permute-start(bf16[2,192,512]{2,1,0:T(8,128)(2,1)S(1)} %maximum_select_fusion.7), channel_id=1, source_target_pairs={{0,15},{1,0},{2,1},{3,2},{4,3},{5,4},{6,5},{7,6},{8,7},{9,8},{10,9... | collective-permute-start | bytes 1179656 | tf_op jit(solution)/shard_map/ppermute | solution.py:22
  141.2 13.5 %collective-permute-start.27 = (bf16[2,192,512]{2,1,0:T(8,128)(2,1)S(1)}, bf16[2,192,512]{2,1,0:T(8,128)(2,1)S(1)}, u32[]{:S(2)}, u32[]{:S(2)}) collective-permute-start(bf16[2,192,512]{2,1,0:T(8,128)(2,1)S(1)} %collective-permute-done.26), channel_id=1, source_target_pairs={{0,15},{1,0},{2,1},{3,2},{4,3},{5,4},{6,5},{7,6},{8,7},{9,8},{10,9... | collective-permute-start | bytes 1179656 | tf_op jit(solution)/shard_map/ppermute | solution.py:22
  148.6 12.0 %collective-permute-start.20 = (bf16[2,192,512]{2,1,0:T(8,128)(2,1)S(1)}, bf16[2,192,512]{2,1,0:T(8,128)(2,1)}, u32[]{:S(2)}, u32[]{:S(2)}) collective-permute-start(bf16[2,192,512]{2,1,0:T(8,128)(2,1)S(1)} %collective-permute-done.19), channel_id=1, source_target_pairs={{0,1},{1,2},{2,3},{3,4},{4,5},{5,6},{6,7},{7,8},{8,9},{9,10},{10,1... | collective-permute-start | bytes 1179656 | tf_op jit(solution)/shard_map/ppermute | solution.py:21
  154.7 11.8 %collective-permute-start.28 = (bf16[2,192,512]{2,1,0:T(8,128)(2,1)S(1)}, bf16[2,192,512]{2,1,0:T(8,128)(2,1)S(1)}, u32[]{:S(2)}, u32[]{:S(2)}) collective-permute-start(bf16[2,192,512]{2,1,0:T(8,128)(2,1)S(1)} %collective-permute-done.27), channel_id=1, source_target_pairs={{0,15},{1,0},{2,1},{3,2},{4,3},{5,4},{6,5},{7,6},{8,7},{9,8},{10,9... | collective-permute-start | bytes 1179656 | tf_op jit(solution)/shard_map/ppermute | solution.py:22
  166.5 12.1 %collective-permute-start.29 = (bf16[2,192,512]{2,1,0:T(8,128)(2,1)S(1)}, bf16[2,192,512]{2,1,0:T(8,128)(2,1)S(1)}, u32[]{:S(2)}, u32[]{:S(2)}) collective-permute-start(bf16[2,192,512]{2,1,0:T(8,128)(2,1)S(1)} %collective-permute-done.28), channel_id=1, source_target_pairs={{0,15},{1,0},{2,1},{3,2},{4,3},{5,4},{6,5},{7,6},{8,7},{9,8},{10,9... | collective-permute-start | bytes 1179656 | tf_op jit(solution)/shard_map/ppermute | solution.py:22
  178.6 12.1 %collective-permute-start.30 = (bf16[2,192,512]{2,1,0:T(8,128)(2,1)S(1)}, bf16[2,192,512]{2,1,0:T(8,128)(2,1)S(1)}, u32[]{:S(2)}, u32[]{:S(2)}) collective-permute-start(bf16[2,192,512]{2,1,0:T(8,128)(2,1)S(1)} %collective-permute-done.29), channel_id=1, source_target_pairs={{0,15},{1,0},{2,1},{3,2},{4,3},{5,4},{6,5},{7,6},{8,7},{9,8},{10,9... | collective-permute-start | bytes 1179656 | tf_op jit(solution)/shard_map/ppermute | solution.py:22
  194.3 11.9 %collective-permute-start.24 = (bf16[2,192,512]{2,1,0:T(8,128)(2,1)S(1)}, bf16[2,192,512]{2,1,0:T(8,128)(2,1)S(1)}, u32[]{:S(2)}, u32[]{:S(2)}) collective-permute-start(bf16[2,192,512]{2,1,0:T(8,128)(2,1)S(1)} %collective-permute-done.23), channel_id=1, source_target_pairs={{0,1},{1,2},{2,3},{3,4},{4,5},{5,6},{6,7},{7,8},{8,9},{9,10},{10,1... | collective-permute-start | bytes 1179656 | tf_op jit(solution)/shard_map/ppermute | solution.py:21
  202.2 12.7 %collective-permute-start.32 = (bf16[2,192,512]{2,1,0:T(8,128)(2,1)S(1)}, bf16[2,192,512]{2,1,0:T(8,128)(2,1)S(1)}, u32[]{:S(2)}, u32[]{:S(2)}) collective-permute-start(bf16[2,192,512]{2,1,0:T(8,128)(2,1)S(1)} %collective-permute-done.31), channel_id=1, source_target_pairs={{0,15},{1,0},{2,1},{3,2},{4,3},{5,4},{6,5},{7,6},{8,7},{9,8},{10,9... | collective-permute-start | bytes 1179656 | tf_op jit(solution)/shard_map/ppermute | solution.py:22
  258.3 14.4 %collective-permute-start.35 = (f32[17,2,12,192]{3,1,2,0:T(2,128)S(1)}, f32[17,2,12,192]{3,1,2,0:T(2,128)S(1)}, u32[]{:S(2)}, u32[]{:S(2)}) collective-permute-start(f32[17,2,12,192]{3,1,2,0:T(2,128)S(1)} %get-tuple-element.38), channel_id=1, source_target_pairs={{0,128},{32,160},{64,192},{96,224},{128,256},{160,288},{192,320},{... | collective-permute-start | bytes 940040 | tf_op jit(solution)/shard_map/ppermute | solution.py:82
  261.7 16.1 %collective-permute-start.36 = (f32[17,2,12,192]{3,1,2,0:T(2,128)S(1)}, f32[17,2,12,192]{3,1,2,0:T(2,128)}, u32[]{:S(2)}, u32[]{:S(2)}) collective-permute-start(f32[17,2,12,192]{3,1,2,0:T(2,128)S(1)} %get-tuple-element.39), channel_id=1, source_target_pairs={{0,256},{32,288},{64,320},{96,352},{128,384},{160,416},{192,448},{... | collective-permute-start | bytes 940040 | tf_op jit(solution)/shard_map/ppermute | solution.py:82
  264.8 20.8 %collective-permute-start.37 = (f32[17,2,12,192]{3,1,2,0:T(2,128)S(1)}, f32[17,2,12,192]{3,1,2,0:T(2,128)}, u32[]{:S(2)}, u32[]{:S(2)}) collective-permute-start(f32[17,2,12,192]{3,1,2,0:T(2,128)S(1)} %get-tuple-element.40), channel_id=1, source_target_pairs={{0,384},{32,416},{64,448},{96,480},{128,0},{160,32},{192,64},{224,... | collective-permute-start | bytes 940040 | tf_op jit(solution)/shard_map/ppermute | solution.py:82
  (19 other events, 326.7 us)

commit v10 on v9

--- a/solution.py
+++ b/solution.py
@@ -75,12 +75,13 @@
     keep = lax.dynamic_slice_in_dim(shaped, c_me * per, per, axis=2)
     send = lax.dynamic_slice_in_dim(shaped, (1 - c_me) * per, per, axis=2)
     on_chip = keep + lax.ppermute(send, "aux", [(i, i ^ 1) for i in range(naux)])
-    on_chip = on_chip.reshape(slots, nx, 2, per, cols)
-    total = jnp.take(on_chip, x_me, axis=1)
+    total = lax.dynamic_slice_in_dim(on_chip, x_me * 2, 2, axis=1)
     for dx in range(1, nx):
         perm = [(i, ((i // 4 + dx) % nx) * 4 + i % 4) for i in range(naux)]
         total = total + lax.ppermute(
-            jnp.take(on_chip, (x_me + dx) % nx, axis=1), "aux", perm
+            lax.dynamic_slice_in_dim(on_chip, ((x_me + dx) % nx) * 2, 2, axis=1),
+            "aux",
+            perm,
         )
     mine = jnp.take(total, y_me, axis=1)
     theirs = jnp.take(total, 1 - y_me, axis=1)

time: 300 us -> 298 us (level)
  the two profiles are of different devices: /device:TPU:106 before, /device:TPU:122 now
where the time goes in v10:
time: 298 us; the launch traced here: 297 us
  starting transfers between devices  136 us (46%)
  waiting for transfers between devices  89.4 us (30%)
  local copies, waits for them, and re-layouts  50 us (17%)
  matrix products  11.6 us (4%)
  other arithmetic  8.56 us (3%)
    ppermute x7, starting transfers between devices, ring_gather(): from_left = lax.ppermute(from_left, 'row', send_right)  35.2 us
    unnamed x40, local copies, waits for them, and re-layouts  26.7 us
    ppermute x7, waiting for transfers between devices, ring_gather(): from_left = lax.ppermute(from_left, 'row', send_right)  22 us
    ppermute x4, starting transfers between devices, ring_gather_jump(): near_r = lax.ppermute(near_r, 'row', shift(1))  19.5 us
    ppermute x3, waiting for transfers between devices, reduce_scatter_aux(): lax.ppermute(lax.dynamic_slice_in_dim(on_chip, (x_me + dx) % nx * 2, 2, a...  16.6 us
    ppermute x4, starting transfers between devices, ring_gather_jump(): far_r = lax.ppermute(far_r, 'row', shift(hop))  15.3 us
    ppermute x7, starting transfers between devices, ring_gather(): from_right = lax.ppermute(from_right, 'row', send_left)  14.2 us
    ppermute x4, waiting for transfers between devices, ring_gather_jump(): far_r = lax.ppermute(far_r, 'row', shift(hop))  14 us
  transfers between devices with their start and end apart: 39, of which 19 were waited for; matrix products, arithmetic and copies ran while one was open for 10% of the time, Pallas kernels for 0%

profile of v10, /device:TPU:122, one launch (start us, length us, event | category | flops | bytes accessed | tf_op | source)
XLA Modules:
  0.0 296.7 jit_solution(7443918574471764210)
XLA Ops:
  4.1 4.8 %collective-permute-done = bf16[192,256]{1,0:T(8,128)(2,1)S(1)} collective-permute-done((bf16[192,256]{1,0:T(8,128)(2,1)S(1)}, bf16[192,256]{1,0:T(8,128)(2,1)S(1)}, u32[]{:S(2)}, u32[]{:S(2)}) %collective-permute-start) | collective-permute-done | bytes 98336 | tf_op jit(solution)/shard_map/ppermute | solution.py:37
  9.0 5.2 %collective-permute-start.1 = (bf16[2,192,256]{2,1,0:T(8,128)(2,1)S(1)}, bf16[2,192,256]{2,1,0:T(8,128)(2,1)S(1)}, u32[]{:S(2)}, u32[]{:S(2)}) collective-permute-start(bf16[2,192,256]{2,1,0:T(8,128)(2,1)S(1)} %maximum_select_fusion.9), channel_id=1, source_target_pairs={{0,1},{1,2},{2,3},{3,4},{4,5},{5,6},{6,7},{7,8},{8,9},{9,10},{10,1... | collective-permute-start | bytes 589832 | tf_op jit(solution)/shard_map/ppermute | solution.py:49
  14.2 9.6 %collective-permute-start.5 = (bf16[2,192,256]{2,1,0:T(8,128)(2,1)S(1)}, bf16[2,192,256]{2,1,0:T(8,128)(2,1)S(1)}, u32[]{:S(2)}, u32[]{:S(2)}) collective-permute-start(bf16[2,192,256]{2,1,0:T(8,128)(2,1)S(1)} %maximum_select_fusion.9), channel_id=1, source_target_pairs={{0,5},{1,6},{2,7},{3,8},{4,9},{5,10},{6,11},{7,12},{8,13},{9,14},{... | collective-permute-start | bytes 589832 | tf_op jit(solution)/shard_map/ppermute | solution.py:51
  33.4 14.0 %collective-permute-done.5 = bf16[2,192,256]{2,1,0:T(8,128)(2,1)S(1)} collective-permute-done((bf16[2,192,256]{2,1,0:T(8,128)(2,1)S(1)}, bf16[2,192,256]{2,1,0:T(8,128)(2,1)S(1)}, u32[]{:S(2)}, u32[]{:S(2)}) %collective-permute-start.5) | collective-permute-done | bytes 196640 | tf_op jit(solution)/shard_map/ppermute | solution.py:51
  51.6 4.5 %collective-permute-start.10 = (bf16[2,192,256]{2,1,0:T(8,128)(2,1)S(1)}, bf16[2,192,256]{2,1,0:T(8,128)(2,1)S(1)}, u32[]{:S(2)}, u32[]{:S(2)}) collective-permute-start(bf16[2,192,256]{2,1,0:T(8,128)(2,1)S(1)} %collective-permute-done.9), channel_id=1, source_target_pairs={{0,15},{1,0},{2,1},{3,2},{4,3},{5,4},{6,5},{7,6},{8,7},{9,8},{10,9... | collective-permute-start | bytes 589832 | tf_op jit(solution)/shard_map/ppermute | solution.py:56
  58.7 5.1 %collective-permute-start.3 = (bf16[2,192,256]{2,1,0:T(8,128)(2,1)S(1)}, bf16[2,192,256]{2,1,0:T(8,128)(2,1)S(1)}, u32[]{:S(2)}, u32[]{:S(2)}) collective-permute-start(bf16[2,192,256]{2,1,0:T(8,128)(2,1)S(1)} %collective-permute-done.2), channel_id=1, source_target_pairs={{0,1},{1,2},{2,3},{3,4},{4,5},{5,6},{6,7},{7,8},{8,9},{9,10},{10,1... | collective-permute-start | bytes 589832 | tf_op jit(solution)/shard_map/ppermute | solution.py:49
  72.4 5.1 %collective-permute-start.4 = (bf16[2,192,256]{2,1,0:T(8,128)(2,1)S(1)}, bf16[2,192,256]{2,1,0:T(8,128)(2,1)S(1)}, u32[]{:S(2)}, u32[]{:S(2)}) collective-permute-start(bf16[2,192,256]{2,1,0:T(8,128)(2,1)S(1)} %collective-permute-done.3), channel_id=1, source_target_pairs={{0,1},{1,2},{2,3},{3,4},{4,5},{5,6},{6,7},{7,8},{8,9},{9,10},{10,1... | collective-permute-start | bytes 589832 | tf_op jit(solution)/shard_map/ppermute | solution.py:49
  94.3 4.6 %reshape_squeeze.3 = bf16[192,32,192]{2,1,0:T(8,128)(2,1)} reshape(bf16[1,192,6144]{2,1,0:T(8,128)(2,1)S(1)} %copy-done.2) | data formatting | bytes 4718592 | tf_op jit(solution)/shard_map/reshape;squeeze | solution.py:113
  105.1 8.4 %fusion.20 = bf16[192,512]{1,0:T(8,128)(2,1)S(1)} fusion(bf16[32,192,256]{2,1,0:T(8,128)(2,1)} %collective-permute-done.16, bf16[32,192,256]{2,1,0:T(8,128)(2,1)} %bitcast.23, pred[]{:T(512)S(6)} %eq.24, bf16[32,192,192]{2,1,0:T(8,128)(2,1)} %gather_fusion, pred[32]{0:T(512)(128)(4,1)S(1)} %compare_and_fusion.2), kind=kOutput, calls=%fused_computation.24 | convolution fusion | flops 1237549056 | bytes 8847393 | tf_op jit(solution)/shard_map/dot_general | solution.py:115
  116.6 7.5 %collective-permute-done.17 = bf16[192,512]{1,0:T(8,128)(2,1)S(1)} collective-permute-done((bf16[192,512]{1,0:T(8,128)(2,1)S(1)}, bf16[192,512]{1,0:T(8,128)(2,1)S(1)}, u32[]{:S(2)}, u32[]{:S(2)}) %collective-permute-start.17) | collective-permute-done | bytes 196640 | tf_op jit(solution)/shard_map/ppermute | solution.py:12
  130.1 6.7 %collective-permute-done.18 = bf16[2,192,512]{2,1,0:T(8,128)(2,1)S(1)} collective-permute-done((bf16[2,192,512]{2,1,0:T(8,128)(2,1)S(1)}, bf16[2,192,512]{2,1,0:T(8,128)(2,1)S(1)}, u32[]{:S(2)}, u32[]{:S(2)}) %collective-permute-start.18) | collective-permute-done | bytes 393248 | tf_op jit(solution)/shard_map/ppermute | solution.py:21
  136.8 4.3 %collective-permute-start.19 = (bf16[2,192,512]{2,1,0:T(8,128)(2,1)S(1)}, bf16[2,192,512]{2,1,0:T(8,128)(2,1)S(1)}, u32[]{:S(2)}, u32[]{:S(2)}) collective-permute-start(bf16[2,192,512]{2,1,0:T(8,128)(2,1)S(1)} %collective-permute-done.18), channel_id=1, source_target_pairs={{0,1},{1,2},{2,3},{3,4},{4,5},{5,6},{6,7},{7,8},{8,9},{9,10},{10,1... | collective-permute-start | bytes 1179656 | tf_op jit(solution)/shard_map/ppermute | solution.py:21
  143.2 5.2 %collective-permute-done.19 = bf16[2,192,512]{2,1,0:T(8,128)(2,1)S(1)} collective-permute-done((bf16[2,192,512]{2,1,0:T(8,128)(2,1)S(1)}, bf16[2,192,512]{2,1,0:T(8,128)(2,1)S(1)}, u32[]{:S(2)}, u32[]{:S(2)}) %collective-permute-start.19) | collective-permute-done | bytes 393248 | tf_op jit(solution)/shard_map/ppermute | solution.py:21
  148.4 5.5 %collective-permute-start.20 = (bf16[2,192,512]{2,1,0:T(8,128)(2,1)S(1)}, bf16[2,192,512]{2,1,0:T(8,128)(2,1)}, u32[]{:S(2)}, u32[]{:S(2)}) collective-permute-start(bf16[2,192,512]{2,1,0:T(8,128)(2,1)S(1)} %collective-permute-done.19), channel_id=1, source_target_pairs={{0,1},{1,2},{2,3},{3,4},{4,5},{5,6},{6,7},{7,8},{8,9},{9,10},{10,1... | collective-permute-start | bytes 1179656 | tf_op jit(solution)/shard_map/ppermute | solution.py:21
  160.4 5.7 %collective-permute-start.21 = (bf16[2,192,512]{2,1,0:T(8,128)(2,1)}, bf16[2,192,512]{2,1,0:T(8,128)(2,1)}, u32[]{:S(2)}, u32[]{:S(2)}) collective-permute-start(bf16[2,192,512]{2,1,0:T(8,128)(2,1)} %collective-permute-done.20), channel_id=1, source_target_pairs={{0,1},{1,2},{2,3},{3,4},{4,5},{5,6},{6,7},{7,8},{8,9},{9,10},{10,1... | collective-permute-start | bytes 1179656 | tf_op jit(solution)/shard_map/ppermute | solution.py:21
  172.0 5.6 %collective-permute-start.22 = (bf16[2,192,512]{2,1,0:T(8,128)(2,1)}, bf16[2,192,512]{2,1,0:T(8,128)(2,1)S(1)}, u32[]{:S(2)}, u32[]{:S(2)}) collective-permute-start(bf16[2,192,512]{2,1,0:T(8,128)(2,1)} %collective-permute-done.21), channel_id=1, source_target_pairs={{0,1},{1,2},{2,3},{3,4},{4,5},{5,6},{6,7},{7,8},{8,9},{9,10},{10,1... | collective-permute-start | bytes 1179656 | tf_op jit(solution)/shard_map/ppermute | solution.py:21
  183.2 5.5 %collective-permute-start.23 = (bf16[2,192,512]{2,1,0:T(8,128)(2,1)S(1)}, bf16[2,192,512]{2,1,0:T(8,128)(2,1)S(1)}, u32[]{:S(2)}, u32[]{:S(2)}) collective-permute-start(bf16[2,192,512]{2,1,0:T(8,128)(2,1)S(1)} %collective-permute-done.22), channel_id=1, source_target_pairs={{0,1},{1,2},{2,3},{3,4},{4,5},{5,6},{6,7},{7,8},{8,9},{9,10},{10,1... | collective-permute-start | bytes 1179656 | tf_op jit(solution)/shard_map/ppermute | solution.py:21
  194.1 5.5 %collective-permute-start.24 = (bf16[2,192,512]{2,1,0:T(8,128)(2,1)S(1)}, bf16[2,192,512]{2,1,0:T(8,128)(2,1)S(1)}, u32[]{:S(2)}, u32[]{:S(2)}) collective-permute-start(bf16[2,192,512]{2,1,0:T(8,128)(2,1)S(1)} %collective-permute-done.23), channel_id=1, source_target_pairs={{0,1},{1,2},{2,3},{3,4},{4,5},{5,6},{6,7},{7,8},{8,9},{9,10},{10,1... | collective-permute-start | bytes 1179656 | tf_op jit(solution)/shard_map/ppermute | solution.py:21
  206.1 5.6 %collective-permute-start.25 = (bf16[192,512]{1,0:T(8,128)(2,1)S(1)}, bf16[192,512]{1,0:T(8,128)(2,1)S(1)}, u32[]{:S(2)}, u32[]{:S(2)}) collective-permute-start(bf16[192,512]{1,0:T(8,128)(2,1)S(1)} %slice_bitcast_fusion.1), channel_id=1, source_target_pairs={{0,1},{1,2},{2,3},{3,4},{4,5},{5,6},{6,7},{7,8},{8,9},{9,10},{10,1... | collective-permute-start | bytes 589832 | tf_op jit(solution)/shard_map/ppermute | solution.py:25
  217.6 5.9 %collective-permute-done.33 = bf16[192,512]{1,0:T(8,128)(2,1)S(1)} collective-permute-done((bf16[192,512]{1,0:T(8,128)(2,1)S(1)}, bf16[192,512]{1,0:T(8,128)(2,1)S(1)}, u32[]{:S(2)}, u32[]{:S(2)}) %collective-permute-start.33) | collective-permute-done | bytes 196640 | tf_op jit(solution)/shard_map/ppermute | solution.py:26
  233.3 5.6 %gather_fusion.3 = bf16[17,192,512]{2,1,0:T(8,128)(2,1)} fusion(bf16[32,192,512]{2,1,0:T(8,128)(2,1)} %bitcast.48, s32[1024]{0:T(1024)S(1)} %pad_clamp_fusion), kind=kCustom, calls=%fused_computation.1.clone | custom fusion | bytes 6684740 | tf_op jit(solution)/shard_map/jit(_take)/gather | solution.py:122
  270.1 5.0 %collective-permute-done.36 = f32[17,2,12,192]{3,1,2,0:T(2,128)S(1)} collective-permute-done((f32[17,2,12,192]{3,1,2,0:T(2,128)S(1)}, f32[17,2,12,192]{3,1,2,0:T(2,128)S(1)}, u32[]{:S(2)}, u32[]{:S(2)}) %collective-permute-start.36) | collective-permute-done | bytes 313376 | tf_op jit(solution)/shard_map/ppermute | solution.py:81
  275.2 7.8 %collective-permute-done.37 = f32[17,2,12,192]{3,1,2,0:T(2,128)S(1)} collective-permute-done((f32[17,2,12,192]{3,1,2,0:T(2,128)S(1)}, f32[17,2,12,192]{3,1,2,0:T(2,128)S(1)}, u32[]{:S(2)}, u32[]{:S(2)}) %collective-permute-start.37) | collective-permute-done | bytes 313376 | tf_op jit(solution)/shard_map/ppermute | solution.py:81
  288.1 7.8 %collective-permute-done.38 = f32[17,12,192]{2,1,0:T(8,128)S(1)} collective-permute-done((f32[17,12,192]{2,1,0:T(8,128)S(1)}, f32[17,12,192]{2,1,0:T(8,128)S(1)}, u32[]{:S(2)}, u32[]{:S(2)}) %collective-permute-start.38) | collective-permute-done | bytes 156704 | tf_op jit(solution)/shard_map/ppermute | solution.py:88
  (129 shorter events, 145.4 us)
Async XLA Ops:
  9.0 20.3 %collective-permute-start.1 = (bf16[2,192,256]{2,1,0:T(8,128)(2,1)S(1)}, bf16[2,192,256]{2,1,0:T(8,128)(2,1)S(1)}, u32[]{:S(2)}, u32[]{:S(2)}) collective-permute-start(bf16[2,192,256]{2,1,0:T(8,128)(2,1)S(1)} %maximum_select_fusion.9), channel_id=1, source_target_pairs={{0,1},{1,2},{2,3},{3,4},{4,5},{5,6},{6,7},{7,8},{8,9},{9,10},{10,1... | collective-permute-start | bytes 589832 | tf_op jit(solution)/shard_map/ppermute | solution.py:49
  14.2 33.3 %collective-permute-start.5 = (bf16[2,192,256]{2,1,0:T(8,128)(2,1)S(1)}, bf16[2,192,256]{2,1,0:T(8,128)(2,1)S(1)}, u32[]{:S(2)}, u32[]{:S(2)}) collective-permute-start(bf16[2,192,256]{2,1,0:T(8,128)(2,1)S(1)} %maximum_select_fusion.9), channel_id=1, source_target_pairs={{0,5},{1,6},{2,7},{3,8},{4,9},{5,10},{6,11},{7,12},{8,13},{9,14},{... | collective-permute-start | bytes 589832 | tf_op jit(solution)/shard_map/ppermute | solution.py:51
  23.7 27.8 %collective-permute-start.9 = (bf16[2,192,256]{2,1,0:T(8,128)(2,1)S(1)}, bf16[2,192,256]{2,1,0:T(8,128)(2,1)S(1)}, u32[]{:S(2)}, u32[]{:S(2)}) collective-permute-start(bf16[2,192,256]{2,1,0:T(8,128)(2,1)S(1)} %maximum_select_fusion.9), channel_id=1, source_target_pairs={{0,11},{1,12},{2,13},{3,14},{4,15},{5,0},{6,1},{7,2},{8,3},{9,4},{... | collective-permute-start | bytes 589832 | tf_op jit(solution)/shard_map/ppermute | solution.py:56
  25.6 30.4 %collective-permute-start.12 = (bf16[2,192,256]{2,1,0:T(8,128)(2,1)S(1)}, bf16[2,192,256]{2,1,0:T(8,128)(2,1)S(1)}, u32[]{:S(2)}, u32[]{:S(2)}) collective-permute-start(bf16[2,192,256]{2,1,0:T(8,128)(2,1)S(1)} %maximum_select_fusion.9), channel_id=1, source_target_pairs={{0,15},{1,0},{2,1},{3,2},{4,3},{5,4},{6,5},{7,6},{8,7},{9,8},{10,9... | collective-permute-start | bytes 589832 | tf_op jit(solution)/shard_map/ppermute | solution.py:50
  29.3 29.4 %collective-permute-start.2 = (bf16[2,192,256]{2,1,0:T(8,128)(2,1)S(1)}, bf16[2,192,256]{2,1,0:T(8,128)(2,1)S(1)}, u32[]{:S(2)}, u32[]{:S(2)}) collective-permute-start(bf16[2,192,256]{2,1,0:T(8,128)(2,1)S(1)} %collective-permute-done.1), channel_id=1, source_target_pairs={{0,1},{1,2},{2,3},{3,4},{4,5},{5,6},{6,7},{7,8},{8,9},{9,10},{10,1... | collective-permute-start | bytes 589832 | tf_op jit(solution)/shard_map/ppermute | solution.py:49
  47.4 16.4 %collective-permute-start.6 = (bf16[2,192,256]{2,1,0:T(8,128)(2,1)S(1)}, bf16[2,192,256]{2,1,0:T(8,128)(2,1)S(1)}, u32[]{:S(2)}, u32[]{:S(2)}) collective-permute-start(bf16[2,192,256]{2,1,0:T(8,128)(2,1)S(1)} %collective-permute-done.5), channel_id=1, source_target_pairs={{0,1},{1,2},{2,3},{3,4},{4,5},{5,6},{6,7},{7,8},{8,9},{9,10},{10,1... | collective-permute-start | bytes 589832 | tf_op jit(solution)/shard_map/ppermute | solution.py:51
  51.6 14.2 %collective-permute-start.10 = (bf16[2,192,256]{2,1,0:T(8,128)(2,1)S(1)}, bf16[2,192,256]{2,1,0:T(8,128)(2,1)S(1)}, u32[]{:S(2)}, u32[]{:S(2)}) collective-permute-start(bf16[2,192,256]{2,1,0:T(8,128)(2,1)S(1)} %collective-permute-done.9), channel_id=1, source_target_pairs={{0,15},{1,0},{2,1},{3,2},{4,3},{5,4},{6,5},{7,6},{8,7},{9,8},{10,9... | collective-permute-start | bytes 589832 | tf_op jit(solution)/shard_map/ppermute | solution.py:56
  56.1 13.7 %collective-permute-start.13 = (bf16[2,192,256]{2,1,0:T(8,128)(2,1)S(1)}, bf16[2,192,256]{2,1,0:T(8,128)(2,1)S(1)}, u32[]{:S(2)}, u32[]{:S(2)}) collective-permute-start(bf16[2,192,256]{2,1,0:T(8,128)(2,1)S(1)} %collective-permute-done.12), channel_id=1, source_target_pairs={{0,15},{1,0},{2,1},{3,2},{4,3},{5,4},{6,5},{7,6},{8,7},{9,8},{10,9... | collective-permute-start | bytes 589832 | tf_op jit(solution)/shard_map/ppermute | solution.py:50
  58.7 13.6 %collective-permute-start.3 = (bf16[2,192,256]{2,1,0:T(8,128)(2,1)S(1)}, bf16[2,192,256]{2,1,0:T(8,128)(2,1)S(1)}, u32[]{:S(2)}, u32[]{:S(2)}) collective-permute-start(bf16[2,192,256]{2,1,0:T(8,128)(2,1)S(1)} %collective-permute-done.2), channel_id=1, source_target_pairs={{0,1},{1,2},{2,3},{3,4},{4,5},{5,6},{6,7},{7,8},{8,9},{9,10},{10,1... | collective-permute-start | bytes 589832 | tf_op jit(solution)/shard_map/ppermute | solution.py:49
  63.9 13.6 %collective-permute-start.7 = (bf16[2,192,256]{2,1,0:T(8,128)(2,1)S(1)}, bf16[2,192,256]{2,1,0:T(8,128)(2,1)S(1)}, u32[]{:S(2)}, u32[]{:S(2)}) collective-permute-start(bf16[2,192,256]{2,1,0:T(8,128)(2,1)S(1)} %collective-permute-done.6), channel_id=1, source_target_pairs={{0,1},{1,2},{2,3},{3,4},{4,5},{5,6},{6,7},{7,8},{8,9},{9,10},{10,1... | collective-permute-start | bytes 589832 | tf_op jit(solution)/shard_map/ppermute | solution.py:51
  65.8 21.7 %collective-permute-start.11 = (bf16[2,192,256]{2,1,0:T(8,128)(2,1)S(1)}, bf16[2,192,256]{2,1,0:T(8,128)(2,1)S(1)}, u32[]{:S(2)}, u32[]{:S(2)}) collective-permute-start(bf16[2,192,256]{2,1,0:T(8,128)(2,1)S(1)} %collective-permute-done.10), channel_id=1, source_target_pairs={{0,15},{1,0},{2,1},{3,2},{4,3},{5,4},{6,5},{7,6},{8,7},{9,8},{10,9... | collective-permute-start | bytes 589832 | tf_op jit(solution)/shard_map/ppermute | solution.py:56
  92.4 12.7 %collective-permute-start.16 = (bf16[32,192,256]{2,1,0:T(8,128)(2,1)}, bf16[32,192,256]{2,1,0:T(8,128)(2,1)}, u32[]{:S(2)}, u32[]{:S(2)}) collective-permute-start(bf16[32,192,256]{2,1,0:T(8,128)(2,1)} %bitcast.23), channel_id=1, source_target_pairs={{0,32},{32,0},{64,96},{96,64},{128,160},{160,128},{192,224},{224,1... | collective-permute-start | bytes 9437192 | tf_op jit(solution)/shard_map/ppermute | solution.py:104
  124.2 12.5 %collective-permute-start.18 = (bf16[2,192,512]{2,1,0:T(8,128)(2,1)S(1)}, bf16[2,192,512]{2,1,0:T(8,128)(2,1)S(1)}, u32[]{:S(2)}, u32[]{:S(2)}) collective-permute-start(bf16[2,192,512]{2,1,0:T(8,128)(2,1)S(1)} %maximum_select_fusion.7), channel_id=1, source_target_pairs={{0,1},{1,2},{2,3},{3,4},{4,5},{5,6},{6,7},{7,8},{8,9},{9,10},{10,1... | collective-permute-start | bytes 1179656 | tf_op jit(solution)/shard_map/ppermute | solution.py:21
  127.4 13.7 %collective-permute-start.26 = (bf16[2,192,512]{2,1,0:T(8,128)(2,1)S(1)}, bf16[2,192,512]{2,1,0:T(8,128)(2,1)S(1)}, u32[]{:S(2)}, u32[]{:S(2)}) collective-permute-start(bf16[2,192,512]{2,1,0:T(8,128)(2,1)S(1)} %maximum_select_fusion.7), channel_id=1, source_target_pairs={{0,15},{1,0},{2,1},{3,2},{4,3},{5,4},{6,5},{7,6},{8,7},{9,8},{10,9... | collective-permute-start | bytes 1179656 | tf_op jit(solution)/shard_map/ppermute | solution.py:22
  141.1 13.5 %collective-permute-start.27 = (bf16[2,192,512]{2,1,0:T(8,128)(2,1)S(1)}, bf16[2,192,512]{2,1,0:T(8,128)(2,1)S(1)}, u32[]{:S(2)}, u32[]{:S(2)}) collective-permute-start(bf16[2,192,512]{2,1,0:T(8,128)(2,1)S(1)} %collective-permute-done.26), channel_id=1, source_target_pairs={{0,15},{1,0},{2,1},{3,2},{4,3},{5,4},{6,5},{7,6},{8,7},{9,8},{10,9... | collective-permute-start | bytes 1179656 | tf_op jit(solution)/shard_map/ppermute | solution.py:22
  148.4 12.0 %collective-permute-start.20 = (bf16[2,192,512]{2,1,0:T(8,128)(2,1)S(1)}, bf16[2,192,512]{2,1,0:T(8,128)(2,1)}, u32[]{:S(2)}, u32[]{:S(2)}) collective-permute-start(bf16[2,192,512]{2,1,0:T(8,128)(2,1)S(1)} %collective-permute-done.19), channel_id=1, source_target_pairs={{0,1},{1,2},{2,3},{3,4},{4,5},{5,6},{6,7},{7,8},{8,9},{9,10},{10,1... | collective-permute-start | bytes 1179656 | tf_op jit(solution)/shard_map/ppermute | solution.py:21
  154.6 11.7 %collective-permute-start.28 = (bf16[2,192,512]{2,1,0:T(8,128)(2,1)S(1)}, bf16[2,192,512]{2,1,0:T(8,128)(2,1)S(1)}, u32[]{:S(2)}, u32[]{:S(2)}) collective-permute-start(bf16[2,192,512]{2,1,0:T(8,128)(2,1)S(1)} %collective-permute-done.27), channel_id=1, source_target_pairs={{0,15},{1,0},{2,1},{3,2},{4,3},{5,4},{6,5},{7,6},{8,7},{9,8},{10,9... | collective-permute-start | bytes 1179656 | tf_op jit(solution)/shard_map/ppermute | solution.py:22
  166.3 12.0 %collective-permute-start.29 = (bf16[2,192,512]{2,1,0:T(8,128)(2,1)S(1)}, bf16[2,192,512]{2,1,0:T(8,128)(2,1)S(1)}, u32[]{:S(2)}, u32[]{:S(2)}) collective-permute-start(bf16[2,192,512]{2,1,0:T(8,128)(2,1)S(1)} %collective-permute-done.28), channel_id=1, source_target_pairs={{0,15},{1,0},{2,1},{3,2},{4,3},{5,4},{6,5},{7,6},{8,7},{9,8},{10,9... | collective-permute-start | bytes 1179656 | tf_op jit(solution)/shard_map/ppermute | solution.py:22
  178.4 12.1 %collective-permute-start.30 = (bf16[2,192,512]{2,1,0:T(8,128)(2,1)S(1)}, bf16[2,192,512]{2,1,0:T(8,128)(2,1)S(1)}, u32[]{:S(2)}, u32[]{:S(2)}) collective-permute-start(bf16[2,192,512]{2,1,0:T(8,128)(2,1)S(1)} %collective-permute-done.29), channel_id=1, source_target_pairs={{0,15},{1,0},{2,1},{3,2},{4,3},{5,4},{6,5},{7,6},{8,7},{9,8},{10,9... | collective-permute-start | bytes 1179656 | tf_op jit(solution)/shard_map/ppermute | solution.py:22
  194.1 12.0 %collective-permute-start.24 = (bf16[2,192,512]{2,1,0:T(8,128)(2,1)S(1)}, bf16[2,192,512]{2,1,0:T(8,128)(2,1)S(1)}, u32[]{:S(2)}, u32[]{:S(2)}) collective-permute-start(bf16[2,192,512]{2,1,0:T(8,128)(2,1)S(1)} %collective-permute-done.23), channel_id=1, source_target_pairs={{0,1},{1,2},{2,3},{3,4},{4,5},{5,6},{6,7},{7,8},{8,9},{9,10},{10,1... | collective-permute-start | bytes 1179656 | tf_op jit(solution)/shard_map/ppermute | solution.py:21
  202.0 12.7 %collective-permute-start.32 = (bf16[2,192,512]{2,1,0:T(8,128)(2,1)S(1)}, bf16[2,192,512]{2,1,0:T(8,128)(2,1)S(1)}, u32[]{:S(2)}, u32[]{:S(2)}) collective-permute-start(bf16[2,192,512]{2,1,0:T(8,128)(2,1)S(1)} %collective-permute-done.31), channel_id=1, source_target_pairs={{0,15},{1,0},{2,1},{3,2},{4,3},{5,4},{6,5},{7,6},{8,7},{9,8},{10,9... | collective-permute-start | bytes 1179656 | tf_op jit(solution)/shard_map/ppermute | solution.py:22
  255.7 14.4 %collective-permute-start.35 = (f32[17,2,12,192]{3,1,2,0:T(2,128)S(1)}, f32[17,2,12,192]{3,1,2,0:T(2,128)S(1)}, u32[]{:S(2)}, u32[]{:S(2)}) collective-permute-start(f32[17,2,12,192]{3,1,2,0:T(2,128)S(1)} %get-tuple-element.26), channel_id=1, source_target_pairs={{0,128},{32,160},{64,192},{96,224},{128,256},{160,288},{192,320},{... | collective-permute-start | bytes 940040 | tf_op jit(solution)/shard_map/ppermute | solution.py:81
  259.2 16.0 %collective-permute-start.36 = (f32[17,2,12,192]{3,1,2,0:T(2,128)S(1)}, f32[17,2,12,192]{3,1,2,0:T(2,128)S(1)}, u32[]{:S(2)}, u32[]{:S(2)}) collective-permute-start(f32[17,2,12,192]{3,1,2,0:T(2,128)S(1)} %get-tuple-element.28), channel_id=1, source_target_pairs={{0,256},{32,288},{64,320},{96,352},{128,384},{160,416},{192,448},{... | collective-permute-start | bytes 940040 | tf_op jit(solution)/shard_map/ppermute | solution.py:81
  262.2 20.7 %collective-permute-start.37 = (f32[17,2,12,192]{3,1,2,0:T(2,128)S(1)}, f32[17,2,12,192]{3,1,2,0:T(2,128)S(1)}, u32[]{:S(2)}, u32[]{:S(2)}) collective-permute-start(f32[17,2,12,192]{3,1,2,0:T(2,128)S(1)} %get-tuple-element.27), channel_id=1, source_target_pairs={{0,384},{32,416},{64,448},{96,480},{128,0},{160,32},{192,64},{224,... | collective-permute-start | bytes 940040 | tf_op jit(solution)/shard_map/ppermute | solution.py:81
  (20 other events, 327.5 us)

commit v11 on v10

--- a/solution.py
+++ b/solution.py
@@ -76,7 +76,7 @@
     send = lax.dynamic_slice_in_dim(shaped, (1 - c_me) * per, per, axis=2)
     on_chip = keep + lax.ppermute(send, "aux", [(i, i ^ 1) for i in range(naux)])
     total = lax.dynamic_slice_in_dim(on_chip, x_me * 2, 2, axis=1)
-    for dx in range(1, nx):
+    for dx in sorted(range(1, nx), key=lambda d: -min(d, nx - d)):
         perm = [(i, ((i // 4 + dx) % nx) * 4 + i % 4) for i in range(naux)]
         total = total + lax.ppermute(
             lax.dynamic_slice_in_dim(on_chip, ((x_me + dx) % nx) * 2, 2, axis=1),

time: 298 us -> 295 us (0.990)
  the two profiles are of different devices: /device:TPU:122 before, /device:TPU:1 now
where the time goes in v11:
time: 295 us; the launch traced here: 291 us
  starting transfers between devices  161 us (55%)
  waiting for transfers between devices  58.5 us (20%)
  local copies, waits for them, and re-layouts  50 us (17%)
  matrix products  11.6 us (4%)
  other arithmetic  8.56 us (3%)
    ppermute x7, starting transfers between devices, ring_gather(): from_right = lax.ppermute(from_right, 'row', send_left)  29.2 us
    unnamed x40, local copies, waits for them, and re-layouts  26.7 us
    ppermute x7, waiting for transfers between devices, ring_gather(): from_left = lax.ppermute(from_left, 'row', send_right)  21.7 us
    ppermute x4, starting transfers between devices, ring_gather_jump(): far_r = lax.ppermute(far_r, 'row', shift(hop))  21 us
    ppermute x3, starting transfers between devices, ring_gather_jump(): far_l = lax.ppermute(far_l, 'row', shift(-hop))  20.5 us
    ppermute x4, starting transfers between devices, ring_gather_jump(): near_l = lax.ppermute(near_l, 'row', shift(-1))  16.5 us
    ppermute x7, starting transfers between devices, ring_gather(): from_left = lax.ppermute(from_left, 'row', send_right)  15.8 us
    ppermute x3, waiting for transfers between devices, reduce_scatter_aux(): lax.ppermute(lax.dynamic_slice_in_dim(on_chip, (x_me + dx) % nx * 2, 2, a...  12.6 us
  transfers between devices with their start and end apart: 39, of which 18 were waited for; matrix products, arithmetic and copies ran while one was open for 10% of the time, Pallas kernels for 0%

profile of v11, /device:TPU:1, one launch (start us, length us, event | category | flops | bytes accessed | tf_op | source)
XLA Modules:
  0.0 290.8 jit_solution(6635387003138993981)
XLA Ops:
  0.9 5.6 %collective-permute-start = (bf16[192,256]{1,0:T(8,128)(2,1)S(1)}, bf16[192,256]{1,0:T(8,128)(2,1)S(1)}, u32[]{:S(2)}, u32[]{:S(2)}) collective-permute-start(bf16[192,256]{1,0:T(8,128)(2,1)S(1)} %constant_dynamic-slice_fusion.6), channel_id=1, source_target_pairs={{0,16},{1,17},{2,18},{3,19},{4,20},{5,21},{6,22},{7,23},{8,24},{9,... | collective-permute-start | bytes 294920 | tf_op jit(solution)/shard_map/ppermute | solution.py:37
  12.3 10.2 %collective-permute-start.5 = (bf16[2,192,256]{2,1,0:T(8,128)(2,1)S(1)}, bf16[2,192,256]{2,1,0:T(8,128)(2,1)S(1)}, u32[]{:S(2)}, u32[]{:S(2)}) collective-permute-start(bf16[2,192,256]{2,1,0:T(8,128)(2,1)S(1)} %maximum_select_fusion.9), channel_id=1, source_target_pairs={{0,5},{1,6},{2,7},{3,8},{4,9},{5,10},{6,11},{7,12},{8,13},{9,14},{... | collective-permute-start | bytes 589832 | tf_op jit(solution)/shard_map/ppermute | solution.py:51
  22.5 5.0 %collective-permute-start.9 = (bf16[2,192,256]{2,1,0:T(8,128)(2,1)S(1)}, bf16[2,192,256]{2,1,0:T(8,128)(2,1)S(1)}, u32[]{:S(2)}, u32[]{:S(2)}) collective-permute-start(bf16[2,192,256]{2,1,0:T(8,128)(2,1)S(1)} %maximum_select_fusion.9), channel_id=1, source_target_pairs={{0,11},{1,12},{2,13},{3,14},{4,15},{5,0},{6,1},{7,2},{8,3},{9,4},{... | collective-permute-start | bytes 589832 | tf_op jit(solution)/shard_map/ppermute | solution.py:56
  27.5 4.5 %collective-permute-start.12 = (bf16[2,192,256]{2,1,0:T(8,128)(2,1)S(1)}, bf16[2,192,256]{2,1,0:T(8,128)(2,1)S(1)}, u32[]{:S(2)}, u32[]{:S(2)}) collective-permute-start(bf16[2,192,256]{2,1,0:T(8,128)(2,1)S(1)} %maximum_select_fusion.9), channel_id=1, source_target_pairs={{0,15},{1,0},{2,1},{3,2},{4,3},{5,4},{6,5},{7,6},{8,7},{9,8},{10,9... | collective-permute-start | bytes 589832 | tf_op jit(solution)/shard_map/ppermute | solution.py:50
  36.3 5.3 %collective-permute-start.6 = (bf16[2,192,256]{2,1,0:T(8,128)(2,1)S(1)}, bf16[2,192,256]{2,1,0:T(8,128)(2,1)S(1)}, u32[]{:S(2)}, u32[]{:S(2)}) collective-permute-start(bf16[2,192,256]{2,1,0:T(8,128)(2,1)S(1)} %collective-permute-done.5), channel_id=1, source_target_pairs={{0,1},{1,2},{2,3},{3,4},{4,5},{5,6},{6,7},{7,8},{8,9},{9,10},{10,1... | collective-permute-start | bytes 589832 | tf_op jit(solution)/shard_map/ppermute | solution.py:51
  41.6 11.5 %collective-permute-start.10 = (bf16[2,192,256]{2,1,0:T(8,128)(2,1)S(1)}, bf16[2,192,256]{2,1,0:T(8,128)(2,1)S(1)}, u32[]{:S(2)}, u32[]{:S(2)}) collective-permute-start(bf16[2,192,256]{2,1,0:T(8,128)(2,1)S(1)} %collective-permute-done.9), channel_id=1, source_target_pairs={{0,15},{1,0},{2,1},{3,2},{4,3},{5,4},{6,5},{7,6},{8,7},{9,8},{10,9... | collective-permute-start | bytes 589832 | tf_op jit(solution)/shard_map/ppermute | solution.py:56
  53.1 4.6 %collective-permute-start.13 = (bf16[2,192,256]{2,1,0:T(8,128)(2,1)S(1)}, bf16[2,192,256]{2,1,0:T(8,128)(2,1)S(1)}, u32[]{:S(2)}, u32[]{:S(2)}) collective-permute-start(bf16[2,192,256]{2,1,0:T(8,128)(2,1)S(1)} %collective-permute-done.12), channel_id=1, source_target_pairs={{0,15},{1,0},{2,1},{3,2},{4,3},{5,4},{6,5},{7,6},{8,7},{9,8},{10,9... | collective-permute-start | bytes 589832 | tf_op jit(solution)/shard_map/ppermute | solution.py:50
  89.0 5.8 %collective-permute-start.16 = (bf16[32,192,256]{2,1,0:T(8,128)(2,1)}, bf16[32,192,256]{2,1,0:T(8,128)(2,1)}, u32[]{:S(2)}, u32[]{:S(2)}) collective-permute-start(bf16[32,192,256]{2,1,0:T(8,128)(2,1)} %bitcast.23), channel_id=1, source_target_pairs={{0,32},{32,0},{64,96},{96,64},{128,160},{160,128},{192,224},{224,1... | collective-permute-start | bytes 9437192 | tf_op jit(solution)/shard_map/ppermute | solution.py:104
  94.9 4.6 %reshape_squeeze.3 = bf16[192,32,192]{2,1,0:T(8,128)(2,1)} reshape(bf16[1,192,6144]{2,1,0:T(8,128)(2,1)S(1)} %copy-done.2) | data formatting | bytes 4718592 | tf_op jit(solution)/shard_map/reshape;squeeze | solution.py:113
  105.7 8.4 %fusion.20 = bf16[192,512]{1,0:T(8,128)(2,1)S(1)} fusion(bf16[32,192,256]{2,1,0:T(8,128)(2,1)} %collective-permute-done.16, bf16[32,192,256]{2,1,0:T(8,128)(2,1)} %bitcast.23, pred[]{:T(512)S(6)} %eq.24, bf16[32,192,192]{2,1,0:T(8,128)(2,1)} %gather_fusion, pred[32]{0:T(512)(128)(4,1)S(1)} %compare_and_fusion.2), kind=kOutput, calls=%fused_computation.24 | convolution fusion | flops 1237549056 | bytes 8847393 | tf_op jit(solution)/shard_map/dot_general | solution.py:115
  114.1 4.9 %collective-permute-start.17 = (bf16[192,512]{1,0:T(8,128)(2,1)S(1)}, bf16[192,512]{1,0:T(8,128)(2,1)S(1)}, u32[]{:S(2)}, u32[]{:S(2)}) collective-permute-start(bf16[192,512]{1,0:T(8,128)(2,1)S(1)} %fusion.20), channel_id=1, source_target_pairs={{0,16},{1,17},{2,18},{3,19},{4,20},{5,21},{6,22},{7,23},{8,24},{9,... | collective-permute-start | bytes 589832 | tf_op jit(solution)/shard_map/ppermute | solution.py:12
  118.9 4.9 %collective-permute-done.17 = bf16[192,512]{1,0:T(8,128)(2,1)S(1)} collective-permute-done((bf16[192,512]{1,0:T(8,128)(2,1)S(1)}, bf16[192,512]{1,0:T(8,128)(2,1)S(1)}, u32[]{:S(2)}, u32[]{:S(2)}) %collective-permute-start.17) | collective-permute-done | bytes 196640 | tf_op jit(solution)/shard_map/ppermute | solution.py:12
  130.4 6.4 %collective-permute-done.18 = bf16[2,192,512]{2,1,0:T(8,128)(2,1)S(1)} collective-permute-done((bf16[2,192,512]{2,1,0:T(8,128)(2,1)S(1)}, bf16[2,192,512]{2,1,0:T(8,128)(2,1)S(1)}, u32[]{:S(2)}, u32[]{:S(2)}) %collective-permute-start.18) | collective-permute-done | bytes 393248 | tf_op jit(solution)/shard_map/ppermute | solution.py:21
  143.5 5.3 %collective-permute-done.19 = bf16[2,192,512]{2,1,0:T(8,128)(2,1)S(1)} collective-permute-done((bf16[2,192,512]{2,1,0:T(8,128)(2,1)S(1)}, bf16[2,192,512]{2,1,0:T(8,128)(2,1)S(1)}, u32[]{:S(2)}, u32[]{:S(2)}) %collective-permute-start.19) | collective-permute-done | bytes 393248 | tf_op jit(solution)/shard_map/ppermute | solution.py:21
  162.0 4.7 %collective-permute-start.29 = (bf16[2,192,512]{2,1,0:T(8,128)(2,1)S(1)}, bf16[2,192,512]{2,1,0:T(8,128)(2,1)S(1)}, u32[]{:S(2)}, u32[]{:S(2)}) collective-permute-start(bf16[2,192,512]{2,1,0:T(8,128)(2,1)S(1)} %collective-permute-done.28), channel_id=1, source_target_pairs={{0,15},{1,0},{2,1},{3,2},{4,3},{5,4},{6,5},{7,6},{8,7},{9,8},{10,9... | collective-permute-start | bytes 1179656 | tf_op jit(solution)/shard_map/ppermute | solution.py:22
  173.4 4.6 %collective-permute-start.30 = (bf16[2,192,512]{2,1,0:T(8,128)(2,1)S(1)}, bf16[2,192,512]{2,1,0:T(8,128)(2,1)S(1)}, u32[]{:S(2)}, u32[]{:S(2)}) collective-permute-start(bf16[2,192,512]{2,1,0:T(8,128)(2,1)S(1)} %collective-permute-done.29), channel_id=1, source_target_pairs={{0,15},{1,0},{2,1},{3,2},{4,3},{5,4},{6,5},{7,6},{8,7},{9,8},{10,9... | collective-permute-start | bytes 1179656 | tf_op jit(solution)/shard_map/ppermute | solution.py:22
  184.3 4.6 %collective-permute-start.31 = (bf16[2,192,512]{2,1,0:T(8,128)(2,1)S(1)}, bf16[2,192,512]{2,1,0:T(8,128)(2,1)S(1)}, u32[]{:S(2)}, u32[]{:S(2)}) collective-permute-start(bf16[2,192,512]{2,1,0:T(8,128)(2,1)S(1)} %collective-permute-done.30), channel_id=1, source_target_pairs={{0,15},{1,0},{2,1},{3,2},{4,3},{5,4},{6,5},{7,6},{8,7},{9,8},{10,9... | collective-permute-start | bytes 1179656 | tf_op jit(solution)/shard_map/ppermute | solution.py:22
  193.6 5.0 %collective-permute-start.32 = (bf16[2,192,512]{2,1,0:T(8,128)(2,1)S(1)}, bf16[2,192,512]{2,1,0:T(8,128)(2,1)S(1)}, u32[]{:S(2)}, u32[]{:S(2)}) collective-permute-start(bf16[2,192,512]{2,1,0:T(8,128)(2,1)S(1)} %collective-permute-done.31), channel_id=1, source_target_pairs={{0,15},{1,0},{2,1},{3,2},{4,3},{5,4},{6,5},{7,6},{8,7},{9,8},{10,9... | collective-permute-start | bytes 1179656 | tf_op jit(solution)/shard_map/ppermute | solution.py:22
  204.0 5.2 %collective-permute-start.33 = (bf16[192,512]{1,0:T(8,128)(2,1)S(1)}, bf16[192,512]{1,0:T(8,128)(2,1)S(1)}, u32[]{:S(2)}, u32[]{:S(2)}) collective-permute-start(bf16[192,512]{1,0:T(8,128)(2,1)S(1)} %slice_bitcast_fusion), channel_id=1, source_target_pairs={{0,15},{1,0},{2,1},{3,2},{4,3},{5,4},{6,5},{7,6},{8,7},{9,8},{10,9... | collective-permute-start | bytes 589832 | tf_op jit(solution)/shard_map/ppermute | solution.py:26
  223.3 5.6 %gather_fusion.3 = bf16[17,192,512]{2,1,0:T(8,128)(2,1)} fusion(bf16[32,192,512]{2,1,0:T(8,128)(2,1)} %bitcast.48, s32[1024]{0:T(1024)S(1)} %pad_clamp_fusion), kind=kCustom, calls=%fused_computation.1.clone | custom fusion | bytes 6684740 | tf_op jit(solution)/shard_map/jit(_take)/gather | solution.py:122
  235.3 10.8 %collective-permute-start.34 = (f32[17,8,12,192]{3,1,2,0:T(8,128)}, f32[17,8,12,192]{3,1,2,0:T(8,128)}, u32[]{:S(2)}, u32[]{:S(2)}) collective-permute-start(f32[17,8,12,192]{3,1,2,0:T(8,128)} %copy.22), channel_id=1, source_target_pairs={{0,32},{32,0},{64,96},{96,64},{128,160},{160,128},{192,224},{224,1... | collective-permute-start | bytes 3760136 | tf_op jit(solution)/shard_map/ppermute | solution.py:77
  254.3 4.7 %collective-permute-start.35 = (f32[17,2,12,192]{3,1,2,0:T(2,128)S(1)}, f32[17,2,12,192]{3,1,2,0:T(2,128)S(1)}, u32[]{:S(2)}, u32[]{:S(2)}) collective-permute-start(f32[17,2,12,192]{3,1,2,0:T(2,128)S(1)} %get-tuple-element.26), channel_id=1, source_target_pairs={{0,256},{32,288},{64,320},{96,352},{128,384},{160,416},{192,448},{... | collective-permute-start | bytes 940040 | tf_op jit(solution)/shard_map/ppermute | solution.py:81
  268.5 9.6 %collective-permute-done.36 = f32[17,2,12,192]{3,1,2,0:T(2,128)S(1)} collective-permute-done((f32[17,2,12,192]{3,1,2,0:T(2,128)S(1)}, f32[17,2,12,192]{3,1,2,0:T(2,128)S(1)}, u32[]{:S(2)}, u32[]{:S(2)}) %collective-permute-start.36) | collective-permute-done | bytes 313376 | tf_op jit(solution)/shard_map/ppermute | solution.py:81
  284.0 6.0 %collective-permute-done.38 = f32[17,12,192]{2,1,0:T(8,128)S(1)} collective-permute-done((f32[17,12,192]{2,1,0:T(8,128)S(1)}, f32[17,12,192]{2,1,0:T(8,128)S(1)}, u32[]{:S(2)}, u32[]{:S(2)}) %collective-permute-start.38) | collective-permute-done | bytes 156704 | tf_op jit(solution)/shard_map/ppermute | solution.py:88
  (129 shorter events, 142.2 us)
Async XLA Ops:
  8.6 24.1 %collective-permute-start.1 = (bf16[2,192,256]{2,1,0:T(8,128)(2,1)S(1)}, bf16[2,192,256]{2,1,0:T(8,128)(2,1)S(1)}, u32[]{:S(2)}, u32[]{:S(2)}) collective-permute-start(bf16[2,192,256]{2,1,0:T(8,128)(2,1)S(1)} %maximum_select_fusion.9), channel_id=1, source_target_pairs={{0,1},{1,2},{2,3},{3,4},{4,5},{5,6},{6,7},{7,8},{8,9},{9,10},{10,1... | collective-permute-start | bytes 589832 | tf_op jit(solution)/shard_map/ppermute | solution.py:49
  12.3 24.0 %collective-permute-start.5 = (bf16[2,192,256]{2,1,0:T(8,128)(2,1)S(1)}, bf16[2,192,256]{2,1,0:T(8,128)(2,1)S(1)}, u32[]{:S(2)}, u32[]{:S(2)}) collective-permute-start(bf16[2,192,256]{2,1,0:T(8,128)(2,1)S(1)} %maximum_select_fusion.9), channel_id=1, source_target_pairs={{0,5},{1,6},{2,7},{3,8},{4,9},{5,10},{6,11},{7,12},{8,13},{9,14},{... | collective-permute-start | bytes 589832 | tf_op jit(solution)/shard_map/ppermute | solution.py:51
  22.5 19.1 %collective-permute-start.9 = (bf16[2,192,256]{2,1,0:T(8,128)(2,1)S(1)}, bf16[2,192,256]{2,1,0:T(8,128)(2,1)S(1)}, u32[]{:S(2)}, u32[]{:S(2)}) collective-permute-start(bf16[2,192,256]{2,1,0:T(8,128)(2,1)S(1)} %maximum_select_fusion.9), channel_id=1, source_target_pairs={{0,11},{1,12},{2,13},{3,14},{4,15},{5,0},{6,1},{7,2},{8,3},{9,4},{... | collective-permute-start | bytes 589832 | tf_op jit(solution)/shard_map/ppermute | solution.py:56
  27.5 25.7 %collective-permute-start.12 = (bf16[2,192,256]{2,1,0:T(8,128)(2,1)S(1)}, bf16[2,192,256]{2,1,0:T(8,128)(2,1)S(1)}, u32[]{:S(2)}, u32[]{:S(2)}) collective-permute-start(bf16[2,192,256]{2,1,0:T(8,128)(2,1)S(1)} %maximum_select_fusion.9), channel_id=1, source_target_pairs={{0,15},{1,0},{2,1},{3,2},{4,3},{5,4},{6,5},{7,6},{8,7},{9,8},{10,9... | collective-permute-start | bytes 589832 | tf_op jit(solution)/shard_map/ppermute | solution.py:50
  32.7 25.8 %collective-permute-start.2 = (bf16[2,192,256]{2,1,0:T(8,128)(2,1)S(1)}, bf16[2,192,256]{2,1,0:T(8,128)(2,1)S(1)}, u32[]{:S(2)}, u32[]{:S(2)}) collective-permute-start(bf16[2,192,256]{2,1,0:T(8,128)(2,1)S(1)} %collective-permute-done.1), channel_id=1, source_target_pairs={{0,1},{1,2},{2,3},{3,4},{4,5},{5,6},{6,7},{7,8},{8,9},{9,10},{10,1... | collective-permute-start | bytes 589832 | tf_op jit(solution)/shard_map/ppermute | solution.py:49
  36.3 24.1 %collective-permute-start.6 = (bf16[2,192,256]{2,1,0:T(8,128)(2,1)S(1)}, bf16[2,192,256]{2,1,0:T(8,128)(2,1)S(1)}, u32[]{:S(2)}, u32[]{:S(2)}) collective-permute-start(bf16[2,192,256]{2,1,0:T(8,128)(2,1)S(1)} %collective-permute-done.5), channel_id=1, source_target_pairs={{0,1},{1,2},{2,3},{3,4},{4,5},{5,6},{6,7},{7,8},{8,9},{9,10},{10,1... | collective-permute-start | bytes 589832 | tf_op jit(solution)/shard_map/ppermute | solution.py:51
  41.6 21.3 %collective-permute-start.10 = (bf16[2,192,256]{2,1,0:T(8,128)(2,1)S(1)}, bf16[2,192,256]{2,1,0:T(8,128)(2,1)S(1)}, u32[]{:S(2)}, u32[]{:S(2)}) collective-permute-start(bf16[2,192,256]{2,1,0:T(8,128)(2,1)S(1)} %collective-permute-done.9), channel_id=1, source_target_pairs={{0,15},{1,0},{2,1},{3,2},{4,3},{5,4},{6,5},{7,6},{8,7},{9,8},{10,9... | collective-permute-start | bytes 589832 | tf_op jit(solution)/shard_map/ppermute | solution.py:56
  53.1 13.7 %collective-permute-start.13 = (bf16[2,192,256]{2,1,0:T(8,128)(2,1)S(1)}, bf16[2,192,256]{2,1,0:T(8,128)(2,1)S(1)}, u32[]{:S(2)}, u32[]{:S(2)}) collective-permute-start(bf16[2,192,256]{2,1,0:T(8,128)(2,1)S(1)} %collective-permute-done.12), channel_id=1, source_target_pairs={{0,15},{1,0},{2,1},{3,2},{4,3},{5,4},{6,5},{7,6},{8,7},{9,8},{10,9... | collective-permute-start | bytes 589832 | tf_op jit(solution)/shard_map/ppermute | solution.py:50
  58.4 12.5 %collective-permute-start.3 = (bf16[2,192,256]{2,1,0:T(8,128)(2,1)S(1)}, bf16[2,192,256]{2,1,0:T(8,128)(2,1)S(1)}, u32[]{:S(2)}, u32[]{:S(2)}) collective-permute-start(bf16[2,192,256]{2,1,0:T(8,128)(2,1)S(1)} %collective-permute-done.2), channel_id=1, source_target_pairs={{0,1},{1,2},{2,3},{3,4},{4,5},{5,6},{6,7},{7,8},{8,9},{9,10},{10,1... | collective-permute-start | bytes 589832 | tf_op jit(solution)/shard_map/ppermute | solution.py:49
  60.4 12.5 %collective-permute-start.7 = (bf16[2,192,256]{2,1,0:T(8,128)(2,1)S(1)}, bf16[2,192,256]{2,1,0:T(8,128)(2,1)S(1)}, u32[]{:S(2)}, u32[]{:S(2)}) collective-permute-start(bf16[2,192,256]{2,1,0:T(8,128)(2,1)S(1)} %collective-permute-done.6), channel_id=1, source_target_pairs={{0,1},{1,2},{2,3},{3,4},{4,5},{5,6},{6,7},{7,8},{8,9},{9,10},{10,1... | collective-permute-start | bytes 589832 | tf_op jit(solution)/shard_map/ppermute | solution.py:51
  62.9 21.3 %collective-permute-start.11 = (bf16[2,192,256]{2,1,0:T(8,128)(2,1)S(1)}, bf16[2,192,256]{2,1,0:T(8,128)(2,1)S(1)}, u32[]{:S(2)}, u32[]{:S(2)}) collective-permute-start(bf16[2,192,256]{2,1,0:T(8,128)(2,1)S(1)} %collective-permute-done.10), channel_id=1, source_target_pairs={{0,15},{1,0},{2,1},{3,2},{4,3},{5,4},{6,5},{7,6},{8,7},{9,8},{10,9... | collective-permute-start | bytes 589832 | tf_op jit(solution)/shard_map/ppermute | solution.py:56
  72.9 10.6 %collective-permute-start.8 = (bf16[2,192,256]{2,1,0:T(8,128)(2,1)S(1)}, bf16[2,192,256]{2,1,0:T(8,128)(2,1)S(1)}, u32[]{:S(2)}, u32[]{:S(2)}) collective-permute-start(bf16[2,192,256]{2,1,0:T(8,128)(2,1)S(1)} %collective-permute-done.7), channel_id=1, source_target_pairs={{0,1},{1,2},{2,3},{3,4},{4,5},{5,6},{6,7},{7,8},{8,9},{9,10},{10,1... | collective-permute-start | bytes 589832 | tf_op jit(solution)/shard_map/ppermute | solution.py:51
  89.0 16.6 %collective-permute-start.16 = (bf16[32,192,256]{2,1,0:T(8,128)(2,1)}, bf16[32,192,256]{2,1,0:T(8,128)(2,1)}, u32[]{:S(2)}, u32[]{:S(2)}) collective-permute-start(bf16[32,192,256]{2,1,0:T(8,128)(2,1)} %bitcast.23), channel_id=1, source_target_pairs={{0,32},{32,0},{64,96},{96,64},{128,160},{160,128},{192,224},{224,1... | collective-permute-start | bytes 9437192 | tf_op jit(solution)/shard_map/ppermute | solution.py:104
  123.9 12.9 %collective-permute-start.18 = (bf16[2,192,512]{2,1,0:T(8,128)(2,1)S(1)}, bf16[2,192,512]{2,1,0:T(8,128)(2,1)S(1)}, u32[]{:S(2)}, u32[]{:S(2)}) collective-permute-start(bf16[2,192,512]{2,1,0:T(8,128)(2,1)S(1)} %maximum_select_fusion.7), channel_id=1, source_target_pairs={{0,1},{1,2},{2,3},{3,4},{4,5},{5,6},{6,7},{7,8},{8,9},{9,10},{10,1... | collective-permute-start | bytes 1179656 | tf_op jit(solution)/shard_map/ppermute | solution.py:21
  127.6 12.6 %collective-permute-start.26 = (bf16[2,192,512]{2,1,0:T(8,128)(2,1)S(1)}, bf16[2,192,512]{2,1,0:T(8,128)(2,1)S(1)}, u32[]{:S(2)}, u32[]{:S(2)}) collective-permute-start(bf16[2,192,512]{2,1,0:T(8,128)(2,1)S(1)} %maximum_select_fusion.7), channel_id=1, source_target_pairs={{0,15},{1,0},{2,1},{3,2},{4,3},{5,4},{6,5},{7,6},{8,7},{9,8},{10,9... | collective-permute-start | bytes 1179656 | tf_op jit(solution)/shard_map/ppermute | solution.py:22
  136.8 12.0 %collective-permute-start.19 = (bf16[2,192,512]{2,1,0:T(8,128)(2,1)S(1)}, bf16[2,192,512]{2,1,0:T(8,128)(2,1)S(1)}, u32[]{:S(2)}, u32[]{:S(2)}) collective-permute-start(bf16[2,192,512]{2,1,0:T(8,128)(2,1)S(1)} %collective-permute-done.18), channel_id=1, source_target_pairs={{0,1},{1,2},{2,3},{3,4},{4,5},{5,6},{6,7},{7,8},{8,9},{9,10},{10,1... | collective-permute-start | bytes 1179656 | tf_op jit(solution)/shard_map/ppermute | solution.py:21
  140.2 11.3 %collective-permute-start.27 = (bf16[2,192,512]{2,1,0:T(8,128)(2,1)S(1)}, bf16[2,192,512]{2,1,0:T(8,128)(2,1)S(1)}, u32[]{:S(2)}, u32[]{:S(2)}) collective-permute-start(bf16[2,192,512]{2,1,0:T(8,128)(2,1)S(1)} %collective-permute-done.26), channel_id=1, source_target_pairs={{0,15},{1,0},{2,1},{3,2},{4,3},{5,4},{6,5},{7,6},{8,7},{9,8},{10,9... | collective-permute-start | bytes 1179656 | tf_op jit(solution)/shard_map/ppermute | solution.py:22
  148.8 11.3 %collective-permute-start.20 = (bf16[2,192,512]{2,1,0:T(8,128)(2,1)S(1)}, bf16[2,192,512]{2,1,0:T(8,128)(2,1)}, u32[]{:S(2)}, u32[]{:S(2)}) collective-permute-start(bf16[2,192,512]{2,1,0:T(8,128)(2,1)S(1)} %collective-permute-done.19), channel_id=1, source_target_pairs={{0,1},{1,2},{2,3},{3,4},{4,5},{5,6},{6,7},{7,8},{8,9},{9,10},{10,1... | collective-permute-start | bytes 1179656 | tf_op jit(solution)/shard_map/ppermute | solution.py:21
  162.0 11.3 %collective-permute-start.29 = (bf16[2,192,512]{2,1,0:T(8,128)(2,1)S(1)}, bf16[2,192,512]{2,1,0:T(8,128)(2,1)S(1)}, u32[]{:S(2)}, u32[]{:S(2)}) collective-permute-start(bf16[2,192,512]{2,1,0:T(8,128)(2,1)S(1)} %collective-permute-done.28), channel_id=1, source_target_pairs={{0,15},{1,0},{2,1},{3,2},{4,3},{5,4},{6,5},{7,6},{8,7},{9,8},{10,9... | collective-permute-start | bytes 1179656 | tf_op jit(solution)/shard_map/ppermute | solution.py:22
  173.4 10.9 %collective-permute-start.30 = (bf16[2,192,512]{2,1,0:T(8,128)(2,1)S(1)}, bf16[2,192,512]{2,1,0:T(8,128)(2,1)S(1)}, u32[]{:S(2)}, u32[]{:S(2)}) collective-permute-start(bf16[2,192,512]{2,1,0:T(8,128)(2,1)S(1)} %collective-permute-done.29), channel_id=1, source_target_pairs={{0,15},{1,0},{2,1},{3,2},{4,3},{5,4},{6,5},{7,6},{8,7},{9,8},{10,9... | collective-permute-start | bytes 1179656 | tf_op jit(solution)/shard_map/ppermute | solution.py:22
  235.3 14.3 %collective-permute-start.34 = (f32[17,8,12,192]{3,1,2,0:T(8,128)}, f32[17,8,12,192]{3,1,2,0:T(8,128)}, u32[]{:S(2)}, u32[]{:S(2)}) collective-permute-start(f32[17,8,12,192]{3,1,2,0:T(8,128)} %copy.22), channel_id=1, source_target_pairs={{0,32},{32,0},{64,96},{96,64},{128,160},{160,128},{192,224},{224,1... | collective-permute-start | bytes 3760136 | tf_op jit(solution)/shard_map/ppermute | solution.py:77
  254.3 14.3 %collective-permute-start.35 = (f32[17,2,12,192]{3,1,2,0:T(2,128)S(1)}, f32[17,2,12,192]{3,1,2,0:T(2,128)S(1)}, u32[]{:S(2)}, u32[]{:S(2)}) collective-permute-start(f32[17,2,12,192]{3,1,2,0:T(2,128)S(1)} %get-tuple-element.26), channel_id=1, source_target_pairs={{0,256},{32,288},{64,320},{96,352},{128,384},{160,416},{192,448},{... | collective-permute-start | bytes 940040 | tf_op jit(solution)/shard_map/ppermute | solution.py:81
  259.0 19.2 %collective-permute-start.36 = (f32[17,2,12,192]{3,1,2,0:T(2,128)S(1)}, f32[17,2,12,192]{3,1,2,0:T(2,128)S(1)}, u32[]{:S(2)}, u32[]{:S(2)}) collective-permute-start(f32[17,2,12,192]{3,1,2,0:T(2,128)S(1)} %get-tuple-element.28), channel_id=1, source_target_pairs={{0,128},{32,160},{64,192},{96,224},{128,256},{160,288},{192,320},{... | collective-permute-start | bytes 940040 | tf_op jit(solution)/shard_map/ppermute | solution.py:81
  261.3 16.9 %collective-permute-start.37 = (f32[17,2,12,192]{3,1,2,0:T(2,128)S(1)}, f32[17,2,12,192]{3,1,2,0:T(2,128)S(1)}, u32[]{:S(2)}, u32[]{:S(2)}) collective-permute-start(f32[17,2,12,192]{3,1,2,0:T(2,128)S(1)} %get-tuple-element.27), channel_id=1, source_target_pairs={{0,384},{32,416},{64,448},{96,480},{128,0},{160,32},{192,64},{224,... | collective-permute-start | bytes 940040 | tf_op jit(solution)/shard_map/ppermute | solution.py:81
  (20 other events, 316.8 us)

commit v12 on v11

--- a/solution.py
+++ b/solution.py
@@ -10,7 +10,7 @@
     yh = r // ring
     z = r % ring
     other = lax.ppermute(x, "row", [(i, i ^ ring) for i in range(nrow)])
-    pair = jnp.where(yh == 0, jnp.stack([x, other]), jnp.stack([other, x]))
+    pair = jnp.stack([x, other])
     send_right = [(i, (i // ring) * ring + (i % ring + 1) % ring) for i in range(nrow)]
     send_left = [(i, (i // ring) * ring + (i % ring - 1) % ring) for i in range(nrow)]
     got = [None] * ring
@@ -35,7 +35,7 @@
     yh = r // ring
     z = r % ring
     other = lax.ppermute(x, "row", [(i, i ^ ring) for i in range(nrow)])
-    pair = jnp.where(yh == 0, jnp.stack([x, other]), jnp.stack([other, x]))
+    pair = jnp.stack([x, other])
 
     def shift(d):
         return [(i, (i // ring) * ring + (i % ring + d) % ring) for i in range(nrow)]
@@ -60,7 +60,8 @@
 
 
 def position_of(k, z, ring):
-    return ((z - k % ring) % ring) * 2 + k // ring
+    yh = lax.axis_index("row") // ring
+    return ((z - k % ring) % ring) * 2 + jnp.where(k // ring == yh, 0, 1)
 
 
 def reduce_scatter_aux(parts, naux):
@@ -109,7 +110,8 @@
     )
 
     p = jnp.arange(nrow)
-    block_at = (p % 2) * ring + (z - p // 2) % ring
+    yh = lax.axis_index("row") // ring
+    block_at = jnp.where(p % 2 == 0, yh, 1 - yh) * ring + (z - p // 2) % ring
     chol = chol_vectors[0].reshape(block, nrow, nbf // nrow)
     chol_ring = jnp.take(chol, block_at, axis=1).reshape(block, nbf)
     half = jnp.dot(

time: 295 us -> 295 us (level)
  transfers between devices with their start and end apart: 39 -> 39, of which waited for: 18 -> 17; matrix products, arithmetic and copies ran while one was open for 10% -> 10% of each run, Pallas kernels for 0% -> 0%
where the time goes in v12:
time: 295 us; the launch traced here: 291 us
  starting transfers between devices  161 us (55%)
  waiting for transfers between devices  59.4 us (20%)
  local copies, waits for them, and re-layouts  50 us (17%)
  matrix products  11.6 us (4%)
  other arithmetic  8.48 us (3%)
    ppermute x7, starting transfers between devices, ring_gather(): from_right = lax.ppermute(from_right, 'row', send_left)  29.8 us
    unnamed x40, local copies, waits for them, and re-layouts  26.7 us
    ppermute x7, waiting for transfers between devices, ring_gather(): from_left = lax.ppermute(from_left, 'row', send_right)  21.9 us
    ppermute x4, starting transfers between devices, ring_gather_jump(): far_r = lax.ppermute(far_r, 'row', shift(hop))  21 us
    ppermute x3, starting transfers between devices, ring_gather_jump(): far_l = lax.ppermute(far_l, 'row', shift(-hop))  20.5 us
    ppermute x4, starting transfers between devices, ring_gather_jump(): near_l = lax.ppermute(near_l, 'row', shift(-1))  16.5 us
    ppermute x7, starting transfers between devices, ring_gather(): from_left = lax.ppermute(from_left, 'row', send_right)  15.4 us
    ppermute x3, waiting for transfers between devices, reduce_scatter_aux(): lax.ppermute(lax.dynamic_slice_in_dim(on_chip, (x_me + dx) % nx * 2, 2, a...  12.8 us
  transfers between devices with their start and end apart: 39, of which 17 were waited for; matrix products, arithmetic and copies ran while one was open for 10% of the time, Pallas kernels for 0%

profile of v12, /device:TPU:1, one launch (start us, length us, event | category | flops | bytes accessed | tf_op | source)
XLA Modules:
  0.0 291.2 jit_solution(17153438418910279959)
XLA Ops:
  0.9 5.6 %collective-permute-start = (bf16[192,256]{1,0:T(8,128)(2,1)S(1)}, bf16[192,256]{1,0:T(8,128)(2,1)S(1)}, u32[]{:S(2)}, u32[]{:S(2)}) collective-permute-start(bf16[192,256]{1,0:T(8,128)(2,1)S(1)} %constant_dynamic-slice_fusion.6), channel_id=1, source_target_pairs={{0,16},{1,17},{2,18},{3,19},{4,20},{5,21},{6,22},{7,23},{8,24},{9,... | collective-permute-start | bytes 294920 | tf_op jit(solution)/shard_map/ppermute | solution.py:37
  12.3 10.2 %collective-permute-start.5 = (bf16[2,192,256]{2,1,0:T(8,128)(2,1)S(1)}, bf16[2,192,256]{2,1,0:T(8,128)(2,1)S(1)}, u32[]{:S(2)}, u32[]{:S(2)}) collective-permute-start(bf16[2,192,256]{2,1,0:T(8,128)(2,1)S(1)} %pad_maximum_fusion.1), channel_id=1, source_target_pairs={{0,5},{1,6},{2,7},{3,8},{4,9},{5,10},{6,11},{7,12},{8,13},{9,14},{... | collective-permute-start | bytes 589832 | tf_op jit(solution)/shard_map/ppermute | solution.py:51
  22.5 5.0 %collective-permute-start.9 = (bf16[2,192,256]{2,1,0:T(8,128)(2,1)S(1)}, bf16[2,192,256]{2,1,0:T(8,128)(2,1)S(1)}, u32[]{:S(2)}, u32[]{:S(2)}) collective-permute-start(bf16[2,192,256]{2,1,0:T(8,128)(2,1)S(1)} %pad_maximum_fusion.1), channel_id=1, source_target_pairs={{0,11},{1,12},{2,13},{3,14},{4,15},{5,0},{6,1},{7,2},{8,3},{9,4},{... | collective-permute-start | bytes 589832 | tf_op jit(solution)/shard_map/ppermute | solution.py:56
  36.3 5.2 %collective-permute-start.6 = (bf16[2,192,256]{2,1,0:T(8,128)(2,1)S(1)}, bf16[2,192,256]{2,1,0:T(8,128)(2,1)S(1)}, u32[]{:S(2)}, u32[]{:S(2)}) collective-permute-start(bf16[2,192,256]{2,1,0:T(8,128)(2,1)S(1)} %collective-permute-done.5), channel_id=1, source_target_pairs={{0,1},{1,2},{2,3},{3,4},{4,5},{5,6},{6,7},{7,8},{8,9},{9,10},{10,1... | collective-permute-start | bytes 589832 | tf_op jit(solution)/shard_map/ppermute | solution.py:51
  41.5 11.6 %collective-permute-start.10 = (bf16[2,192,256]{2,1,0:T(8,128)(2,1)S(1)}, bf16[2,192,256]{2,1,0:T(8,128)(2,1)S(1)}, u32[]{:S(2)}, u32[]{:S(2)}) collective-permute-start(bf16[2,192,256]{2,1,0:T(8,128)(2,1)S(1)} %collective-permute-done.9), channel_id=1, source_target_pairs={{0,15},{1,0},{2,1},{3,2},{4,3},{5,4},{6,5},{7,6},{8,7},{9,8},{10,9... | collective-permute-start | bytes 589832 | tf_op jit(solution)/shard_map/ppermute | solution.py:56
  53.1 4.6 %collective-permute-start.13 = (bf16[2,192,256]{2,1,0:T(8,128)(2,1)S(1)}, bf16[2,192,256]{2,1,0:T(8,128)(2,1)S(1)}, u32[]{:S(2)}, u32[]{:S(2)}) collective-permute-start(bf16[2,192,256]{2,1,0:T(8,128)(2,1)S(1)} %collective-permute-done.12), channel_id=1, source_target_pairs={{0,15},{1,0},{2,1},{3,2},{4,3},{5,4},{6,5},{7,6},{8,7},{9,8},{10,9... | collective-permute-start | bytes 589832 | tf_op jit(solution)/shard_map/ppermute | solution.py:50
  89.0 5.9 %collective-permute-start.16 = (bf16[32,192,256]{2,1,0:T(8,128)(2,1)}, bf16[32,192,256]{2,1,0:T(8,128)(2,1)}, u32[]{:S(2)}, u32[]{:S(2)}) collective-permute-start(bf16[32,192,256]{2,1,0:T(8,128)(2,1)} %bitcast.22), channel_id=1, source_target_pairs={{0,32},{32,0},{64,96},{96,64},{128,160},{160,128},{192,224},{224,1... | collective-permute-start | bytes 9437192 | tf_op jit(solution)/shard_map/ppermute | solution.py:105
  94.9 4.6 %reshape_squeeze.3 = bf16[192,32,192]{2,1,0:T(8,128)(2,1)} reshape(bf16[1,192,6144]{2,1,0:T(8,128)(2,1)S(1)} %copy-done.2) | data formatting | bytes 4718592 | tf_op jit(solution)/shard_map/reshape;squeeze | solution.py:115
  105.7 8.4 %fusion.20 = bf16[192,512]{1,0:T(8,128)(2,1)S(1)} fusion(bf16[32,192,256]{2,1,0:T(8,128)(2,1)} %collective-permute-done.16, bf16[32,192,256]{2,1,0:T(8,128)(2,1)} %bitcast.22, pred[]{:T(512)S(6)} %eq.46, bf16[32,192,192]{2,1,0:T(8,128)(2,1)} %gather_fusion, pred[32]{0:T(512)(128)(4,1)S(1)} %compare_and_fusion.2), kind=kOutput, calls=%fused_computation.24 | convolution fusion | flops 1237549056 | bytes 8847393 | tf_op jit(solution)/shard_map/dot_general | solution.py:117
  114.1 4.8 %collective-permute-start.17 = (bf16[192,512]{1,0:T(8,128)(2,1)S(1)}, bf16[192,512]{1,0:T(8,128)(2,1)S(1)}, u32[]{:S(2)}, u32[]{:S(2)}) collective-permute-start(bf16[192,512]{1,0:T(8,128)(2,1)S(1)} %fusion.20), channel_id=1, source_target_pairs={{0,16},{1,17},{2,18},{3,19},{4,20},{5,21},{6,22},{7,23},{8,24},{9,... | collective-permute-start | bytes 589832 | tf_op jit(solution)/shard_map/ppermute | solution.py:12
  118.9 5.1 %collective-permute-done.17 = bf16[192,512]{1,0:T(8,128)(2,1)S(1)} collective-permute-done((bf16[192,512]{1,0:T(8,128)(2,1)S(1)}, bf16[192,512]{1,0:T(8,128)(2,1)S(1)}, u32[]{:S(2)}, u32[]{:S(2)}) %collective-permute-start.17) | collective-permute-done | bytes 196640 | tf_op jit(solution)/shard_map/ppermute | solution.py:12
  130.6 6.4 %collective-permute-done.18 = bf16[2,192,512]{2,1,0:T(8,128)(2,1)S(1)} collective-permute-done((bf16[2,192,512]{2,1,0:T(8,128)(2,1)S(1)}, bf16[2,192,512]{2,1,0:T(8,128)(2,1)S(1)}, u32[]{:S(2)}, u32[]{:S(2)}) %collective-permute-start.18) | collective-permute-done | bytes 393248 | tf_op jit(solution)/shard_map/ppermute | solution.py:21
  143.7 5.4 %collective-permute-done.19 = bf16[2,192,512]{2,1,0:T(8,128)(2,1)S(1)} collective-permute-done((bf16[2,192,512]{2,1,0:T(8,128)(2,1)S(1)}, bf16[2,192,512]{2,1,0:T(8,128)(2,1)S(1)}, u32[]{:S(2)}, u32[]{:S(2)}) %collective-permute-start.19) | collective-permute-done | bytes 393248 | tf_op jit(solution)/shard_map/ppermute | solution.py:21
  151.6 4.6 %collective-permute-start.28 = (bf16[2,192,512]{2,1,0:T(8,128)(2,1)S(1)}, bf16[2,192,512]{2,1,0:T(8,128)(2,1)S(1)}, u32[]{:S(2)}, u32[]{:S(2)}) collective-permute-start(bf16[2,192,512]{2,1,0:T(8,128)(2,1)S(1)} %collective-permute-done.27), channel_id=1, source_target_pairs={{0,15},{1,0},{2,1},{3,2},{4,3},{5,4},{6,5},{7,6},{8,7},{9,8},{10,9... | collective-permute-start | bytes 1179656 | tf_op jit(solution)/shard_map/ppermute | solution.py:22
  162.4 4.7 %collective-permute-start.29 = (bf16[2,192,512]{2,1,0:T(8,128)(2,1)S(1)}, bf16[2,192,512]{2,1,0:T(8,128)(2,1)S(1)}, u32[]{:S(2)}, u32[]{:S(2)}) collective-permute-start(bf16[2,192,512]{2,1,0:T(8,128)(2,1)S(1)} %collective-permute-done.28), channel_id=1, source_target_pairs={{0,15},{1,0},{2,1},{3,2},{4,3},{5,4},{6,5},{7,6},{8,7},{9,8},{10,9... | collective-permute-start | bytes 1179656 | tf_op jit(solution)/shard_map/ppermute | solution.py:22
  173.8 4.6 %collective-permute-start.30 = (bf16[2,192,512]{2,1,0:T(8,128)(2,1)S(1)}, bf16[2,192,512]{2,1,0:T(8,128)(2,1)S(1)}, u32[]{:S(2)}, u32[]{:S(2)}) collective-permute-start(bf16[2,192,512]{2,1,0:T(8,128)(2,1)S(1)} %collective-permute-done.29), channel_id=1, source_target_pairs={{0,15},{1,0},{2,1},{3,2},{4,3},{5,4},{6,5},{7,6},{8,7},{9,8},{10,9... | collective-permute-start | bytes 1179656 | tf_op jit(solution)/shard_map/ppermute | solution.py:22
  184.7 4.6 %collective-permute-start.31 = (bf16[2,192,512]{2,1,0:T(8,128)(2,1)S(1)}, bf16[2,192,512]{2,1,0:T(8,128)(2,1)S(1)}, u32[]{:S(2)}, u32[]{:S(2)}) collective-permute-start(bf16[2,192,512]{2,1,0:T(8,128)(2,1)S(1)} %collective-permute-done.30), channel_id=1, source_target_pairs={{0,15},{1,0},{2,1},{3,2},{4,3},{5,4},{6,5},{7,6},{8,7},{9,8},{10,9... | collective-permute-start | bytes 1179656 | tf_op jit(solution)/shard_map/ppermute | solution.py:22
  194.0 5.0 %collective-permute-start.32 = (bf16[2,192,512]{2,1,0:T(8,128)(2,1)S(1)}, bf16[2,192,512]{2,1,0:T(8,128)(2,1)S(1)}, u32[]{:S(2)}, u32[]{:S(2)}) collective-permute-start(bf16[2,192,512]{2,1,0:T(8,128)(2,1)S(1)} %collective-permute-done.31), channel_id=1, source_target_pairs={{0,15},{1,0},{2,1},{3,2},{4,3},{5,4},{6,5},{7,6},{8,7},{9,8},{10,9... | collective-permute-start | bytes 1179656 | tf_op jit(solution)/shard_map/ppermute | solution.py:22
  204.3 5.2 %collective-permute-start.33 = (bf16[192,512]{1,0:T(8,128)(2,1)S(1)}, bf16[192,512]{1,0:T(8,128)(2,1)S(1)}, u32[]{:S(2)}, u32[]{:S(2)}) collective-permute-start(bf16[192,512]{1,0:T(8,128)(2,1)S(1)} %slice_bitcast_fusion), channel_id=1, source_target_pairs={{0,15},{1,0},{2,1},{3,2},{4,3},{5,4},{6,5},{7,6},{8,7},{9,8},{10,9... | collective-permute-start | bytes 589832 | tf_op jit(solution)/shard_map/ppermute | solution.py:26
  223.5 5.6 %gather_fusion.3 = bf16[17,192,512]{2,1,0:T(8,128)(2,1)} fusion(bf16[32,192,512]{2,1,0:T(8,128)(2,1)} %bitcast.46, s32[1024]{0:T(1024)S(1)} %pad_clamp_fusion), kind=kCustom, calls=%fused_computation.1.clone | custom fusion | bytes 6684740 | tf_op jit(solution)/shard_map/jit(_take)/gather | solution.py:124
  235.5 10.7 %collective-permute-start.34 = (f32[17,8,12,192]{3,1,2,0:T(8,128)}, f32[17,8,12,192]{3,1,2,0:T(8,128)}, u32[]{:S(2)}, u32[]{:S(2)}) collective-permute-start(f32[17,8,12,192]{3,1,2,0:T(8,128)} %copy.22), channel_id=1, source_target_pairs={{0,32},{32,0},{64,96},{96,64},{128,160},{160,128},{192,224},{224,1... | collective-permute-start | bytes 3760136 | tf_op jit(solution)/shard_map/ppermute | solution.py:78
  254.4 4.6 %collective-permute-start.35 = (f32[17,2,12,192]{3,1,2,0:T(2,128)S(1)}, f32[17,2,12,192]{3,1,2,0:T(2,128)S(1)}, u32[]{:S(2)}, u32[]{:S(2)}) collective-permute-start(f32[17,2,12,192]{3,1,2,0:T(2,128)S(1)} %get-tuple-element.26), channel_id=1, source_target_pairs={{0,256},{32,288},{64,320},{96,352},{128,384},{160,416},{192,448},{... | collective-permute-start | bytes 940040 | tf_op jit(solution)/shard_map/ppermute | solution.py:82
  268.7 9.6 %collective-permute-done.36 = f32[17,2,12,192]{3,1,2,0:T(2,128)S(1)} collective-permute-done((f32[17,2,12,192]{3,1,2,0:T(2,128)S(1)}, f32[17,2,12,192]{3,1,2,0:T(2,128)S(1)}, u32[]{:S(2)}, u32[]{:S(2)}) %collective-permute-start.36) | collective-permute-done | bytes 313376 | tf_op jit(solution)/shard_map/ppermute | solution.py:82
  283.9 6.5 %collective-permute-done.38 = f32[17,12,192]{2,1,0:T(8,128)S(1)} collective-permute-done((f32[17,12,192]{2,1,0:T(8,128)S(1)}, f32[17,12,192]{2,1,0:T(8,128)S(1)}, u32[]{:S(2)}, u32[]{:S(2)}) %collective-permute-start.38) | collective-permute-done | bytes 156704 | tf_op jit(solution)/shard_map/ppermute | solution.py:89
  (128 shorter events, 142.0 us)
Async XLA Ops:
  8.6 24.0 %collective-permute-start.1 = (bf16[2,192,256]{2,1,0:T(8,128)(2,1)S(1)}, bf16[2,192,256]{2,1,0:T(8,128)(2,1)S(1)}, u32[]{:S(2)}, u32[]{:S(2)}) collective-permute-start(bf16[2,192,256]{2,1,0:T(8,128)(2,1)S(1)} %pad_maximum_fusion.1), channel_id=1, source_target_pairs={{0,1},{1,2},{2,3},{3,4},{4,5},{5,6},{6,7},{7,8},{8,9},{9,10},{10,1... | collective-permute-start | bytes 589832 | tf_op jit(solution)/shard_map/ppermute | solution.py:49
  12.3 24.0 %collective-permute-start.5 = (bf16[2,192,256]{2,1,0:T(8,128)(2,1)S(1)}, bf16[2,192,256]{2,1,0:T(8,128)(2,1)S(1)}, u32[]{:S(2)}, u32[]{:S(2)}) collective-permute-start(bf16[2,192,256]{2,1,0:T(8,128)(2,1)S(1)} %pad_maximum_fusion.1), channel_id=1, source_target_pairs={{0,5},{1,6},{2,7},{3,8},{4,9},{5,10},{6,11},{7,12},{8,13},{9,14},{... | collective-permute-start | bytes 589832 | tf_op jit(solution)/shard_map/ppermute | solution.py:51
  22.5 19.0 %collective-permute-start.9 = (bf16[2,192,256]{2,1,0:T(8,128)(2,1)S(1)}, bf16[2,192,256]{2,1,0:T(8,128)(2,1)S(1)}, u32[]{:S(2)}, u32[]{:S(2)}) collective-permute-start(bf16[2,192,256]{2,1,0:T(8,128)(2,1)S(1)} %pad_maximum_fusion.1), channel_id=1, source_target_pairs={{0,11},{1,12},{2,13},{3,14},{4,15},{5,0},{6,1},{7,2},{8,3},{9,4},{... | collective-permute-start | bytes 589832 | tf_op jit(solution)/shard_map/ppermute | solution.py:56
  27.5 25.7 %collective-permute-start.12 = (bf16[2,192,256]{2,1,0:T(8,128)(2,1)S(1)}, bf16[2,192,256]{2,1,0:T(8,128)(2,1)S(1)}, u32[]{:S(2)}, u32[]{:S(2)}) collective-permute-start(bf16[2,192,256]{2,1,0:T(8,128)(2,1)S(1)} %pad_maximum_fusion.1), channel_id=1, source_target_pairs={{0,15},{1,0},{2,1},{3,2},{4,3},{5,4},{6,5},{7,6},{8,7},{9,8},{10,9... | collective-permute-start | bytes 589832 | tf_op jit(solution)/shard_map/ppermute | solution.py:50
  32.6 25.8 %collective-permute-start.2 = (bf16[2,192,256]{2,1,0:T(8,128)(2,1)S(1)}, bf16[2,192,256]{2,1,0:T(8,128)(2,1)S(1)}, u32[]{:S(2)}, u32[]{:S(2)}) collective-permute-start(bf16[2,192,256]{2,1,0:T(8,128)(2,1)S(1)} %collective-permute-done.1), channel_id=1, source_target_pairs={{0,1},{1,2},{2,3},{3,4},{4,5},{5,6},{6,7},{7,8},{8,9},{9,10},{10,1... | collective-permute-start | bytes 589832 | tf_op jit(solution)/shard_map/ppermute | solution.py:49
  36.3 24.1 %collective-permute-start.6 = (bf16[2,192,256]{2,1,0:T(8,128)(2,1)S(1)}, bf16[2,192,256]{2,1,0:T(8,128)(2,1)S(1)}, u32[]{:S(2)}, u32[]{:S(2)}) collective-permute-start(bf16[2,192,256]{2,1,0:T(8,128)(2,1)S(1)} %collective-permute-done.5), channel_id=1, source_target_pairs={{0,1},{1,2},{2,3},{3,4},{4,5},{5,6},{6,7},{7,8},{8,9},{9,10},{10,1... | collective-permute-start | bytes 589832 | tf_op jit(solution)/shard_map/ppermute | solution.py:51
  41.5 21.4 %collective-permute-start.10 = (bf16[2,192,256]{2,1,0:T(8,128)(2,1)S(1)}, bf16[2,192,256]{2,1,0:T(8,128)(2,1)S(1)}, u32[]{:S(2)}, u32[]{:S(2)}) collective-permute-start(bf16[2,192,256]{2,1,0:T(8,128)(2,1)S(1)} %collective-permute-done.9), channel_id=1, source_target_pairs={{0,15},{1,0},{2,1},{3,2},{4,3},{5,4},{6,5},{7,6},{8,7},{9,8},{10,9... | collective-permute-start | bytes 589832 | tf_op jit(solution)/shard_map/ppermute | solution.py:56
  53.1 13.7 %collective-permute-start.13 = (bf16[2,192,256]{2,1,0:T(8,128)(2,1)S(1)}, bf16[2,192,256]{2,1,0:T(8,128)(2,1)S(1)}, u32[]{:S(2)}, u32[]{:S(2)}) collective-permute-start(bf16[2,192,256]{2,1,0:T(8,128)(2,1)S(1)} %collective-permute-done.12), channel_id=1, source_target_pairs={{0,15},{1,0},{2,1},{3,2},{4,3},{5,4},{6,5},{7,6},{8,7},{9,8},{10,9... | collective-permute-start | bytes 589832 | tf_op jit(solution)/shard_map/ppermute | solution.py:50
  58.4 12.5 %collective-permute-start.3 = (bf16[2,192,256]{2,1,0:T(8,128)(2,1)S(1)}, bf16[2,192,256]{2,1,0:T(8,128)(2,1)S(1)}, u32[]{:S(2)}, u32[]{:S(2)}) collective-permute-start(bf16[2,192,256]{2,1,0:T(8,128)(2,1)S(1)} %collective-permute-done.2), channel_id=1, source_target_pairs={{0,1},{1,2},{2,3},{3,4},{4,5},{5,6},{6,7},{7,8},{8,9},{9,10},{10,1... | collective-permute-start | bytes 589832 | tf_op jit(solution)/shard_map/ppermute | solution.py:49
  60.4 12.5 %collective-permute-start.7 = (bf16[2,192,256]{2,1,0:T(8,128)(2,1)S(1)}, bf16[2,192,256]{2,1,0:T(8,128)(2,1)S(1)}, u32[]{:S(2)}, u32[]{:S(2)}) collective-permute-start(bf16[2,192,256]{2,1,0:T(8,128)(2,1)S(1)} %collective-permute-done.6), channel_id=1, source_target_pairs={{0,1},{1,2},{2,3},{3,4},{4,5},{5,6},{6,7},{7,8},{8,9},{9,10},{10,1... | collective-permute-start | bytes 589832 | tf_op jit(solution)/shard_map/ppermute | solution.py:51
  62.9 21.2 %collective-permute-start.11 = (bf16[2,192,256]{2,1,0:T(8,128)(2,1)S(1)}, bf16[2,192,256]{2,1,0:T(8,128)(2,1)S(1)}, u32[]{:S(2)}, u32[]{:S(2)}) collective-permute-start(bf16[2,192,256]{2,1,0:T(8,128)(2,1)S(1)} %collective-permute-done.10), channel_id=1, source_target_pairs={{0,15},{1,0},{2,1},{3,2},{4,3},{5,4},{6,5},{7,6},{8,7},{9,8},{10,9... | collective-permute-start | bytes 589832 | tf_op jit(solution)/shard_map/ppermute | solution.py:56
  89.0 16.7 %collective-permute-start.16 = (bf16[32,192,256]{2,1,0:T(8,128)(2,1)}, bf16[32,192,256]{2,1,0:T(8,128)(2,1)}, u32[]{:S(2)}, u32[]{:S(2)}) collective-permute-start(bf16[32,192,256]{2,1,0:T(8,128)(2,1)} %bitcast.22), channel_id=1, source_target_pairs={{0,32},{32,0},{64,96},{96,64},{128,160},{160,128},{192,224},{224,1... | collective-permute-start | bytes 9437192 | tf_op jit(solution)/shard_map/ppermute | solution.py:105
  124.0 12.9 %collective-permute-start.18 = (bf16[2,192,512]{2,1,0:T(8,128)(2,1)S(1)}, bf16[2,192,512]{2,1,0:T(8,128)(2,1)S(1)}, u32[]{:S(2)}, u32[]{:S(2)}) collective-permute-start(bf16[2,192,512]{2,1,0:T(8,128)(2,1)S(1)} %pad_maximum_fusion), channel_id=1, source_target_pairs={{0,1},{1,2},{2,3},{3,4},{4,5},{5,6},{6,7},{7,8},{8,9},{9,10},{10,1... | collective-permute-start | bytes 1179656 | tf_op jit(solution)/shard_map/ppermute | solution.py:21
  127.5 12.6 %collective-permute-start.26 = (bf16[2,192,512]{2,1,0:T(8,128)(2,1)S(1)}, bf16[2,192,512]{2,1,0:T(8,128)(2,1)S(1)}, u32[]{:S(2)}, u32[]{:S(2)}) collective-permute-start(bf16[2,192,512]{2,1,0:T(8,128)(2,1)S(1)} %pad_maximum_fusion), channel_id=1, source_target_pairs={{0,15},{1,0},{2,1},{3,2},{4,3},{5,4},{6,5},{7,6},{8,7},{9,8},{10,9... | collective-permute-start | bytes 1179656 | tf_op jit(solution)/shard_map/ppermute | solution.py:22
  137.0 12.1 %collective-permute-start.19 = (bf16[2,192,512]{2,1,0:T(8,128)(2,1)S(1)}, bf16[2,192,512]{2,1,0:T(8,128)(2,1)S(1)}, u32[]{:S(2)}, u32[]{:S(2)}) collective-permute-start(bf16[2,192,512]{2,1,0:T(8,128)(2,1)S(1)} %collective-permute-done.18), channel_id=1, source_target_pairs={{0,1},{1,2},{2,3},{3,4},{4,5},{5,6},{6,7},{7,8},{8,9},{9,10},{10,1... | collective-permute-start | bytes 1179656 | tf_op jit(solution)/shard_map/ppermute | solution.py:21
  140.1 11.5 %collective-permute-start.27 = (bf16[2,192,512]{2,1,0:T(8,128)(2,1)S(1)}, bf16[2,192,512]{2,1,0:T(8,128)(2,1)S(1)}, u32[]{:S(2)}, u32[]{:S(2)}) collective-permute-start(bf16[2,192,512]{2,1,0:T(8,128)(2,1)S(1)} %collective-permute-done.26), channel_id=1, source_target_pairs={{0,15},{1,0},{2,1},{3,2},{4,3},{5,4},{6,5},{7,6},{8,7},{9,8},{10,9... | collective-permute-start | bytes 1179656 | tf_op jit(solution)/shard_map/ppermute | solution.py:22
  149.1 11.3 %collective-permute-start.20 = (bf16[2,192,512]{2,1,0:T(8,128)(2,1)S(1)}, bf16[2,192,512]{2,1,0:T(8,128)(2,1)}, u32[]{:S(2)}, u32[]{:S(2)}) collective-permute-start(bf16[2,192,512]{2,1,0:T(8,128)(2,1)S(1)} %collective-permute-done.19), channel_id=1, source_target_pairs={{0,1},{1,2},{2,3},{3,4},{4,5},{5,6},{6,7},{7,8},{8,9},{9,10},{10,1... | collective-permute-start | bytes 1179656 | tf_op jit(solution)/shard_map/ppermute | solution.py:21
  151.6 10.8 %collective-permute-start.28 = (bf16[2,192,512]{2,1,0:T(8,128)(2,1)S(1)}, bf16[2,192,512]{2,1,0:T(8,128)(2,1)S(1)}, u32[]{:S(2)}, u32[]{:S(2)}) collective-permute-start(bf16[2,192,512]{2,1,0:T(8,128)(2,1)S(1)} %collective-permute-done.27), channel_id=1, source_target_pairs={{0,15},{1,0},{2,1},{3,2},{4,3},{5,4},{6,5},{7,6},{8,7},{9,8},{10,9... | collective-permute-start | bytes 1179656 | tf_op jit(solution)/shard_map/ppermute | solution.py:22
  162.4 11.4 %collective-permute-start.29 = (bf16[2,192,512]{2,1,0:T(8,128)(2,1)S(1)}, bf16[2,192,512]{2,1,0:T(8,128)(2,1)S(1)}, u32[]{:S(2)}, u32[]{:S(2)}) collective-permute-start(bf16[2,192,512]{2,1,0:T(8,128)(2,1)S(1)} %collective-permute-done.28), channel_id=1, source_target_pairs={{0,15},{1,0},{2,1},{3,2},{4,3},{5,4},{6,5},{7,6},{8,7},{9,8},{10,9... | collective-permute-start | bytes 1179656 | tf_op jit(solution)/shard_map/ppermute | solution.py:22
  173.8 10.9 %collective-permute-start.30 = (bf16[2,192,512]{2,1,0:T(8,128)(2,1)S(1)}, bf16[2,192,512]{2,1,0:T(8,128)(2,1)S(1)}, u32[]{:S(2)}, u32[]{:S(2)}) collective-permute-start(bf16[2,192,512]{2,1,0:T(8,128)(2,1)S(1)} %collective-permute-done.29), channel_id=1, source_target_pairs={{0,15},{1,0},{2,1},{3,2},{4,3},{5,4},{6,5},{7,6},{8,7},{9,8},{10,9... | collective-permute-start | bytes 1179656 | tf_op jit(solution)/shard_map/ppermute | solution.py:22
  235.5 14.2 %collective-permute-start.34 = (f32[17,8,12,192]{3,1,2,0:T(8,128)}, f32[17,8,12,192]{3,1,2,0:T(8,128)}, u32[]{:S(2)}, u32[]{:S(2)}) collective-permute-start(f32[17,8,12,192]{3,1,2,0:T(8,128)} %copy.22), channel_id=1, source_target_pairs={{0,32},{32,0},{64,96},{96,64},{128,160},{160,128},{192,224},{224,1... | collective-permute-start | bytes 3760136 | tf_op jit(solution)/shard_map/ppermute | solution.py:78
  254.4 14.3 %collective-permute-start.35 = (f32[17,2,12,192]{3,1,2,0:T(2,128)S(1)}, f32[17,2,12,192]{3,1,2,0:T(2,128)S(1)}, u32[]{:S(2)}, u32[]{:S(2)}) collective-permute-start(f32[17,2,12,192]{3,1,2,0:T(2,128)S(1)} %get-tuple-element.26), channel_id=1, source_target_pairs={{0,256},{32,288},{64,320},{96,352},{128,384},{160,416},{192,448},{... | collective-permute-start | bytes 940040 | tf_op jit(solution)/shard_map/ppermute | solution.py:82
  259.0 19.3 %collective-permute-start.36 = (f32[17,2,12,192]{3,1,2,0:T(2,128)S(1)}, f32[17,2,12,192]{3,1,2,0:T(2,128)S(1)}, u32[]{:S(2)}, u32[]{:S(2)}) collective-permute-start(f32[17,2,12,192]{3,1,2,0:T(2,128)S(1)} %get-tuple-element.28), channel_id=1, source_target_pairs={{0,128},{32,160},{64,192},{96,224},{128,256},{160,288},{192,320},{... | collective-permute-start | bytes 940040 | tf_op jit(solution)/shard_map/ppermute | solution.py:82
  261.2 17.1 %collective-permute-start.37 = (f32[17,2,12,192]{3,1,2,0:T(2,128)S(1)}, f32[17,2,12,192]{3,1,2,0:T(2,128)S(1)}, u32[]{:S(2)}, u32[]{:S(2)}) collective-permute-start(f32[17,2,12,192]{3,1,2,0:T(2,128)S(1)} %get-tuple-element.27), channel_id=1, source_target_pairs={{0,384},{32,416},{64,448},{96,480},{128,0},{160,32},{192,64},{224,... | collective-permute-start | bytes 940040 | tf_op jit(solution)/shard_map/ppermute | solution.py:82
  (20 other events, 317.4 us)
